TPU v7x, 512 devices: a whole 4x4x16 slice. The times are simulated.
512 devices in a mesh: cluster: 128 (over z, y, x_lo), feat: 4 (over x_hi, core).
Axes of the slice: x: 4 (x_hi: 2, x_lo: 2; x = x_hi * 2 + x_lo), y: 4, z: 16, core: 2. Of those that a mesh axis runs over, the one named last changes fastest.
Arguments:
- queries: bfloat16 [32768, 1024], P('cluster', 'feat'), may hold values from -6 to 6
- assign: int32 [32768, 1], P('cluster'), may hold values from 0 to 127, as said below
- band_mask: int32 [128, 7], replicated, may hold values from 0 to 1, as said below
- keys: bfloat16 [65536, 1024], P(('cluster', 'feat')), may hold values from -6 to 6
- labels: bfloat16 [65536, 1000], P(('cluster', 'feat')), may hold values from -24 to 24
- prior: bfloat16 [65536], P(('cluster', 'feat')), may hold values from -2 to 506
Outputs:
- propagated: bfloat16 [32768, 1000], P('cluster', 'feat')
Inputs may be any that keep to these rules, and one draw needn't show every extreme that they name: `assign`: in each aligned block of 256 rows at most 4 rows name one cluster. `band_mask`: entry 3 of every row is 1.
All inputs are finite; a program needn't handle non-finite values.
Results may differ from a plain program's by a relative error of at most 0.014.
Values may be sent and summed in bfloat16 or wider, within the bound.
No kernel may reach another device: no remote copies, remote signals or barrier semaphores. Data moves between devices by JAX's collectives and lax.ppermute only.
A program may use at most 64 MiB of HBM per device.

v0:
```python
import math

import jax
import jax.numpy as jnp
from jax import lax
from jax.sharding import PartitionSpec as P

REACH = 3


temper = 2.0


def from_behind(array, axis, by):
    peers = lax.axis_size(axis)
    return lax.ppermute(array, axis, [(i, (i + by) % peers) for i in range(peers)])


def combined_all(part, axis, combine):
    gathered = jax.tree.map(lambda a: lax.all_gather(a, axis), part)

    def take(source):
        return jax.tree.map(lambda a: lax.dynamic_index_in_dim(a, source, 0, False), gathered)

    return lax.fori_loop(
        1, lax.axis_size(axis), lambda source, state: combine(state, take(source)), take(0)
    )


def combine_totals(first, second):
    top_first, sum_first = first
    top_second, sum_second = second
    highest = jnp.maximum(top_first, top_second)
    return (
        highest,
        sum_first * jnp.exp(top_first - highest) + sum_second * jnp.exp(top_second - highest),
    )


def absorb(state, block, query_full, enabled):
    running, total, accum = state
    block_keys, block_labels, block_prior = block
    scale = temper / math.sqrt(query_full.shape[1])
    scores = (
        jnp.einsum("qd,kd->qk", query_full, block_keys, preferred_element_type=jnp.float32) * scale
    )
    scores = scores + block_prior.astype(jnp.float32)[None, :]
    scores = jnp.where(enabled, scores, jnp.float32(-1e30))
    highest = jnp.maximum(running, jnp.max(scores, axis=1))
    carried = jnp.exp(running - highest)
    weight = jnp.exp(scores - highest[:, None])
    total = total * carried + jnp.sum(weight, axis=1)
    accum = accum * carried[:, None] + jnp.dot(
        weight.astype(jnp.bfloat16), block_labels, preferred_element_type=jnp.float32
    )
    return (highest, total, accum)


def body(queries, assign, band_mask, keys, labels, prior):
    clusters = lax.axis_size("cluster")
    cluster_index = lax.axis_index("cluster")
    local_rows = queries.shape[0]
    capacity = 2 * local_rows // clusters
    slots = clusters * capacity
    target = assign[:, 0]
    onehot = (target[:, None] == jnp.arange(clusters, dtype=jnp.int32)[None, :]).astype(jnp.int32)
    before = jnp.cumsum(onehot, axis=0) - onehot
    position = target * capacity + jnp.sum(before * onehot, axis=1)
    outgoing = jnp.zeros((slots, queries.shape[1]), queries.dtype).at[position].set(queries)
    arrived = lax.all_to_all(
        outgoing.reshape(clusters, capacity, queries.shape[1]),
        "cluster",
        split_axis=0,
        concat_axis=0,
        tiled=True,
    )
    query_full = lax.all_gather(
        arrived.reshape(slots, queries.shape[1]), "feat", axis=1, tiled=True
    )
    mask_row = band_mask[cluster_index]
    classes = labels.shape[1]
    state = (
        jnp.full((slots,), -1e30, jnp.float32),
        jnp.zeros((slots,), jnp.float32),
        jnp.zeros((slots, classes), jnp.float32),
    )
    state = absorb(state, (keys, labels, prior), query_full, jnp.bool_(True))

    def visit(current, block, offset):
        enabled = mask_row[REACH + offset] > 0
        return absorb(current, block, query_full, enabled)

    up_keys, up_labels, up_prior = (keys, labels, prior)
    down_keys, down_labels, down_prior = (keys, labels, prior)
    for reach in range(1, REACH + 1):
        up_keys, up_labels, up_prior = from_behind((up_keys, up_labels, up_prior), "cluster", -1)
        state = visit(state, (up_keys, up_labels, up_prior), reach)
        down_keys, down_labels, down_prior = from_behind(
            (down_keys, down_labels, down_prior), "cluster", 1
        )
        state = visit(state, (down_keys, down_labels, down_prior), -reach)
    running, total, accum = state
    highest, grand_total = combined_all((running, total), "feat", combine_totals)
    factor = jnp.exp(running - highest) / grand_total
    shares = lax.psum_scatter(
        (accum * factor[:, None]).astype(jnp.bfloat16), "feat", scatter_dimension=1, tiled=True
    )
    returned = lax.all_to_all(
        shares.reshape(clusters, capacity, shares.shape[1]),
        "cluster",
        split_axis=0,
        concat_axis=0,
        tiled=True,
    )
    return returned.reshape(slots, shares.shape[1])[position]


def solution(mesh):
    in_specs = (
        P("cluster", "feat"),
        P("cluster", None),
        P(),
        P(("cluster", "feat"), None),
        P(("cluster", "feat"), None),
        P(("cluster", "feat")),
    )
    out_specs = P("cluster", "feat")
    return jax.shard_map(body, mesh=mesh, in_specs=in_specs, out_specs=out_specs, check_vma=False)
```

profile of v0, /device:TPU:32, one launch (start us, length us, event | category | flops | bytes accessed | tf_op | source)
XLA Modules:
  0.0 298.2 jit_solution(2191758470256113544)
XLA Ops:
  6.6 0.8 copy.10
  7.4 0.2 fusion.43
  7.7 0.9 fusion.45
  8.6 0.7 compare_select_fusion
  9.3 1.9 scatter_custom_fusion
  11.2 0.1 reshape.386
  11.3 43.1 %all_to_all.10 = bf16[128,4,256]{2,1,0:T(4,128)(2,1)S(1)} all-to-all(bf16[128,4,256]{2,1,0:T(4,128)(2,1)S(1)} %reshape.386), channel_id=1, replica_groups=mesh['cluster'=128,'feat'=4] {'cluster'}, dimensions={0} | all-to-all | bytes 524288 | tf_op jit(solution)/shard_map/all_to_all | solution.py:70
  54.3 0.8 reshape.387
  55.2 3.4 %collective-permute-start = (bf16[128,1024]{1,0:T(8,128)(2,1)S(1)}, bf16[128,1024]{1,0:T(8,128)(2,1)S(1)}, u32[]{:S(2)}, u32[]{:S(2)}) collective-permute-start(bf16[128,1024]{1,0:T(8,128)(2,1)S(1)} %copy-done.3), channel_id=1, source_target_pairs={{0,508},{4,0},{8,4},{12,8},{16,12},{20,16},{24,20},{28,24},{32,28}... | collective-permute-start | bytes 786440 | tf_op jit(solution)/shard_map/ppermute | solution.py:16
  58.5 2.5 collective-permute-start.3
  61.0 6.4 %collective-permute-start.2 = (bf16[128,1000]{0,1:T(8,128)(2,1)S(1)}, bf16[128,1000]{0,1:T(8,128)(2,1)S(1)}, u32[]{:S(2)}, u32[]{:S(2)}) collective-permute-start(bf16[128,1000]{0,1:T(8,128)(2,1)S(1)} %copy-done.4), channel_id=1, source_target_pairs={{0,508},{4,0},{8,4},{12,8},{16,12},{20,16},{24,20},{28,24},{32,28}... | collective-permute-start | bytes 768008 | tf_op jit(solution)/shard_map/ppermute | solution.py:16
  67.4 1.9 collective-permute-start.5
  69.4 8.8 %collective-permute-start.6 = (bf16[128,1024]{1,0:T(8,128)(2,1)S(1)}, bf16[128,1024]{1,0:T(8,128)(2,1)S(1)}, u32[]{:S(2)}, u32[]{:S(2)}) collective-permute-start(bf16[128,1024]{1,0:T(8,128)(2,1)S(1)} %collective-permute-done), channel_id=1, source_target_pairs={{0,508},{4,0},{8,4},{12,8},{16,12},{20,16},{24,20},{28,24},{32,28}... | collective-permute-start | bytes 786440 | tf_op jit(solution)/shard_map/ppermute | solution.py:16
  78.1 6.5 %collective-permute-done.3 = bf16[128,1024]{1,0:T(8,128)(2,1)S(1)} collective-permute-done((bf16[128,1024]{1,0:T(8,128)(2,1)S(1)}, bf16[128,1024]{1,0:T(8,128)(2,1)S(1)}, u32[]{:S(2)}, u32[]{:S(2)}) %collective-permute-start.3) | collective-permute-done | bytes 262176 | tf_op jit(solution)/shard_map/ppermute | solution.py:16
  84.6 4.4 %collective-permute-start.9 = (bf16[128,1024]{1,0:T(8,128)(2,1)S(1)}, bf16[128,1024]{1,0:T(8,128)(2,1)S(1)}, u32[]{:S(2)}, u32[]{:S(2)}) collective-permute-start(bf16[128,1024]{1,0:T(8,128)(2,1)S(1)} %collective-permute-done.3), channel_id=1, source_target_pairs={{0,4},{4,8},{8,12},{12,16},{16,20},{20,24},{24,28},{28,32},{32,36}... | collective-permute-start | bytes 786440 | tf_op jit(solution)/shard_map/ppermute | solution.py:16
  89.0 6.3 %collective-permute-start.8 = (bf16[128,1000]{0,1:T(8,128)(2,1)S(1)}, bf16[128,1000]{0,1:T(8,128)(2,1)}, u32[]{:S(2)}, u32[]{:S(2)}) collective-permute-start(bf16[128,1000]{0,1:T(8,128)(2,1)S(1)} %collective-permute-done.2), channel_id=1, source_target_pairs={{0,508},{4,0},{8,4},{12,8},{16,12},{20,16},{24,20},{28,24},{32,28}... | collective-permute-start | bytes 768008 | tf_op jit(solution)/shard_map/ppermute | solution.py:16
  95.4 1.9 collective-permute-start.11
  97.3 6.9 %collective-permute-start.1 = (bf16[128]{0:T(256)(128)(2,1)S(1)}, bf16[128]{0:T(256)(128)(2,1)S(1)}, u32[]{:S(2)}, u32[]{:S(2)}) collective-permute-start(bf16[128]{0:T(256)(128)(2,1)S(1)} %copy-done.10), channel_id=1, source_target_pairs={{0,508},{4,0},{8,4},{12,8},{16,12},{20,16},{24,20},{28,24},{32,28}... | collective-permute-start | bytes 776 | tf_op jit(solution)/shard_map/ppermute | solution.py:16
  104.2 3.7 %collective-permute-done.1 = bf16[128]{0:T(256)(128)(2,1)S(1)} collective-permute-done((bf16[128]{0:T(256)(128)(2,1)S(1)}, bf16[128]{0:T(256)(128)(2,1)S(1)}, u32[]{:S(2)}, u32[]{:S(2)}) %collective-permute-start.1) | collective-permute-done | bytes 288 | tf_op jit(solution)/shard_map/ppermute | solution.py:16
  108.0 3.0 collective-permute-start.4
  110.9 0.1 constant_dynamic-slice_fusion.3
  111.0 5.4 %collective-permute-done.4 = bf16[128]{0:T(256)(128)(2,1)S(1)} collective-permute-done((bf16[128]{0:T(256)(128)(2,1)S(1)}, bf16[128]{0:T(256)(128)(2,1)S(1)}, u32[]{:S(2)}, u32[]{:S(2)}) %collective-permute-start.4) | collective-permute-done | bytes 288 | tf_op jit(solution)/shard_map/ppermute | solution.py:16
  116.4 1.9 collective-permute-start.7
  118.3 0.6 fusion.59
  118.9 2.9 collective-permute-done.7
  121.8 1.9 collective-permute-start.10
  125.6 4.6 %collective-permute-done.10 = bf16[128]{0:T(256)(128)(2,1)S(1)} collective-permute-done((bf16[128]{0:T(256)(128)(2,1)S(1)}, bf16[128]{0:T(256)(128)(2,1)S(1)}, u32[]{:S(2)}, u32[]{:S(2)}) %collective-permute-start.10) | collective-permute-done | bytes 288 | tf_op jit(solution)/shard_map/ppermute | solution.py:16
  130.2 2.3 collective-permute-start.13
  134.5 1.2 collective-permute-done.13
  135.7 2.3 collective-permute-start.16
  138.1 6.0 %collective-permute-done.16 = bf16[128]{0:T(256)(128)(2,1)S(1)} collective-permute-done((bf16[128]{0:T(256)(128)(2,1)S(1)}, bf16[128]{0:T(256)(128)(2,1)S(1)}, u32[]{:S(2)}, u32[]{:S(2)}) %collective-permute-start.16) | collective-permute-done | bytes 288 | tf_op jit(solution)/shard_map/ppermute | solution.py:16
  144.1 2.3 collective-permute-start.14
  146.4 3.5 %collective-permute-start.17 = (bf16[128,1000]{0,1:T(8,128)(2,1)}, bf16[128,1000]{0,1:T(8,128)(2,1)}, u32[]{:S(2)}, u32[]{:S(2)}) collective-permute-start(bf16[128,1000]{0,1:T(8,128)(2,1)} %collective-permute-done.11), channel_id=1, source_target_pairs={{0,4},{4,8},{8,12},{12,16},{16,20},{20,24},{24,28},{28,32},{32,36}... | collective-permute-start | bytes 768008 | tf_op jit(solution)/shard_map/ppermute | solution.py:16
  150.0 5.3 %collective-permute-start.12 = (bf16[128,1024]{1,0:T(8,128)(2,1)S(1)}, bf16[128,1024]{1,0:T(8,128)(2,1)S(1)}, u32[]{:S(2)}, u32[]{:S(2)}) collective-permute-start(bf16[128,1024]{1,0:T(8,128)(2,1)S(1)} %collective-permute-done.6), channel_id=1, source_target_pairs={{0,508},{4,0},{8,4},{12,8},{16,12},{20,16},{24,20},{28,24},{32,28}... | collective-permute-start | bytes 786440 | tf_op jit(solution)/shard_map/ppermute | solution.py:16
  155.3 1.9 collective-permute-start.15
  157.3 1.8 fusion.60
  159.1 1.7 fusion.61
  160.9 0.5 fusion.62
  161.4 0.5 fusion.63
  161.9 0.5 fusion.64
  162.5 0.5 fusion.65
  163.0 3.6 %collective-permute-done.15 = bf16[128,1024]{1,0:T(8,128)(2,1)S(1)} collective-permute-done((bf16[128,1024]{1,0:T(8,128)(2,1)S(1)}, bf16[128,1024]{1,0:T(8,128)(2,1)S(1)}, u32[]{:S(2)}, u32[]{:S(2)}) %collective-permute-start.15) | collective-permute-done | bytes 262176 | tf_op jit(solution)/shard_map/ppermute | solution.py:16
  166.6 0.5 fusion.66
  167.1 0.1 fusion.23
  167.2 0.1 fusion.21
  167.4 0.1 fusion.13
  167.6 6.7 %all-gather = f32[4,1,512]{2,1,0:T(1,128)S(1)} all-gather(f32[1,1,512]{2,1,0:T(1,128)S(1)} %get-tuple-element.167), channel_id=1, replica_groups=mesh['cluster'=128,'feat'=4] {'feat'}, dimensions={0}, use_global_device_ids=true | all-gather | bytes 10240 | tf_op jit(solution)/shard_map/all_gather | solution.py:20
  174.3 6.8 %all-gather.1 = f32[4,1,512]{2,1,0:T(1,128)S(1)} all-gather(f32[1,1,512]{2,1,0:T(1,128)S(1)} %get-tuple-element.166), channel_id=1, replica_groups=mesh['cluster'=128,'feat'=4] {'feat'}, dimensions={0}, use_global_device_ids=true | all-gather | bytes 10240 | tf_op jit(solution)/shard_map/all_gather | solution.py:20
  181.1 0.5 fusion.41
  181.6 0.2 while.17
  181.8 1.5 fusion.33
  183.3 1.5 fusion.35
  184.8 0.5 fusion.37
  185.3 0.5 fusion.39
  185.8 1.4 fusion.31
  187.3 3.5 %multiply_convert_fusion = bf16[512,1000]{1,0:T(8,128)(2,1)} fusion(f32[512,1000]{1,0:T(8,128)S(1)} %fusion.31, f32[512,1000]{1,0:T(8,128)S(1)} %fusion.33, f32[512,1000]{1,0:T(8,128)S(1)} %fusion.35, f32[512,1000]{1,0:T(8,128)S(1)} %fusion.37, f32[512,1000]{1,0:T(8,128)S(1)} %fusion.39, f32[512,1000]{1,0:T(8,128)S(1)} %fusion.41, ...), kind=kOutput, calls=%fused_computation.5 | convolution fusion | flops 138883072 | bytes 13848576 | tf_op jit(solution)/shard_map/dot_general | solution.py:53
  190.8 1.3 dynamic-slice
  192.7 54.7 %all-reduce.3.cloned.1.call-done = bf16[512,1000]{1,0:T(8,128)(2,1)} async-done(((bf16[512,1000]{1,0:T(8,128)(2,1)}), bf16[512,1000]{1,0:T(8,128)(2,1)}) %all-reduce.3.cloned.1.call-update) | async-done | bytes 1024016
  247.4 1.1 constant_dynamic-slice_fusion.2
  248.5 0.8 reshape.388
  249.3 16.5 %all-to-all-start.1 = ((bf16[128,4,250]{2,1,0:T(4,128)(2,1)}), bf16[128,4,250]{2,1,0:T(4,128)(2,1)S(1)}, u32[]{:S(2)}, u32[]{:S(2)}) async-start(bf16[128,4,250]{2,1,0:T(4,128)(2,1)} %reshape.388), calls=%async_computation.1 | async-start | bytes 524288 | tf_op jit(solution)/shard_map/all_to_all | solution.py:108
  265.8 23.7 %all-to-all-done.1 = bf16[128,4,250]{2,1,0:T(4,128)(2,1)S(1)} async-done(((bf16[128,4,250]{2,1,0:T(4,128)(2,1)}), bf16[128,4,250]{2,1,0:T(4,128)(2,1)S(1)}, u32[]{:S(2)}, u32[]{:S(2)}) %all-to-all-start.1) | async-done | bytes 256032 | tf_op jit(solution)/shard_map/all_to_all | solution.py:108
  289.4 0.2 reshape.389
  289.6 1.8 gather_fusion
  (72 shorter events, 0.7 us)
Async XLA Ops:
  6.5 104.4 %copy-start = (s32[128,7]{0,1:T(8,128)S(1)}, s32[128,7]{0,1:T(8,128)}, u32[]{:S(2)}) copy-start(s32[128,7]{0,1:T(8,128)} %param.10) | copy-start | bytes 10756
  6.5 48.6 %copy-start.3 = (bf16[128,1024]{1,0:T(8,128)(2,1)S(1)}, bf16[128,1024]{1,0:T(8,128)(2,1)}, u32[]{:S(2)}) copy-start(bf16[128,1024]{1,0:T(8,128)(2,1)} %param.11) | copy-start | bytes 786436
  6.5 54.5 %copy-start.4 = (bf16[128,1000]{0,1:T(8,128)(2,1)S(1)}, bf16[128,1000]{0,1:T(8,128)(2,1)}, u32[]{:S(2)}) copy-start(bf16[128,1000]{0,1:T(8,128)(2,1)} %param.12) | copy-start | bytes 768004
  6.5 90.8 %copy-start.10 = (bf16[128]{0:T(256)(128)(2,1)S(1)}, bf16[128]{0:T(256)(128)(2,1)}, u32[]{:S(2)}) copy-start(bf16[128]{0:T(256)(128)(2,1)} %param.13) | copy-start | bytes 772
  6.5 150.7 %all-gather.4.cloned.1.call-start = ((), (), s32[]{:S(2)}) async-start(), calls=%async_computation.2 | async-start | bytes 1310720 | tf_op jit(solution)/shard_map/all_gather | solution.py:77
  55.1 192.3 %all-reduce.3.cloned.1.call-start = ((), (), s32[]{:S(2)}) async-start(), calls=%async_computation.3 | async-start | bytes 2097152
  55.2 14.2 %collective-permute-start = (bf16[128,1024]{1,0:T(8,128)(2,1)S(1)}, bf16[128,1024]{1,0:T(8,128)(2,1)S(1)}, u32[]{:S(2)}, u32[]{:S(2)}) collective-permute-start(bf16[128,1024]{1,0:T(8,128)(2,1)S(1)} %copy-done.3), channel_id=1, source_target_pairs={{0,508},{4,0},{8,4},{12,8},{16,12},{20,16},{24,20},{28,24},{32,28}... | collective-permute-start | bytes 786440 | tf_op jit(solution)/shard_map/ppermute | solution.py:16
  58.5 26.1 %collective-permute-start.3 = (bf16[128,1024]{1,0:T(8,128)(2,1)S(1)}, bf16[128,1024]{1,0:T(8,128)(2,1)S(1)}, u32[]{:S(2)}, u32[]{:S(2)}) collective-permute-start(bf16[128,1024]{1,0:T(8,128)(2,1)S(1)} %copy-done.3), channel_id=1, source_target_pairs={{0,4},{4,8},{8,12},{12,16},{16,20},{20,24},{24,28},{28,32},{32,36}... | collective-permute-start | bytes 786440 | tf_op jit(solution)/shard_map/ppermute | solution.py:16
  61.0 28.0 %collective-permute-start.2 = (bf16[128,1000]{0,1:T(8,128)(2,1)S(1)}, bf16[128,1000]{0,1:T(8,128)(2,1)S(1)}, u32[]{:S(2)}, u32[]{:S(2)}) collective-permute-start(bf16[128,1000]{0,1:T(8,128)(2,1)S(1)} %copy-done.4), channel_id=1, source_target_pairs={{0,508},{4,0},{8,4},{12,8},{16,12},{20,16},{24,20},{28,24},{32,28}... | collective-permute-start | bytes 768008 | tf_op jit(solution)/shard_map/ppermute | solution.py:16
  67.4 27.9 %collective-permute-start.5 = (bf16[128,1000]{0,1:T(8,128)(2,1)S(1)}, bf16[128,1000]{0,1:T(8,128)(2,1)S(1)}, u32[]{:S(2)}, u32[]{:S(2)}) collective-permute-start(bf16[128,1000]{0,1:T(8,128)(2,1)S(1)} %copy-done.4), channel_id=1, source_target_pairs={{0,4},{4,8},{8,12},{12,16},{16,20},{20,24},{24,28},{28,32},{32,36}... | collective-permute-start | bytes 768008 | tf_op jit(solution)/shard_map/ppermute | solution.py:16
  69.4 80.6 %collective-permute-start.6 = (bf16[128,1024]{1,0:T(8,128)(2,1)S(1)}, bf16[128,1024]{1,0:T(8,128)(2,1)S(1)}, u32[]{:S(2)}, u32[]{:S(2)}) collective-permute-start(bf16[128,1024]{1,0:T(8,128)(2,1)S(1)} %collective-permute-done), channel_id=1, source_target_pairs={{0,508},{4,0},{8,4},{12,8},{16,12},{20,16},{24,20},{28,24},{32,28}... | collective-permute-start | bytes 786440 | tf_op jit(solution)/shard_map/ppermute | solution.py:16
  84.6 70.7 %collective-permute-start.9 = (bf16[128,1024]{1,0:T(8,128)(2,1)S(1)}, bf16[128,1024]{1,0:T(8,128)(2,1)S(1)}, u32[]{:S(2)}, u32[]{:S(2)}) collective-permute-start(bf16[128,1024]{1,0:T(8,128)(2,1)S(1)} %collective-permute-done.3), channel_id=1, source_target_pairs={{0,4},{4,8},{8,12},{12,16},{16,20},{20,24},{24,28},{28,32},{32,36}... | collective-permute-start | bytes 786440 | tf_op jit(solution)/shard_map/ppermute | solution.py:16
  89.0 70.1 %copy-start.6 = (bf16[128,1000]{0,1:T(8,128)(2,1)}, bf16[128,1000]{0,1:T(8,128)(2,1)S(1)}, u32[]{:S(2)}) copy-start(bf16[128,1000]{0,1:T(8,128)(2,1)S(1)} %collective-permute-done.2) | copy-start | bytes 768004
  89.0 55.1 %collective-permute-start.8 = (bf16[128,1000]{0,1:T(8,128)(2,1)S(1)}, bf16[128,1000]{0,1:T(8,128)(2,1)}, u32[]{:S(2)}, u32[]{:S(2)}) collective-permute-start(bf16[128,1000]{0,1:T(8,128)(2,1)S(1)} %collective-permute-done.2), channel_id=1, source_target_pairs={{0,508},{4,0},{8,4},{12,8},{16,12},{20,16},{24,20},{28,24},{32,28}... | collective-permute-start | bytes 768008 | tf_op jit(solution)/shard_map/ppermute | solution.py:16
  95.4 63.8 %copy-start.8 = (bf16[128,1000]{0,1:T(8,128)(2,1)}, bf16[128,1000]{0,1:T(8,128)(2,1)S(1)}, u32[]{:S(2)}) copy-start(bf16[128,1000]{0,1:T(8,128)(2,1)S(1)} %collective-permute-done.5) | copy-start | bytes 768004
  95.4 51.1 %collective-permute-start.11 = (bf16[128,1000]{0,1:T(8,128)(2,1)S(1)}, bf16[128,1000]{0,1:T(8,128)(2,1)}, u32[]{:S(2)}, u32[]{:S(2)}) collective-permute-start(bf16[128,1000]{0,1:T(8,128)(2,1)S(1)} %collective-permute-done.5), channel_id=1, source_target_pairs={{0,4},{4,8},{8,12},{12,16},{16,20},{20,24},{24,28},{28,32},{32,36}... | collective-permute-start | bytes 768008 | tf_op jit(solution)/shard_map/ppermute | solution.py:16
  97.3 10.6 %collective-permute-start.1 = (bf16[128]{0:T(256)(128)(2,1)S(1)}, bf16[128]{0:T(256)(128)(2,1)S(1)}, u32[]{:S(2)}, u32[]{:S(2)}) collective-permute-start(bf16[128]{0:T(256)(128)(2,1)S(1)} %copy-done.10), channel_id=1, source_target_pairs={{0,508},{4,0},{8,4},{12,8},{16,12},{20,16},{24,20},{28,24},{32,28}... | collective-permute-start | bytes 776 | tf_op jit(solution)/shard_map/ppermute | solution.py:16
  108.0 8.4 %collective-permute-start.4 = (bf16[128]{0:T(256)(128)(2,1)S(1)}, bf16[128]{0:T(256)(128)(2,1)S(1)}, u32[]{:S(2)}, u32[]{:S(2)}) collective-permute-start(bf16[128]{0:T(256)(128)(2,1)S(1)} %copy-done.10), channel_id=1, source_target_pairs={{0,4},{4,8},{8,12},{12,16},{16,20},{20,24},{24,28},{28,32},{32,36}... | collective-permute-start | bytes 776 | tf_op jit(solution)/shard_map/ppermute | solution.py:16
  116.4 5.4 %collective-permute-start.7 = (bf16[128]{0:T(256)(128)(2,1)S(1)}, bf16[128]{0:T(256)(128)(2,1)S(1)}, u32[]{:S(2)}, u32[]{:S(2)}) collective-permute-start(bf16[128]{0:T(256)(128)(2,1)S(1)} %collective-permute-done.1), channel_id=1, source_target_pairs={{0,508},{4,0},{8,4},{12,8},{16,12},{20,16},{24,20},{28,24},{32,28}... | collective-permute-start | bytes 776 | tf_op jit(solution)/shard_map/ppermute | solution.py:16
  121.8 8.4 %collective-permute-start.10 = (bf16[128]{0:T(256)(128)(2,1)S(1)}, bf16[128]{0:T(256)(128)(2,1)S(1)}, u32[]{:S(2)}, u32[]{:S(2)}) collective-permute-start(bf16[128]{0:T(256)(128)(2,1)S(1)} %collective-permute-done.4), channel_id=1, source_target_pairs={{0,4},{4,8},{8,12},{12,16},{16,20},{20,24},{24,28},{28,32},{32,36}... | collective-permute-start | bytes 776 | tf_op jit(solution)/shard_map/ppermute | solution.py:16
  130.2 5.4 %collective-permute-start.13 = (bf16[128]{0:T(256)(128)(2,1)S(1)}, bf16[128]{0:T(256)(128)(2,1)S(1)}, u32[]{:S(2)}, u32[]{:S(2)}) collective-permute-start(bf16[128]{0:T(256)(128)(2,1)S(1)} %collective-permute-done.7), channel_id=1, source_target_pairs={{0,508},{4,0},{8,4},{12,8},{16,12},{20,16},{24,20},{28,24},{32,28}... | collective-permute-start | bytes 776 | tf_op jit(solution)/shard_map/ppermute | solution.py:16
  135.7 8.4 %collective-permute-start.16 = (bf16[128]{0:T(256)(128)(2,1)S(1)}, bf16[128]{0:T(256)(128)(2,1)S(1)}, u32[]{:S(2)}, u32[]{:S(2)}) collective-permute-start(bf16[128]{0:T(256)(128)(2,1)S(1)} %collective-permute-done.10), channel_id=1, source_target_pairs={{0,4},{4,8},{8,12},{12,16},{16,20},{20,24},{24,28},{28,32},{32,36}... | collective-permute-start | bytes 776 | tf_op jit(solution)/shard_map/ppermute | solution.py:16
  144.1 41.7 %collective-permute-start.14 = (bf16[128,1000]{0,1:T(8,128)(2,1)}, bf16[128,1000]{0,1:T(8,128)(2,1)}, u32[]{:S(2)}, u32[]{:S(2)}) collective-permute-start(bf16[128,1000]{0,1:T(8,128)(2,1)} %collective-permute-done.8), channel_id=1, source_target_pairs={{0,508},{4,0},{8,4},{12,8},{16,12},{20,16},{24,20},{28,24},{32,28}... | collective-permute-start | bytes 768008 | tf_op jit(solution)/shard_map/ppermute | solution.py:16
  146.4 40.8 %collective-permute-start.17 = (bf16[128,1000]{0,1:T(8,128)(2,1)}, bf16[128,1000]{0,1:T(8,128)(2,1)}, u32[]{:S(2)}, u32[]{:S(2)}) collective-permute-start(bf16[128,1000]{0,1:T(8,128)(2,1)} %collective-permute-done.11), channel_id=1, source_target_pairs={{0,4},{4,8},{8,12},{12,16},{16,20},{20,24},{24,28},{28,32},{32,36}... | collective-permute-start | bytes 768008 | tf_op jit(solution)/shard_map/ppermute | solution.py:16
  150.0 12.5 %collective-permute-start.12 = (bf16[128,1024]{1,0:T(8,128)(2,1)S(1)}, bf16[128,1024]{1,0:T(8,128)(2,1)S(1)}, u32[]{:S(2)}, u32[]{:S(2)}) collective-permute-start(bf16[128,1024]{1,0:T(8,128)(2,1)S(1)} %collective-permute-done.6), channel_id=1, source_target_pairs={{0,508},{4,0},{8,4},{12,8},{16,12},{20,16},{24,20},{28,24},{32,28}... | collective-permute-start | bytes 786440 | tf_op jit(solution)/shard_map/ppermute | solution.py:16
  155.3 11.3 %collective-permute-start.15 = (bf16[128,1024]{1,0:T(8,128)(2,1)S(1)}, bf16[128,1024]{1,0:T(8,128)(2,1)S(1)}, u32[]{:S(2)}, u32[]{:S(2)}) collective-permute-start(bf16[128,1024]{1,0:T(8,128)(2,1)S(1)} %collective-permute-done.9), channel_id=1, source_target_pairs={{0,4},{4,8},{8,12},{12,16},{16,20},{20,24},{24,28},{28,32},{32,36}... | collective-permute-start | bytes 786440 | tf_op jit(solution)/shard_map/ppermute | solution.py:16
  157.3 3.6 %copy-start.2 = (bf16[512,1024]{1,0:T(8,128)(2,1)S(1)}, bf16[512,1024]{1,0:T(8,128)(2,1)}, u32[]{:S(2)}) copy-start(bf16[512,1024]{1,0:T(8,128)(2,1)} %all-gather.4.cloned.1.call-done) | copy-start | bytes 3145732
  162.4 4.9 %copy-start.1 = (f32[512,128]{0,1:T(8,128)}, f32[512,128]{0,1:T(8,128)S(1)}, u32[]{:S(2)}) copy-start(f32[512,128]{0,1:T(8,128)S(1)} %get-tuple-element.185) | copy-start | bytes 786436
  163.0 18.1 %copy-start.5 = (bf16[128,1000]{0,1:T(8,128)(2,1)S(1)}, bf16[128,1000]{0,1:T(8,128)(2,1)}, u32[]{:S(2)}) copy-start(bf16[128,1000]{0,1:T(8,128)(2,1)} %param.12) | copy-start | bytes 768004
  181.8 3.0 %copy-start.9 = (bf16[128,1000]{0,1:T(8,128)(2,1)S(1)}, bf16[128,1000]{0,1:T(8,128)(2,1)}, u32[]{:S(2)}) copy-start(bf16[128,1000]{0,1:T(8,128)(2,1)} %copy-done.8) | copy-start | bytes 768004
  183.3 2.0 copy-start.7
  249.3 40.1 %all-to-all-start.1 = ((bf16[128,4,250]{2,1,0:T(4,128)(2,1)}), bf16[128,4,250]{2,1,0:T(4,128)(2,1)S(1)}, u32[]{:S(2)}, u32[]{:S(2)}) async-start(bf16[128,4,250]{2,1,0:T(4,128)(2,1)} %reshape.388), calls=%async_computation.1 | async-start | bytes 524288 | tf_op jit(solution)/shard_map/all_to_all | solution.py:108
Sparse Core Ops, SparseCore 0:
  55.2 35.7 all-gather.3
  190.9 56.4 all-reduce.2
where the time goes:
time: 299 us; the launch traced here: 298 us
  waiting for transfers between devices  112 us (37%)
  starting transfers between devices  83.5 us (28%)
  blocking collectives  56.6 us (19%)
  between operations  18.4 us (6%)
  matrix products  15.4 us (5%)
  local copies, waits for them, and re-layouts  9.51 us (3%)
    ppermute x18, starting transfers between devices, from_behind(): lax.ppermute(array, axis, [(i, (i + by) % peers) for i in range(peers)])  66.9 us
    unnamed x3, waiting for transfers between devices  54.7 us
    all_to_all x1, blocking collectives, body(): lax.all_to_all(outgoing.reshape(clusters, capacity, queries.shape[1]), 'c...  43.1 us
    ppermute x18, waiting for transfers between devices, from_behind(): lax.ppermute(array, axis, [(i, (i + by) % peers) for i in range(peers)])  34 us
    all_to_all x1, waiting for transfers between devices, body(): lax.all_to_all(shares.reshape(clusters, capacity, shares.shape[1]), 'clus...  23.7 us
    all_to_all x1, starting transfers between devices, body(): lax.all_to_all(shares.reshape(clusters, capacity, shares.shape[1]), 'clus...  16.5 us
    all_gather x2, blocking collectives, combined_all(): gathered = jax.tree.map(lambda a: lax.all_gather(a, axis), part)  13.5 us
    dot_general x7, matrix products, absorb(): jnp.dot(weight.astype(jnp.bfloat16), block_labels, preferred_element_type...  9.34 us
  transfers between devices with their start and end apart: 21, of which 10 were waited for; matrix products, arithmetic and copies ran while one was open for 5% of the time, Pallas kernels for 0%

commit v1 on v0

v1 whole, which is shorter than its diff:
```python
import math

import jax
import jax.numpy as jnp
from jax import lax
from jax.sharding import PartitionSpec as P

REACH = 3


temper = 2.0


def shifted(array, axis, by):
    peers = lax.axis_size(axis)
    return lax.ppermute(array, axis, [(i, (i - by) % peers) for i in range(peers)])


def swapped(array, axis, bit):
    peers = lax.axis_size(axis)
    return lax.ppermute(array, axis, [(i, i ^ bit) for i in range(peers)])


def round_bf16(x):
    return lax.reduce_precision(x, exponent_bits=8, mantissa_bits=7)


def split3(x):
    hi = round_bf16(x)
    rest = x - hi
    mid = round_bf16(rest)
    lo = rest - mid
    return [part.astype(jnp.bfloat16) for part in (hi, mid, lo)]


def join3(parts):
    hi, mid, lo = [p.astype(jnp.float32) for p in parts]
    return (hi + mid) + lo


def pack(part, top, total, width):
    rows = part.shape[0]
    codes = split3(top) + split3(total)
    columns = [part.astype(jnp.bfloat16)] + [c[:, None] for c in codes]
    pad = width - part.shape[1] - len(codes)
    columns.append(jnp.zeros((rows, pad), jnp.bfloat16))
    return jnp.concatenate(columns, axis=1)


def merge(kept, top, total, message, width):
    other = message[:, :width].astype(jnp.float32)
    codes = [message[:, width + i] for i in range(6)]
    other_top = join3(codes[:3])
    other_total = join3(codes[3:])
    highest = jnp.maximum(top, other_top)
    mine = jnp.exp(top - highest)
    theirs = jnp.exp(other_top - highest)
    merged = kept * mine[:, None] + other * theirs[:, None]
    return merged, highest, total * mine + other_total * theirs


def body(queries, assign, band_mask, keys, labels, prior):
    clusters = lax.axis_size("cluster")
    cluster_index = lax.axis_index("cluster")
    feat_index = lax.axis_index("feat")
    local_rows = queries.shape[0]
    depth = keys.shape[1]
    classes = labels.shape[1]
    rows = keys.shape[0]
    capacity = 2 * local_rows // clusters
    slots = clusters * capacity

    width = depth + classes + 1
    padded = -(-width // 128) * 128
    block = jnp.concatenate(
        [keys, labels, prior[:, None], jnp.zeros((rows, padded - width), keys.dtype)], axis=1
    )
    offsets = [0]
    for reach in range(1, REACH + 1):
        offsets += [reach, -reach]
    blocks = [block] + [shifted(block, "cluster", o) for o in offsets[1:]]

    target = assign[:, 0]
    onehot = (target[:, None] == jnp.arange(clusters, dtype=jnp.int32)[None, :]).astype(jnp.int32)
    before = jnp.cumsum(onehot, axis=0) - onehot
    position = target * capacity + jnp.sum(before * onehot, axis=1)
    outgoing = jnp.zeros((slots, queries.shape[1]), queries.dtype).at[position].set(queries)
    arrived = lax.all_to_all(
        outgoing.reshape(clusters, capacity, queries.shape[1]),
        "cluster",
        split_axis=0,
        concat_axis=0,
        tiled=True,
    )
    query_full = lax.all_gather(
        arrived.reshape(slots, queries.shape[1]), "feat", axis=1, tiled=True
    )

    stacked = jnp.stack(blocks)
    band_keys = stacked[:, :, :depth].reshape(len(offsets) * rows, depth)
    band_labels = stacked[:, :, depth : depth + classes].reshape(len(offsets) * rows, classes)
    band_prior = stacked[:, :, depth + classes].reshape(len(offsets) * rows)
    mask_row = band_mask[cluster_index]
    live_blocks = jnp.stack([mask_row[REACH + o] > 0 for o in offsets])
    live = jnp.repeat(live_blocks, rows)
    scale = temper / math.sqrt(depth)
    scores = jnp.einsum("qd,kd->qk", query_full, band_keys, preferred_element_type=jnp.float32) * scale
    scores = scores + band_prior.astype(jnp.float32)[None, :]
    scores = jnp.where(live[None, :], scores, -jnp.inf)
    top = jnp.max(scores, axis=1)
    weight = jnp.exp(scores - top[:, None])
    total = jnp.sum(weight, axis=1)
    accum = jnp.dot(weight.astype(jnp.bfloat16), band_labels, preferred_element_type=jnp.float32)

    quarter = classes // 4
    core = feat_index % 2
    side = feat_index // 2
    grid = accum.reshape(slots, 2, 2, quarter)
    kept = lax.dynamic_index_in_dim(grid, core, axis=2, keepdims=False)
    sent = lax.dynamic_index_in_dim(grid, 1 - core, axis=2, keepdims=False)
    message = swapped(pack(sent.reshape(slots, 2 * quarter), top, total, 2 * quarter + 12), "feat", 1)
    kept, top, total = merge(kept.reshape(slots, 2 * quarter), top, total, message, 2 * quarter)
    grid = kept.reshape(slots, 2, quarter)
    kept = lax.dynamic_index_in_dim(grid, side, axis=1, keepdims=False)
    sent = lax.dynamic_index_in_dim(grid, 1 - side, axis=1, keepdims=False)
    message = swapped(pack(sent, top, total, quarter + 6), "feat", 2)
    kept, top, total = merge(kept, top, total, message, quarter)
    shares = (kept / total[:, None]).astype(jnp.bfloat16)

    returned = lax.all_to_all(
        shares.reshape(clusters, capacity, quarter),
        "cluster",
        split_axis=0,
        concat_axis=0,
        tiled=True,
    )
    return returned.reshape(slots, quarter)[position]


def solution(mesh):
    in_specs = (
        P("cluster", "feat"),
        P("cluster", None),
        P(),
        P(("cluster", "feat"), None),
        P(("cluster", "feat"), None),
        P(("cluster", "feat")),
    )
    out_specs = P("cluster", "feat")
    return jax.shard_map(body, mesh=mesh, in_specs=in_specs, out_specs=out_specs, check_vma=False)
```

time: 299 us -> 179 us (0.60)
  blocking collectives: 56.6 us -> 0 us
  waiting for transfers between devices: 112 us -> 56.9 us
  local copies, waits for them, and re-layouts: 9.51 us -> 29.4 us
  starting transfers between devices: 83.5 us -> 66.8 us
  matrix products: 15.4 us -> 4.64 us
    unnamed x3 -> x1, waiting for transfers between devices: 54.7 us -> 0.02 us
    all_to_all x1 -> x0, blocking collectives: 43.1 us -> none  [body(): lax.all_to_all(outgoing.reshape(clusters, capacity, queries.shape[1]), 'c...]
    ppermute x18 -> x8, starting transfers between devices: 66.9 us -> 28.4 us  [the longest x6 23.8 us: shifted(): lax.ppermute(array, axis, [(i, (i - by) % peers) for i in range(peers)])]
    ppermute x18 -> x8, waiting for transfers between devices: 34 us -> 9.59 us  [the longest x2 9.57 us: swapped(): return lax.ppermute(array, axis, [(i, i ^ bit) for i in range(peers)])]
    all_to_all x1 -> x2, starting transfers between devices: 16.5 us -> 38.4 us  [the longest x1 21.9 us: body(): lax.all_to_all(outgoing.reshape(clusters, capacity, queries.shape[1]), 'c...]
    all_gather x2 -> x0, blocking collectives: 13.5 us -> none  [combined_all(): gathered = jax.tree.map(lambda a: lax.all_gather(a, axis), part)]
    all_gather x1, waiting for transfers between devices: 0.02 us -> 13.3 us  [body(): lax.all_gather(arrived.reshape(slots, queries.shape[1]), 'feat', axis=1,...]
    dot_general x14 -> x2, matrix products: 15.4 us -> 4.64 us  [the longest x1 3.19 us: body(): jnp.einsum('qd,kd->qk', query_full, band_keys, preferred_element_type=jnp...]
  transfers between devices with their start and end apart: 21 -> 11, of which waited for: 10 -> 5; matrix products, arithmetic and copies ran while one was open for 5% -> 12% of each run, Pallas kernels for 0% -> 0%
where the time goes in v1:
time: 179 us; the launch traced here: 178 us
  starting transfers between devices  66.8 us (37%)
  waiting for transfers between devices  56.9 us (32%)
  local copies, waits for them, and re-layouts  29.4 us (16%)
  between operations  18.2 us (10%)
  matrix products  4.64 us (3%)
  other arithmetic  2.49 us (1%)
    ppermute x6, starting transfers between devices, shifted(): lax.ppermute(array, axis, [(i, (i - by) % peers) for i in range(peers)])  23.8 us
    all_to_all x1, waiting for transfers between devices, body(): lax.all_to_all(shares.reshape(clusters, capacity, quarter), 'cluster', sp...  22.7 us
    all_to_all x1, starting transfers between devices, body(): lax.all_to_all(outgoing.reshape(clusters, capacity, queries.shape[1]), 'c...  21.9 us
    all_to_all x1, starting transfers between devices, body(): lax.all_to_all(shares.reshape(clusters, capacity, quarter), 'cluster', sp...  16.5 us
    all_gather x1, waiting for transfers between devices, body(): lax.all_gather(arrived.reshape(slots, queries.shape[1]), 'feat', axis=1,...  13.3 us
    all_to_all x1, waiting for transfers between devices, body(): lax.all_to_all(outgoing.reshape(clusters, capacity, queries.shape[1]), 'c...  11.2 us
    ppermute x2, waiting for transfers between devices, swapped(): return lax.ppermute(array, axis, [(i, i ^ bit) for i in range(peers)])  9.57 us
    unnamed x18, local copies, waits for them, and re-layouts  9.28 us
  transfers between devices with their start and end apart: 11, of which 5 were waited for; matrix products, arithmetic and copies ran while one was open for 12% of the time, Pallas kernels for 0%

profile of v1, /device:TPU:32, one launch (start us, length us, event | category | flops | bytes accessed | tf_op | source)
XLA Modules:
  0.0 178.4 jit_solution(16442998857804492078)
XLA Ops:
  6.5 1.1 copy.24
  7.7 0.8 copy.25
  8.5 1.1 concatenate.9
  9.6 5.4 %collective-permute-start = (bf16[128,2048]{1,0:T(8,128)(2,1)S(1)}, bf16[128,2048]{1,0:T(8,128)(2,1)S(1)}, u32[]{:S(2)}, u32[]{:S(2)}) collective-permute-start(bf16[128,2048]{1,0:T(8,128)(2,1)S(1)} %concatenate.9), channel_id=1, source_target_pairs={{0,508},{4,0},{8,4},{12,8},{16,12},{20,16},{24,20},{28,24},{32,28}... | collective-permute-start | bytes 1572872 | tf_op jit(solution)/shard_map/ppermute | solution.py:16
  15.0 1.9 %collective-permute-start.1 = (bf16[128,2048]{1,0:T(8,128)(2,1)S(1)}, bf16[128,2048]{1,0:T(8,128)(2,1)S(1)}, u32[]{:S(2)}, u32[]{:S(2)}) collective-permute-start(bf16[128,2048]{1,0:T(8,128)(2,1)S(1)} %concatenate.9), channel_id=1, source_target_pairs={{0,4},{4,8},{8,12},{12,16},{16,20},{20,24},{24,28},{28,32},{32,36}... | collective-permute-start | bytes 1572872 | tf_op jit(solution)/shard_map/ppermute | solution.py:16
  16.9 3.0 %collective-permute-start.2 = (bf16[128,2048]{1,0:T(8,128)(2,1)S(1)}, bf16[128,2048]{1,0:T(8,128)(2,1)S(1)}, u32[]{:S(2)}, u32[]{:S(2)}) collective-permute-start(bf16[128,2048]{1,0:T(8,128)(2,1)S(1)} %concatenate.9), channel_id=1, source_target_pairs={{0,504},{4,508},{8,0},{12,4},{16,8},{20,12},{24,16},{28,20},{32,24... | collective-permute-start | bytes 1572872 | tf_op jit(solution)/shard_map/ppermute | solution.py:16
  19.9 2.8 %collective-permute-start.3 = (bf16[128,2048]{1,0:T(8,128)(2,1)S(1)}, bf16[128,2048]{1,0:T(8,128)(2,1)S(1)}, u32[]{:S(2)}, u32[]{:S(2)}) collective-permute-start(bf16[128,2048]{1,0:T(8,128)(2,1)S(1)} %concatenate.9), channel_id=1, source_target_pairs={{0,8},{4,12},{8,16},{12,20},{16,24},{20,28},{24,32},{28,36},{32,40... | collective-permute-start | bytes 1572872 | tf_op jit(solution)/shard_map/ppermute | solution.py:16
  22.8 6.4 %collective-permute-start.4 = (bf16[128,2048]{1,0:T(8,128)(2,1)S(1)}, bf16[128,2048]{1,0:T(8,128)(2,1)S(1)}, u32[]{:S(2)}, u32[]{:S(2)}) collective-permute-start(bf16[128,2048]{1,0:T(8,128)(2,1)S(1)} %concatenate.9), channel_id=1, source_target_pairs={{0,500},{4,504},{8,508},{12,0},{16,4},{20,8},{24,12},{28,16},{32,2... | collective-permute-start | bytes 1572872 | tf_op jit(solution)/shard_map/ppermute | solution.py:16
  29.2 0.8 copy.22
  30.0 0.2 fusion.11
  30.3 0.2 fusion.13
  30.5 1.9 %scatter_custom_fusion = bf16[512,256]{1,0:T(8,128)(2,1)S(1)} fusion(s32[256]{0:T(256)S(1)} %bitcast.96, bf16[256,256]{1,0:T(8,128)(2,1)} %param.6, bf16[]{:T(256)} %constant.68.clone.1), kind=kCustom, calls=%fused_computation.33 | custom fusion | bytes 262656 | tf_op jit(solution)/shard_map/scatter | solution.py:87
  32.4 0.8 reshape.174
  33.2 21.9 %all-to-all-start = ((bf16[128,4,256]{2,1,0:T(4,128)(2,1)}), bf16[128,4,256]{2,1,0:T(4,128)(2,1)S(1)}, u32[]{:S(2)}, u32[]{:S(2)}) async-start(bf16[128,4,256]{2,1,0:T(4,128)(2,1)} %reshape.174), calls=%async_computation | async-start | bytes 524288 | tf_op jit(solution)/shard_map/all_to_all | solution.py:88
  55.1 0.0 all-gather.2.cloned.1.call-start
  55.1 0.1 constant_dynamic-slice_fusion.1
  55.2 0.6 fusion.39
  60.2 0.1 stack.55
  60.3 0.8 bitcast_dynamic-update-slice_fusion.6
  61.2 0.1 broadcast_bitcast_fusion
  61.2 0.0 collective-permute-done
  61.2 4.3 %collective-permute-start.5 = (bf16[128,2048]{1,0:T(8,128)(2,1)S(1)}, bf16[128,2048]{1,0:T(8,128)(2,1)}, u32[]{:S(2)}, u32[]{:S(2)}) collective-permute-start(bf16[128,2048]{1,0:T(8,128)(2,1)S(1)} %concatenate.9), channel_id=1, source_target_pairs={{0,12},{4,16},{8,20},{12,24},{16,28},{20,32},{24,36},{28,40},{32,4... | collective-permute-start | bytes 1572872 | tf_op jit(solution)/shard_map/ppermute | solution.py:16
  65.5 0.8 bitcast_dynamic-update-slice_fusion.5
  66.3 0.8 bitcast_dynamic-update-slice_fusion.4
  67.2 11.2 %all-to-all-done = bf16[128,4,256]{2,1,0:T(4,128)(2,1)S(1)} async-done(((bf16[128,4,256]{2,1,0:T(4,128)(2,1)}), bf16[128,4,256]{2,1,0:T(4,128)(2,1)S(1)}, u32[]{:S(2)}, u32[]{:S(2)}) %all-to-all-start) | async-done | bytes 262176 | tf_op jit(solution)/shard_map/all_to_all | solution.py:88
  78.4 0.8 reshape.175
  79.2 0.0 all-gather.2.cloned.1.call-update
  79.2 0.8 bitcast_dynamic-update-slice_fusion.3
  80.1 0.0 collective-permute-done.3
  80.1 0.8 bitcast_dynamic-update-slice_fusion.2
  80.9 0.0 collective-permute-done.4
  80.9 0.8 bitcast_dynamic-update-slice_fusion.1
  81.8 0.0 collective-permute-done.5
  81.8 1.9 %bitcast_dynamic-update-slice_fusion = bf16[7,128,2048]{2,1,0:T(8,128)(2,1)} fusion(bf16[7,128,2048]{2,1,0:T(8,128)(2,1)} %bitcast_dynamic-update-slice_fusion.1, bf16[128,2048]{1,0:T(8,128)(2,1)} %collective-permute-done.5), kind=kLoop, calls=%fused_computation.16 | loop fusion | bytes 1048576 | tf_op jit(solution)/shard_map/stack | solution.py:99
  83.6 1.8 %slice.116 = bf16[7,128,1000]{2,1,0:T(8,128)(2,1)S(1)} slice(bf16[7,128,2048]{2,1,0:T(8,128)(2,1)} %bitcast_dynamic-update-slice_fusion), slice={[0:7], [0:128], [1024:2024]} | slice | bytes 3584000 | tf_op jit(solution)/shard_map/slice | solution.py:101
  85.5 0.8 copy-done.1
  86.2 1.4 slice.114
  87.6 3.0 %reshape.200 = bf16[2,2,250,896]{2,1,0,3:T(2,128)(2,1)} reshape(bf16[1000,896]{0,1:T(8,128)(2,1)S(1)} %bitcast.78) | data formatting | bytes 3584000 | tf_op jit(solution)/shard_map/dot_general | solution.py:113
  90.6 1.2 convert_reduce_fusion
  91.8 13.3 %all-gather.2.cloned.1.call-done = bf16[512,1024]{1,0:T(8,128)(2,1)} async-done(((bf16[512,256]{1,0:T(8,128)(2,1)}), bf16[512,1024]{1,0:T(8,128)(2,1)}) %all-gather.2.cloned.1.call-update) | async-done | bytes 1048592 | tf_op jit(solution)/shard_map/all_gather | solution.py:95
  105.0 3.2 %fusion.40 = (f32[512]{0:T(512)S(1)}, f32[512,896]{1,0:T(8,128)S(1)}) fusion(f32[896]{0:T(1024)S(1)} %bitcast.94, bf16[512,1024]{1,0:T(8,128)(2,1)} %all-gather.2.cloned.1.call-done, bf16[896,1024]{1,0:T(8,128)(2,1)} %bitcast.79, pred[896]{0:T(1024)(128)(4,1)S(1)} %broadcast_bitcast_fusion), kind=kOutput, calls=%fused_computation.94 | convolution fusion | flops 941358592 | bytes 4725120 | tf_op jit(solution)/shard_map/qd,kd->qk/dot_general | solution.py:107
  108.2 0.5 fusion.2
  108.7 1.0 copy-done.2
  109.7 1.4 fusion
  111.2 1.3 copy-done.3
  112.5 0.1 dynamic-slice_convert_fusion
  112.6 0.1 convert_element_type.224
  112.8 0.4 concatenate.10
  113.1 2.2 %collective-permute-start.6 = (bf16[512,512]{0,1:T(8,128)(2,1)S(1)}, bf16[512,512]{0,1:T(8,128)(2,1)S(1)}, u32[]{:S(2)}, u32[]{:S(2)}) collective-permute-start(bf16[512,512]{0,1:T(8,128)(2,1)S(1)} %concatenate.10), channel_id=1, source_target_pairs={{0,1},{1,0},{2,3},{3,2},{4,5},{5,4},{6,7},{7,6},{8,9},{9,8},{10,11... | collective-permute-start | bytes 1572872 | tf_op jit(solution)/shard_map/ppermute | solution.py:21
  115.3 1.3 constant_dynamic-slice_fusion
  116.6 0.1 reshape.178
  116.7 0.2 collective-permute-done.6
  116.9 0.2 multiply_add_fusion
  117.1 0.1 reshape.179
  117.3 0.1 concatenate.11
  117.4 2.5 %collective-permute-start.7 = (bf16[512,256]{0,1:T(8,128)(2,1)S(1)}, bf16[512,256]{0,1:T(8,128)(2,1)S(1)}, u32[]{:S(2)}, u32[]{:S(2)}) collective-permute-start(bf16[512,256]{0,1:T(8,128)(2,1)S(1)} %concatenate.11), channel_id=1, source_target_pairs={{0,2},{1,3},{2,0},{3,1},{4,6},{5,7},{6,4},{7,5},{8,10},{9,11},{10,... | collective-permute-start | bytes 786440 | tf_op jit(solution)/shard_map/ppermute | solution.py:21
  119.9 9.4 %collective-permute-done.7 = bf16[512,256]{0,1:T(8,128)(2,1)S(1)} collective-permute-done((bf16[512,256]{0,1:T(8,128)(2,1)S(1)}, bf16[512,256]{0,1:T(8,128)(2,1)S(1)}, u32[]{:S(2)}, u32[]{:S(2)}) %collective-permute-start.7) | collective-permute-done | bytes 262176 | tf_op jit(solution)/shard_map/ppermute | solution.py:21
  129.3 0.1 fusion.9
  129.4 0.1 copy.27
  129.6 0.8 reshape.180
  130.4 16.5 %all-to-all-start.1 = ((bf16[128,4,250]{2,1,0:T(4,128)(2,1)}), bf16[128,4,250]{2,1,0:T(4,128)(2,1)S(1)}, u32[]{:S(2)}, u32[]{:S(2)}) async-start(bf16[128,4,250]{2,1,0:T(4,128)(2,1)} %reshape.180), calls=%async_computation.1 | async-start | bytes 524288 | tf_op jit(solution)/shard_map/all_to_all | solution.py:130
  146.8 22.7 %all-to-all-done.1 = bf16[128,4,250]{2,1,0:T(4,128)(2,1)S(1)} async-done(((bf16[128,4,250]{2,1,0:T(4,128)(2,1)}), bf16[128,4,250]{2,1,0:T(4,128)(2,1)S(1)}, u32[]{:S(2)}, u32[]{:S(2)}) %all-to-all-start.1) | async-done | bytes 256032 | tf_op jit(solution)/shard_map/all_to_all | solution.py:130
  169.6 0.2 reshape.181
  169.7 1.8 %gather_fusion = bf16[256,250]{1,0:T(8,128)(2,1)} fusion(bf16[512,250]{1,0:T(8,128)(2,1)S(1)} %reshape.181, s32[1024]{0:T(1024)S(1)} %pad_clamp_fusion), kind=kCustom, calls=%fused_computation | custom fusion | bytes 257024 | tf_op jit(solution)/shard_map/gather | solution.py:137
  (25 shorter events, 0.2 us)
Async XLA Ops:
  6.5 48.6 %copy-start = (s32[128,7]{0,1:T(8,128)S(1)}, s32[128,7]{0,1:T(8,128)}, u32[]{:S(2)}) copy-start(s32[128,7]{0,1:T(8,128)} %param.8) | copy-start | bytes 10756
  6.5 23.7 %copy-start.4 = (s32[256,1]{0,1:T(1,128)S(1)}, s32[256,1]{0,1:T(1,128)}, u32[]{:S(2)}) copy-start(s32[256,1]{0,1:T(1,128)} %param.7) | copy-start | bytes 3076
  9.6 51.6 %collective-permute-start = (bf16[128,2048]{1,0:T(8,128)(2,1)S(1)}, bf16[128,2048]{1,0:T(8,128)(2,1)S(1)}, u32[]{:S(2)}, u32[]{:S(2)}) collective-permute-start(bf16[128,2048]{1,0:T(8,128)(2,1)S(1)} %concatenate.9), channel_id=1, source_target_pairs={{0,508},{4,0},{8,4},{12,8},{16,12},{20,16},{24,20},{28,24},{32,28}... | collective-permute-start | bytes 1572872 | tf_op jit(solution)/shard_map/ppermute | solution.py:16
  15.0 51.3 %collective-permute-start.1 = (bf16[128,2048]{1,0:T(8,128)(2,1)S(1)}, bf16[128,2048]{1,0:T(8,128)(2,1)S(1)}, u32[]{:S(2)}, u32[]{:S(2)}) collective-permute-start(bf16[128,2048]{1,0:T(8,128)(2,1)S(1)} %concatenate.9), channel_id=1, source_target_pairs={{0,4},{4,8},{8,12},{12,16},{16,20},{20,24},{24,28},{28,32},{32,36}... | collective-permute-start | bytes 1572872 | tf_op jit(solution)/shard_map/ppermute | solution.py:16
  16.9 62.3 %collective-permute-start.2 = (bf16[128,2048]{1,0:T(8,128)(2,1)S(1)}, bf16[128,2048]{1,0:T(8,128)(2,1)S(1)}, u32[]{:S(2)}, u32[]{:S(2)}) collective-permute-start(bf16[128,2048]{1,0:T(8,128)(2,1)S(1)} %concatenate.9), channel_id=1, source_target_pairs={{0,504},{4,508},{8,0},{12,4},{16,8},{20,12},{24,16},{28,20},{32,24... | collective-permute-start | bytes 1572872 | tf_op jit(solution)/shard_map/ppermute | solution.py:16
  19.9 60.1 %collective-permute-start.3 = (bf16[128,2048]{1,0:T(8,128)(2,1)S(1)}, bf16[128,2048]{1,0:T(8,128)(2,1)S(1)}, u32[]{:S(2)}, u32[]{:S(2)}) collective-permute-start(bf16[128,2048]{1,0:T(8,128)(2,1)S(1)} %concatenate.9), channel_id=1, source_target_pairs={{0,8},{4,12},{8,16},{12,20},{16,24},{20,28},{24,32},{28,36},{32,40... | collective-permute-start | bytes 1572872 | tf_op jit(solution)/shard_map/ppermute | solution.py:16
  22.8 58.1 %collective-permute-start.4 = (bf16[128,2048]{1,0:T(8,128)(2,1)S(1)}, bf16[128,2048]{1,0:T(8,128)(2,1)S(1)}, u32[]{:S(2)}, u32[]{:S(2)}) collective-permute-start(bf16[128,2048]{1,0:T(8,128)(2,1)S(1)} %concatenate.9), channel_id=1, source_target_pairs={{0,500},{4,504},{8,508},{12,0},{16,4},{20,8},{24,12},{28,16},{32,2... | collective-permute-start | bytes 1572872 | tf_op jit(solution)/shard_map/ppermute | solution.py:16
  33.2 45.3 %all-to-all-start = ((bf16[128,4,256]{2,1,0:T(4,128)(2,1)}), bf16[128,4,256]{2,1,0:T(4,128)(2,1)S(1)}, u32[]{:S(2)}, u32[]{:S(2)}) async-start(bf16[128,4,256]{2,1,0:T(4,128)(2,1)} %reshape.174), calls=%async_computation | async-start | bytes 524288 | tf_op jit(solution)/shard_map/all_to_all | solution.py:88
  55.1 50.0 %all-gather.2.cloned.1.call-start = ((), (), s32[]{:S(2)}) async-start(), calls=%async_computation.2 | async-start | bytes 1310720 | tf_op jit(solution)/shard_map/all_gather | solution.py:95
  61.2 20.5 %collective-permute-start.5 = (bf16[128,2048]{1,0:T(8,128)(2,1)S(1)}, bf16[128,2048]{1,0:T(8,128)(2,1)}, u32[]{:S(2)}, u32[]{:S(2)}) collective-permute-start(bf16[128,2048]{1,0:T(8,128)(2,1)S(1)} %concatenate.9), channel_id=1, source_target_pairs={{0,12},{4,16},{8,20},{12,24},{16,28},{20,32},{24,36},{28,40},{32,4... | collective-permute-start | bytes 1572872 | tf_op jit(solution)/shard_map/ppermute | solution.py:16
  83.6 2.6 %copy-start.1 = (bf16[7,128,2048]{2,1,0:T(8,128)(2,1)S(1)}, bf16[7,128,2048]{2,1,0:T(8,128)(2,1)}, u32[]{:S(2)}) copy-start(bf16[7,128,2048]{2,1,0:T(8,128)(2,1)} %bitcast_dynamic-update-slice_fusion) | copy-start | bytes 11010052
  108.2 1.5 copy-start.2
  111.2 1.3 copy-start.3
  113.1 3.8 %collective-permute-start.6 = (bf16[512,512]{0,1:T(8,128)(2,1)S(1)}, bf16[512,512]{0,1:T(8,128)(2,1)S(1)}, u32[]{:S(2)}, u32[]{:S(2)}) collective-permute-start(bf16[512,512]{0,1:T(8,128)(2,1)S(1)} %concatenate.10), channel_id=1, source_target_pairs={{0,1},{1,0},{2,3},{3,2},{4,5},{5,4},{6,7},{7,6},{8,9},{9,8},{10,11... | collective-permute-start | bytes 1572872 | tf_op jit(solution)/shard_map/ppermute | solution.py:21
  117.4 11.9 %collective-permute-start.7 = (bf16[512,256]{0,1:T(8,128)(2,1)S(1)}, bf16[512,256]{0,1:T(8,128)(2,1)S(1)}, u32[]{:S(2)}, u32[]{:S(2)}) collective-permute-start(bf16[512,256]{0,1:T(8,128)(2,1)S(1)} %concatenate.11), channel_id=1, source_target_pairs={{0,2},{1,3},{2,0},{3,1},{4,6},{5,7},{6,4},{7,5},{8,10},{9,11},{10,... | collective-permute-start | bytes 786440 | tf_op jit(solution)/shard_map/ppermute | solution.py:21
  130.4 39.2 %all-to-all-start.1 = ((bf16[128,4,250]{2,1,0:T(4,128)(2,1)}), bf16[128,4,250]{2,1,0:T(4,128)(2,1)S(1)}, u32[]{:S(2)}, u32[]{:S(2)}) async-start(bf16[128,4,250]{2,1,0:T(4,128)(2,1)} %reshape.180), calls=%async_computation.1 | async-start | bytes 524288 | tf_op jit(solution)/shard_map/all_to_all | solution.py:130
Sparse Core Ops, SparseCore 0:
  79.3 25.6 all-gather.1

commit v2 on v1

--- a/solution.py
+++ b/solution.py
@@ -70,10 +70,9 @@
     capacity = 2 * local_rows // clusters
     slots = clusters * capacity
 
-    width = depth + classes + 1
-    padded = -(-width // 128) * 128
-    block = jnp.concatenate(
-        [keys, labels, prior[:, None], jnp.zeros((rows, padded - width), keys.dtype)], axis=1
+    spare = depth - classes - 1
+    block = jnp.stack(
+        [keys, jnp.concatenate([labels, prior[:, None], jnp.zeros((rows, spare), keys.dtype)], axis=1)]
     )
     offsets = [0]
     for reach in range(1, REACH + 1):
@@ -96,21 +95,27 @@
         arrived.reshape(slots, queries.shape[1]), "feat", axis=1, tiled=True
     )
 
-    stacked = jnp.stack(blocks)
-    band_keys = stacked[:, :, :depth].reshape(len(offsets) * rows, depth)
-    band_labels = stacked[:, :, depth : depth + classes].reshape(len(offsets) * rows, classes)
-    band_prior = stacked[:, :, depth + classes].reshape(len(offsets) * rows)
     mask_row = band_mask[cluster_index]
     live_blocks = jnp.stack([mask_row[REACH + o] > 0 for o in offsets])
     live = jnp.repeat(live_blocks, rows)
     scale = temper / math.sqrt(depth)
-    scores = jnp.einsum("qd,kd->qk", query_full, band_keys, preferred_element_type=jnp.float32) * scale
-    scores = scores + band_prior.astype(jnp.float32)[None, :]
+    scores = jnp.concatenate(
+        [
+            jnp.einsum("qd,kd->qk", query_full, b[0], preferred_element_type=jnp.float32) * scale
+            + b[1][:, classes].astype(jnp.float32)[None, :]
+            for b in blocks
+        ],
+        axis=1,
+    )
     scores = jnp.where(live[None, :], scores, -jnp.inf)
     top = jnp.max(scores, axis=1)
     weight = jnp.exp(scores - top[:, None])
     total = jnp.sum(weight, axis=1)
-    accum = jnp.dot(weight.astype(jnp.bfloat16), band_labels, preferred_element_type=jnp.float32)
+    rounded = weight.astype(jnp.bfloat16)
+    accum = sum(
+        jnp.dot(rounded[:, i * rows : (i + 1) * rows], b[1], preferred_element_type=jnp.float32)
+        for i, b in enumerate(blocks)
+    )[:, :classes]
 
     quarter = classes // 4
     core = feat_index % 2

time: 179 us -> 192 us (1.073)
  waiting for transfers between devices: 56.9 us -> 72.4 us
  local copies, waits for them, and re-layouts: 29.4 us -> 16.7 us
  other arithmetic: 2.49 us -> 7.9 us
  matrix products: 4.64 us -> 8.91 us
    all_gather x1, waiting for transfers between devices: 13.3 us -> 24.7 us  [body(): lax.all_gather(arrived.reshape(slots, queries.shape[1]), 'feat', axis=1,...]
    unnamed x18 -> x14, local copies, waits for them, and re-layouts: 9.28 us -> 1.46 us
    dot_general x2 -> x14, matrix products: 4.64 us -> 8.91 us  [the longest x7 5.97 us: body(): jnp.einsum('qd,kd->qk', query_full, b[0], preferred_element_type=jnp.floa...]
    slice x2 -> x0, local copies, waits for them, and re-layouts: 3.22 us -> none  [the longest x1 1.83 us: body(): stacked[:, :, depth:depth + classes].reshape(len(offsets) * rows, classes)]
    concatenate x2, local copies, waits for them, and re-layouts: 0.48 us -> 3.59 us  [pack(): return jnp.concatenate(columns, axis=1)]
    dot_general x1 -> x0, local copies, waits for them, and re-layouts: 2.96 us -> none  [body(): jnp.dot(weight.astype(jnp.bfloat16), band_labels, preferred_element_type=...]
    all_to_all x1, waiting for transfers between devices: 11.2 us -> 13.8 us  [body(): lax.all_to_all(outgoing.reshape(clusters, capacity, queries.shape[1]), 'c...]
    another operation x3 -> x5, other arithmetic: 0.25 us -> 2.28 us  [the longest x2 2.03 us: body(): jnp.stack([keys, jnp.concatenate([labels, prior[:, None], jnp.zeros((rows...]
  transfers between devices with their start and end apart: 11 -> 11, of which waited for: 5 -> 5; matrix products, arithmetic and copies ran while one was open for 12% -> 3% of each run, Pallas kernels for 0% -> 0%
where the time goes in v2:
time: 192 us; the launch traced here: 191 us
  waiting for transfers between devices  72.4 us (38%)
  starting transfers between devices  67 us (35%)
  between operations  18.4 us (10%)
  local copies, waits for them, and re-layouts  16.7 us (9%)
  matrix products  8.91 us (5%)
  other arithmetic  7.9 us (4%)
    all_gather x1, waiting for transfers between devices, body(): lax.all_gather(arrived.reshape(slots, queries.shape[1]), 'feat', axis=1,...  24.7 us
    ppermute x6, starting transfers between devices, shifted(): lax.ppermute(array, axis, [(i, (i - by) % peers) for i in range(peers)])  24 us
    all_to_all x1, waiting for transfers between devices, body(): lax.all_to_all(shares.reshape(clusters, capacity, quarter), 'cluster', sp...  22.7 us
    all_to_all x1, starting transfers between devices, body(): lax.all_to_all(outgoing.reshape(clusters, capacity, queries.shape[1]), 'c...  21.9 us
    all_to_all x1, starting transfers between devices, body(): lax.all_to_all(shares.reshape(clusters, capacity, quarter), 'cluster', sp...  16.5 us
    all_to_all x1, waiting for transfers between devices, body(): lax.all_to_all(outgoing.reshape(clusters, capacity, queries.shape[1]), 'c...  13.8 us
    ppermute x2, waiting for transfers between devices, swapped(): return lax.ppermute(array, axis, [(i, i ^ bit) for i in range(peers)])  11.1 us
    dot_general x7, matrix products, body(): jnp.einsum('qd,kd->qk', query_full, b[0], preferred_element_type=jnp.floa...  5.97 us
  transfers between devices with their start and end apart: 11, of which 5 were waited for; matrix products, arithmetic and copies ran while one was open for 3% of the time, Pallas kernels for 0%

profile of v2, /device:TPU:32, one launch (start us, length us, event | category | flops | bytes accessed | tf_op | source)
XLA Modules:
  0.0 191.3 jit_solution(4619953975214828033)
XLA Ops:
  6.5 1.1 copy.12
  7.7 0.1 pad.4.clone
  7.8 1.2 fusion.21
  9.0 0.9 pad_maximum_fusion
  9.8 5.4 %collective-permute-start = (bf16[2,128,1024]{1,2,0:T(8,128)(2,1)}, bf16[2,128,1024]{1,2,0:T(8,128)(2,1)S(1)}, u32[]{:S(2)}, u32[]{:S(2)}) collective-permute-start(bf16[2,128,1024]{1,2,0:T(8,128)(2,1)} %pad_maximum_fusion), channel_id=1, source_target_pairs={{0,508},{4,0},{8,4},{12,8},{16,12},{20,16},{24,20},{28,24},{32,28}... | collective-permute-start | bytes 1572872 | tf_op jit(solution)/shard_map/ppermute | solution.py:16
  15.2 1.9 %collective-permute-start.1 = (bf16[2,128,1024]{1,2,0:T(8,128)(2,1)}, bf16[2,128,1024]{1,2,0:T(8,128)(2,1)S(1)}, u32[]{:S(2)}, u32[]{:S(2)}) collective-permute-start(bf16[2,128,1024]{1,2,0:T(8,128)(2,1)} %pad_maximum_fusion), channel_id=1, source_target_pairs={{0,4},{4,8},{8,12},{12,16},{16,20},{20,24},{24,28},{28,32},{32,36}... | collective-permute-start | bytes 1572872 | tf_op jit(solution)/shard_map/ppermute | solution.py:16
  17.1 3.0 %collective-permute-start.2 = (bf16[2,128,1024]{1,2,0:T(8,128)(2,1)}, bf16[2,128,1024]{1,2,0:T(8,128)(2,1)S(1)}, u32[]{:S(2)}, u32[]{:S(2)}) collective-permute-start(bf16[2,128,1024]{1,2,0:T(8,128)(2,1)} %pad_maximum_fusion), channel_id=1, source_target_pairs={{0,504},{4,508},{8,0},{12,4},{16,8},{20,12},{24,16},{28,20},{32,24... | collective-permute-start | bytes 1572872 | tf_op jit(solution)/shard_map/ppermute | solution.py:16
  20.1 2.8 %collective-permute-start.3 = (bf16[2,128,1024]{1,2,0:T(8,128)(2,1)}, bf16[2,128,1024]{1,2,0:T(8,128)(2,1)S(1)}, u32[]{:S(2)}, u32[]{:S(2)}) collective-permute-start(bf16[2,128,1024]{1,2,0:T(8,128)(2,1)} %pad_maximum_fusion), channel_id=1, source_target_pairs={{0,8},{4,12},{8,16},{12,20},{16,24},{20,28},{24,32},{28,36},{32,40... | collective-permute-start | bytes 1572872 | tf_op jit(solution)/shard_map/ppermute | solution.py:16
  23.0 6.4 %collective-permute-start.4 = (bf16[2,128,1024]{1,2,0:T(8,128)(2,1)}, bf16[2,128,1024]{1,2,0:T(8,128)(2,1)S(1)}, u32[]{:S(2)}, u32[]{:S(2)}) collective-permute-start(bf16[2,128,1024]{1,2,0:T(8,128)(2,1)} %pad_maximum_fusion), channel_id=1, source_target_pairs={{0,500},{4,504},{8,508},{12,0},{16,4},{20,8},{24,12},{28,16},{32,2... | collective-permute-start | bytes 1572872 | tf_op jit(solution)/shard_map/ppermute | solution.py:16
  29.4 0.1 copy.10
  29.5 0.2 fusion.22
  29.8 0.2 fusion.38
  30.0 1.9 scatter_custom_fusion
  31.9 0.8 reshape.205
  32.7 21.9 %all-to-all-start = ((bf16[128,4,256]{2,1,0:T(4,128)(2,1)}), bf16[128,4,256]{2,1,0:T(4,128)(2,1)S(1)}, u32[]{:S(2)}, u32[]{:S(2)}) async-start(bf16[128,4,256]{2,1,0:T(4,128)(2,1)} %reshape.205), calls=%async_computation | async-start | bytes 524288 | tf_op jit(solution)/shard_map/all_to_all | solution.py:87
  54.7 0.1 constant_dynamic-slice_fusion.1
  54.8 0.6 fusion.71
  59.8 0.1 stack.40
  60.0 0.1 broadcast_bitcast_fusion
  60.0 4.5 %collective-permute-start.5 = (bf16[2,128,1024]{1,2,0:T(8,128)(2,1)}, bf16[2,128,1024]{1,2,0:T(8,128)(2,1)S(1)}, u32[]{:S(2)}, u32[]{:S(2)}) collective-permute-start(bf16[2,128,1024]{1,2,0:T(8,128)(2,1)} %pad_maximum_fusion), channel_id=1, source_target_pairs={{0,12},{4,16},{8,20},{12,24},{16,28},{20,32},{24,36},{28,40},{32,4... | collective-permute-start | bytes 1572872 | tf_op jit(solution)/shard_map/ppermute | solution.py:16
  64.6 0.7 slice_bitcast_fusion.9
  65.3 13.8 %all-to-all-done = bf16[128,4,256]{2,1,0:T(4,128)(2,1)S(1)} async-done(((bf16[128,4,256]{2,1,0:T(4,128)(2,1)}), bf16[128,4,256]{2,1,0:T(4,128)(2,1)S(1)}, u32[]{:S(2)}, u32[]{:S(2)}) %all-to-all-start) | async-done | bytes 262176 | tf_op jit(solution)/shard_map/all_to_all | solution.py:87
  79.1 0.8 reshape.206
  79.9 0.7 fusion.64
  80.7 24.7 %all-gather.2.cloned.1.call-done = bf16[512,1024]{1,0:T(8,128)(2,1)} async-done(((bf16[512,256]{1,0:T(8,128)(2,1)}), bf16[512,1024]{1,0:T(8,128)(2,1)}) %all-gather.2.cloned.1.call-update) | async-done | bytes 1048592 | tf_op jit(solution)/shard_map/all_gather | solution.py:94
  105.4 1.8 fusion.15
  107.3 1.7 fusion.13
  109.0 0.5 fusion.11
  109.5 0.5 fusion.9
  110.0 0.5 fusion.7
  110.5 0.5 fusion.5
  111.0 0.5 fusion.3
  111.5 0.2 select_reduce_fusion
  111.7 0.4 fusion
  112.1 0.3 copy-done.3
  112.4 0.5 fusion.20
  112.9 0.4 fusion.25
  113.3 0.4 fusion.27
  113.7 0.4 fusion.29
  114.1 0.4 fusion.31
  114.6 0.4 fusion.33
  115.0 0.4 fusion.23
  115.4 1.8 slice_add_fusion
  117.2 1.6 reshape.207
  118.7 1.4 dynamic-slice_convert_fusion
  120.2 0.1 convert_element_type.288
  120.3 3.5 %concatenate.14 = bf16[512,512]{0,1:T(8,128)(2,1)} concatenate(bf16[512,500]{0,1:T(8,128)(2,1)S(1)} %convert_element_type.288, bf16[512,1]{0,1:T(2,128)(2,1)S(1)} %get-tuple-element.32, bf16[512,1]{0,1:T(2,128)(2,1)S(1)} %get-tuple-element.31, bf16[512,1]{0,1:T(2,128)(2,1)S(1)} %get-tuple-element.30, bf16[512,1]{0,1:T(2,128)(2,1)S(1)} %get-tuple-element.33, ...), dimensions={1} | concatenate | bytes 1048576 | tf_op jit(solution)/shard_map/concatenate | solution.py:47
  123.8 2.1 %collective-permute-start.6 = (bf16[512,512]{0,1:T(8,128)(2,1)}, bf16[512,512]{0,1:T(8,128)(2,1)}, u32[]{:S(2)}, u32[]{:S(2)}) collective-permute-start(bf16[512,512]{0,1:T(8,128)(2,1)} %concatenate.14), channel_id=1, source_target_pairs={{0,1},{1,0},{2,3},{3,2},{4,5},{5,4},{6,7},{7,6},{8,9},{9,8},{10,11... | collective-permute-start | bytes 1572872 | tf_op jit(solution)/shard_map/ppermute | solution.py:21
  126.0 0.1 constant_dynamic-slice_fusion
  126.1 0.1 reshape.208
  126.2 1.8 collective-permute-done.6
  127.9 0.9 fusion.46
  128.8 1.2 multiply_add_fusion
  130.1 0.1 reshape.209
  130.2 0.1 concatenate.15
  130.4 2.5 %collective-permute-start.7 = (bf16[512,256]{0,1:T(8,128)(2,1)S(1)}, bf16[512,256]{0,1:T(8,128)(2,1)S(1)}, u32[]{:S(2)}, u32[]{:S(2)}) collective-permute-start(bf16[512,256]{0,1:T(8,128)(2,1)S(1)} %concatenate.15), channel_id=1, source_target_pairs={{0,2},{1,3},{2,0},{3,1},{4,6},{5,7},{6,4},{7,5},{8,10},{9,11},{10,... | collective-permute-start | bytes 786440 | tf_op jit(solution)/shard_map/ppermute | solution.py:21
  132.8 9.4 %collective-permute-done.7 = bf16[512,256]{0,1:T(8,128)(2,1)S(1)} collective-permute-done((bf16[512,256]{0,1:T(8,128)(2,1)S(1)}, bf16[512,256]{0,1:T(8,128)(2,1)S(1)}, u32[]{:S(2)}, u32[]{:S(2)}) %collective-permute-start.7) | collective-permute-done | bytes 262176 | tf_op jit(solution)/shard_map/ppermute | solution.py:21
  142.3 0.1 fusion.18
  142.4 0.1 copy.13
  142.5 0.8 reshape.210
  143.3 16.5 %all-to-all-start.1 = ((bf16[128,4,250]{2,1,0:T(4,128)(2,1)}), bf16[128,4,250]{2,1,0:T(4,128)(2,1)S(1)}, u32[]{:S(2)}, u32[]{:S(2)}) async-start(bf16[128,4,250]{2,1,0:T(4,128)(2,1)} %reshape.210), calls=%async_computation.1 | async-start | bytes 524288 | tf_op jit(solution)/shard_map/all_to_all | solution.py:135
  159.8 22.7 %all-to-all-done.1 = bf16[128,4,250]{2,1,0:T(4,128)(2,1)S(1)} async-done(((bf16[128,4,250]{2,1,0:T(4,128)(2,1)}), bf16[128,4,250]{2,1,0:T(4,128)(2,1)S(1)}, u32[]{:S(2)}, u32[]{:S(2)}) %all-to-all-start.1) | async-done | bytes 256032 | tf_op jit(solution)/shard_map/all_to_all | solution.py:135
  182.5 0.2 reshape.211
  182.7 1.8 gather_fusion
  (45 shorter events, 0.4 us)
Async XLA Ops:
  6.5 48.1 %copy-start = (s32[128,7]{0,1:T(8,128)S(1)}, s32[128,7]{0,1:T(8,128)}, u32[]{:S(2)}) copy-start(s32[128,7]{0,1:T(8,128)} %param.8) | copy-start | bytes 10756
  6.5 22.9 %copy-start.4 = (s32[256,1]{0,1:T(1,128)S(1)}, s32[256,1]{0,1:T(1,128)}, u32[]{:S(2)}) copy-start(s32[256,1]{0,1:T(1,128)} %param.7) | copy-start | bytes 3076
  7.7 52.3 %copy-start.5 = (bf16[128]{0:T(256)(128)(2,1)S(1)}, bf16[128]{0:T(256)(128)(2,1)}, u32[]{:S(2)}) copy-start(bf16[128]{0:T(256)(128)(2,1)} %param.11) | copy-start | bytes 772
  9.8 50.2 %collective-permute-start = (bf16[2,128,1024]{1,2,0:T(8,128)(2,1)}, bf16[2,128,1024]{1,2,0:T(8,128)(2,1)S(1)}, u32[]{:S(2)}, u32[]{:S(2)}) collective-permute-start(bf16[2,128,1024]{1,2,0:T(8,128)(2,1)} %pad_maximum_fusion), channel_id=1, source_target_pairs={{0,508},{4,0},{8,4},{12,8},{16,12},{20,16},{24,20},{28,24},{32,28}... | collective-permute-start | bytes 1572872 | tf_op jit(solution)/shard_map/ppermute | solution.py:16
  15.2 49.3 %collective-permute-start.1 = (bf16[2,128,1024]{1,2,0:T(8,128)(2,1)}, bf16[2,128,1024]{1,2,0:T(8,128)(2,1)S(1)}, u32[]{:S(2)}, u32[]{:S(2)}) collective-permute-start(bf16[2,128,1024]{1,2,0:T(8,128)(2,1)} %pad_maximum_fusion), channel_id=1, source_target_pairs={{0,4},{4,8},{8,12},{12,16},{16,20},{20,24},{24,28},{28,32},{32,36}... | collective-permute-start | bytes 1572872 | tf_op jit(solution)/shard_map/ppermute | solution.py:16
  17.1 47.4 %collective-permute-start.2 = (bf16[2,128,1024]{1,2,0:T(8,128)(2,1)}, bf16[2,128,1024]{1,2,0:T(8,128)(2,1)S(1)}, u32[]{:S(2)}, u32[]{:S(2)}) collective-permute-start(bf16[2,128,1024]{1,2,0:T(8,128)(2,1)} %pad_maximum_fusion), channel_id=1, source_target_pairs={{0,504},{4,508},{8,0},{12,4},{16,8},{20,12},{24,16},{28,20},{32,24... | collective-permute-start | bytes 1572872 | tf_op jit(solution)/shard_map/ppermute | solution.py:16
  20.1 60.4 %collective-permute-start.3 = (bf16[2,128,1024]{1,2,0:T(8,128)(2,1)}, bf16[2,128,1024]{1,2,0:T(8,128)(2,1)S(1)}, u32[]{:S(2)}, u32[]{:S(2)}) collective-permute-start(bf16[2,128,1024]{1,2,0:T(8,128)(2,1)} %pad_maximum_fusion), channel_id=1, source_target_pairs={{0,8},{4,12},{8,16},{12,20},{16,24},{20,28},{24,32},{28,36},{32,40... | collective-permute-start | bytes 1572872 | tf_op jit(solution)/shard_map/ppermute | solution.py:16
  23.0 57.6 %collective-permute-start.4 = (bf16[2,128,1024]{1,2,0:T(8,128)(2,1)}, bf16[2,128,1024]{1,2,0:T(8,128)(2,1)S(1)}, u32[]{:S(2)}, u32[]{:S(2)}) collective-permute-start(bf16[2,128,1024]{1,2,0:T(8,128)(2,1)} %pad_maximum_fusion), channel_id=1, source_target_pairs={{0,500},{4,504},{8,508},{12,0},{16,4},{20,8},{24,12},{28,16},{32,2... | collective-permute-start | bytes 1572872 | tf_op jit(solution)/shard_map/ppermute | solution.py:16
  32.7 46.4 %all-to-all-start = ((bf16[128,4,256]{2,1,0:T(4,128)(2,1)}), bf16[128,4,256]{2,1,0:T(4,128)(2,1)S(1)}, u32[]{:S(2)}, u32[]{:S(2)}) async-start(bf16[128,4,256]{2,1,0:T(4,128)(2,1)} %reshape.205), calls=%async_computation | async-start | bytes 524288 | tf_op jit(solution)/shard_map/all_to_all | solution.py:87
  54.6 50.8 %all-gather.2.cloned.1.call-start = ((), (), s32[]{:S(2)}) async-start(), calls=%async_computation.2 | async-start | bytes 1310720 | tf_op jit(solution)/shard_map/all_gather | solution.py:94
  60.0 20.6 %collective-permute-start.5 = (bf16[2,128,1024]{1,2,0:T(8,128)(2,1)}, bf16[2,128,1024]{1,2,0:T(8,128)(2,1)S(1)}, u32[]{:S(2)}, u32[]{:S(2)}) collective-permute-start(bf16[2,128,1024]{1,2,0:T(8,128)(2,1)} %pad_maximum_fusion), channel_id=1, source_target_pairs={{0,12},{4,16},{8,20},{12,24},{16,28},{20,32},{24,36},{28,40},{32,4... | collective-permute-start | bytes 1572872 | tf_op jit(solution)/shard_map/ppermute | solution.py:16
  105.4 3.6 %copy-start.1 = (bf16[512,1024]{1,0:T(8,128)(2,1)S(1)}, bf16[512,1024]{1,0:T(8,128)(2,1)}, u32[]{:S(2)}) copy-start(bf16[512,1024]{1,0:T(8,128)(2,1)} %all-gather.2.cloned.1.call-done) | copy-start | bytes 3145732
  111.5 1.0 copy-start.3
  118.7 7.2 %copy-start.2 = (f32[512,2,2,250]{0,3,2,1:T(8,128)S(1)}, f32[512,2,2,250]{0,3,2,1:T(8,128)}, u32[]{:S(2)}) copy-start(f32[512,2,2,250]{0,3,2,1:T(8,128)} %reshape.207) | copy-start | bytes 6144004
  123.8 4.1 %collective-permute-start.6 = (bf16[512,512]{0,1:T(8,128)(2,1)}, bf16[512,512]{0,1:T(8,128)(2,1)}, u32[]{:S(2)}, u32[]{:S(2)}) collective-permute-start(bf16[512,512]{0,1:T(8,128)(2,1)} %concatenate.14), channel_id=1, source_target_pairs={{0,1},{1,0},{2,3},{3,2},{4,5},{5,4},{6,7},{7,6},{8,9},{9,8},{10,11... | collective-permute-start | bytes 1572872 | tf_op jit(solution)/shard_map/ppermute | solution.py:21
  130.4 11.9 %collective-permute-start.7 = (bf16[512,256]{0,1:T(8,128)(2,1)S(1)}, bf16[512,256]{0,1:T(8,128)(2,1)S(1)}, u32[]{:S(2)}, u32[]{:S(2)}) collective-permute-start(bf16[512,256]{0,1:T(8,128)(2,1)S(1)} %concatenate.15), channel_id=1, source_target_pairs={{0,2},{1,3},{2,0},{3,1},{4,6},{5,7},{6,4},{7,5},{8,10},{9,11},{10,... | collective-permute-start | bytes 786440 | tf_op jit(solution)/shard_map/ppermute | solution.py:21
  143.3 39.2 %all-to-all-start.1 = ((bf16[128,4,250]{2,1,0:T(4,128)(2,1)}), bf16[128,4,250]{2,1,0:T(4,128)(2,1)S(1)}, u32[]{:S(2)}, u32[]{:S(2)}) async-start(bf16[128,4,250]{2,1,0:T(4,128)(2,1)} %reshape.210), calls=%async_computation.1 | async-start | bytes 524288 | tf_op jit(solution)/shard_map/all_to_all | solution.py:135
Sparse Core Ops, SparseCore 0:
  80.0 25.3 all-gather.1

commit v3 on v1

--- a/solution.py
+++ b/solution.py
@@ -3,12 +3,29 @@
 import jax
 import jax.numpy as jnp
 from jax import lax
+from jax.sharding import Mesh
 from jax.sharding import PartitionSpec as P
 
 REACH = 3
 
 
 temper = 2.0
+CLUSTER = ("outer", "inner")
+
+
+def routed(array, forward):
+    outer = lax.axis_size("outer")
+    inner = lax.axis_size("inner")
+    tail = array.shape[1:]
+    grid = array.reshape((outer, inner) + tail)
+    stages = ("inner", "outer") if forward else ("outer", "inner")
+    for axis in stages:
+        if axis == "inner":
+            grid = jnp.swapaxes(grid, 0, 1)
+        grid = lax.all_to_all(grid, axis, split_axis=0, concat_axis=0, tiled=True)
+        if axis == "inner":
+            grid = jnp.swapaxes(grid, 0, 1)
+    return grid.reshape(array.shape)
 
 
 def shifted(array, axis, by):
@@ -60,8 +77,8 @@
 
 
 def body(queries, assign, band_mask, keys, labels, prior):
-    clusters = lax.axis_size("cluster")
-    cluster_index = lax.axis_index("cluster")
+    clusters = lax.axis_size(CLUSTER)
+    cluster_index = lax.axis_index(CLUSTER)
     feat_index = lax.axis_index("feat")
     local_rows = queries.shape[0]
     depth = keys.shape[1]
@@ -78,20 +95,14 @@
     offsets = [0]
     for reach in range(1, REACH + 1):
         offsets += [reach, -reach]
-    blocks = [block] + [shifted(block, "cluster", o) for o in offsets[1:]]
+    blocks = [block] + [shifted(block, CLUSTER, o) for o in offsets[1:]]
 
     target = assign[:, 0]
     onehot = (target[:, None] == jnp.arange(clusters, dtype=jnp.int32)[None, :]).astype(jnp.int32)
     before = jnp.cumsum(onehot, axis=0) - onehot
     position = target * capacity + jnp.sum(before * onehot, axis=1)
     outgoing = jnp.zeros((slots, queries.shape[1]), queries.dtype).at[position].set(queries)
-    arrived = lax.all_to_all(
-        outgoing.reshape(clusters, capacity, queries.shape[1]),
-        "cluster",
-        split_axis=0,
-        concat_axis=0,
-        tiled=True,
-    )
+    arrived = routed(outgoing.reshape(clusters, capacity, queries.shape[1]), True)
     query_full = lax.all_gather(
         arrived.reshape(slots, queries.shape[1]), "feat", axis=1, tiled=True
     )
@@ -127,24 +138,23 @@
     kept, top, total = merge(kept, top, total, message, quarter)
     shares = (kept / total[:, None]).astype(jnp.bfloat16)
 
-    returned = lax.all_to_all(
-        shares.reshape(clusters, capacity, quarter),
-        "cluster",
-        split_axis=0,
-        concat_axis=0,
-        tiled=True,
-    )
+    returned = routed(shares.reshape(clusters, capacity, quarter), False)
     return returned.reshape(slots, quarter)[position]
 
 
 def solution(mesh):
+    clusters = mesh.shape["cluster"]
+    inner = 8 if clusters % 8 == 0 else 1
+    split = Mesh(
+        mesh.devices.reshape(clusters // inner, inner, mesh.shape["feat"]), ("outer", "inner", "feat")
+    )
     in_specs = (
-        P("cluster", "feat"),
-        P("cluster", None),
+        P(CLUSTER, "feat"),
+        P(CLUSTER, None),
         P(),
-        P(("cluster", "feat"), None),
-        P(("cluster", "feat"), None),
-        P(("cluster", "feat")),
+        P(CLUSTER + ("feat",), None),
+        P(CLUSTER + ("feat",), None),
+        P(CLUSTER + ("feat",)),
     )
-    out_specs = P("cluster", "feat")
-    return jax.shard_map(body, mesh=mesh, in_specs=in_specs, out_specs=out_specs, check_vma=False)
+    out_specs = P(CLUSTER, "feat")
+    return jax.shard_map(body, mesh=split, in_specs=in_specs, out_specs=out_specs, check_vma=False)

time: 179 us -> 195 us (1.089)
  the two profiles are of different devices: /device:TPU:32 before, /device:TPU:64 now
where the time goes in v3:
time: 195 us; the launch traced here: 194 us
  starting transfers between devices  59.6 us (31%)
  waiting for transfers between devices  47.1 us (24%)
  local copies, waits for them, and re-layouts  31.7 us (16%)
  blocking collectives  30.7 us (16%)
  between operations  18.1 us (9%)
  matrix products  4.64 us (2%)
  other arithmetic  2.49 us (1%)
    ppermute x6, starting transfers between devices, shifted(): lax.ppermute(array, axis, [(i, (i - by) % peers) for i in range(peers)])  31 us
    all_to_all x1, blocking collectives, routed(): grid = lax.all_to_all(grid, axis, split_axis=0, concat_axis=0, tiled=True)  30.7 us
    all_to_all x3, starting transfers between devices, routed(): grid = lax.all_to_all(grid, axis, split_axis=0, concat_axis=0, tiled=True)  24 us
    all_to_all x3, waiting for transfers between devices, routed(): grid = lax.all_to_all(grid, axis, split_axis=0, concat_axis=0, tiled=True)  19.9 us
    ppermute x6, waiting for transfers between devices, shifted(): lax.ppermute(array, axis, [(i, (i - by) % peers) for i in range(peers)])  11.3 us
    unnamed x18, local copies, waits for them, and re-layouts  10.4 us
    ppermute x2, waiting for transfers between devices, swapped(): return lax.ppermute(array, axis, [(i, i ^ bit) for i in range(peers)])  9.58 us
    all_gather x1, waiting for transfers between devices, body(): lax.all_gather(arrived.reshape(slots, queries.shape[1]), 'feat', axis=1,...  6.28 us
  transfers between devices with their start and end apart: 12, of which 7 were waited for; matrix products, arithmetic and copies ran while one was open for 12% of the time, Pallas kernels for 0%

profile of v3, /device:TPU:64, one launch (start us, length us, event | category | flops | bytes accessed | tf_op | source)
XLA Modules:
  0.0 194.4 jit_solution(8708139541104495941)
XLA Ops:
  6.5 1.1 copy.51
  7.7 0.8 copy.52
  8.5 1.1 concatenate.9
  9.6 5.4 %collective-permute-start = (bf16[128,2048]{1,0:T(8,128)(2,1)S(1)}, bf16[128,2048]{1,0:T(8,128)(2,1)}, u32[]{:S(2)}, u32[]{:S(2)}) collective-permute-start(bf16[128,2048]{1,0:T(8,128)(2,1)S(1)} %concatenate.9), channel_id=1, source_target_pairs={{0,508},{4,0},{8,4},{12,8},{16,12},{20,16},{24,20},{28,24},{32,28}... | collective-permute-start | bytes 1572872 | tf_op jit(solution)/shard_map/ppermute | solution.py:33
  15.0 1.9 collective-permute-start.1
  16.9 3.0 %collective-permute-start.2 = (bf16[128,2048]{1,0:T(8,128)(2,1)S(1)}, bf16[128,2048]{1,0:T(8,128)(2,1)S(1)}, u32[]{:S(2)}, u32[]{:S(2)}) collective-permute-start(bf16[128,2048]{1,0:T(8,128)(2,1)S(1)} %concatenate.9), channel_id=1, source_target_pairs={{0,504},{4,508},{8,0},{12,4},{16,8},{20,12},{24,16},{28,20},{32,24... | collective-permute-start | bytes 1572872 | tf_op jit(solution)/shard_map/ppermute | solution.py:33
  19.9 2.8 %collective-permute-start.3 = (bf16[128,2048]{1,0:T(8,128)(2,1)S(1)}, bf16[128,2048]{1,0:T(8,128)(2,1)S(1)}, u32[]{:S(2)}, u32[]{:S(2)}) collective-permute-start(bf16[128,2048]{1,0:T(8,128)(2,1)S(1)} %concatenate.9), channel_id=1, source_target_pairs={{0,8},{4,12},{8,16},{12,20},{16,24},{20,28},{24,32},{28,36},{32,40... | collective-permute-start | bytes 1572872 | tf_op jit(solution)/shard_map/ppermute | solution.py:33
  22.8 6.4 %collective-permute-start.4 = (bf16[128,2048]{1,0:T(8,128)(2,1)S(1)}, bf16[128,2048]{1,0:T(8,128)(2,1)S(1)}, u32[]{:S(2)}, u32[]{:S(2)}) collective-permute-start(bf16[128,2048]{1,0:T(8,128)(2,1)S(1)} %concatenate.9), channel_id=1, source_target_pairs={{0,500},{4,504},{8,508},{12,0},{16,4},{20,8},{24,12},{28,16},{32,2... | collective-permute-start | bytes 1572872 | tf_op jit(solution)/shard_map/ppermute | solution.py:33
  29.2 0.8 copy.47
  30.0 0.2 fusion.11
  30.3 0.2 fusion.13
  30.5 1.9 scatter_custom_fusion
  32.5 0.8 copy.62
  33.3 4.8 %all-to-all-start = ((bf16[8,16,4,256]{3,2,1,0:T(4,128)(2,1)}), bf16[8,16,4,256]{3,2,1,0:T(4,128)(2,1)S(1)}, u32[]{:S(2)}, u32[]{:S(2)}) async-start(bf16[8,16,4,256]{3,2,1,0:T(4,128)(2,1)} %bitcast.80), calls=%async_computation | async-start | bytes 524288 | tf_op jit(solution)/shard_map/all_to_all | solution.py:25
  38.0 0.8 bitcast_dynamic-update-slice_fusion.6
  38.9 0.1 constant_dynamic-slice_fusion.1
  39.0 0.6 fusion.39
  43.9 0.1 stack.55
  44.0 8.9 %all-to-all-done = bf16[8,16,4,256]{3,2,1,0:T(4,128)(2,1)S(1)} async-done(((bf16[8,16,4,256]{3,2,1,0:T(4,128)(2,1)}), bf16[8,16,4,256]{3,2,1,0:T(4,128)(2,1)S(1)}, u32[]{:S(2)}, u32[]{:S(2)}) %all-to-all-start) | async-done | bytes 262176 | tf_op jit(solution)/shard_map/all_to_all | solution.py:25
  52.9 0.8 copy.50
  53.8 14.9 %all-to-all-start.1 = ((bf16[16,8,4,256]{3,2,1,0:T(4,128)(2,1)}), bf16[16,8,4,256]{3,2,1,0:T(4,128)(2,1)S(1)}, u32[]{:S(2)}, u32[]{:S(2)}) async-start(bf16[16,8,4,256]{3,2,1,0:T(4,128)(2,1)} %copy.50), calls=%async_computation.1 | async-start | bytes 524288 | tf_op jit(solution)/shard_map/all_to_all | solution.py:25
  68.7 0.1 broadcast_bitcast_fusion
  68.8 11.5 %collective-permute-start.5 = (bf16[128,2048]{1,0:T(8,128)(2,1)S(1)}, bf16[128,2048]{1,0:T(8,128)(2,1)}, u32[]{:S(2)}, u32[]{:S(2)}) collective-permute-start(bf16[128,2048]{1,0:T(8,128)(2,1)S(1)} %concatenate.9), channel_id=1, source_target_pairs={{0,12},{4,16},{8,20},{12,24},{16,28},{20,32},{24,36},{28,40},{32,4... | collective-permute-start | bytes 1572872 | tf_op jit(solution)/shard_map/ppermute | solution.py:33
  80.3 1.9 bitcast_dynamic-update-slice_fusion.5
  82.1 0.9 bitcast_dynamic-update-slice_fusion.4
  83.0 3.7 %all-to-all-done.1 = bf16[16,8,4,256]{3,2,1,0:T(4,128)(2,1)S(1)} async-done(((bf16[16,8,4,256]{3,2,1,0:T(4,128)(2,1)}), bf16[16,8,4,256]{3,2,1,0:T(4,128)(2,1)S(1)}, u32[]{:S(2)}, u32[]{:S(2)}) %all-to-all-start.1) | async-done | bytes 262176 | tf_op jit(solution)/shard_map/all_to_all | solution.py:25
  86.7 0.8 reshape_reshape.13
  87.5 0.8 bitcast_dynamic-update-slice_fusion.3
  88.4 0.8 bitcast_dynamic-update-slice_fusion.2
  89.2 0.8 bitcast_dynamic-update-slice_fusion.1
  90.1 11.3 %collective-permute-done.5 = bf16[128,2048]{1,0:T(8,128)(2,1)} collective-permute-done((bf16[128,2048]{1,0:T(8,128)(2,1)S(1)}, bf16[128,2048]{1,0:T(8,128)(2,1)}, u32[]{:S(2)}, u32[]{:S(2)}) %collective-permute-start.5) | collective-permute-done | bytes 524320 | tf_op jit(solution)/shard_map/ppermute | solution.py:33
  101.3 1.9 bitcast_dynamic-update-slice_fusion
  103.2 1.8 slice.116
  105.1 0.8 copy-done.1
  105.9 1.4 slice.114
  107.3 3.0 %reshape.184 = bf16[2,2,250,896]{2,1,0,3:T(2,128)(2,1)} reshape(bf16[1000,896]{0,1:T(8,128)(2,1)S(1)} %bitcast.84) | data formatting | bytes 3584000 | tf_op jit(solution)/shard_map/dot_general | solution.py:124
  110.2 1.2 convert_reduce_fusion
  111.4 6.3 %all-gather.2.cloned.1.call-done = bf16[512,1024]{1,0:T(8,128)(2,1)} async-done(((bf16[512,256]{1,0:T(8,128)(2,1)}), bf16[512,1024]{1,0:T(8,128)(2,1)}) %all-gather.2.cloned.1.call-update) | async-done | bytes 1048592 | tf_op jit(solution)/shard_map/all_gather | solution.py:106
  117.7 3.2 %fusion.40 = (f32[512]{0:T(512)S(1)}, f32[512,896]{1,0:T(8,128)S(1)}) fusion(f32[896]{0:T(1024)S(1)} %bitcast.103, bf16[512,1024]{1,0:T(8,128)(2,1)} %all-gather.2.cloned.1.call-done, bf16[896,1024]{1,0:T(8,128)(2,1)} %bitcast.85, pred[896]{0:T(1024)(128)(4,1)S(1)} %broadcast_bitcast_fusion), kind=kOutput, calls=%fused_computation.95 | convolution fusion | flops 941358592 | bytes 4725120 | tf_op jit(solution)/shard_map/qd,kd->qk/dot_general | solution.py:118
  120.9 0.5 fusion.2
  121.4 1.0 copy-done.2
  122.4 1.4 fusion
  123.8 1.3 copy-done.3
  125.2 0.1 convert_element_type.224
  125.4 0.4 concatenate.10
  125.7 2.2 %collective-permute-start.6 = (bf16[512,512]{0,1:T(8,128)(2,1)S(1)}, bf16[512,512]{0,1:T(8,128)(2,1)S(1)}, u32[]{:S(2)}, u32[]{:S(2)}) collective-permute-start(bf16[512,512]{0,1:T(8,128)(2,1)S(1)} %concatenate.10), channel_id=1, source_target_pairs={{0,1},{1,0},{2,3},{3,2},{4,5},{5,4},{6,7},{7,6},{8,9},{9,8},{10,11... | collective-permute-start | bytes 1572872 | tf_op jit(solution)/shard_map/ppermute | solution.py:38
  127.9 1.3 constant_dynamic-slice_fusion
  129.2 0.1 reshape.164
  129.4 0.2 collective-permute-done.6
  129.6 0.2 multiply_add_fusion
  129.8 0.1 reshape.165
  130.0 0.1 concatenate.11
  130.1 2.5 %collective-permute-start.7 = (bf16[512,256]{0,1:T(8,128)(2,1)S(1)}, bf16[512,256]{0,1:T(8,128)(2,1)S(1)}, u32[]{:S(2)}, u32[]{:S(2)}) collective-permute-start(bf16[512,256]{0,1:T(8,128)(2,1)S(1)} %concatenate.11), channel_id=1, source_target_pairs={{0,2},{1,3},{2,0},{3,1},{4,6},{5,7},{6,4},{7,5},{8,10},{9,11},{10,... | collective-permute-start | bytes 786440 | tf_op jit(solution)/shard_map/ppermute | solution.py:38
  132.6 9.4 %collective-permute-done.7 = bf16[512,256]{0,1:T(8,128)(2,1)S(1)} collective-permute-done((bf16[512,256]{0,1:T(8,128)(2,1)S(1)}, bf16[512,256]{0,1:T(8,128)(2,1)S(1)}, u32[]{:S(2)}, u32[]{:S(2)}) %collective-permute-start.7) | collective-permute-done | bytes 262176 | tf_op jit(solution)/shard_map/ppermute | solution.py:38
  142.0 0.1 fusion.9
  142.1 0.1 copy.54
  142.2 0.1 reshape_reshape.14
  142.3 30.7 %all_to_all.20 = bf16[16,8,4,250]{3,2,1,0:T(4,128)(2,1)S(1)} all-to-all(bf16[16,8,4,250]{3,2,1,0:T(4,128)(2,1)S(1)} %reshape_reshape.14), channel_id=1, replica_groups=mesh['outer'=16,'inner'=8,'feat'=4] {'outer'}, dimensions={0} | all-to-all | bytes 512000 | tf_op jit(solution)/shard_map/all_to_all | solution.py:25
  173.0 0.8 copy.55
  173.8 4.3 %all-to-all-start.3 = ((bf16[8,16,4,250]{3,2,1,0:T(4,128)(2,1)}), bf16[8,16,4,250]{3,2,1,0:T(4,128)(2,1)S(1)}, u32[]{:S(2)}, u32[]{:S(2)}) async-start(bf16[8,16,4,250]{3,2,1,0:T(4,128)(2,1)} %copy.55), calls=%async_computation.3 | async-start | bytes 524288 | tf_op jit(solution)/shard_map/all_to_all | solution.py:25
  178.1 7.3 %all-to-all-done.3 = bf16[8,16,4,250]{3,2,1,0:T(4,128)(2,1)S(1)} async-done(((bf16[8,16,4,250]{3,2,1,0:T(4,128)(2,1)}), bf16[8,16,4,250]{3,2,1,0:T(4,128)(2,1)S(1)}, u32[]{:S(2)}, u32[]{:S(2)}) %all-to-all-start.3) | async-done | bytes 256032 | tf_op jit(solution)/shard_map/all_to_all | solution.py:25
  185.4 0.1 copy.56
  185.5 0.2 reshape_reshape.15
  185.7 1.8 gather_fusion
  (32 shorter events, 0.4 us)
Async XLA Ops:
  6.5 32.4 %copy-start = (s32[128,7]{0,1:T(8,128)S(1)}, s32[128,7]{0,1:T(8,128)}, u32[]{:S(2)}) copy-start(s32[128,7]{0,1:T(8,128)} %param.8) | copy-start | bytes 10756
  6.5 23.7 %copy-start.4 = (s32[256,1]{0,1:T(1,128)S(1)}, s32[256,1]{0,1:T(1,128)}, u32[]{:S(2)}) copy-start(s32[256,1]{0,1:T(1,128)} %param.7) | copy-start | bytes 3076
  9.6 59.2 %collective-permute-start = (bf16[128,2048]{1,0:T(8,128)(2,1)S(1)}, bf16[128,2048]{1,0:T(8,128)(2,1)}, u32[]{:S(2)}, u32[]{:S(2)}) collective-permute-start(bf16[128,2048]{1,0:T(8,128)(2,1)S(1)} %concatenate.9), channel_id=1, source_target_pairs={{0,508},{4,0},{8,4},{12,8},{16,12},{20,16},{24,20},{28,24},{32,28}... | collective-permute-start | bytes 1572872 | tf_op jit(solution)/shard_map/ppermute | solution.py:33
  15.0 67.1 %collective-permute-start.1 = (bf16[128,2048]{1,0:T(8,128)(2,1)S(1)}, bf16[128,2048]{1,0:T(8,128)(2,1)S(1)}, u32[]{:S(2)}, u32[]{:S(2)}) collective-permute-start(bf16[128,2048]{1,0:T(8,128)(2,1)S(1)} %concatenate.9), channel_id=1, source_target_pairs={{0,4},{4,8},{8,12},{12,16},{16,20},{20,24},{24,28},{28,32},{32,36}... | collective-permute-start | bytes 1572872 | tf_op jit(solution)/shard_map/ppermute | solution.py:33
  16.9 70.6 %collective-permute-start.2 = (bf16[128,2048]{1,0:T(8,128)(2,1)S(1)}, bf16[128,2048]{1,0:T(8,128)(2,1)S(1)}, u32[]{:S(2)}, u32[]{:S(2)}) collective-permute-start(bf16[128,2048]{1,0:T(8,128)(2,1)S(1)} %concatenate.9), channel_id=1, source_target_pairs={{0,504},{4,508},{8,0},{12,4},{16,8},{20,12},{24,16},{28,20},{32,24... | collective-permute-start | bytes 1572872 | tf_op jit(solution)/shard_map/ppermute | solution.py:33
  19.9 68.4 %collective-permute-start.3 = (bf16[128,2048]{1,0:T(8,128)(2,1)S(1)}, bf16[128,2048]{1,0:T(8,128)(2,1)S(1)}, u32[]{:S(2)}, u32[]{:S(2)}) collective-permute-start(bf16[128,2048]{1,0:T(8,128)(2,1)S(1)} %concatenate.9), channel_id=1, source_target_pairs={{0,8},{4,12},{8,16},{12,20},{16,24},{20,28},{24,32},{28,36},{32,40... | collective-permute-start | bytes 1572872 | tf_op jit(solution)/shard_map/ppermute | solution.py:33
  22.8 66.4 %collective-permute-start.4 = (bf16[128,2048]{1,0:T(8,128)(2,1)S(1)}, bf16[128,2048]{1,0:T(8,128)(2,1)S(1)}, u32[]{:S(2)}, u32[]{:S(2)}) collective-permute-start(bf16[128,2048]{1,0:T(8,128)(2,1)S(1)} %concatenate.9), channel_id=1, source_target_pairs={{0,500},{4,504},{8,508},{12,0},{16,4},{20,8},{24,12},{28,16},{32,2... | collective-permute-start | bytes 1572872 | tf_op jit(solution)/shard_map/ppermute | solution.py:33
  33.3 19.7 %all-to-all-start = ((bf16[8,16,4,256]{3,2,1,0:T(4,128)(2,1)}), bf16[8,16,4,256]{3,2,1,0:T(4,128)(2,1)S(1)}, u32[]{:S(2)}, u32[]{:S(2)}) async-start(bf16[8,16,4,256]{3,2,1,0:T(4,128)(2,1)} %bitcast.80), calls=%async_computation | async-start | bytes 524288 | tf_op jit(solution)/shard_map/all_to_all | solution.py:25
  53.8 33.0 %all-to-all-start.1 = ((bf16[16,8,4,256]{3,2,1,0:T(4,128)(2,1)}), bf16[16,8,4,256]{3,2,1,0:T(4,128)(2,1)S(1)}, u32[]{:S(2)}, u32[]{:S(2)}) async-start(bf16[16,8,4,256]{3,2,1,0:T(4,128)(2,1)} %copy.50), calls=%async_computation.1 | async-start | bytes 524288 | tf_op jit(solution)/shard_map/all_to_all | solution.py:25
  68.7 49.0 %all-gather.2.cloned.1.call-start = ((), (), s32[]{:S(2)}) async-start(), calls=%async_computation.4 | async-start | bytes 1310720 | tf_op jit(solution)/shard_map/all_gather | solution.py:106
  68.8 32.6 %collective-permute-start.5 = (bf16[128,2048]{1,0:T(8,128)(2,1)S(1)}, bf16[128,2048]{1,0:T(8,128)(2,1)}, u32[]{:S(2)}, u32[]{:S(2)}) collective-permute-start(bf16[128,2048]{1,0:T(8,128)(2,1)S(1)} %concatenate.9), channel_id=1, source_target_pairs={{0,12},{4,16},{8,20},{12,24},{16,28},{20,32},{24,36},{28,40},{32,4... | collective-permute-start | bytes 1572872 | tf_op jit(solution)/shard_map/ppermute | solution.py:33
  103.2 2.6 %copy-start.1 = (bf16[7,128,2048]{2,1,0:T(8,128)(2,1)S(1)}, bf16[7,128,2048]{2,1,0:T(8,128)(2,1)}, u32[]{:S(2)}) copy-start(bf16[7,128,2048]{2,1,0:T(8,128)(2,1)} %bitcast_dynamic-update-slice_fusion) | copy-start | bytes 11010052
  120.9 1.5 copy-start.2
  123.8 1.3 copy-start.3
  125.7 3.8 %collective-permute-start.6 = (bf16[512,512]{0,1:T(8,128)(2,1)S(1)}, bf16[512,512]{0,1:T(8,128)(2,1)S(1)}, u32[]{:S(2)}, u32[]{:S(2)}) collective-permute-start(bf16[512,512]{0,1:T(8,128)(2,1)S(1)} %concatenate.10), channel_id=1, source_target_pairs={{0,1},{1,0},{2,3},{3,2},{4,5},{5,4},{6,7},{7,6},{8,9},{9,8},{10,11... | collective-permute-start | bytes 1572872 | tf_op jit(solution)/shard_map/ppermute | solution.py:38
  130.1 11.9 %collective-permute-start.7 = (bf16[512,256]{0,1:T(8,128)(2,1)S(1)}, bf16[512,256]{0,1:T(8,128)(2,1)S(1)}, u32[]{:S(2)}, u32[]{:S(2)}) collective-permute-start(bf16[512,256]{0,1:T(8,128)(2,1)S(1)} %concatenate.11), channel_id=1, source_target_pairs={{0,2},{1,3},{2,0},{3,1},{4,6},{5,7},{6,4},{7,5},{8,10},{9,11},{10,... | collective-permute-start | bytes 786440 | tf_op jit(solution)/shard_map/ppermute | solution.py:38
  173.8 11.6 %all-to-all-start.3 = ((bf16[8,16,4,250]{3,2,1,0:T(4,128)(2,1)}), bf16[8,16,4,250]{3,2,1,0:T(4,128)(2,1)S(1)}, u32[]{:S(2)}, u32[]{:S(2)}) async-start(bf16[8,16,4,250]{3,2,1,0:T(4,128)(2,1)} %copy.55), calls=%async_computation.3 | async-start | bytes 524288 | tf_op jit(solution)/shard_map/all_to_all | solution.py:25
Sparse Core Ops, SparseCore 0:
  87.7 29.9 all-gather.1

commit v4 on v1

--- a/solution.py
+++ b/solution.py
@@ -63,6 +63,7 @@
     clusters = lax.axis_size("cluster")
     cluster_index = lax.axis_index("cluster")
     feat_index = lax.axis_index("feat")
+    feats = lax.axis_size("feat")
     local_rows = queries.shape[0]
     depth = keys.shape[1]
     classes = labels.shape[1]
@@ -92,9 +93,10 @@
         concat_axis=0,
         tiled=True,
     )
-    query_full = lax.all_gather(
-        arrived.reshape(slots, queries.shape[1]), "feat", axis=1, tiled=True
-    )
+    own = arrived.reshape(slots, queries.shape[1])
+    parts = jnp.stack([own] + [swapped(own, "feat", k) for k in range(1, feats)])
+    order = jnp.arange(feats, dtype=jnp.int32) ^ feat_index
+    query_full = jnp.swapaxes(jnp.take(parts, order, axis=0), 0, 1).reshape(slots, feats * queries.shape[1])
 
     stacked = jnp.stack(blocks)
     band_keys = stacked[:, :, :depth].reshape(len(offsets) * rows, depth)
@@ -112,19 +114,19 @@
     total = jnp.sum(weight, axis=1)
     accum = jnp.dot(weight.astype(jnp.bfloat16), band_labels, preferred_element_type=jnp.float32)
 
-    quarter = classes // 4
-    core = feat_index % 2
-    side = feat_index // 2
-    grid = accum.reshape(slots, 2, 2, quarter)
-    kept = lax.dynamic_index_in_dim(grid, core, axis=2, keepdims=False)
-    sent = lax.dynamic_index_in_dim(grid, 1 - core, axis=2, keepdims=False)
-    message = swapped(pack(sent.reshape(slots, 2 * quarter), top, total, 2 * quarter + 12), "feat", 1)
-    kept, top, total = merge(kept.reshape(slots, 2 * quarter), top, total, message, 2 * quarter)
-    grid = kept.reshape(slots, 2, quarter)
-    kept = lax.dynamic_index_in_dim(grid, side, axis=1, keepdims=False)
-    sent = lax.dynamic_index_in_dim(grid, 1 - side, axis=1, keepdims=False)
-    message = swapped(pack(sent, top, total, quarter + 6), "feat", 2)
-    kept, top, total = merge(kept, top, total, message, quarter)
+    quarter = classes // feats
+    grid = accum.reshape(slots, feats, quarter)
+    kept = lax.dynamic_index_in_dim(grid, feat_index, axis=1, keepdims=False)
+    messages = [
+        swapped(
+            pack(lax.dynamic_index_in_dim(grid, feat_index ^ k, axis=1, keepdims=False), top, total, quarter + 6),
+            "feat",
+            k,
+        )
+        for k in range(1, feats)
+    ]
+    for message in messages:
+        kept, top, total = merge(kept, top, total, message, quarter)
     shares = (kept / total[:, None]).astype(jnp.bfloat16)
 
     returned = lax.all_to_all(

time: 179 us -> 166 us (0.927)
  waiting for transfers between devices: 56.9 us -> 40.1 us
  between operations: 18.2 us -> 4.81 us
  starting transfers between devices: 66.8 us -> 76.6 us
  local copies, waits for them, and re-layouts: 29.4 us -> 33.1 us
  other arithmetic: 2.49 us -> 5.7 us
    ppermute x2 -> x6, starting transfers between devices: 4.62 us -> 18.4 us  [swapped(): return lax.ppermute(array, axis, [(i, i ^ bit) for i in range(peers)])]
    all_gather x1 -> x0, waiting for transfers between devices: 13.3 us -> none  [body(): lax.all_gather(arrived.reshape(slots, queries.shape[1]), 'feat', axis=1,...]
    concatenate x2 -> x3, local copies, waits for them, and re-layouts: 0.48 us -> 6.23 us  [pack(): return jnp.concatenate(columns, axis=1)]
    all_to_all x1, starting transfers between devices: 16.5 us -> 12.5 us  [body(): lax.all_to_all(shares.reshape(clusters, capacity, quarter), 'cluster', sp...]
    all_to_all x1, waiting for transfers between devices: 11.2 us -> 8.67 us  [body(): lax.all_to_all(outgoing.reshape(clusters, capacity, queries.shape[1]), 'c...]
    unnamed x18 -> x19, local copies, waits for them, and re-layouts: 9.28 us -> 8.36 us
    ppermute x2 -> x6, waiting for transfers between devices: 9.57 us -> 8.95 us  [swapped(): return lax.ppermute(array, axis, [(i, i ^ bit) for i in range(peers)])]
  transfers between devices with their start and end apart: 11 -> 14, of which waited for: 5 -> 4; matrix products, arithmetic and copies ran while one was open for 12% -> 14% of each run, Pallas kernels for 0% -> 0%
where the time goes in v4:
time: 166 us; the launch traced here: 165 us
  starting transfers between devices  76.6 us (46%)
  waiting for transfers between devices  40.1 us (24%)
  local copies, waits for them, and re-layouts  33.1 us (20%)
  other arithmetic  5.7 us (3%)
  between operations  4.81 us (3%)
  matrix products  4.27 us (3%)
    ppermute x6, starting transfers between devices, shifted(): lax.ppermute(array, axis, [(i, (i - by) % peers) for i in range(peers)])  23.8 us
    all_to_all x1, waiting for transfers between devices, body(): lax.all_to_all(shares.reshape(clusters, capacity, quarter), 'cluster', sp...  22.5 us
    all_to_all x1, starting transfers between devices, body(): lax.all_to_all(outgoing.reshape(clusters, capacity, queries.shape[1]), 'c...  21.9 us
    ppermute x6, starting transfers between devices, swapped(): return lax.ppermute(array, axis, [(i, i ^ bit) for i in range(peers)])  18.4 us
    all_to_all x1, starting transfers between devices, body(): lax.all_to_all(shares.reshape(clusters, capacity, quarter), 'cluster', sp...  12.5 us
    ppermute x6, waiting for transfers between devices, swapped(): return lax.ppermute(array, axis, [(i, i ^ bit) for i in range(peers)])  8.95 us
    all_to_all x1, waiting for transfers between devices, body(): lax.all_to_all(outgoing.reshape(clusters, capacity, queries.shape[1]), 'c...  8.67 us
    unnamed x19, local copies, waits for them, and re-layouts  8.36 us
  transfers between devices with their start and end apart: 14, of which 4 were waited for; matrix products, arithmetic and copies ran while one was open for 14% of the time, Pallas kernels for 0%

profile of v4, /device:TPU:32, one launch (start us, length us, event | category | flops | bytes accessed | tf_op | source)
XLA Modules:
  0.0 164.7 jit_solution(12092170682655889416)
XLA Ops:
  0.0 1.1 copy.43
  1.2 0.8 copy.44
  1.9 1.1 concatenate.12
  3.1 5.4 %collective-permute-start.3 = (bf16[128,2048]{1,0:T(8,128)(2,1)S(1)}, bf16[128,2048]{1,0:T(8,128)(2,1)S(1)}, u32[]{:S(2)}, u32[]{:S(2)}) collective-permute-start(bf16[128,2048]{1,0:T(8,128)(2,1)S(1)} %concatenate.12), channel_id=1, source_target_pairs={{0,508},{4,0},{8,4},{12,8},{16,12},{20,16},{24,20},{28,24},{32,28}... | collective-permute-start | bytes 1572872 | tf_op jit(solution)/shard_map/ppermute | solution.py:16
  8.5 1.9 %collective-permute-start.4 = (bf16[128,2048]{1,0:T(8,128)(2,1)S(1)}, bf16[128,2048]{1,0:T(8,128)(2,1)S(1)}, u32[]{:S(2)}, u32[]{:S(2)}) collective-permute-start(bf16[128,2048]{1,0:T(8,128)(2,1)S(1)} %concatenate.12), channel_id=1, source_target_pairs={{0,4},{4,8},{8,12},{12,16},{16,20},{20,24},{24,28},{28,32},{32,36}... | collective-permute-start | bytes 1572872 | tf_op jit(solution)/shard_map/ppermute | solution.py:16
  10.4 3.0 %collective-permute-start.5 = (bf16[128,2048]{1,0:T(8,128)(2,1)S(1)}, bf16[128,2048]{1,0:T(8,128)(2,1)S(1)}, u32[]{:S(2)}, u32[]{:S(2)}) collective-permute-start(bf16[128,2048]{1,0:T(8,128)(2,1)S(1)} %concatenate.12), channel_id=1, source_target_pairs={{0,504},{4,508},{8,0},{12,4},{16,8},{20,12},{24,16},{28,20},{32,24... | collective-permute-start | bytes 1572872 | tf_op jit(solution)/shard_map/ppermute | solution.py:16
  13.4 2.8 %collective-permute-start.6 = (bf16[128,2048]{1,0:T(8,128)(2,1)S(1)}, bf16[128,2048]{1,0:T(8,128)(2,1)S(1)}, u32[]{:S(2)}, u32[]{:S(2)}) collective-permute-start(bf16[128,2048]{1,0:T(8,128)(2,1)S(1)} %concatenate.12), channel_id=1, source_target_pairs={{0,8},{4,12},{8,16},{12,20},{16,24},{20,28},{24,32},{28,36},{32,40... | collective-permute-start | bytes 1572872 | tf_op jit(solution)/shard_map/ppermute | solution.py:16
  16.3 6.4 %collective-permute-start.7 = (bf16[128,2048]{1,0:T(8,128)(2,1)S(1)}, bf16[128,2048]{1,0:T(8,128)(2,1)S(1)}, u32[]{:S(2)}, u32[]{:S(2)}) collective-permute-start(bf16[128,2048]{1,0:T(8,128)(2,1)S(1)} %concatenate.12), channel_id=1, source_target_pairs={{0,500},{4,504},{8,508},{12,0},{16,4},{20,8},{24,12},{28,16},{32,2... | collective-permute-start | bytes 1572872 | tf_op jit(solution)/shard_map/ppermute | solution.py:16
  22.6 0.8 copy.40
  23.4 0.2 fusion.14
  23.7 0.2 fusion.16
  23.9 1.9 %scatter_custom_fusion = bf16[512,256]{1,0:T(8,128)(2,1)S(1)} fusion(s32[256]{0:T(256)S(1)} %bitcast.122, bf16[256,256]{1,0:T(8,128)(2,1)} %param.6, bf16[]{:T(256)} %constant.60.clone.1), kind=kCustom, calls=%fused_computation.39 | custom fusion | bytes 262656 | tf_op jit(solution)/shard_map/scatter | solution.py:88
  25.8 0.8 reshape.183
  26.6 21.9 %all-to-all-start = ((bf16[128,4,256]{2,1,0:T(4,128)(2,1)}), bf16[128,4,256]{2,1,0:T(4,128)(2,1)S(1)}, u32[]{:S(2)}, u32[]{:S(2)}) async-start(bf16[128,4,256]{2,1,0:T(4,128)(2,1)} %reshape.183), calls=%async_computation | async-start | bytes 524288 | tf_op jit(solution)/shard_map/all_to_all | solution.py:89
  48.6 0.1 constant_dynamic-slice_fusion.4
  48.7 0.6 fusion.48
  53.7 0.1 stack.67
  53.8 0.1 broadcast_bitcast_fusion
  53.9 0.8 bitcast_dynamic-update-slice_fusion.6
  54.7 4.3 %collective-permute-start.8 = (bf16[128,2048]{1,0:T(8,128)(2,1)S(1)}, bf16[128,2048]{1,0:T(8,128)(2,1)}, u32[]{:S(2)}, u32[]{:S(2)}) collective-permute-start(bf16[128,2048]{1,0:T(8,128)(2,1)S(1)} %concatenate.12), channel_id=1, source_target_pairs={{0,12},{4,16},{8,20},{12,24},{16,28},{20,32},{24,36},{28,40},{32,4... | collective-permute-start | bytes 1572872 | tf_op jit(solution)/shard_map/ppermute | solution.py:16
  59.0 0.8 bitcast_dynamic-update-slice_fusion.5
  59.8 0.8 bitcast_dynamic-update-slice_fusion.4
  60.7 0.8 bitcast_dynamic-update-slice_fusion.3
  61.5 0.8 bitcast_dynamic-update-slice_fusion.2
  62.4 0.8 bitcast_dynamic-update-slice_fusion.1
  63.2 8.7 %all-to-all-done = bf16[128,4,256]{2,1,0:T(4,128)(2,1)S(1)} async-done(((bf16[128,4,256]{2,1,0:T(4,128)(2,1)}), bf16[128,4,256]{2,1,0:T(4,128)(2,1)S(1)}, u32[]{:S(2)}, u32[]{:S(2)}) %all-to-all-start) | async-done | bytes 262176 | tf_op jit(solution)/shard_map/all_to_all | solution.py:89
  71.9 1.9 %collective-permute-start.2 = (bf16[512,256]{1,0:T(8,128)(2,1)S(1)}, bf16[512,256]{1,0:T(8,128)(2,1)S(1)}, u32[]{:S(2)}, u32[]{:S(2)}) collective-permute-start(bf16[512,256]{1,0:T(8,128)(2,1)S(1)} %reshape.184), channel_id=1, source_target_pairs={{0,3},{1,2},{2,1},{3,0},{4,7},{5,6},{6,5},{7,4},{8,11},{9,10},{10,... | collective-permute-start | bytes 786440 | tf_op jit(solution)/shard_map/ppermute | solution.py:21
  73.9 4.6 %collective-permute-start.1 = (bf16[512,256]{1,0:T(8,128)(2,1)S(1)}, bf16[512,256]{1,0:T(8,128)(2,1)S(1)}, u32[]{:S(2)}, u32[]{:S(2)}) collective-permute-start(bf16[512,256]{1,0:T(8,128)(2,1)S(1)} %reshape.184), channel_id=1, source_target_pairs={{0,2},{1,3},{2,0},{3,1},{4,6},{5,7},{6,4},{7,5},{8,10},{9,11},{10,... | collective-permute-start | bytes 786440 | tf_op jit(solution)/shard_map/ppermute | solution.py:21
  78.5 2.5 %collective-permute-start = (bf16[512,256]{1,0:T(8,128)(2,1)S(1)}, bf16[512,256]{1,0:T(8,128)(2,1)}, u32[]{:S(2)}, u32[]{:S(2)}) collective-permute-start(bf16[512,256]{1,0:T(8,128)(2,1)S(1)} %reshape.184), channel_id=1, source_target_pairs={{0,1},{1,0},{2,3},{3,2},{4,5},{5,4},{6,7},{7,6},{8,9},{9,8},{10,11... | collective-permute-start | bytes 786440 | tf_op jit(solution)/shard_map/ppermute | solution.py:21
  81.1 1.9 %bitcast_dynamic-update-slice_fusion = bf16[7,128,2048]{2,1,0:T(8,128)(2,1)} fusion(bf16[7,128,2048]{2,1,0:T(8,128)(2,1)} %bitcast_dynamic-update-slice_fusion.1, bf16[128,2048]{1,0:T(8,128)(2,1)} %collective-permute-done.8), kind=kLoop, calls=%fused_computation.20 | loop fusion | bytes 1048576 | tf_op jit(solution)/shard_map/stack | solution.py:101
  82.9 1.8 %slice.146 = bf16[7,128,1000]{2,1,0:T(8,128)(2,1)S(1)} slice(bf16[7,128,2048]{2,1,0:T(8,128)(2,1)} %bitcast_dynamic-update-slice_fusion), slice={[0:7], [0:128], [1024:2024]} | slice | bytes 3584000 | tf_op jit(solution)/shard_map/slice | solution.py:103
  84.8 0.8 copy-done.1
  85.5 1.4 slice.144
  86.9 2.7 %reshape.216 = bf16[4,250,896]{1,0,2:T(4,128)(2,1)} reshape(bf16[1000,896]{0,1:T(8,128)(2,1)S(1)} %bitcast.95) | data formatting | bytes 3584000 | tf_op jit(solution)/shard_map/dot_general | solution.py:115
  89.6 1.2 convert_reduce_fusion
  90.9 1.1 pad_maximum_fusion
  92.0 0.6 gather_fusion
  92.6 0.2 select_bitcast_fusion
  92.8 0.5 copy.42
  93.3 2.9 %fusion.49 = (f32[512]{0:T(512)S(1)}, f32[512,896]{1,0:T(8,128)S(1)}) fusion(f32[896]{0:T(1024)S(1)} %bitcast.120, bf16[512,1024]{0,1:T(8,128)(2,1)S(1)} %bitcast.97, bf16[896,1024]{1,0:T(8,128)(2,1)} %bitcast.96, pred[896]{0:T(1024)(128)(4,1)S(1)} %broadcast_bitcast_fusion), kind=kOutput, calls=%fused_computation.113 | convolution fusion | flops 941358592 | bytes 4725120 | tf_op jit(solution)/shard_map/qd,kd->qk/dot_general | solution.py:109
  96.2 0.5 fusion.2
  96.7 1.0 copy-done.2
  97.7 1.4 fusion
  99.1 0.1 constant_dynamic-slice_fusion.1
  99.2 0.1 copy.52
  99.4 2.1 %concatenate.13 = bf16[512,256]{0,1:T(8,128)(2,1)} concatenate(bf16[512,250]{0,1:T(8,128)(2,1)S(1)} %bitcast.98, bf16[512,1]{0,1:T(2,128)(2,1)S(1)} %get-tuple-element.29, bf16[512,1]{0,1:T(2,128)(2,1)S(1)} %get-tuple-element.28, bf16[512,1]{0,1:T(2,128)(2,1)S(1)} %get-tuple-element.27, bf16[512,1]{0,1:T(2,128)(2,1)S(1)} %get-tuple-element.32, ...), dimensions={1} | concatenate | bytes 524288 | tf_op jit(solution)/shard_map/concatenate | solution.py:47
  101.5 1.9 %collective-permute-start.9 = (bf16[512,256]{0,1:T(8,128)(2,1)}, bf16[512,256]{0,1:T(8,128)(2,1)S(1)}, u32[]{:S(2)}, u32[]{:S(2)}) collective-permute-start(bf16[512,256]{0,1:T(8,128)(2,1)} %concatenate.13), channel_id=1, source_target_pairs={{0,1},{1,0},{2,3},{3,2},{4,5},{5,4},{6,7},{7,6},{8,9},{9,8},{10,11... | collective-permute-start | bytes 786440 | tf_op jit(solution)/shard_map/ppermute | solution.py:21
  103.4 0.1 copy.54
  103.5 2.1 %concatenate.15 = bf16[512,256]{0,1:T(8,128)(2,1)} concatenate(bf16[512,250]{0,1:T(8,128)(2,1)S(1)} %bitcast.100, bf16[512,1]{0,1:T(2,128)(2,1)S(1)} %get-tuple-element.29, bf16[512,1]{0,1:T(2,128)(2,1)S(1)} %get-tuple-element.28, bf16[512,1]{0,1:T(2,128)(2,1)S(1)} %get-tuple-element.27, bf16[512,1]{0,1:T(2,128)(2,1)S(1)} %get-tuple-element.32, ...), dimensions={1} | concatenate | bytes 524288 | tf_op jit(solution)/shard_map/concatenate | solution.py:47
  105.6 4.7 %collective-permute-start.11 = (bf16[512,256]{0,1:T(8,128)(2,1)}, bf16[512,256]{0,1:T(8,128)(2,1)}, u32[]{:S(2)}, u32[]{:S(2)}) collective-permute-start(bf16[512,256]{0,1:T(8,128)(2,1)} %concatenate.15), channel_id=1, source_target_pairs={{0,3},{1,2},{2,1},{3,0},{4,7},{5,6},{6,5},{7,4},{8,11},{9,10},{10,... | collective-permute-start | bytes 786440 | tf_op jit(solution)/shard_map/ppermute | solution.py:21
  110.3 0.1 copy.53
  110.5 2.1 %concatenate.14 = bf16[512,256]{0,1:T(8,128)(2,1)} concatenate(bf16[512,250]{0,1:T(8,128)(2,1)S(1)} %bitcast.99, bf16[512,1]{0,1:T(2,128)(2,1)S(1)} %get-tuple-element.29, bf16[512,1]{0,1:T(2,128)(2,1)S(1)} %get-tuple-element.28, bf16[512,1]{0,1:T(2,128)(2,1)S(1)} %get-tuple-element.27, bf16[512,1]{0,1:T(2,128)(2,1)S(1)} %get-tuple-element.32, ...), dimensions={1} | concatenate | bytes 524288 | tf_op jit(solution)/shard_map/concatenate | solution.py:47
  112.6 2.7 %collective-permute-start.10 = (bf16[512,256]{0,1:T(8,128)(2,1)}, bf16[512,256]{0,1:T(8,128)(2,1)}, u32[]{:S(2)}, u32[]{:S(2)}) collective-permute-start(bf16[512,256]{0,1:T(8,128)(2,1)} %concatenate.14), channel_id=1, source_target_pairs={{0,2},{1,3},{2,0},{3,1},{4,6},{5,7},{6,4},{7,5},{8,10},{9,11},{10,... | collective-permute-start | bytes 786440 | tf_op jit(solution)/shard_map/ppermute | solution.py:21
  115.3 0.2 copy.46
  115.6 1.7 %collective-permute-done.11 = bf16[512,256]{0,1:T(8,128)(2,1)} collective-permute-done((bf16[512,256]{0,1:T(8,128)(2,1)}, bf16[512,256]{0,1:T(8,128)(2,1)}, u32[]{:S(2)}, u32[]{:S(2)}) %collective-permute-start.11) | collective-permute-done | bytes 262176 | tf_op jit(solution)/shard_map/ppermute | solution.py:21
  117.3 7.2 %collective-permute-done.10 = bf16[512,256]{0,1:T(8,128)(2,1)} collective-permute-done((bf16[512,256]{0,1:T(8,128)(2,1)}, bf16[512,256]{0,1:T(8,128)(2,1)}, u32[]{:S(2)}, u32[]{:S(2)}) %collective-permute-start.10) | collective-permute-done | bytes 262176 | tf_op jit(solution)/shard_map/ppermute | solution.py:21
  124.5 1.0 fusion.27
  125.5 1.3 fusion.13
  126.8 0.1 copy.50
  126.9 0.8 reshape.188
  127.7 12.5 %all-to-all-start.1 = ((bf16[128,4,250]{2,1,0:T(4,128)(2,1)}), bf16[128,4,250]{2,1,0:T(4,128)(2,1)S(1)}, u32[]{:S(2)}, u32[]{:S(2)}) async-start(bf16[128,4,250]{2,1,0:T(4,128)(2,1)} %reshape.188), calls=%async_computation.1 | async-start | bytes 524288 | tf_op jit(solution)/shard_map/all_to_all | solution.py:132
  140.2 22.5 %all-to-all-done.1 = bf16[128,4,250]{2,1,0:T(4,128)(2,1)S(1)} async-done(((bf16[128,4,250]{2,1,0:T(4,128)(2,1)}), bf16[128,4,250]{2,1,0:T(4,128)(2,1)S(1)}, u32[]{:S(2)}, u32[]{:S(2)}) %all-to-all-start.1) | async-done | bytes 256032 | tf_op jit(solution)/shard_map/all_to_all | solution.py:132
  162.7 0.2 reshape.189
  162.9 1.8 %gather_fusion.1 = bf16[256,250]{1,0:T(8,128)(2,1)} fusion(bf16[512,250]{1,0:T(8,128)(2,1)S(1)} %reshape.189, s32[1024]{0:T(1024)S(1)} %pad_clamp_fusion), kind=kCustom, calls=%fused_computation.1 | custom fusion | bytes 257024 | tf_op jit(solution)/shard_map/gather | solution.py:139
  (33 shorter events, 0.4 us)
Async XLA Ops:
  0.0 48.6 %copy-start = (s32[128,7]{0,1:T(8,128)S(1)}, s32[128,7]{0,1:T(8,128)}, u32[]{:S(2)}) copy-start(s32[128,7]{0,1:T(8,128)} %param.8) | copy-start | bytes 10756
  0.0 23.7 %copy-start.3 = (s32[256,1]{0,1:T(1,128)S(1)}, s32[256,1]{0,1:T(1,128)}, u32[]{:S(2)}) copy-start(s32[256,1]{0,1:T(1,128)} %param.7) | copy-start | bytes 3076
  3.1 51.7 %collective-permute-start.3 = (bf16[128,2048]{1,0:T(8,128)(2,1)S(1)}, bf16[128,2048]{1,0:T(8,128)(2,1)S(1)}, u32[]{:S(2)}, u32[]{:S(2)}) collective-permute-start(bf16[128,2048]{1,0:T(8,128)(2,1)S(1)} %concatenate.12), channel_id=1, source_target_pairs={{0,508},{4,0},{8,4},{12,8},{16,12},{20,16},{24,20},{28,24},{32,28}... | collective-permute-start | bytes 1572872 | tf_op jit(solution)/shard_map/ppermute | solution.py:16
  8.5 51.4 %collective-permute-start.4 = (bf16[128,2048]{1,0:T(8,128)(2,1)S(1)}, bf16[128,2048]{1,0:T(8,128)(2,1)S(1)}, u32[]{:S(2)}, u32[]{:S(2)}) collective-permute-start(bf16[128,2048]{1,0:T(8,128)(2,1)S(1)} %concatenate.12), channel_id=1, source_target_pairs={{0,4},{4,8},{8,12},{12,16},{16,20},{20,24},{24,28},{28,32},{32,36}... | collective-permute-start | bytes 1572872 | tf_op jit(solution)/shard_map/ppermute | solution.py:16
  10.4 50.3 %collective-permute-start.5 = (bf16[128,2048]{1,0:T(8,128)(2,1)S(1)}, bf16[128,2048]{1,0:T(8,128)(2,1)S(1)}, u32[]{:S(2)}, u32[]{:S(2)}) collective-permute-start(bf16[128,2048]{1,0:T(8,128)(2,1)S(1)} %concatenate.12), channel_id=1, source_target_pairs={{0,504},{4,508},{8,0},{12,4},{16,8},{20,12},{24,16},{28,20},{32,24... | collective-permute-start | bytes 1572872 | tf_op jit(solution)/shard_map/ppermute | solution.py:16
  13.4 48.1 %collective-permute-start.6 = (bf16[128,2048]{1,0:T(8,128)(2,1)S(1)}, bf16[128,2048]{1,0:T(8,128)(2,1)S(1)}, u32[]{:S(2)}, u32[]{:S(2)}) collective-permute-start(bf16[128,2048]{1,0:T(8,128)(2,1)S(1)} %concatenate.12), channel_id=1, source_target_pairs={{0,8},{4,12},{8,16},{12,20},{16,24},{20,28},{24,32},{28,36},{32,40... | collective-permute-start | bytes 1572872 | tf_op jit(solution)/shard_map/ppermute | solution.py:16
  16.3 46.1 %collective-permute-start.7 = (bf16[128,2048]{1,0:T(8,128)(2,1)S(1)}, bf16[128,2048]{1,0:T(8,128)(2,1)S(1)}, u32[]{:S(2)}, u32[]{:S(2)}) collective-permute-start(bf16[128,2048]{1,0:T(8,128)(2,1)S(1)} %concatenate.12), channel_id=1, source_target_pairs={{0,500},{4,504},{8,508},{12,0},{16,4},{20,8},{24,12},{28,16},{32,2... | collective-permute-start | bytes 1572872 | tf_op jit(solution)/shard_map/ppermute | solution.py:16
  26.6 45.2 %all-to-all-start = ((bf16[128,4,256]{2,1,0:T(4,128)(2,1)}), bf16[128,4,256]{2,1,0:T(4,128)(2,1)S(1)}, u32[]{:S(2)}, u32[]{:S(2)}) async-start(bf16[128,4,256]{2,1,0:T(4,128)(2,1)} %reshape.183), calls=%async_computation | async-start | bytes 524288 | tf_op jit(solution)/shard_map/all_to_all | solution.py:89
  54.7 26.3 %collective-permute-start.8 = (bf16[128,2048]{1,0:T(8,128)(2,1)S(1)}, bf16[128,2048]{1,0:T(8,128)(2,1)}, u32[]{:S(2)}, u32[]{:S(2)}) collective-permute-start(bf16[128,2048]{1,0:T(8,128)(2,1)S(1)} %concatenate.12), channel_id=1, source_target_pairs={{0,12},{4,16},{8,20},{12,24},{16,28},{20,32},{24,36},{28,40},{32,4... | collective-permute-start | bytes 1572872 | tf_op jit(solution)/shard_map/ppermute | solution.py:16
  71.9 18.9 %collective-permute-start.2 = (bf16[512,256]{1,0:T(8,128)(2,1)S(1)}, bf16[512,256]{1,0:T(8,128)(2,1)S(1)}, u32[]{:S(2)}, u32[]{:S(2)}) collective-permute-start(bf16[512,256]{1,0:T(8,128)(2,1)S(1)} %reshape.184), channel_id=1, source_target_pairs={{0,3},{1,2},{2,1},{3,0},{4,7},{5,6},{6,5},{7,4},{8,11},{9,10},{10,... | collective-permute-start | bytes 786440 | tf_op jit(solution)/shard_map/ppermute | solution.py:21
  73.9 17.0 %collective-permute-start.1 = (bf16[512,256]{1,0:T(8,128)(2,1)S(1)}, bf16[512,256]{1,0:T(8,128)(2,1)S(1)}, u32[]{:S(2)}, u32[]{:S(2)}) collective-permute-start(bf16[512,256]{1,0:T(8,128)(2,1)S(1)} %reshape.184), channel_id=1, source_target_pairs={{0,2},{1,3},{2,0},{3,1},{4,6},{5,7},{6,4},{7,5},{8,10},{9,11},{10,... | collective-permute-start | bytes 786440 | tf_op jit(solution)/shard_map/ppermute | solution.py:21
  78.5 12.4 %collective-permute-start = (bf16[512,256]{1,0:T(8,128)(2,1)S(1)}, bf16[512,256]{1,0:T(8,128)(2,1)}, u32[]{:S(2)}, u32[]{:S(2)}) collective-permute-start(bf16[512,256]{1,0:T(8,128)(2,1)S(1)} %reshape.184), channel_id=1, source_target_pairs={{0,1},{1,0},{2,3},{3,2},{4,5},{5,4},{6,7},{7,6},{8,9},{9,8},{10,11... | collective-permute-start | bytes 786440 | tf_op jit(solution)/shard_map/ppermute | solution.py:21
  82.9 2.6 %copy-start.1 = (bf16[7,128,2048]{2,1,0:T(8,128)(2,1)S(1)}, bf16[7,128,2048]{2,1,0:T(8,128)(2,1)}, u32[]{:S(2)}) copy-start(bf16[7,128,2048]{2,1,0:T(8,128)(2,1)} %bitcast_dynamic-update-slice_fusion) | copy-start | bytes 11010052
  96.2 1.5 copy-start.2
  101.5 14.1 %collective-permute-start.9 = (bf16[512,256]{0,1:T(8,128)(2,1)}, bf16[512,256]{0,1:T(8,128)(2,1)S(1)}, u32[]{:S(2)}, u32[]{:S(2)}) collective-permute-start(bf16[512,256]{0,1:T(8,128)(2,1)} %concatenate.13), channel_id=1, source_target_pairs={{0,1},{1,0},{2,3},{3,2},{4,5},{5,4},{6,7},{7,6},{8,9},{9,8},{10,11... | collective-permute-start | bytes 786440 | tf_op jit(solution)/shard_map/ppermute | solution.py:21
  105.6 11.7 %collective-permute-start.11 = (bf16[512,256]{0,1:T(8,128)(2,1)}, bf16[512,256]{0,1:T(8,128)(2,1)}, u32[]{:S(2)}, u32[]{:S(2)}) collective-permute-start(bf16[512,256]{0,1:T(8,128)(2,1)} %concatenate.15), channel_id=1, source_target_pairs={{0,3},{1,2},{2,1},{3,0},{4,7},{5,6},{6,5},{7,4},{8,11},{9,10},{10,... | collective-permute-start | bytes 786440 | tf_op jit(solution)/shard_map/ppermute | solution.py:21
  112.6 11.9 %collective-permute-start.10 = (bf16[512,256]{0,1:T(8,128)(2,1)}, bf16[512,256]{0,1:T(8,128)(2,1)}, u32[]{:S(2)}, u32[]{:S(2)}) collective-permute-start(bf16[512,256]{0,1:T(8,128)(2,1)} %concatenate.14), channel_id=1, source_target_pairs={{0,2},{1,3},{2,0},{3,1},{4,6},{5,7},{6,4},{7,5},{8,10},{9,11},{10,... | collective-permute-start | bytes 786440 | tf_op jit(solution)/shard_map/ppermute | solution.py:21
  127.7 35.0 %all-to-all-start.1 = ((bf16[128,4,250]{2,1,0:T(4,128)(2,1)}), bf16[128,4,250]{2,1,0:T(4,128)(2,1)S(1)}, u32[]{:S(2)}, u32[]{:S(2)}) async-start(bf16[128,4,250]{2,1,0:T(4,128)(2,1)} %reshape.188), calls=%async_computation.1 | async-start | bytes 524288 | tf_op jit(solution)/shard_map/all_to_all | solution.py:132

commit v5 on v4

--- a/solution.py
+++ b/solution.py
@@ -38,20 +38,10 @@
     return (hi + mid) + lo
 
 
-def pack(part, top, total, width):
-    rows = part.shape[0]
-    codes = split3(top) + split3(total)
-    columns = [part.astype(jnp.bfloat16)] + [c[:, None] for c in codes]
-    pad = width - part.shape[1] - len(codes)
-    columns.append(jnp.zeros((rows, pad), jnp.bfloat16))
-    return jnp.concatenate(columns, axis=1)
-
-
 def merge(kept, top, total, message, width):
-    other = message[:, :width].astype(jnp.float32)
-    codes = [message[:, width + i] for i in range(6)]
-    other_top = join3(codes[:3])
-    other_total = join3(codes[3:])
+    other = message.astype(jnp.float32)
+    other_top = join3([other[:, width + i] for i in range(3)])
+    other_total = join3([other[:, width + 3 + i] for i in range(3)])
     highest = jnp.maximum(top, other_top)
     mine = jnp.exp(top - highest)
     theirs = jnp.exp(other_top - highest)
@@ -71,11 +61,11 @@
     capacity = 2 * local_rows // clusters
     slots = clusters * capacity
 
-    width = depth + classes + 1
-    padded = -(-width // 128) * 128
-    block = jnp.concatenate(
-        [keys, labels, prior[:, None], jnp.zeros((rows, padded - width), keys.dtype)], axis=1
-    )
+    quarter = classes // feats
+    group = -(-(quarter + 6) // 128) * 128
+    grouped = jnp.pad(labels.reshape(rows, feats, quarter), ((0, 0), (0, 0), (0, group - quarter)))
+    grouped = grouped.at[:, 0, quarter].set(prior)
+    block = jnp.stack([keys, grouped.reshape(rows, feats * group)])
     offsets = [0]
     for reach in range(1, REACH + 1):
         offsets += [reach, -reach]
@@ -98,10 +88,9 @@
     order = jnp.arange(feats, dtype=jnp.int32) ^ feat_index
     query_full = jnp.swapaxes(jnp.take(parts, order, axis=0), 0, 1).reshape(slots, feats * queries.shape[1])
 
-    stacked = jnp.stack(blocks)
-    band_keys = stacked[:, :, :depth].reshape(len(offsets) * rows, depth)
-    band_labels = stacked[:, :, depth : depth + classes].reshape(len(offsets) * rows, classes)
-    band_prior = stacked[:, :, depth + classes].reshape(len(offsets) * rows)
+    band_keys = jnp.stack([b[0] for b in blocks]).reshape(len(offsets) * rows, depth)
+    band_labels = jnp.stack([b[1] for b in blocks]).reshape(len(offsets) * rows, feats * group)
+    band_prior = band_labels[:, quarter]
     mask_row = band_mask[cluster_index]
     live_blocks = jnp.stack([mask_row[REACH + o] > 0 for o in offsets])
     live = jnp.repeat(live_blocks, rows)
@@ -114,19 +103,20 @@
     total = jnp.sum(weight, axis=1)
     accum = jnp.dot(weight.astype(jnp.bfloat16), band_labels, preferred_element_type=jnp.float32)
 
-    quarter = classes // feats
-    grid = accum.reshape(slots, feats, quarter)
-    kept = lax.dynamic_index_in_dim(grid, feat_index, axis=1, keepdims=False)
-    messages = [
-        swapped(
-            pack(lax.dynamic_index_in_dim(grid, feat_index ^ k, axis=1, keepdims=False), top, total, quarter + 6),
-            "feat",
-            k,
-        )
-        for k in range(1, feats)
-    ]
+    column = lax.broadcasted_iota(jnp.int32, (slots, group), 1)
+    codes = split3(top) + split3(total)
+
+    def pack(g):
+        part = lax.dynamic_slice_in_dim(accum, g * group, group, axis=1)
+        for i, c in enumerate(codes):
+            part = jnp.where(column == quarter + i, c.astype(jnp.float32)[:, None], part)
+        return part.astype(jnp.bfloat16)
+
+    kept = lax.dynamic_slice_in_dim(accum, feat_index * group, group, axis=1)
+    messages = [swapped(pack(feat_index ^ k), "feat", k) for k in range(1, feats)]
     for message in messages:
         kept, top, total = merge(kept, top, total, message, quarter)
+    kept = kept[:, :quarter]
     shares = (kept / total[:, None]).astype(jnp.bfloat16)
 
     returned = lax.all_to_all(

time: 166 us -> 164 us (0.988)
  local copies, waits for them, and re-layouts: 33.1 us -> 21.2 us
  waiting for transfers between devices: 40.1 us -> 49 us
  other arithmetic: 5.7 us -> 7.58 us
    ppermute x6, waiting for transfers between devices: 8.95 us -> 17.7 us  [swapped(): return lax.ppermute(array, axis, [(i, i ^ bit) for i in range(peers)])]
    concatenate x4 -> x0, local copies, waits for them, and re-layouts: 7.33 us -> none  [the longest x3 6.23 us: pack(): return jnp.concatenate(columns, axis=1)]
    another operation x3 -> x7, other arithmetic: 0.25 us -> 4.25 us
    dot_general x1 -> x0, local copies, waits for them, and re-layouts: 2.7 us -> none  [body(): jnp.dot(weight.astype(jnp.bfloat16), band_labels, preferred_element_type=...]
    slice x2 -> x1, local copies, waits for them, and re-layouts: 3.23 us -> 1.06 us  [body(): band_prior = band_labels[:, quarter]]
    convert_element_type x1 -> x6, other arithmetic: 0.01 us -> 1.95 us  [the longest x1 1.77 us: pack(): return part.astype(jnp.bfloat16)]
    unnamed x19 -> x16, local copies, waits for them, and re-layouts: 8.36 us -> 8.34 us
  transfers between devices with their start and end apart: 14 -> 14, of which waited for: 4 -> 6; matrix products, arithmetic and copies ran while one was open for 14% -> 8% of each run, Pallas kernels for 0% -> 0%
where the time goes in v5:
time: 164 us; the launch traced here: 163 us
  starting transfers between devices  76.3 us (47%)
  waiting for transfers between devices  49 us (30%)
  local copies, waits for them, and re-layouts  21.2 us (13%)
  other arithmetic  7.58 us (5%)
  between operations  4.77 us (3%)
  matrix products  4.36 us (3%)
    ppermute x6, starting transfers between devices, shifted(): lax.ppermute(array, axis, [(i, (i - by) % peers) for i in range(peers)])  23.8 us
    all_to_all x1, waiting for transfers between devices, body(): lax.all_to_all(shares.reshape(clusters, capacity, quarter), 'cluster', sp...  23.8 us
    all_to_all x1, starting transfers between devices, body(): lax.all_to_all(outgoing.reshape(clusters, capacity, queries.shape[1]), 'c...  21.9 us
    ppermute x6, starting transfers between devices, swapped(): return lax.ppermute(array, axis, [(i, i ^ bit) for i in range(peers)])  18.2 us
    ppermute x6, waiting for transfers between devices, swapped(): return lax.ppermute(array, axis, [(i, i ^ bit) for i in range(peers)])  17.7 us
    all_to_all x1, starting transfers between devices, body(): lax.all_to_all(shares.reshape(clusters, capacity, quarter), 'cluster', sp...  12.4 us
    unnamed x16, local copies, waits for them, and re-layouts  8.34 us
    all_to_all x1, waiting for transfers between devices, body(): lax.all_to_all(outgoing.reshape(clusters, capacity, queries.shape[1]), 'c...  7.43 us
  transfers between devices with their start and end apart: 14, of which 6 were waited for; matrix products, arithmetic and copies ran while one was open for 8% of the time, Pallas kernels for 0%

profile of v5, /device:TPU:32, one launch (start us, length us, event | category | flops | bytes accessed | tf_op | source)
XLA Modules:
  0.0 163.2 jit_solution(13318312621471434308)
XLA Ops:
  0.0 0.6 fusion.40
  0.7 1.0 reshape.188
  1.7 1.4 and_reduce_fusion
  3.1 2.6 %broadcast_select_fusion = bf16[128,1,1]{0,2,1:T(2,128)(2,1)S(1)} fusion(pred[]{:T(512)} %and_reduce_fusion, s32[]{:T(128)} %bitcast.23, s32[]{:T(128)} %bitcast.24, bf16[128]{0:T(256)(128)(2,1)} %param.13, bf16[128,4,250]{0,2,1:T(8,128)(2,1)S(1)} %reshape.188), kind=kLoop, calls=%fused_computation.111 | loop fusion | flops 128 | bytes 256521 | tf_op jit(solution)/shard_map/select.1
  5.7 1.3 scatter.13
  6.9 0.1 copy.30
  7.1 0.1 pad_maximum_fusion.1
  7.2 5.4 %collective-permute-start.3 = (bf16[2,128,1024]{2,1,0:T(8,128)(2,1)S(1)}, bf16[2,128,1024]{2,1,0:T(8,128)(2,1)}, u32[]{:S(2)}, u32[]{:S(2)}) collective-permute-start(bf16[2,128,1024]{2,1,0:T(8,128)(2,1)S(1)} %pad_maximum_fusion.1), channel_id=1, source_target_pairs={{0,508},{4,0},{8,4},{12,8},{16,12},{20,16},{24,20},{28,24},{32,28}... | collective-permute-start | bytes 1572872 | tf_op jit(solution)/shard_map/ppermute | solution.py:16
  12.6 1.9 %collective-permute-start.4 = (bf16[2,128,1024]{2,1,0:T(8,128)(2,1)S(1)}, bf16[2,128,1024]{2,1,0:T(8,128)(2,1)}, u32[]{:S(2)}, u32[]{:S(2)}) collective-permute-start(bf16[2,128,1024]{2,1,0:T(8,128)(2,1)S(1)} %pad_maximum_fusion.1), channel_id=1, source_target_pairs={{0,4},{4,8},{8,12},{12,16},{16,20},{20,24},{24,28},{28,32},{32,36}... | collective-permute-start | bytes 1572872 | tf_op jit(solution)/shard_map/ppermute | solution.py:16
  14.5 3.0 %collective-permute-start.5 = (bf16[2,128,1024]{2,1,0:T(8,128)(2,1)S(1)}, bf16[2,128,1024]{2,1,0:T(8,128)(2,1)S(1)}, u32[]{:S(2)}, u32[]{:S(2)}) collective-permute-start(bf16[2,128,1024]{2,1,0:T(8,128)(2,1)S(1)} %pad_maximum_fusion.1), channel_id=1, source_target_pairs={{0,504},{4,508},{8,0},{12,4},{16,8},{20,12},{24,16},{28,20},{32,24... | collective-permute-start | bytes 1572872 | tf_op jit(solution)/shard_map/ppermute | solution.py:16
  17.5 2.8 %collective-permute-start.6 = (bf16[2,128,1024]{2,1,0:T(8,128)(2,1)S(1)}, bf16[2,128,1024]{2,1,0:T(8,128)(2,1)S(1)}, u32[]{:S(2)}, u32[]{:S(2)}) collective-permute-start(bf16[2,128,1024]{2,1,0:T(8,128)(2,1)S(1)} %pad_maximum_fusion.1), channel_id=1, source_target_pairs={{0,8},{4,12},{8,16},{12,20},{16,24},{20,28},{24,32},{28,36},{32,40... | collective-permute-start | bytes 1572872 | tf_op jit(solution)/shard_map/ppermute | solution.py:16
  20.4 6.4 %collective-permute-start.7 = (bf16[2,128,1024]{2,1,0:T(8,128)(2,1)S(1)}, bf16[2,128,1024]{2,1,0:T(8,128)(2,1)S(1)}, u32[]{:S(2)}, u32[]{:S(2)}) collective-permute-start(bf16[2,128,1024]{2,1,0:T(8,128)(2,1)S(1)} %pad_maximum_fusion.1), channel_id=1, source_target_pairs={{0,500},{4,504},{8,508},{12,0},{16,4},{20,8},{24,12},{28,16},{32,2... | collective-permute-start | bytes 1572872 | tf_op jit(solution)/shard_map/ppermute | solution.py:16
  26.8 0.1 copy.27
  26.9 0.2 fusion.12
  27.2 0.2 fusion.14
  27.4 1.9 %scatter_custom_fusion = bf16[512,256]{1,0:T(8,128)(2,1)S(1)} fusion(s32[256]{0:T(256)S(1)} %bitcast.82, bf16[256,256]{1,0:T(8,128)(2,1)} %param.8, bf16[]{:T(256)} %constant.81.clone.1), kind=kCustom, calls=%fused_computation.45 | custom fusion | bytes 262656 | tf_op jit(solution)/shard_map/scatter | solution.py:78
  29.3 0.8 reshape.185
  30.1 21.9 %all-to-all-start = ((bf16[128,4,256]{2,1,0:T(4,128)(2,1)}), bf16[128,4,256]{2,1,0:T(4,128)(2,1)S(1)}, u32[]{:S(2)}, u32[]{:S(2)}) async-start(bf16[128,4,256]{2,1,0:T(4,128)(2,1)} %reshape.185), calls=%async_computation | async-start | bytes 524288 | tf_op jit(solution)/shard_map/all_to_all | solution.py:79
  52.0 0.9 constant_dynamic-update-slice_fusion
  52.9 0.1 constant_dynamic-slice_fusion.1
  53.0 0.6 fusion.39
  57.9 0.1 stack.55
  58.0 0.1 broadcast_bitcast_fusion
  58.2 4.3 %collective-permute-start.8 = (bf16[2,128,1024]{2,1,0:T(8,128)(2,1)S(1)}, bf16[2,128,1024]{2,1,0:T(8,128)(2,1)S(1)}, u32[]{:S(2)}, u32[]{:S(2)}) collective-permute-start(bf16[2,128,1024]{2,1,0:T(8,128)(2,1)S(1)} %pad_maximum_fusion.1), channel_id=1, source_target_pairs={{0,12},{4,16},{8,20},{12,24},{16,28},{20,32},{24,36},{28,40},{32,4... | collective-permute-start | bytes 1572872 | tf_op jit(solution)/shard_map/ppermute | solution.py:16
  62.5 1.9 %slice_dynamic-update-slice_fusion.11 = (bf16[7,128,1024]{2,1,0:T(8,128)(2,1)}, bf16[7,128,1024]{2,1,0:T(8,128)(2,1)}) fusion(bf16[7,128,1024]{2,1,0:T(8,128)(2,1)} %get-tuple-element.58, bf16[2,128,1024]{2,1,0:T(8,128)(2,1)} %collective-permute-done.3, bf16[7,128,1024]{2,1,0:T(8,128)(2,1)} %get-tuple-element.59), kind=kLoop, calls=%fused_computation.37 | loop fusion | bytes 1048576
  64.3 1.9 %slice_dynamic-update-slice_fusion.10 = (bf16[7,128,1024]{2,1,0:T(8,128)(2,1)}, bf16[7,128,1024]{2,1,0:T(8,128)(2,1)}) fusion(bf16[7,128,1024]{2,1,0:T(8,128)(2,1)} %get-tuple-element.39, bf16[2,128,1024]{2,1,0:T(8,128)(2,1)} %collective-permute-done.4, bf16[7,128,1024]{2,1,0:T(8,128)(2,1)} %get-tuple-element.40), kind=kLoop, calls=%fused_computation.36 | loop fusion | bytes 1048576
  66.2 0.9 slice_dynamic-update-slice_fusion.9
  67.1 0.9 slice_dynamic-update-slice_fusion.8
  68.0 0.8 slice_dynamic-update-slice_fusion.7
  68.8 7.4 %all-to-all-done = bf16[128,4,256]{2,1,0:T(4,128)(2,1)S(1)} async-done(((bf16[128,4,256]{2,1,0:T(4,128)(2,1)}), bf16[128,4,256]{2,1,0:T(4,128)(2,1)S(1)}, u32[]{:S(2)}, u32[]{:S(2)}) %all-to-all-start) | async-done | bytes 262176 | tf_op jit(solution)/shard_map/all_to_all | solution.py:79
  76.2 0.1 reshape.186
  76.3 1.9 %collective-permute-start = (bf16[512,256]{1,0:T(8,128)(2,1)S(1)}, bf16[512,256]{1,0:T(8,128)(2,1)S(1)}, u32[]{:S(2)}, u32[]{:S(2)}) collective-permute-start(bf16[512,256]{1,0:T(8,128)(2,1)S(1)} %reshape.186), channel_id=1, source_target_pairs={{0,1},{1,0},{2,3},{3,2},{4,5},{5,4},{6,7},{7,6},{8,9},{9,8},{10,11... | collective-permute-start | bytes 786440 | tf_op jit(solution)/shard_map/ppermute | solution.py:21
  78.2 4.6 %collective-permute-start.1 = (bf16[512,256]{1,0:T(8,128)(2,1)S(1)}, bf16[512,256]{1,0:T(8,128)(2,1)S(1)}, u32[]{:S(2)}, u32[]{:S(2)}) collective-permute-start(bf16[512,256]{1,0:T(8,128)(2,1)S(1)} %reshape.186), channel_id=1, source_target_pairs={{0,2},{1,3},{2,0},{3,1},{4,6},{5,7},{6,4},{7,5},{8,10},{9,11},{10,... | collective-permute-start | bytes 786440 | tf_op jit(solution)/shard_map/ppermute | solution.py:21
  82.9 2.5 %collective-permute-start.2 = (bf16[512,256]{1,0:T(8,128)(2,1)S(1)}, bf16[512,256]{1,0:T(8,128)(2,1)S(1)}, u32[]{:S(2)}, u32[]{:S(2)}) collective-permute-start(bf16[512,256]{1,0:T(8,128)(2,1)S(1)} %reshape.186), channel_id=1, source_target_pairs={{0,3},{1,2},{2,1},{3,0},{4,7},{5,6},{6,5},{7,4},{8,11},{9,10},{10,... | collective-permute-start | bytes 786440 | tf_op jit(solution)/shard_map/ppermute | solution.py:21
  85.4 0.8 slice_dynamic-update-slice_fusion.6
  86.2 1.1 slice.215
  87.3 0.1 copy.39
  87.5 0.1 stack_reshape.6
  87.6 3.2 %collective-permute-done.1 = bf16[512,256]{1,0:T(8,128)(2,1)S(1)} collective-permute-done((bf16[512,256]{1,0:T(8,128)(2,1)S(1)}, bf16[512,256]{1,0:T(8,128)(2,1)S(1)}, u32[]{:S(2)}, u32[]{:S(2)}) %collective-permute-start.1) | collective-permute-done | bytes 262176 | tf_op jit(solution)/shard_map/ppermute | solution.py:21
  90.7 4.8 %collective-permute-done.2 = bf16[512,256]{1,0:T(8,128)(2,1)S(1)} collective-permute-done((bf16[512,256]{1,0:T(8,128)(2,1)S(1)}, bf16[512,256]{1,0:T(8,128)(2,1)S(1)}, u32[]{:S(2)}, u32[]{:S(2)}) %collective-permute-start.2) | collective-permute-done | bytes 262176 | tf_op jit(solution)/shard_map/ppermute | solution.py:21
  95.5 0.1 pad_maximum_fusion
  95.7 0.6 gather_fusion
  96.3 0.2 select_bitcast_fusion
  96.5 0.5 copy.29
  97.0 2.9 %fusion.41 = (f32[512]{0:T(512)S(1)}, f32[512,896]{1,0:T(8,128)S(1)}) fusion(f32[896]{0:T(1024)S(1)} %convert_reduce_fusion, bf16[512,1024]{0,1:T(8,128)(2,1)S(1)} %bitcast.58, bf16[896,1024]{1,0:T(8,128)(2,1)} %bitcast.67, pred[896]{0:T(1024)(128)(4,1)S(1)} %broadcast_bitcast_fusion), kind=kOutput, calls=%fused_computation.117 | convolution fusion | flops 941358592 | bytes 4725120 | tf_op jit(solution)/shard_map/qd,kd->qk/dot_general | solution.py:98
  99.9 0.5 fusion
  100.4 1.0 copy-done.2
  101.4 1.4 fusion.2
  102.9 1.8 %select_convert_fusion.2 = (bf16[512,256]{0,1:T(8,128)(2,1)}, bf16[512,256]{0,1:T(8,128)(2,1)S(1)}, bf16[512,256]{0,1:T(8,128)(2,1)S(1)}) fusion(f32[512,1024]{0,1:T(8,128)S(1)} %fusion.2, s32[]{:T(128)S(6)} %select_n.111, bf16[512]{0:T(512)(128)(2,1)S(1)} %get-tuple-element.53, bf16[512]{0:T(512)(128)(2,1)S(1)} %get-tuple-element.52, ...), kind=kLoop, calls=%fused_computation.24 | loop fusion | flops 2359296 | bytes 1580556 | tf_op jit(solution)/shard_map/convert_element_type | solution.py:113
  104.7 2.1 %collective-permute-start.9 = (bf16[512,256]{0,1:T(8,128)(2,1)}, bf16[512,256]{0,1:T(8,128)(2,1)S(1)}, u32[]{:S(2)}, u32[]{:S(2)}) collective-permute-start(bf16[512,256]{0,1:T(8,128)(2,1)} %get-tuple-element.26), channel_id=1, source_target_pairs={{0,1},{1,0},{2,3},{3,2},{4,5},{5,4},{6,7},{7,6},{8,9},{9,8},{10,11... | collective-permute-start | bytes 786440 | tf_op jit(solution)/shard_map/ppermute | solution.py:21
  106.8 4.6 %collective-permute-start.10 = (bf16[512,256]{0,1:T(8,128)(2,1)S(1)}, bf16[512,256]{0,1:T(8,128)(2,1)S(1)}, u32[]{:S(2)}, u32[]{:S(2)}) collective-permute-start(bf16[512,256]{0,1:T(8,128)(2,1)S(1)} %get-tuple-element.27), channel_id=1, source_target_pairs={{0,2},{1,3},{2,0},{3,1},{4,6},{5,7},{6,4},{7,5},{8,10},{9,11},{10,... | collective-permute-start | bytes 786440 | tf_op jit(solution)/shard_map/ppermute | solution.py:21
  111.5 2.3 %collective-permute-start.11 = (bf16[512,256]{0,1:T(8,128)(2,1)S(1)}, bf16[512,256]{0,1:T(8,128)(2,1)S(1)}, u32[]{:S(2)}, u32[]{:S(2)}) collective-permute-start(bf16[512,256]{0,1:T(8,128)(2,1)S(1)} %get-tuple-element.28), channel_id=1, source_target_pairs={{0,3},{1,2},{2,1},{3,0},{4,7},{5,6},{6,5},{7,4},{8,11},{9,10},{10,... | collective-permute-start | bytes 786440 | tf_op jit(solution)/shard_map/ppermute | solution.py:21
  113.8 0.1 convert_element_type.157
  113.9 5.5 %collective-permute-done.10 = bf16[512,256]{0,1:T(8,128)(2,1)S(1)} collective-permute-done((bf16[512,256]{0,1:T(8,128)(2,1)S(1)}, bf16[512,256]{0,1:T(8,128)(2,1)S(1)}, u32[]{:S(2)}, u32[]{:S(2)}) %collective-permute-start.10) | collective-permute-done | bytes 262176 | tf_op jit(solution)/shard_map/ppermute | solution.py:21
  119.3 0.1 convert_element_type.159
  119.4 4.3 %collective-permute-done.11 = bf16[512,256]{0,1:T(8,128)(2,1)S(1)} collective-permute-done((bf16[512,256]{0,1:T(8,128)(2,1)S(1)}, bf16[512,256]{0,1:T(8,128)(2,1)S(1)}, u32[]{:S(2)}, u32[]{:S(2)}) %collective-permute-start.11) | collective-permute-done | bytes 262176 | tf_op jit(solution)/shard_map/ppermute | solution.py:21
  123.7 0.1 convert_element_type.161
  123.8 0.3 fusion.11
  124.1 0.1 copy.37
  124.2 0.8 reshape.194
  125.0 12.4 %all-to-all-start.1 = ((bf16[128,4,250]{2,1,0:T(4,128)(2,1)}), bf16[128,4,250]{2,1,0:T(4,128)(2,1)S(1)}, u32[]{:S(2)}, u32[]{:S(2)}) async-start(bf16[128,4,250]{2,1,0:T(4,128)(2,1)} %reshape.194), calls=%async_computation.1 | async-start | bytes 524288 | tf_op jit(solution)/shard_map/all_to_all | solution.py:122
  137.4 23.8 %all-to-all-done.1 = bf16[128,4,250]{2,1,0:T(4,128)(2,1)S(1)} async-done(((bf16[128,4,250]{2,1,0:T(4,128)(2,1)}), bf16[128,4,250]{2,1,0:T(4,128)(2,1)S(1)}, u32[]{:S(2)}, u32[]{:S(2)}) %all-to-all-start.1) | async-done | bytes 256032 | tf_op jit(solution)/shard_map/all_to_all | solution.py:122
  161.2 0.2 reshape.195
  161.4 1.8 %gather_fusion.1 = bf16[256,250]{1,0:T(8,128)(2,1)} fusion(bf16[512,250]{1,0:T(8,128)(2,1)S(1)} %reshape.195, s32[1024]{0:T(1024)S(1)} %pad_clamp_fusion), kind=kCustom, calls=%fused_computation.1 | custom fusion | bytes 257024 | tf_op jit(solution)/shard_map/gather | solution.py:129
  (36 shorter events, 0.3 us)
Async XLA Ops:
  0.0 52.9 %copy-start = (s32[128,7]{0,1:T(8,128)S(1)}, s32[128,7]{0,1:T(8,128)}, u32[]{:S(2)}) copy-start(s32[128,7]{0,1:T(8,128)} %param.10) | copy-start | bytes 10756
  0.0 7.1 %copy-start.1 = (bf16[128,1024]{1,0:T(8,128)(2,1)S(1)}, bf16[128,1024]{1,0:T(8,128)(2,1)}, u32[]{:S(2)}) copy-start(bf16[128,1024]{1,0:T(8,128)(2,1)} %param.11) | copy-start | bytes 786436
  0.0 26.7 %copy-start.3 = (s32[256,1]{0,1:T(1,128)S(1)}, s32[256,1]{0,1:T(1,128)}, u32[]{:S(2)}) copy-start(s32[256,1]{0,1:T(1,128)} %param.9) | copy-start | bytes 3076
  7.2 51.0 %collective-permute-start.3 = (bf16[2,128,1024]{2,1,0:T(8,128)(2,1)S(1)}, bf16[2,128,1024]{2,1,0:T(8,128)(2,1)}, u32[]{:S(2)}, u32[]{:S(2)}) collective-permute-start(bf16[2,128,1024]{2,1,0:T(8,128)(2,1)S(1)} %pad_maximum_fusion.1), channel_id=1, source_target_pairs={{0,508},{4,0},{8,4},{12,8},{16,12},{20,16},{24,20},{28,24},{32,28}... | collective-permute-start | bytes 1572872 | tf_op jit(solution)/shard_map/ppermute | solution.py:16
  12.6 51.8 %collective-permute-start.4 = (bf16[2,128,1024]{2,1,0:T(8,128)(2,1)S(1)}, bf16[2,128,1024]{2,1,0:T(8,128)(2,1)}, u32[]{:S(2)}, u32[]{:S(2)}) collective-permute-start(bf16[2,128,1024]{2,1,0:T(8,128)(2,1)S(1)} %pad_maximum_fusion.1), channel_id=1, source_target_pairs={{0,4},{4,8},{8,12},{12,16},{16,20},{20,24},{24,28},{28,32},{32,36}... | collective-permute-start | bytes 1572872 | tf_op jit(solution)/shard_map/ppermute | solution.py:16
  14.5 51.7 %collective-permute-start.5 = (bf16[2,128,1024]{2,1,0:T(8,128)(2,1)S(1)}, bf16[2,128,1024]{2,1,0:T(8,128)(2,1)S(1)}, u32[]{:S(2)}, u32[]{:S(2)}) collective-permute-start(bf16[2,128,1024]{2,1,0:T(8,128)(2,1)S(1)} %pad_maximum_fusion.1), channel_id=1, source_target_pairs={{0,504},{4,508},{8,0},{12,4},{16,8},{20,12},{24,16},{28,20},{32,24... | collective-permute-start | bytes 1572872 | tf_op jit(solution)/shard_map/ppermute | solution.py:16
  17.5 49.6 %collective-permute-start.6 = (bf16[2,128,1024]{2,1,0:T(8,128)(2,1)S(1)}, bf16[2,128,1024]{2,1,0:T(8,128)(2,1)S(1)}, u32[]{:S(2)}, u32[]{:S(2)}) collective-permute-start(bf16[2,128,1024]{2,1,0:T(8,128)(2,1)S(1)} %pad_maximum_fusion.1), channel_id=1, source_target_pairs={{0,8},{4,12},{8,16},{12,20},{16,24},{20,28},{24,32},{28,36},{32,40... | collective-permute-start | bytes 1572872 | tf_op jit(solution)/shard_map/ppermute | solution.py:16
  20.4 47.6 %collective-permute-start.7 = (bf16[2,128,1024]{2,1,0:T(8,128)(2,1)S(1)}, bf16[2,128,1024]{2,1,0:T(8,128)(2,1)S(1)}, u32[]{:S(2)}, u32[]{:S(2)}) collective-permute-start(bf16[2,128,1024]{2,1,0:T(8,128)(2,1)S(1)} %pad_maximum_fusion.1), channel_id=1, source_target_pairs={{0,500},{4,504},{8,508},{12,0},{16,4},{20,8},{24,12},{28,16},{32,2... | collective-permute-start | bytes 1572872 | tf_op jit(solution)/shard_map/ppermute | solution.py:16
  30.1 46.1 %all-to-all-start = ((bf16[128,4,256]{2,1,0:T(4,128)(2,1)}), bf16[128,4,256]{2,1,0:T(4,128)(2,1)S(1)}, u32[]{:S(2)}, u32[]{:S(2)}) async-start(bf16[128,4,256]{2,1,0:T(4,128)(2,1)} %reshape.185), calls=%async_computation | async-start | bytes 524288 | tf_op jit(solution)/shard_map/all_to_all | solution.py:79
  58.2 27.2 %collective-permute-start.8 = (bf16[2,128,1024]{2,1,0:T(8,128)(2,1)S(1)}, bf16[2,128,1024]{2,1,0:T(8,128)(2,1)S(1)}, u32[]{:S(2)}, u32[]{:S(2)}) collective-permute-start(bf16[2,128,1024]{2,1,0:T(8,128)(2,1)S(1)} %pad_maximum_fusion.1), channel_id=1, source_target_pairs={{0,12},{4,16},{8,20},{12,24},{16,28},{20,32},{24,36},{28,40},{32,4... | collective-permute-start | bytes 1572872 | tf_op jit(solution)/shard_map/ppermute | solution.py:16
  76.3 11.3 %collective-permute-start = (bf16[512,256]{1,0:T(8,128)(2,1)S(1)}, bf16[512,256]{1,0:T(8,128)(2,1)S(1)}, u32[]{:S(2)}, u32[]{:S(2)}) collective-permute-start(bf16[512,256]{1,0:T(8,128)(2,1)S(1)} %reshape.186), channel_id=1, source_target_pairs={{0,1},{1,0},{2,3},{3,2},{4,5},{5,4},{6,7},{7,6},{8,9},{9,8},{10,11... | collective-permute-start | bytes 786440 | tf_op jit(solution)/shard_map/ppermute | solution.py:21
  78.2 12.5 %collective-permute-start.1 = (bf16[512,256]{1,0:T(8,128)(2,1)S(1)}, bf16[512,256]{1,0:T(8,128)(2,1)S(1)}, u32[]{:S(2)}, u32[]{:S(2)}) collective-permute-start(bf16[512,256]{1,0:T(8,128)(2,1)S(1)} %reshape.186), channel_id=1, source_target_pairs={{0,2},{1,3},{2,0},{3,1},{4,6},{5,7},{6,4},{7,5},{8,10},{9,11},{10,... | collective-permute-start | bytes 786440 | tf_op jit(solution)/shard_map/ppermute | solution.py:21
  82.9 12.7 %collective-permute-start.2 = (bf16[512,256]{1,0:T(8,128)(2,1)S(1)}, bf16[512,256]{1,0:T(8,128)(2,1)S(1)}, u32[]{:S(2)}, u32[]{:S(2)}) collective-permute-start(bf16[512,256]{1,0:T(8,128)(2,1)S(1)} %reshape.186), channel_id=1, source_target_pairs={{0,3},{1,2},{2,1},{3,0},{4,7},{5,6},{6,5},{7,4},{8,11},{9,10},{10,... | collective-permute-start | bytes 786440 | tf_op jit(solution)/shard_map/ppermute | solution.py:21
  99.9 1.5 copy-start.2
  104.7 9.1 %collective-permute-start.9 = (bf16[512,256]{0,1:T(8,128)(2,1)}, bf16[512,256]{0,1:T(8,128)(2,1)S(1)}, u32[]{:S(2)}, u32[]{:S(2)}) collective-permute-start(bf16[512,256]{0,1:T(8,128)(2,1)} %get-tuple-element.26), channel_id=1, source_target_pairs={{0,1},{1,0},{2,3},{3,2},{4,5},{5,4},{6,7},{7,6},{8,9},{9,8},{10,11... | collective-permute-start | bytes 786440 | tf_op jit(solution)/shard_map/ppermute | solution.py:21
  106.8 12.5 %collective-permute-start.10 = (bf16[512,256]{0,1:T(8,128)(2,1)S(1)}, bf16[512,256]{0,1:T(8,128)(2,1)S(1)}, u32[]{:S(2)}, u32[]{:S(2)}) collective-permute-start(bf16[512,256]{0,1:T(8,128)(2,1)S(1)} %get-tuple-element.27), channel_id=1, source_target_pairs={{0,2},{1,3},{2,0},{3,1},{4,6},{5,7},{6,4},{7,5},{8,10},{9,11},{10,... | collective-permute-start | bytes 786440 | tf_op jit(solution)/shard_map/ppermute | solution.py:21
  111.5 12.2 %collective-permute-start.11 = (bf16[512,256]{0,1:T(8,128)(2,1)S(1)}, bf16[512,256]{0,1:T(8,128)(2,1)S(1)}, u32[]{:S(2)}, u32[]{:S(2)}) collective-permute-start(bf16[512,256]{0,1:T(8,128)(2,1)S(1)} %get-tuple-element.28), channel_id=1, source_target_pairs={{0,3},{1,2},{2,1},{3,0},{4,7},{5,6},{6,5},{7,4},{8,11},{9,10},{10,... | collective-permute-start | bytes 786440 | tf_op jit(solution)/shard_map/ppermute | solution.py:21
  125.0 36.2 %all-to-all-start.1 = ((bf16[128,4,250]{2,1,0:T(4,128)(2,1)}), bf16[128,4,250]{2,1,0:T(4,128)(2,1)S(1)}, u32[]{:S(2)}, u32[]{:S(2)}) async-start(bf16[128,4,250]{2,1,0:T(4,128)(2,1)} %reshape.194), calls=%async_computation.1 | async-start | bytes 524288 | tf_op jit(solution)/shard_map/all_to_all | solution.py:122

commit v6 on v5

--- a/solution.py
+++ b/solution.py
@@ -63,8 +63,11 @@
 
     quarter = classes // feats
     group = -(-(quarter + 6) // 128) * 128
-    grouped = jnp.pad(labels.reshape(rows, feats, quarter), ((0, 0), (0, 0), (0, group - quarter)))
-    grouped = grouped.at[:, 0, quarter].set(prior)
+    first = (lax.broadcasted_iota(jnp.int32, (rows, feats, group - quarter), 1) == 0) & (
+        lax.broadcasted_iota(jnp.int32, (rows, feats, group - quarter), 2) == 0
+    )
+    spare = jnp.where(first, prior[:, None, None], jnp.zeros((), prior.dtype))
+    grouped = jnp.concatenate([labels.reshape(rows, feats, quarter), spare], axis=2)
     block = jnp.stack([keys, grouped.reshape(rows, feats * group)])
     offsets = [0]
     for reach in range(1, REACH + 1):
@@ -84,9 +87,10 @@
         tiled=True,
     )
     own = arrived.reshape(slots, queries.shape[1])
-    parts = jnp.stack([own] + [swapped(own, "feat", k) for k in range(1, feats)])
-    order = jnp.arange(feats, dtype=jnp.int32) ^ feat_index
-    query_full = jnp.swapaxes(jnp.take(parts, order, axis=0), 0, 1).reshape(slots, feats * queries.shape[1])
+    parts = lax.all_to_all(
+        jnp.broadcast_to(own[None], (feats,) + own.shape), "feat", split_axis=0, concat_axis=0, tiled=True
+    )
+    query_full = jnp.swapaxes(parts, 0, 1).reshape(slots, feats * queries.shape[1])
 
     band_keys = jnp.stack([b[0] for b in blocks]).reshape(len(offsets) * rows, depth)
     band_labels = jnp.stack([b[1] for b in blocks]).reshape(len(offsets) * rows, feats * group)
@@ -113,8 +117,10 @@
         return part.astype(jnp.bfloat16)
 
     kept = lax.dynamic_slice_in_dim(accum, feat_index * group, group, axis=1)
-    messages = [swapped(pack(feat_index ^ k), "feat", k) for k in range(1, feats)]
-    for message in messages:
+    outbox = jnp.stack([pack(g) for g in range(feats)])
+    inbox = lax.all_to_all(outbox, "feat", split_axis=0, concat_axis=0, tiled=True)
+    for k in range(1, feats):
+        message = lax.dynamic_index_in_dim(inbox, feat_index ^ k, axis=0, keepdims=False)
         kept, top, total = merge(kept, top, total, message, quarter)
     kept = kept[:, :quarter]
     shares = (kept / total[:, None]).astype(jnp.bfloat16)

time: 164 us -> 160 us (0.976)
  starting transfers between devices: 76.3 us -> 65.5 us
  waiting for transfers between devices: 49 us -> 59.3 us
  other arithmetic: 7.58 us -> 5.29 us
    all_to_all x0 -> x2, waiting for transfers between devices: none -> 27.1 us  [the longest x1 15.9 us: body(): lax.all_to_all(outbox, 'feat', split_axis=0, concat_axis=0, tiled=True)]
    ppermute x6 -> x0, starting transfers between devices: 18.2 us -> none  [swapped(): return lax.ppermute(array, axis, [(i, i ^ bit) for i in range(peers)])]
    ppermute x6 -> x0, waiting for transfers between devices: 17.7 us -> none  [swapped(): return lax.ppermute(array, axis, [(i, i ^ bit) for i in range(peers)])]
    all_to_all x0 -> x2, starting transfers between devices: none -> 7.51 us  [the longest x1 4 us: body(): lax.all_to_all(jnp.broadcast_to(own[None], (feats,) + own.shape), 'feat',...]
    another operation x7 -> x5, other arithmetic: 4.33 us -> 2.23 us  [the longest x2 1.97 us: body(): outbox = jnp.stack([pack(g) for g in range(feats)])]
    all_to_all x1, waiting for transfers between devices: 7.43 us -> 9.26 us  [body(): lax.all_to_all(outgoing.reshape(clusters, capacity, queries.shape[1]), 'c...]
    convert_element_type x1 -> x0, other arithmetic: 1.77 us -> none  [pack(): return part.astype(jnp.bfloat16)]
  transfers between devices with their start and end apart: 14 -> 10, of which waited for: 6 -> 4; matrix products, arithmetic and copies ran while one was open for 8% -> 10% of each run, Pallas kernels for 0% -> 0%
where the time goes in v6:
time: 160 us; the launch traced here: 159 us
  starting transfers between devices  65.5 us (41%)
  waiting for transfers between devices  59.3 us (37%)
  local copies, waits for them, and re-layouts  20.3 us (13%)
  other arithmetic  5.29 us (3%)
  between operations  4.6 us (3%)
  matrix products  4.35 us (3%)
    ppermute x6, starting transfers between devices, shifted(): lax.ppermute(array, axis, [(i, (i - by) % peers) for i in range(peers)])  23.8 us
    all_to_all x1, waiting for transfers between devices, body(): lax.all_to_all(shares.reshape(clusters, capacity, quarter), 'cluster', sp...  22.9 us
    all_to_all x1, starting transfers between devices, body(): lax.all_to_all(outgoing.reshape(clusters, capacity, queries.shape[1]), 'c...  21.9 us
    all_to_all x1, waiting for transfers between devices, body(): lax.all_to_all(outbox, 'feat', split_axis=0, concat_axis=0, tiled=True)  15.9 us
    all_to_all x1, starting transfers between devices, body(): lax.all_to_all(shares.reshape(clusters, capacity, quarter), 'cluster', sp...  12.2 us
    all_to_all x1, waiting for transfers between devices, body(): lax.all_to_all(jnp.broadcast_to(own[None], (feats,) + own.shape), 'feat',...  11.2 us
    all_to_all x1, waiting for transfers between devices, body(): lax.all_to_all(outgoing.reshape(clusters, capacity, queries.shape[1]), 'c...  9.26 us
    unnamed x16, local copies, waits for them, and re-layouts  8.35 us
  transfers between devices with their start and end apart: 10, of which 4 were waited for; matrix products, arithmetic and copies ran while one was open for 10% of the time, Pallas kernels for 0%

profile of v6, /device:TPU:32, one launch (start us, length us, event | category | flops | bytes accessed | tf_op | source)
XLA Modules:
  0.0 159.3 jit_solution(12107093720195952577)
XLA Ops:
  0.0 0.0 copy-start
  0.0 0.0 copy-start.3
  0.0 1.0 reshape.133
  1.1 0.7 and_select_fusion
  1.8 0.0 copy-start.1
  1.8 0.1 copy.21
  2.0 1.0 pad_maximum_fusion.1
  3.0 5.4 %collective-permute-start = (bf16[2,128,1024]{2,1,0:T(8,128)(2,1)S(1)}, bf16[2,128,1024]{2,1,0:T(8,128)(2,1)}, u32[]{:S(2)}, u32[]{:S(2)}) collective-permute-start(bf16[2,128,1024]{2,1,0:T(8,128)(2,1)S(1)} %pad_maximum_fusion.1), channel_id=1, source_target_pairs={{0,508},{4,0},{8,4},{12,8},{16,12},{20,16},{24,20},{28,24},{32,28}... | collective-permute-start | bytes 1572872 | tf_op jit(solution)/shard_map/ppermute | solution.py:16
  8.4 1.9 %collective-permute-start.1 = (bf16[2,128,1024]{2,1,0:T(8,128)(2,1)S(1)}, bf16[2,128,1024]{2,1,0:T(8,128)(2,1)}, u32[]{:S(2)}, u32[]{:S(2)}) collective-permute-start(bf16[2,128,1024]{2,1,0:T(8,128)(2,1)S(1)} %pad_maximum_fusion.1), channel_id=1, source_target_pairs={{0,4},{4,8},{8,12},{12,16},{16,20},{20,24},{24,28},{28,32},{32,36}... | collective-permute-start | bytes 1572872 | tf_op jit(solution)/shard_map/ppermute | solution.py:16
  10.3 3.0 %collective-permute-start.2 = (bf16[2,128,1024]{2,1,0:T(8,128)(2,1)S(1)}, bf16[2,128,1024]{2,1,0:T(8,128)(2,1)S(1)}, u32[]{:S(2)}, u32[]{:S(2)}) collective-permute-start(bf16[2,128,1024]{2,1,0:T(8,128)(2,1)S(1)} %pad_maximum_fusion.1), channel_id=1, source_target_pairs={{0,504},{4,508},{8,0},{12,4},{16,8},{20,12},{24,16},{28,20},{32,24... | collective-permute-start | bytes 1572872 | tf_op jit(solution)/shard_map/ppermute | solution.py:16
  13.3 2.8 %collective-permute-start.3 = (bf16[2,128,1024]{2,1,0:T(8,128)(2,1)S(1)}, bf16[2,128,1024]{2,1,0:T(8,128)(2,1)S(1)}, u32[]{:S(2)}, u32[]{:S(2)}) collective-permute-start(bf16[2,128,1024]{2,1,0:T(8,128)(2,1)S(1)} %pad_maximum_fusion.1), channel_id=1, source_target_pairs={{0,8},{4,12},{8,16},{12,20},{16,24},{20,28},{24,32},{28,36},{32,40... | collective-permute-start | bytes 1572872 | tf_op jit(solution)/shard_map/ppermute | solution.py:16
  16.2 6.4 %collective-permute-start.4 = (bf16[2,128,1024]{2,1,0:T(8,128)(2,1)S(1)}, bf16[2,128,1024]{2,1,0:T(8,128)(2,1)S(1)}, u32[]{:S(2)}, u32[]{:S(2)}) collective-permute-start(bf16[2,128,1024]{2,1,0:T(8,128)(2,1)S(1)} %pad_maximum_fusion.1), channel_id=1, source_target_pairs={{0,500},{4,504},{8,508},{12,0},{16,4},{20,8},{24,12},{28,16},{32,2... | collective-permute-start | bytes 1572872 | tf_op jit(solution)/shard_map/ppermute | solution.py:16
  22.6 0.0 copy-done.3
  22.6 0.1 copy.18
  22.7 0.2 fusion.40
  23.0 0.2 fusion.42
  23.2 1.9 %scatter_custom_fusion = bf16[512,256]{1,0:T(8,128)(2,1)S(1)} fusion(s32[256]{0:T(256)S(1)} %bitcast.87, bf16[256,256]{1,0:T(8,128)(2,1)} %param.6, bf16[]{:T(256)} %constant.28.clone.1), kind=kCustom, calls=%fused_computation.76 | custom fusion | bytes 262656 | tf_op jit(solution)/shard_map/scatter | solution.py:81
  25.1 0.8 reshape.131
  25.9 21.9 %all-to-all-start = ((bf16[128,4,256]{2,1,0:T(4,128)(2,1)}), bf16[128,4,256]{2,1,0:T(4,128)(2,1)S(1)}, u32[]{:S(2)}, u32[]{:S(2)}) async-start(bf16[128,4,256]{2,1,0:T(4,128)(2,1)} %reshape.131), calls=%async_computation | async-start | bytes 524288 | tf_op jit(solution)/shard_map/all_to_all | solution.py:82
  47.8 0.0 copy-done.1
  47.8 0.9 constant_dynamic-update-slice_fusion
  48.7 0.0 copy-done
  48.7 0.1 constant_dynamic-slice_fusion
  48.8 0.6 fusion.66
  53.7 0.1 stack.58
  53.8 0.1 broadcast_bitcast_fusion
  53.9 0.0 collective-permute-done
  53.9 4.3 %collective-permute-start.5 = (bf16[2,128,1024]{2,1,0:T(8,128)(2,1)S(1)}, bf16[2,128,1024]{2,1,0:T(8,128)(2,1)}, u32[]{:S(2)}, u32[]{:S(2)}) collective-permute-start(bf16[2,128,1024]{2,1,0:T(8,128)(2,1)S(1)} %pad_maximum_fusion.1), channel_id=1, source_target_pairs={{0,12},{4,16},{8,20},{12,24},{16,28},{20,32},{24,36},{28,40},{32,4... | collective-permute-start | bytes 1572872 | tf_op jit(solution)/shard_map/ppermute | solution.py:16
  58.2 1.9 %slice_dynamic-update-slice_fusion.11 = (bf16[7,128,1024]{2,1,0:T(8,128)(2,1)}, bf16[7,128,1024]{2,1,0:T(8,128)(2,1)}) fusion(bf16[7,128,1024]{2,1,0:T(8,128)(2,1)} %get-tuple-element.48, bf16[2,128,1024]{2,1,0:T(8,128)(2,1)} %collective-permute-done, bf16[7,128,1024]{2,1,0:T(8,128)(2,1)} %get-tuple-element.49), kind=kLoop, calls=%fused_computation.64 | loop fusion | bytes 1048576
  60.0 0.0 collective-permute-done.1
  60.0 1.9 %slice_dynamic-update-slice_fusion.10 = (bf16[7,128,1024]{2,1,0:T(8,128)(2,1)}, bf16[7,128,1024]{2,1,0:T(8,128)(2,1)}) fusion(bf16[7,128,1024]{2,1,0:T(8,128)(2,1)} %get-tuple-element.31, bf16[2,128,1024]{2,1,0:T(8,128)(2,1)} %collective-permute-done.1, bf16[7,128,1024]{2,1,0:T(8,128)(2,1)} %get-tuple-element.32), kind=kLoop, calls=%fused_computation.63 | loop fusion | bytes 1048576
  61.9 0.0 collective-permute-done.2
  61.9 0.8 slice_dynamic-update-slice_fusion.9
  62.8 9.3 %all-to-all-done = bf16[128,4,256]{2,1,0:T(4,128)(2,1)S(1)} async-done(((bf16[128,4,256]{2,1,0:T(4,128)(2,1)}), bf16[128,4,256]{2,1,0:T(4,128)(2,1)S(1)}, u32[]{:S(2)}, u32[]{:S(2)}) %all-to-all-start) | async-done | bytes 262176 | tf_op jit(solution)/shard_map/all_to_all | solution.py:82
  72.0 0.1 broadcast_in_dim.167
  72.1 0.1 copy.20
  72.3 1.1 broadcast_in_dim.168
  73.3 4.0 %all-to-all-start.1 = ((bf16[4,512,256]{1,2,0:T(8,128)(2,1)}), bf16[4,512,256]{1,2,0:T(8,128)(2,1)S(1)}, u32[]{:S(2)}, u32[]{:S(2)}) async-start(bf16[4,512,256]{1,2,0:T(8,128)(2,1)} %broadcast_in_dim.168), calls=%async_computation.1 | async-start | bytes 2097152 | tf_op jit(solution)/shard_map/all_to_all | solution.py:90
  77.3 0.0 collective-permute-done.3
  77.3 0.9 slice_dynamic-update-slice_fusion.8
  78.2 0.0 collective-permute-done.4
  78.2 0.8 slice_dynamic-update-slice_fusion.7
  79.0 0.0 collective-permute-done.5
  79.0 1.9 %slice_dynamic-update-slice_fusion.6 = (bf16[7,128,1024]{2,1,0:T(8,128)(2,1)}, bf16[7,128,1024]{2,1,0:T(8,128)(2,1)}) fusion(bf16[7,128,1024]{2,1,0:T(8,128)(2,1)} %get-tuple-element.23, bf16[2,128,1024]{2,1,0:T(8,128)(2,1)} %collective-permute-done.5, bf16[7,128,1024]{2,1,0:T(8,128)(2,1)} %get-tuple-element.24), kind=kLoop, calls=%fused_computation.59 | loop fusion | bytes 1048576 | tf_op jit(solution)/shard_map/stack | solution.py:95
  80.9 1.1 slice.186
  82.0 0.1 copy.31
  82.1 11.2 %all-to-all-done.1 = bf16[4,512,256]{1,2,0:T(8,128)(2,1)S(1)} async-done(((bf16[4,512,256]{1,2,0:T(8,128)(2,1)}), bf16[4,512,256]{1,2,0:T(8,128)(2,1)S(1)}, u32[]{:S(2)}, u32[]{:S(2)}) %all-to-all-start.1) | async-done | bytes 1048608 | tf_op jit(solution)/shard_map/all_to_all | solution.py:90
  93.3 2.9 %fusion.67 = (f32[512]{0:T(512)S(1)}, f32[512,896]{1,0:T(8,128)S(1)}) fusion(f32[896]{0:T(1024)S(1)} %convert_reduce_fusion, bf16[512,1024]{0,1:T(8,128)(2,1)S(1)} %bitcast.65, bf16[896,1024]{1,0:T(8,128)(2,1)} %bitcast.72, pred[896]{0:T(1024)(128)(4,1)S(1)} %broadcast_bitcast_fusion), kind=kOutput, calls=%fused_computation.141 | convolution fusion | flops 941358592 | bytes 4725120 | tf_op jit(solution)/shard_map/qd,kd->qk/dot_general | solution.py:102
  96.2 0.0 copy-start.2
  96.2 0.5 fusion
  96.7 1.0 copy-done.2
  97.7 1.4 fusion.2
  99.2 0.9 fusion.36
  100.1 1.1 pad_maximum_fusion
  101.2 3.5 %all-to-all-start.2 = ((bf16[4,512,256]{1,2,0:T(8,128)(2,1)}), bf16[4,512,256]{1,2,0:T(8,128)(2,1)S(1)}, u32[]{:S(2)}, u32[]{:S(2)}) async-start(bf16[4,512,256]{1,2,0:T(8,128)(2,1)} %pad_maximum_fusion), calls=%async_computation.2 | async-start | bytes 2097152 | tf_op jit(solution)/shard_map/all_to_all | solution.py:121
  104.7 15.9 %all-to-all-done.2 = bf16[4,512,256]{1,2,0:T(8,128)(2,1)S(1)} async-done(((bf16[4,512,256]{1,2,0:T(8,128)(2,1)}), bf16[4,512,256]{1,2,0:T(8,128)(2,1)S(1)}, u32[]{:S(2)}, u32[]{:S(2)}) %all-to-all-start.2) | async-done | bytes 1048608 | tf_op jit(solution)/shard_map/all_to_all | solution.py:121
  120.6 0.2 bitcast_convert_fusion.2
  120.9 0.3 fusion.35
  121.2 0.1 copy.29
  121.3 0.8 reshape.136
  122.1 12.2 %all-to-all-start.3 = ((bf16[128,4,250]{2,1,0:T(4,128)(2,1)}), bf16[128,4,250]{2,1,0:T(4,128)(2,1)S(1)}, u32[]{:S(2)}, u32[]{:S(2)}) async-start(bf16[128,4,250]{2,1,0:T(4,128)(2,1)} %reshape.136), calls=%async_computation.3 | async-start | bytes 524288 | tf_op jit(solution)/shard_map/all_to_all | solution.py:128
  134.4 22.9 %all-to-all-done.3 = bf16[128,4,250]{2,1,0:T(4,128)(2,1)S(1)} async-done(((bf16[128,4,250]{2,1,0:T(4,128)(2,1)}), bf16[128,4,250]{2,1,0:T(4,128)(2,1)S(1)}, u32[]{:S(2)}, u32[]{:S(2)}) %all-to-all-start.3) | async-done | bytes 256032 | tf_op jit(solution)/shard_map/all_to_all | solution.py:128
  157.3 0.2 reshape.137
  157.5 1.8 %gather_fusion = bf16[256,250]{1,0:T(8,128)(2,1)} fusion(bf16[512,250]{1,0:T(8,128)(2,1)S(1)} %reshape.137, s32[1024]{0:T(1024)S(1)} %pad_clamp_fusion), kind=kCustom, calls=%fused_computation | custom fusion | bytes 257024 | tf_op jit(solution)/shard_map/gather | solution.py:135
  (19 shorter events, 0.2 us)
Async XLA Ops:
  0.0 48.7 %copy-start = (s32[128,7]{0,1:T(8,128)S(1)}, s32[128,7]{0,1:T(8,128)}, u32[]{:S(2)}) copy-start(s32[128,7]{0,1:T(8,128)} %param.8) | copy-start | bytes 10756
  0.0 22.6 %copy-start.3 = (s32[256,1]{0,1:T(1,128)S(1)}, s32[256,1]{0,1:T(1,128)}, u32[]{:S(2)}) copy-start(s32[256,1]{0,1:T(1,128)} %param.7) | copy-start | bytes 3076
  1.8 46.0 %copy-start.1 = (bf16[128,1024]{1,0:T(8,128)(2,1)S(1)}, bf16[128,1024]{1,0:T(8,128)(2,1)}, u32[]{:S(2)}) copy-start(bf16[128,1024]{1,0:T(8,128)(2,1)} %param.9) | copy-start | bytes 786436
  3.0 50.9 %collective-permute-start = (bf16[2,128,1024]{2,1,0:T(8,128)(2,1)S(1)}, bf16[2,128,1024]{2,1,0:T(8,128)(2,1)}, u32[]{:S(2)}, u32[]{:S(2)}) collective-permute-start(bf16[2,128,1024]{2,1,0:T(8,128)(2,1)S(1)} %pad_maximum_fusion.1), channel_id=1, source_target_pairs={{0,508},{4,0},{8,4},{12,8},{16,12},{20,16},{24,20},{28,24},{32,28}... | collective-permute-start | bytes 1572872 | tf_op jit(solution)/shard_map/ppermute | solution.py:16
  8.4 51.7 %collective-permute-start.1 = (bf16[2,128,1024]{2,1,0:T(8,128)(2,1)S(1)}, bf16[2,128,1024]{2,1,0:T(8,128)(2,1)}, u32[]{:S(2)}, u32[]{:S(2)}) collective-permute-start(bf16[2,128,1024]{2,1,0:T(8,128)(2,1)S(1)} %pad_maximum_fusion.1), channel_id=1, source_target_pairs={{0,4},{4,8},{8,12},{12,16},{16,20},{20,24},{24,28},{28,32},{32,36}... | collective-permute-start | bytes 1572872 | tf_op jit(solution)/shard_map/ppermute | solution.py:16
  10.3 51.6 %collective-permute-start.2 = (bf16[2,128,1024]{2,1,0:T(8,128)(2,1)S(1)}, bf16[2,128,1024]{2,1,0:T(8,128)(2,1)S(1)}, u32[]{:S(2)}, u32[]{:S(2)}) collective-permute-start(bf16[2,128,1024]{2,1,0:T(8,128)(2,1)S(1)} %pad_maximum_fusion.1), channel_id=1, source_target_pairs={{0,504},{4,508},{8,0},{12,4},{16,8},{20,12},{24,16},{28,20},{32,24... | collective-permute-start | bytes 1572872 | tf_op jit(solution)/shard_map/ppermute | solution.py:16
  13.3 64.0 %collective-permute-start.3 = (bf16[2,128,1024]{2,1,0:T(8,128)(2,1)S(1)}, bf16[2,128,1024]{2,1,0:T(8,128)(2,1)S(1)}, u32[]{:S(2)}, u32[]{:S(2)}) collective-permute-start(bf16[2,128,1024]{2,1,0:T(8,128)(2,1)S(1)} %pad_maximum_fusion.1), channel_id=1, source_target_pairs={{0,8},{4,12},{8,16},{12,20},{16,24},{20,28},{24,32},{28,36},{32,40... | collective-permute-start | bytes 1572872 | tf_op jit(solution)/shard_map/ppermute | solution.py:16
  16.2 62.0 %collective-permute-start.4 = (bf16[2,128,1024]{2,1,0:T(8,128)(2,1)S(1)}, bf16[2,128,1024]{2,1,0:T(8,128)(2,1)S(1)}, u32[]{:S(2)}, u32[]{:S(2)}) collective-permute-start(bf16[2,128,1024]{2,1,0:T(8,128)(2,1)S(1)} %pad_maximum_fusion.1), channel_id=1, source_target_pairs={{0,500},{4,504},{8,508},{12,0},{16,4},{20,8},{24,12},{28,16},{32,2... | collective-permute-start | bytes 1572872 | tf_op jit(solution)/shard_map/ppermute | solution.py:16
  25.9 46.2 %all-to-all-start = ((bf16[128,4,256]{2,1,0:T(4,128)(2,1)}), bf16[128,4,256]{2,1,0:T(4,128)(2,1)S(1)}, u32[]{:S(2)}, u32[]{:S(2)}) async-start(bf16[128,4,256]{2,1,0:T(4,128)(2,1)} %reshape.131), calls=%async_computation | async-start | bytes 524288 | tf_op jit(solution)/shard_map/all_to_all | solution.py:82
  53.9 25.1 %collective-permute-start.5 = (bf16[2,128,1024]{2,1,0:T(8,128)(2,1)S(1)}, bf16[2,128,1024]{2,1,0:T(8,128)(2,1)}, u32[]{:S(2)}, u32[]{:S(2)}) collective-permute-start(bf16[2,128,1024]{2,1,0:T(8,128)(2,1)S(1)} %pad_maximum_fusion.1), channel_id=1, source_target_pairs={{0,12},{4,16},{8,20},{12,24},{16,28},{20,32},{24,36},{28,40},{32,4... | collective-permute-start | bytes 1572872 | tf_op jit(solution)/shard_map/ppermute | solution.py:16
  73.3 20.0 %all-to-all-start.1 = ((bf16[4,512,256]{1,2,0:T(8,128)(2,1)}), bf16[4,512,256]{1,2,0:T(8,128)(2,1)S(1)}, u32[]{:S(2)}, u32[]{:S(2)}) async-start(bf16[4,512,256]{1,2,0:T(8,128)(2,1)} %broadcast_in_dim.168), calls=%async_computation.1 | async-start | bytes 2097152 | tf_op jit(solution)/shard_map/all_to_all | solution.py:90
  96.2 1.5 copy-start.2
  101.2 19.5 %all-to-all-start.2 = ((bf16[4,512,256]{1,2,0:T(8,128)(2,1)}), bf16[4,512,256]{1,2,0:T(8,128)(2,1)S(1)}, u32[]{:S(2)}, u32[]{:S(2)}) async-start(bf16[4,512,256]{1,2,0:T(8,128)(2,1)} %pad_maximum_fusion), calls=%async_computation.2 | async-start | bytes 2097152 | tf_op jit(solution)/shard_map/all_to_all | solution.py:121
  122.1 35.2 %all-to-all-start.3 = ((bf16[128,4,250]{2,1,0:T(4,128)(2,1)}), bf16[128,4,250]{2,1,0:T(4,128)(2,1)S(1)}, u32[]{:S(2)}, u32[]{:S(2)}) async-start(bf16[128,4,250]{2,1,0:T(4,128)(2,1)} %reshape.136), calls=%async_computation.3 | async-start | bytes 524288 | tf_op jit(solution)/shard_map/all_to_all | solution.py:128

commit v7 on v6

--- a/solution.py
+++ b/solution.py
@@ -72,7 +72,6 @@
     offsets = [0]
     for reach in range(1, REACH + 1):
         offsets += [reach, -reach]
-    blocks = [block] + [shifted(block, "cluster", o) for o in offsets[1:]]
 
     target = assign[:, 0]
     onehot = (target[:, None] == jnp.arange(clusters, dtype=jnp.int32)[None, :]).astype(jnp.int32)
@@ -86,6 +85,8 @@
         concat_axis=0,
         tiled=True,
     )
+    block, arrived = lax.optimization_barrier((block, arrived))
+    blocks = [block] + [shifted(block, "cluster", o) for o in offsets[1:]]
     own = arrived.reshape(slots, queries.shape[1])
     parts = lax.all_to_all(
         jnp.broadcast_to(own[None], (feats,) + own.shape), "feat", split_axis=0, concat_axis=0, tiled=True

time: 160 us -> 183 us (1.14)
  waiting for transfers between devices: 59.3 us -> 82.4 us
    ppermute x6, waiting for transfers between devices: 0.02 us -> 26 us  [shifted(): lax.ppermute(array, axis, [(i, (i - by) % peers) for i in range(peers)])]
    all_to_all x1, waiting for transfers between devices: 11.2 us -> 0.01 us  [body(): lax.all_to_all(jnp.broadcast_to(own[None], (feats,) + own.shape), 'feat',...]
    all_to_all x1, waiting for transfers between devices: 9.26 us -> 17.5 us  [body(): lax.all_to_all(outgoing.reshape(clusters, capacity, queries.shape[1]), 'c...]
    all_to_all x1, starting transfers between devices: 12.2 us -> 19.1 us  [body(): lax.all_to_all(shares.reshape(clusters, capacity, quarter), 'cluster', sp...]
    ppermute x6, starting transfers between devices: 23.8 us -> 19.4 us  [shifted(): lax.ppermute(array, axis, [(i, (i - by) % peers) for i in range(peers)])]
    unnamed x16 -> x18, local copies, waits for them, and re-layouts: 8.35 us -> 8.35 us
  transfers between devices with their start and end apart: 10 -> 10, of which waited for: 4 -> 6; matrix products, arithmetic and copies ran while one was open for 10% -> 6% of each run, Pallas kernels for 0% -> 0%
where the time goes in v7:
time: 183 us; the launch traced here: 182 us
  waiting for transfers between devices  82.4 us (45%)
  starting transfers between devices  66.6 us (36%)
  local copies, waits for them, and re-layouts  18.9 us (10%)
  other arithmetic  5.03 us (3%)
  between operations  4.7 us (3%)
  matrix products  4.37 us (2%)
    ppermute x6, waiting for transfers between devices, shifted(): lax.ppermute(array, axis, [(i, (i - by) % peers) for i in range(peers)])  26 us
    all_to_all x1, waiting for transfers between devices, body(): lax.all_to_all(shares.reshape(clusters, capacity, quarter), 'cluster', sp...  22.9 us
    all_to_all x1, starting transfers between devices, body(): lax.all_to_all(outgoing.reshape(clusters, capacity, queries.shape[1]), 'c...  20.1 us
    ppermute x6, starting transfers between devices, shifted(): lax.ppermute(array, axis, [(i, (i - by) % peers) for i in range(peers)])  19.4 us
    all_to_all x1, starting transfers between devices, body(): lax.all_to_all(shares.reshape(clusters, capacity, quarter), 'cluster', sp...  19.1 us
    all_to_all x1, waiting for transfers between devices, body(): lax.all_to_all(outgoing.reshape(clusters, capacity, queries.shape[1]), 'c...  17.5 us
    all_to_all x1, waiting for transfers between devices, body(): lax.all_to_all(outbox, 'feat', split_axis=0, concat_axis=0, tiled=True)  16 us
    unnamed x18, local copies, waits for them, and re-layouts  8.35 us
  transfers between devices with their start and end apart: 10, of which 6 were waited for; matrix products, arithmetic and copies ran while one was open for 6% of the time, Pallas kernels for 0%

profile of v7, /device:TPU:32, one launch (start us, length us, event | category | flops | bytes accessed | tf_op | source)
XLA Modules:
  0.0 182.1 jit_solution(10381719688241749218)
XLA Ops:
  0.0 0.0 copy-start
  0.0 0.8 copy.18
  0.8 0.2 fusion.40
  1.1 0.0 copy-start.1
  1.2 0.9 fusion.42
  2.0 0.7 compare_select_fusion
  2.7 1.9 %scatter_custom_fusion = bf16[512,256]{1,0:T(8,128)(2,1)S(1)} fusion(s32[256]{0:T(256)S(1)} %bitcast.86, bf16[256,256]{1,0:T(8,128)(2,1)} %param.6, bf16[]{:T(256)} %constant.28.clone.1), kind=kCustom, calls=%fused_computation.78 | custom fusion | bytes 262656 | tf_op jit(solution)/shard_map/scatter | solution.py:80
  4.6 0.8 reshape.132
  5.4 20.1 %all-to-all-start = ((bf16[128,4,256]{2,1,0:T(4,128)(2,1)}), bf16[128,4,256]{2,1,0:T(4,128)(2,1)S(1)}, u32[]{:S(2)}, u32[]{:S(2)}) async-start(bf16[128,4,256]{2,1,0:T(4,128)(2,1)} %reshape.132), calls=%async_computation | async-start | bytes 524288 | tf_op jit(solution)/shard_map/all_to_all | solution.py:81
  25.5 0.0 copy-done.2
  25.5 0.1 reshape.130
  25.6 0.0 copy-done.4
  25.6 0.1 and_select_fusion
  25.7 0.1 copy.17
  25.9 0.0 copy-done
  25.9 0.1 constant_dynamic-slice_fusion
  26.0 0.6 fusion.66
  30.9 0.1 stack.58
  31.0 0.1 pad_maximum_fusion.1
  31.1 0.1 broadcast_bitcast_fusion
  31.2 17.5 %all-to-all-done = bf16[128,4,256]{2,1,0:T(4,128)(2,1)S(1)} async-done(((bf16[128,4,256]{2,1,0:T(4,128)(2,1)}), bf16[128,4,256]{2,1,0:T(4,128)(2,1)S(1)}, u32[]{:S(2)}, u32[]{:S(2)}) %all-to-all-start) | async-done | bytes 262176 | tf_op jit(solution)/shard_map/all_to_all | solution.py:81
  48.6 3.3 %collective-permute-start = (bf16[2,128,1024]{2,1,0:T(8,128)(2,1)S(1)}, bf16[2,128,1024]{2,1,0:T(8,128)(2,1)}, u32[]{:S(2)}, u32[]{:S(2)}) collective-permute-start(bf16[2,128,1024]{2,1,0:T(8,128)(2,1)S(1)} %pad_maximum_fusion.1), channel_id=1, source_target_pairs={{0,508},{4,0},{8,4},{12,8},{16,12},{20,16},{24,20},{28,24},{32,28}... | collective-permute-start | bytes 1572872 | tf_op jit(solution)/shard_map/ppermute | solution.py:16
  52.0 2.5 %collective-permute-start.1 = (bf16[2,128,1024]{2,1,0:T(8,128)(2,1)S(1)}, bf16[2,128,1024]{2,1,0:T(8,128)(2,1)}, u32[]{:S(2)}, u32[]{:S(2)}) collective-permute-start(bf16[2,128,1024]{2,1,0:T(8,128)(2,1)S(1)} %pad_maximum_fusion.1), channel_id=1, source_target_pairs={{0,4},{4,8},{8,12},{12,16},{16,20},{20,24},{24,28},{28,32},{32,36}... | collective-permute-start | bytes 1572872 | tf_op jit(solution)/shard_map/ppermute | solution.py:16
  54.5 4.1 %collective-permute-start.2 = (bf16[2,128,1024]{2,1,0:T(8,128)(2,1)S(1)}, bf16[2,128,1024]{2,1,0:T(8,128)(2,1)S(1)}, u32[]{:S(2)}, u32[]{:S(2)}) collective-permute-start(bf16[2,128,1024]{2,1,0:T(8,128)(2,1)S(1)} %pad_maximum_fusion.1), channel_id=1, source_target_pairs={{0,504},{4,508},{8,0},{12,4},{16,8},{20,12},{24,16},{28,20},{32,24... | collective-permute-start | bytes 1572872 | tf_op jit(solution)/shard_map/ppermute | solution.py:16
  58.6 0.9 slice_dynamic-update-slice_fusion.13
  59.5 1.9 %collective-permute-start.3 = (bf16[2,128,1024]{2,1,0:T(8,128)(2,1)S(1)}, bf16[2,128,1024]{2,1,0:T(8,128)(2,1)S(1)}, u32[]{:S(2)}, u32[]{:S(2)}) collective-permute-start(bf16[2,128,1024]{2,1,0:T(8,128)(2,1)S(1)} %pad_maximum_fusion.1), channel_id=1, source_target_pairs={{0,8},{4,12},{8,16},{12,20},{16,24},{20,28},{24,32},{28,36},{32,40... | collective-permute-start | bytes 1572872 | tf_op jit(solution)/shard_map/ppermute | solution.py:16
  61.4 5.6 %collective-permute-start.4 = (bf16[2,128,1024]{2,1,0:T(8,128)(2,1)S(1)}, bf16[2,128,1024]{2,1,0:T(8,128)(2,1)S(1)}, u32[]{:S(2)}, u32[]{:S(2)}) collective-permute-start(bf16[2,128,1024]{2,1,0:T(8,128)(2,1)S(1)} %pad_maximum_fusion.1), channel_id=1, source_target_pairs={{0,500},{4,504},{8,508},{12,0},{16,4},{20,8},{24,12},{28,16},{32,2... | collective-permute-start | bytes 1572872 | tf_op jit(solution)/shard_map/ppermute | solution.py:16
  67.1 0.1 broadcast_in_dim.169
  67.1 0.1 copy.20
  67.3 1.1 broadcast_in_dim.170
  68.3 4.0 %all-to-all-start.1 = ((bf16[4,512,256]{1,2,0:T(8,128)(2,1)}), bf16[4,512,256]{1,2,0:T(8,128)(2,1)S(1)}, u32[]{:S(2)}, u32[]{:S(2)}) async-start(bf16[4,512,256]{1,2,0:T(8,128)(2,1)} %broadcast_in_dim.170), calls=%async_computation.1 | async-start | bytes 2097152 | tf_op jit(solution)/shard_map/all_to_all | solution.py:91
  72.3 0.0 collective-permute-done
  72.4 1.9 %collective-permute-start.5 = (bf16[2,128,1024]{2,1,0:T(8,128)(2,1)S(1)}, bf16[2,128,1024]{2,1,0:T(8,128)(2,1)S(1)}, u32[]{:S(2)}, u32[]{:S(2)}) collective-permute-start(bf16[2,128,1024]{2,1,0:T(8,128)(2,1)S(1)} %pad_maximum_fusion.1), channel_id=1, source_target_pairs={{0,12},{4,16},{8,20},{12,24},{16,28},{20,32},{24,36},{28,40},{32,4... | collective-permute-start | bytes 1572872 | tf_op jit(solution)/shard_map/ppermute | solution.py:16
  74.3 1.9 %slice_dynamic-update-slice_fusion.11 = (bf16[7,128,1024]{2,1,0:T(8,128)(2,1)}, bf16[7,128,1024]{2,1,0:T(8,128)(2,1)}) fusion(bf16[7,128,1024]{2,1,0:T(8,128)(2,1)} %get-tuple-element.37, bf16[2,128,1024]{2,1,0:T(8,128)(2,1)} %collective-permute-done, bf16[7,128,1024]{2,1,0:T(8,128)(2,1)} %get-tuple-element.38), kind=kLoop, calls=%fused_computation.64 | loop fusion | bytes 1048576
  76.1 0.0 collective-permute-done.1
  76.2 1.9 %slice_dynamic-update-slice_fusion.10 = (bf16[7,128,1024]{2,1,0:T(8,128)(2,1)}, bf16[7,128,1024]{2,1,0:T(8,128)(2,1)}) fusion(bf16[7,128,1024]{2,1,0:T(8,128)(2,1)} %get-tuple-element.35, bf16[2,128,1024]{2,1,0:T(8,128)(2,1)} %collective-permute-done.1, bf16[7,128,1024]{2,1,0:T(8,128)(2,1)} %get-tuple-element.36), kind=kLoop, calls=%fused_computation.63 | loop fusion | bytes 1048576
  78.0 0.0 collective-permute-done.2
  78.0 0.8 slice_dynamic-update-slice_fusion.9
  78.9 2.4 %collective-permute-done.3 = bf16[2,128,1024]{2,1,0:T(8,128)(2,1)S(1)} collective-permute-done((bf16[2,128,1024]{2,1,0:T(8,128)(2,1)S(1)}, bf16[2,128,1024]{2,1,0:T(8,128)(2,1)S(1)}, u32[]{:S(2)}, u32[]{:S(2)}) %collective-permute-start.3) | collective-permute-done | bytes 524320 | tf_op jit(solution)/shard_map/ppermute | solution.py:16
  81.2 0.9 slice_dynamic-update-slice_fusion.8
  82.1 5.8 %collective-permute-done.4 = bf16[2,128,1024]{2,1,0:T(8,128)(2,1)S(1)} collective-permute-done((bf16[2,128,1024]{2,1,0:T(8,128)(2,1)S(1)}, bf16[2,128,1024]{2,1,0:T(8,128)(2,1)S(1)}, u32[]{:S(2)}, u32[]{:S(2)}) %collective-permute-start.4) | collective-permute-done | bytes 524320 | tf_op jit(solution)/shard_map/ppermute | solution.py:16
  87.9 0.8 slice_dynamic-update-slice_fusion.7
  88.7 17.8 %collective-permute-done.5 = bf16[2,128,1024]{2,1,0:T(8,128)(2,1)S(1)} collective-permute-done((bf16[2,128,1024]{2,1,0:T(8,128)(2,1)S(1)}, bf16[2,128,1024]{2,1,0:T(8,128)(2,1)S(1)}, u32[]{:S(2)}, u32[]{:S(2)}) %collective-permute-start.5) | collective-permute-done | bytes 524320 | tf_op jit(solution)/shard_map/ppermute | solution.py:16
  106.6 0.8 slice_dynamic-update-slice_fusion.6
  107.4 1.1 slice.194
  108.5 0.1 copy.29
  108.6 0.0 all-to-all-done.1
  108.6 2.9 %fusion.67 = (f32[512]{0:T(512)S(1)}, f32[512,896]{1,0:T(8,128)S(1)}) fusion(f32[896]{0:T(1024)S(1)} %convert_reduce_fusion, bf16[512,1024]{0,1:T(8,128)(2,1)S(1)} %bitcast.64, bf16[896,1024]{1,0:T(8,128)(2,1)} %bitcast.71, pred[896]{0:T(1024)(128)(4,1)S(1)} %broadcast_bitcast_fusion), kind=kOutput, calls=%fused_computation.141 | convolution fusion | flops 941358592 | bytes 4725120 | tf_op jit(solution)/shard_map/qd,kd->qk/dot_general | solution.py:103
  111.6 0.5 fusion
  112.1 1.0 copy-done.3
  113.1 1.4 fusion.2
  114.5 0.9 fusion.36
  115.4 1.1 pad_maximum_fusion
  116.5 4.0 %all-to-all-start.2 = ((bf16[4,512,256]{1,2,0:T(8,128)(2,1)}), bf16[4,512,256]{1,2,0:T(8,128)(2,1)S(1)}, u32[]{:S(2)}, u32[]{:S(2)}) async-start(bf16[4,512,256]{1,2,0:T(8,128)(2,1)} %pad_maximum_fusion), calls=%async_computation.2 | async-start | bytes 2097152 | tf_op jit(solution)/shard_map/all_to_all | solution.py:122
  120.5 16.0 %all-to-all-done.2 = bf16[4,512,256]{1,2,0:T(8,128)(2,1)S(1)} async-done(((bf16[4,512,256]{1,2,0:T(8,128)(2,1)}), bf16[4,512,256]{1,2,0:T(8,128)(2,1)S(1)}, u32[]{:S(2)}, u32[]{:S(2)}) %all-to-all-start.2) | async-done | bytes 1048608 | tf_op jit(solution)/shard_map/all_to_all | solution.py:122
  136.5 0.2 bitcast_convert_fusion.2
  136.7 0.1 fusion.52
  136.8 0.3 fusion.35
  137.1 0.1 copy.27
  137.2 0.8 reshape.136
  138.0 19.1 %all-to-all-start.3 = ((bf16[128,4,250]{2,1,0:T(4,128)(2,1)}), bf16[128,4,250]{2,1,0:T(4,128)(2,1)S(1)}, u32[]{:S(2)}, u32[]{:S(2)}) async-start(bf16[128,4,250]{2,1,0:T(4,128)(2,1)} %reshape.136), calls=%async_computation.3 | async-start | bytes 524288 | tf_op jit(solution)/shard_map/all_to_all | solution.py:129
  157.1 22.9 %all-to-all-done.3 = bf16[128,4,250]{2,1,0:T(4,128)(2,1)S(1)} async-done(((bf16[128,4,250]{2,1,0:T(4,128)(2,1)}), bf16[128,4,250]{2,1,0:T(4,128)(2,1)S(1)}, u32[]{:S(2)}, u32[]{:S(2)}) %all-to-all-start.3) | async-done | bytes 256032 | tf_op jit(solution)/shard_map/all_to_all | solution.py:129
  180.1 0.2 reshape.137
  180.2 1.8 gather_fusion
  (20 shorter events, 0.2 us)
Async XLA Ops:
  0.0 25.9 %copy-start = (s32[128,7]{0,1:T(8,128)S(1)}, s32[128,7]{0,1:T(8,128)}, u32[]{:S(2)}) copy-start(s32[128,7]{0,1:T(8,128)} %param.8) | copy-start | bytes 10756
  0.0 25.5 %copy-start.2 = (bf16[128,1000]{0,1:T(8,128)(2,1)S(1)}, bf16[128,1000]{0,1:T(8,128)(2,1)}, u32[]{:S(2)}) copy-start(bf16[128,1000]{0,1:T(8,128)(2,1)} %param.10) | copy-start | bytes 768004
  0.0 25.6 %copy-start.4 = (bf16[128]{0:T(256)(128)(2,1)S(1)}, bf16[128]{0:T(256)(128)(2,1)}, u32[]{:S(2)}) copy-start(bf16[128]{0:T(256)(128)(2,1)} %param.11) | copy-start | bytes 772
  1.1 30.0 %copy-start.1 = (bf16[128,1024]{1,0:T(8,128)(2,1)S(1)}, bf16[128,1024]{1,0:T(8,128)(2,1)}, u32[]{:S(2)}) copy-start(bf16[128,1024]{1,0:T(8,128)(2,1)} %param.9) | copy-start | bytes 786436
  5.4 43.3 %all-to-all-start = ((bf16[128,4,256]{2,1,0:T(4,128)(2,1)}), bf16[128,4,256]{2,1,0:T(4,128)(2,1)S(1)}, u32[]{:S(2)}, u32[]{:S(2)}) async-start(bf16[128,4,256]{2,1,0:T(4,128)(2,1)} %reshape.132), calls=%async_computation | async-start | bytes 524288 | tf_op jit(solution)/shard_map/all_to_all | solution.py:81
  48.6 23.7 %collective-permute-start = (bf16[2,128,1024]{2,1,0:T(8,128)(2,1)S(1)}, bf16[2,128,1024]{2,1,0:T(8,128)(2,1)}, u32[]{:S(2)}, u32[]{:S(2)}) collective-permute-start(bf16[2,128,1024]{2,1,0:T(8,128)(2,1)S(1)} %pad_maximum_fusion.1), channel_id=1, source_target_pairs={{0,508},{4,0},{8,4},{12,8},{16,12},{20,16},{24,20},{28,24},{32,28}... | collective-permute-start | bytes 1572872 | tf_op jit(solution)/shard_map/ppermute | solution.py:16
  52.0 24.1 %collective-permute-start.1 = (bf16[2,128,1024]{2,1,0:T(8,128)(2,1)S(1)}, bf16[2,128,1024]{2,1,0:T(8,128)(2,1)}, u32[]{:S(2)}, u32[]{:S(2)}) collective-permute-start(bf16[2,128,1024]{2,1,0:T(8,128)(2,1)S(1)} %pad_maximum_fusion.1), channel_id=1, source_target_pairs={{0,4},{4,8},{8,12},{12,16},{16,20},{20,24},{24,28},{28,32},{32,36}... | collective-permute-start | bytes 1572872 | tf_op jit(solution)/shard_map/ppermute | solution.py:16
  54.5 23.5 %collective-permute-start.2 = (bf16[2,128,1024]{2,1,0:T(8,128)(2,1)S(1)}, bf16[2,128,1024]{2,1,0:T(8,128)(2,1)S(1)}, u32[]{:S(2)}, u32[]{:S(2)}) collective-permute-start(bf16[2,128,1024]{2,1,0:T(8,128)(2,1)S(1)} %pad_maximum_fusion.1), channel_id=1, source_target_pairs={{0,504},{4,508},{8,0},{12,4},{16,8},{20,12},{24,16},{28,20},{32,24... | collective-permute-start | bytes 1572872 | tf_op jit(solution)/shard_map/ppermute | solution.py:16
  59.5 21.7 %collective-permute-start.3 = (bf16[2,128,1024]{2,1,0:T(8,128)(2,1)S(1)}, bf16[2,128,1024]{2,1,0:T(8,128)(2,1)S(1)}, u32[]{:S(2)}, u32[]{:S(2)}) collective-permute-start(bf16[2,128,1024]{2,1,0:T(8,128)(2,1)S(1)} %pad_maximum_fusion.1), channel_id=1, source_target_pairs={{0,8},{4,12},{8,16},{12,20},{16,24},{20,28},{24,32},{28,36},{32,40... | collective-permute-start | bytes 1572872 | tf_op jit(solution)/shard_map/ppermute | solution.py:16
  61.4 26.5 %collective-permute-start.4 = (bf16[2,128,1024]{2,1,0:T(8,128)(2,1)S(1)}, bf16[2,128,1024]{2,1,0:T(8,128)(2,1)S(1)}, u32[]{:S(2)}, u32[]{:S(2)}) collective-permute-start(bf16[2,128,1024]{2,1,0:T(8,128)(2,1)S(1)} %pad_maximum_fusion.1), channel_id=1, source_target_pairs={{0,500},{4,504},{8,508},{12,0},{16,4},{20,8},{24,12},{28,16},{32,2... | collective-permute-start | bytes 1572872 | tf_op jit(solution)/shard_map/ppermute | solution.py:16
  68.3 40.3 %all-to-all-start.1 = ((bf16[4,512,256]{1,2,0:T(8,128)(2,1)}), bf16[4,512,256]{1,2,0:T(8,128)(2,1)S(1)}, u32[]{:S(2)}, u32[]{:S(2)}) async-start(bf16[4,512,256]{1,2,0:T(8,128)(2,1)} %broadcast_in_dim.170), calls=%async_computation.1 | async-start | bytes 2097152 | tf_op jit(solution)/shard_map/all_to_all | solution.py:91
  72.4 34.2 %collective-permute-start.5 = (bf16[2,128,1024]{2,1,0:T(8,128)(2,1)S(1)}, bf16[2,128,1024]{2,1,0:T(8,128)(2,1)S(1)}, u32[]{:S(2)}, u32[]{:S(2)}) collective-permute-start(bf16[2,128,1024]{2,1,0:T(8,128)(2,1)S(1)} %pad_maximum_fusion.1), channel_id=1, source_target_pairs={{0,12},{4,16},{8,20},{12,24},{16,28},{20,32},{24,36},{28,40},{32,4... | collective-permute-start | bytes 1572872 | tf_op jit(solution)/shard_map/ppermute | solution.py:16
  111.6 1.5 copy-start.3
  116.5 20.0 %all-to-all-start.2 = ((bf16[4,512,256]{1,2,0:T(8,128)(2,1)}), bf16[4,512,256]{1,2,0:T(8,128)(2,1)S(1)}, u32[]{:S(2)}, u32[]{:S(2)}) async-start(bf16[4,512,256]{1,2,0:T(8,128)(2,1)} %pad_maximum_fusion), calls=%async_computation.2 | async-start | bytes 2097152 | tf_op jit(solution)/shard_map/all_to_all | solution.py:122
  138.0 42.1 %all-to-all-start.3 = ((bf16[128,4,250]{2,1,0:T(4,128)(2,1)}), bf16[128,4,250]{2,1,0:T(4,128)(2,1)S(1)}, u32[]{:S(2)}, u32[]{:S(2)}) async-start(bf16[128,4,250]{2,1,0:T(4,128)(2,1)} %reshape.136), calls=%async_computation.3 | async-start | bytes 524288 | tf_op jit(solution)/shard_map/all_to_all | solution.py:129

commit v8 on v6

--- a/solution.py
+++ b/solution.py
@@ -87,10 +87,11 @@
         tiled=True,
     )
     own = arrived.reshape(slots, queries.shape[1])
-    parts = lax.all_to_all(
-        jnp.broadcast_to(own[None], (feats,) + own.shape), "feat", split_axis=0, concat_axis=0, tiled=True
-    )
-    query_full = jnp.swapaxes(parts, 0, 1).reshape(slots, feats * queries.shape[1])
+    far = swapped(own, "feat", 2)
+    near = swapped(jnp.stack([own, far]), "feat", 1)
+    parts = jnp.stack([own, far, near[0], near[1]])
+    order = jnp.array([0, 2, 1, 3], jnp.int32)[jnp.arange(feats, dtype=jnp.int32) ^ feat_index]
+    query_full = jnp.swapaxes(jnp.take(parts, order, axis=0), 0, 1).reshape(slots, feats * queries.shape[1])
 
     band_keys = jnp.stack([b[0] for b in blocks]).reshape(len(offsets) * rows, depth)
     band_labels = jnp.stack([b[1] for b in blocks]).reshape(len(offsets) * rows, feats * group)
@@ -108,20 +109,26 @@
     accum = jnp.dot(weight.astype(jnp.bfloat16), band_labels, preferred_element_type=jnp.float32)
 
     column = lax.broadcasted_iota(jnp.int32, (slots, group), 1)
-    codes = split3(top) + split3(total)
 
-    def pack(g):
-        part = lax.dynamic_slice_in_dim(accum, g * group, group, axis=1)
-        for i, c in enumerate(codes):
+    def pack(part, top, total):
+        for i, c in enumerate(split3(top) + split3(total)):
             part = jnp.where(column == quarter + i, c.astype(jnp.float32)[:, None], part)
         return part.astype(jnp.bfloat16)
 
-    kept = lax.dynamic_slice_in_dim(accum, feat_index * group, group, axis=1)
-    outbox = jnp.stack([pack(g) for g in range(feats)])
-    inbox = lax.all_to_all(outbox, "feat", split_axis=0, concat_axis=0, tiled=True)
-    for k in range(1, feats):
-        message = lax.dynamic_index_in_dim(inbox, feat_index ^ k, axis=0, keepdims=False)
-        kept, top, total = merge(kept, top, total, message, quarter)
+    grid = accum.reshape(slots, feats, group)
+    pick = lambda g: lax.dynamic_index_in_dim(grid, g, axis=1, keepdims=False)
+    kept = jnp.stack([pick(feat_index), pick(feat_index ^ 2)])
+    sent = jnp.stack([pack(pick(feat_index ^ 1), top, total), pack(pick(feat_index ^ 3), top, total)])
+    message = swapped(sent, "feat", 1).astype(jnp.float32)
+    other_top = join3([message[0, :, quarter + i] for i in range(3)])
+    other_total = join3([message[0, :, quarter + 3 + i] for i in range(3)])
+    highest = jnp.maximum(top, other_top)
+    mine = jnp.exp(top - highest)
+    theirs = jnp.exp(other_top - highest)
+    kept = kept * mine[None, :, None] + message * theirs[None, :, None]
+    top, total = highest, total * mine + other_total * theirs
+    message = swapped(pack(kept[1], top, total), "feat", 2)
+    kept, top, total = merge(kept[0], top, total, message, quarter)
     kept = kept[:, :quarter]
     shares = (kept / total[:, None]).astype(jnp.bfloat16)
 

time: 160 us -> 159 us (level)
  waiting for transfers between devices: 59.3 us -> 41 us
  local copies, waits for them, and re-layouts: 20.3 us -> 27.8 us
  starting transfers between devices: 65.5 us -> 72.7 us
    all_to_all x2 -> x0, waiting for transfers between devices: 27.1 us -> none  [the longest x1 15.9 us: body(): lax.all_to_all(outbox, 'feat', split_axis=0, concat_axis=0, tiled=True)]
    ppermute x0 -> x4, starting transfers between devices: none -> 13.6 us  [swapped(): return lax.ppermute(array, axis, [(i, i ^ bit) for i in range(peers)])]
    ppermute x0 -> x4, waiting for transfers between devices: none -> 8.61 us  [swapped(): return lax.ppermute(array, axis, [(i, i ^ bit) for i in range(peers)])]
    all_to_all x2 -> x0, starting transfers between devices: 7.51 us -> none  [the longest x1 4 us: body(): lax.all_to_all(jnp.broadcast_to(own[None], (feats,) + own.shape), 'feat',...]
    unnamed x16 -> x19, local copies, waits for them, and re-layouts: 8.35 us -> 11.9 us
    reshape x0 -> x2, local copies, waits for them, and re-layouts: none -> 2.53 us  [the longest x1 2.46 us: body(): jnp.stack([b[1] for b in blocks])]
    another operation x3 -> x7, local copies, waits for them, and re-layouts: 0.02 us -> 1.75 us  [the longest x3 1.67 us: body(): kept = jnp.stack([pick(feat_index), pick(feat_index ^ 2)])]
  transfers between devices with their start and end apart: 10 -> 12, of which waited for: 4 -> 4; matrix products, arithmetic and copies ran while one was open for 10% -> 14% of each run, Pallas kernels for 0% -> 0%
where the time goes in v8:
time: 159 us; the launch traced here: 158 us
  starting transfers between devices  72.7 us (46%)
  waiting for transfers between devices  41 us (26%)
  local copies, waits for them, and re-layouts  27.8 us (17%)
  other arithmetic  6.87 us (4%)
  between operations  4.98 us (3%)
  matrix products  4.32 us (3%)
    ppermute x6, starting transfers between devices, shifted(): lax.ppermute(array, axis, [(i, (i - by) % peers) for i in range(peers)])  23.8 us
    all_to_all x1, waiting for transfers between devices, body(): lax.all_to_all(shares.reshape(clusters, capacity, quarter), 'cluster', sp...  22.7 us
    all_to_all x1, starting transfers between devices, body(): lax.all_to_all(outgoing.reshape(clusters, capacity, queries.shape[1]), 'c...  21.9 us
    ppermute x4, starting transfers between devices, swapped(): return lax.ppermute(array, axis, [(i, i ^ bit) for i in range(peers)])  13.6 us
    all_to_all x1, starting transfers between devices, body(): lax.all_to_all(shares.reshape(clusters, capacity, quarter), 'cluster', sp...  13.3 us
    unnamed x19, local copies, waits for them, and re-layouts  11.9 us
    all_to_all x1, waiting for transfers between devices, body(): lax.all_to_all(outgoing.reshape(clusters, capacity, queries.shape[1]), 'c...  9.68 us
    ppermute x4, waiting for transfers between devices, swapped(): return lax.ppermute(array, axis, [(i, i ^ bit) for i in range(peers)])  8.61 us
  transfers between devices with their start and end apart: 12, of which 4 were waited for; matrix products, arithmetic and copies ran while one was open for 14% of the time, Pallas kernels for 0%

profile of v8, /device:TPU:32, one launch (start us, length us, event | category | flops | bytes accessed | tf_op | source)
XLA Modules:
  0.0 157.6 jit_solution(10371939418786758671)
XLA Ops:
  0.0 1.0 reshape.919
  1.1 0.7 and_select_fusion
  1.8 0.1 copy.33
  2.0 1.0 pad_maximum_fusion.2
  3.0 5.4 %collective-permute-start.2 = (bf16[2,128,1024]{2,1,0:T(8,128)(2,1)S(1)}, bf16[2,128,1024]{2,1,0:T(8,128)(2,1)}, u32[]{:S(2)}, u32[]{:S(2)}) collective-permute-start(bf16[2,128,1024]{2,1,0:T(8,128)(2,1)S(1)} %pad_maximum_fusion.2), channel_id=1, source_target_pairs={{0,508},{4,0},{8,4},{12,8},{16,12},{20,16},{24,20},{28,24},{32,28}... | collective-permute-start | bytes 1572872 | tf_op jit(solution)/shard_map/ppermute | solution.py:16
  8.4 1.9 %collective-permute-start.3 = (bf16[2,128,1024]{2,1,0:T(8,128)(2,1)S(1)}, bf16[2,128,1024]{2,1,0:T(8,128)(2,1)}, u32[]{:S(2)}, u32[]{:S(2)}) collective-permute-start(bf16[2,128,1024]{2,1,0:T(8,128)(2,1)S(1)} %pad_maximum_fusion.2), channel_id=1, source_target_pairs={{0,4},{4,8},{8,12},{12,16},{16,20},{20,24},{24,28},{28,32},{32,36}... | collective-permute-start | bytes 1572872 | tf_op jit(solution)/shard_map/ppermute | solution.py:16
  10.3 3.0 %collective-permute-start.4 = (bf16[2,128,1024]{2,1,0:T(8,128)(2,1)S(1)}, bf16[2,128,1024]{2,1,0:T(8,128)(2,1)}, u32[]{:S(2)}, u32[]{:S(2)}) collective-permute-start(bf16[2,128,1024]{2,1,0:T(8,128)(2,1)S(1)} %pad_maximum_fusion.2), channel_id=1, source_target_pairs={{0,504},{4,508},{8,0},{12,4},{16,8},{20,12},{24,16},{28,20},{32,24... | collective-permute-start | bytes 1572872 | tf_op jit(solution)/shard_map/ppermute | solution.py:16
  13.3 2.8 %collective-permute-start.5 = (bf16[2,128,1024]{2,1,0:T(8,128)(2,1)S(1)}, bf16[2,128,1024]{2,1,0:T(8,128)(2,1)}, u32[]{:S(2)}, u32[]{:S(2)}) collective-permute-start(bf16[2,128,1024]{2,1,0:T(8,128)(2,1)S(1)} %pad_maximum_fusion.2), channel_id=1, source_target_pairs={{0,8},{4,12},{8,16},{12,20},{16,24},{20,28},{24,32},{28,36},{32,40... | collective-permute-start | bytes 1572872 | tf_op jit(solution)/shard_map/ppermute | solution.py:16
  16.2 6.4 %collective-permute-start.6 = (bf16[2,128,1024]{2,1,0:T(8,128)(2,1)S(1)}, bf16[2,128,1024]{2,1,0:T(8,128)(2,1)}, u32[]{:S(2)}, u32[]{:S(2)}) collective-permute-start(bf16[2,128,1024]{2,1,0:T(8,128)(2,1)S(1)} %pad_maximum_fusion.2), channel_id=1, source_target_pairs={{0,500},{4,504},{8,508},{12,0},{16,4},{20,8},{24,12},{28,16},{32,2... | collective-permute-start | bytes 1572872 | tf_op jit(solution)/shard_map/ppermute | solution.py:16
  22.6 0.1 copy.30
  22.7 0.2 fusion.17
  23.0 0.2 fusion.19
  23.2 1.9 %scatter_custom_fusion = bf16[512,256]{1,0:T(8,128)(2,1)S(1)} fusion(s32[256]{0:T(256)S(1)} %bitcast.139, bf16[256,256]{1,0:T(8,128)(2,1)} %param.7, bf16[]{:T(256)} %constant.71.clone.1), kind=kCustom, calls=%fused_computation.58 | custom fusion | bytes 262656 | tf_op jit(solution)/shard_map/scatter | solution.py:81
  25.1 0.8 reshape.916
  25.9 21.9 %all-to-all-start = ((bf16[128,4,256]{2,1,0:T(4,128)(2,1)}), bf16[128,4,256]{2,1,0:T(4,128)(2,1)S(1)}, u32[]{:S(2)}, u32[]{:S(2)}) async-start(bf16[128,4,256]{2,1,0:T(4,128)(2,1)} %reshape.916), calls=%async_computation | async-start | bytes 524288 | tf_op jit(solution)/shard_map/all_to_all | solution.py:82
  47.9 0.7 constant_dynamic-update-slice_fusion
  48.6 0.1 constant_dynamic-slice_fusion
  48.7 0.6 fusion.52
  53.7 0.1 stack.68
  53.9 0.1 broadcast_bitcast_fusion
  54.0 0.6 gather_fusion
  54.7 4.3 %collective-permute-start.7 = (bf16[2,128,1024]{2,1,0:T(8,128)(2,1)S(1)}, bf16[2,128,1024]{2,1,0:T(8,128)(2,1)}, u32[]{:S(2)}, u32[]{:S(2)}) collective-permute-start(bf16[2,128,1024]{2,1,0:T(8,128)(2,1)S(1)} %pad_maximum_fusion.2), channel_id=1, source_target_pairs={{0,12},{4,16},{8,20},{12,24},{16,28},{20,32},{24,36},{28,40},{32,4... | collective-permute-start | bytes 1572872 | tf_op jit(solution)/shard_map/ppermute | solution.py:16
  58.9 1.8 %slice_dynamic-update-slice_fusion.11 = (bf16[7,128,1024]{2,1,0:T(8,128)(2,1)}, bf16[7,128,1024]{2,1,0:T(8,128)(2,1)S(1)}) fusion(bf16[7,128,1024]{2,1,0:T(8,128)(2,1)} %get-tuple-element.52, bf16[2,128,1024]{2,1,0:T(8,128)(2,1)} %collective-permute-done.2, bf16[7,128,1024]{2,1,0:T(8,128)(2,1)S(1)} %get-tuple-element.53), kind=kLoop, calls=%fused_computation.49 | loop fusion | bytes 1048576
  60.7 1.8 %slice_dynamic-update-slice_fusion.10 = (bf16[7,128,1024]{2,1,0:T(8,128)(2,1)}, bf16[7,128,1024]{2,1,0:T(8,128)(2,1)S(1)}) fusion(bf16[7,128,1024]{2,1,0:T(8,128)(2,1)} %get-tuple-element.26, bf16[2,128,1024]{2,1,0:T(8,128)(2,1)} %collective-permute-done.3, bf16[7,128,1024]{2,1,0:T(8,128)(2,1)S(1)} %get-tuple-element.27), kind=kLoop, calls=%fused_computation.48 | loop fusion | bytes 1048576
  62.5 9.7 %all-to-all-done = bf16[128,4,256]{2,1,0:T(4,128)(2,1)S(1)} async-done(((bf16[128,4,256]{2,1,0:T(4,128)(2,1)}), bf16[128,4,256]{2,1,0:T(4,128)(2,1)S(1)}, u32[]{:S(2)}, u32[]{:S(2)}) %all-to-all-start) | async-done | bytes 262176 | tf_op jit(solution)/shard_map/all_to_all | solution.py:82
  72.2 0.1 reshape.917
  72.2 4.6 %collective-permute-start = (bf16[512,256]{1,0:T(8,128)(2,1)S(1)}, bf16[512,256]{1,0:T(8,128)(2,1)S(1)}, u32[]{:S(2)}, u32[]{:S(2)}) collective-permute-start(bf16[512,256]{1,0:T(8,128)(2,1)S(1)} %reshape.917), channel_id=1, source_target_pairs={{0,2},{1,3},{2,0},{3,1},{4,6},{5,7},{6,4},{7,5},{8,10},{9,11},{10,... | collective-permute-start | bytes 786440 | tf_op jit(solution)/shard_map/ppermute | solution.py:21
  76.9 1.8 %slice_dynamic-update-slice_fusion.9 = (bf16[7,128,1024]{2,1,0:T(8,128)(2,1)}, bf16[7,128,1024]{2,1,0:T(8,128)(2,1)S(1)}) fusion(bf16[7,128,1024]{2,1,0:T(8,128)(2,1)} %get-tuple-element.24, bf16[2,128,1024]{2,1,0:T(8,128)(2,1)} %collective-permute-done.4, bf16[7,128,1024]{2,1,0:T(8,128)(2,1)S(1)} %get-tuple-element.25), kind=kLoop, calls=%fused_computation.47 | loop fusion | bytes 1048576
  78.7 1.8 %slice_dynamic-update-slice_fusion.8 = (bf16[7,128,1024]{2,1,0:T(8,128)(2,1)}, bf16[7,128,1024]{2,1,0:T(8,128)(2,1)S(1)}) fusion(bf16[7,128,1024]{2,1,0:T(8,128)(2,1)} %get-tuple-element.22, bf16[2,128,1024]{2,1,0:T(8,128)(2,1)} %collective-permute-done.5, bf16[7,128,1024]{2,1,0:T(8,128)(2,1)S(1)} %get-tuple-element.23), kind=kLoop, calls=%fused_computation.46 | loop fusion | bytes 1048576
  80.5 1.5 collective-permute-done
  82.0 0.9 pad_maximum_fusion.1
  82.9 1.9 %collective-permute-start.1 = (bf16[2,512,256]{2,1,0:T(8,128)(2,1)}, bf16[2,512,256]{2,1,0:T(8,128)(2,1)}, u32[]{:S(2)}, u32[]{:S(2)}) collective-permute-start(bf16[2,512,256]{2,1,0:T(8,128)(2,1)} %pad_maximum_fusion.1), channel_id=1, source_target_pairs={{0,1},{1,0},{2,3},{3,2},{4,5},{5,4},{6,7},{7,6},{8,9},{9,8},{10,11... | collective-permute-start | bytes 1572872 | tf_op jit(solution)/shard_map/ppermute | solution.py:21
  84.8 1.8 %slice_dynamic-update-slice_fusion.7 = (bf16[7,128,1024]{2,1,0:T(8,128)(2,1)}, bf16[7,128,1024]{2,1,0:T(8,128)(2,1)S(1)}) fusion(bf16[7,128,1024]{2,1,0:T(8,128)(2,1)} %get-tuple-element.20, bf16[2,128,1024]{2,1,0:T(8,128)(2,1)} %collective-permute-done.6, bf16[7,128,1024]{2,1,0:T(8,128)(2,1)S(1)} %get-tuple-element.21), kind=kLoop, calls=%fused_computation.45 | loop fusion | bytes 1048576
  86.5 1.8 %slice_dynamic-update-slice_fusion.6 = (bf16[7,128,1024]{2,1,0:T(8,128)(2,1)}, bf16[7,128,1024]{2,1,0:T(8,128)(2,1)S(1)}) fusion(bf16[7,128,1024]{2,1,0:T(8,128)(2,1)} %get-tuple-element.18, bf16[2,128,1024]{2,1,0:T(8,128)(2,1)} %collective-permute-done.7, bf16[7,128,1024]{2,1,0:T(8,128)(2,1)S(1)} %get-tuple-element.19), kind=kLoop, calls=%fused_computation.44 | loop fusion | bytes 1048576 | tf_op jit(solution)/shard_map/stack | solution.py:96
  88.3 2.5 %copy.35 = bf16[896,1024]{0,1:T(8,128)(2,1)} copy(bf16[896,1024]{1,0:T(8,128)(2,1)S(1)} %bitcast.113) | data formatting | bytes 3670016 | tf_op jit(solution)/shard_map/reshape | solution.py:97
  90.8 0.7 fusion.24
  91.5 1.1 pad_maximum_fusion
  92.7 0.6 gather_fusion.1
  93.3 0.2 select_bitcast_fusion
  93.5 0.5 copy.32
  94.0 2.9 %fusion.53 = (f32[512]{0:T(512)S(1)}, f32[512,896]{1,0:T(8,128)S(1)}) fusion(f32[896]{0:T(1024)S(1)} %fusion.24, bf16[512,1024]{0,1:T(8,128)(2,1)S(1)} %bitcast.115, bf16[896,1024]{1,0:T(8,128)(2,1)} %bitcast.127, pred[896]{0:T(1024)(128)(4,1)S(1)} %broadcast_bitcast_fusion), kind=kOutput, calls=%fused_computation.146 | convolution fusion | flops 941358592 | bytes 4725120 | tf_op jit(solution)/shard_map/qd,kd->qk/dot_general | solution.py:103
  96.9 0.5 fusion
  97.4 1.0 copy-done.2
  98.4 1.4 fusion.4
  99.9 1.3 copy-done.3
  101.2 0.1 copy.39
  101.4 0.1 copy.40
  101.5 0.3 select_convert_fusion.1
  101.9 2.4 %collective-permute-start.8 = (bf16[2,512,256]{1,2,0:T(8,128)(2,1)S(1)}, bf16[2,512,256]{1,2,0:T(8,128)(2,1)S(1)}, u32[]{:S(2)}, u32[]{:S(2)}) collective-permute-start(bf16[2,512,256]{1,2,0:T(8,128)(2,1)S(1)} %pad_maximum_fusion.3), channel_id=1, source_target_pairs={{0,1},{1,0},{2,3},{3,2},{4,5},{5,4},{6,7},{7,6},{8,9},{9,8},{10,11... | collective-permute-start | bytes 1572872 | tf_op jit(solution)/shard_map/ppermute | solution.py:21
  104.3 1.3 dynamic-slice_bitcast_fusion.3
  105.6 0.2 copy.37
  105.8 0.2 copy.38
  106.0 0.1 convert_element_type.251
  106.2 0.2 fusion.2
  106.4 0.3 fusion.15
  106.7 4.6 %collective-permute-start.9 = (bf16[512,256]{0,1:T(8,128)(2,1)S(1)}, bf16[512,256]{0,1:T(8,128)(2,1)S(1)}, u32[]{:S(2)}, u32[]{:S(2)}) collective-permute-start(bf16[512,256]{0,1:T(8,128)(2,1)S(1)} %fusion.15), channel_id=1, source_target_pairs={{0,2},{1,3},{2,0},{3,1},{4,6},{5,7},{6,4},{7,5},{8,10},{9,11},{10,... | collective-permute-start | bytes 786440 | tf_op jit(solution)/shard_map/ppermute | solution.py:21
  111.4 7.1 %collective-permute-done.9 = bf16[512,256]{0,1:T(8,128)(2,1)S(1)} collective-permute-done((bf16[512,256]{0,1:T(8,128)(2,1)S(1)}, bf16[512,256]{0,1:T(8,128)(2,1)S(1)}, u32[]{:S(2)}, u32[]{:S(2)}) %collective-permute-start.9) | collective-permute-done | bytes 262176 | tf_op jit(solution)/shard_map/ppermute | solution.py:21
  118.6 0.1 fusion.16
  118.7 0.1 copy.41
  118.9 0.8 reshape.922
  119.6 13.3 %all-to-all-start.1 = ((bf16[128,4,250]{2,1,0:T(4,128)(2,1)}), bf16[128,4,250]{2,1,0:T(4,128)(2,1)S(1)}, u32[]{:S(2)}, u32[]{:S(2)}) async-start(bf16[128,4,250]{2,1,0:T(4,128)(2,1)} %reshape.922), calls=%async_computation.1 | async-start | bytes 524288 | tf_op jit(solution)/shard_map/all_to_all | solution.py:135
  133.0 22.7 %all-to-all-done.1 = bf16[128,4,250]{2,1,0:T(4,128)(2,1)S(1)} async-done(((bf16[128,4,250]{2,1,0:T(4,128)(2,1)}), bf16[128,4,250]{2,1,0:T(4,128)(2,1)S(1)}, u32[]{:S(2)}, u32[]{:S(2)}) %all-to-all-start.1) | async-done | bytes 256032 | tf_op jit(solution)/shard_map/all_to_all | solution.py:135
  155.7 0.2 reshape.923
  155.8 1.8 %gather_fusion.2 = bf16[256,250]{1,0:T(8,128)(2,1)} fusion(bf16[512,250]{1,0:T(8,128)(2,1)S(1)} %reshape.923, s32[1024]{0:T(1024)S(1)} %pad_clamp_fusion), kind=kCustom, calls=%fused_computation.2 | custom fusion | bytes 257024 | tf_op jit(solution)/shard_map/gather | solution.py:142
  (50 shorter events, 0.6 us)
Async XLA Ops:
  0.0 48.6 %copy-start = (s32[128,7]{0,1:T(8,128)S(1)}, s32[128,7]{0,1:T(8,128)}, u32[]{:S(2)}) copy-start(s32[128,7]{0,1:T(8,128)} %param.9) | copy-start | bytes 10756
  0.0 22.6 %copy-start.5 = (s32[256,1]{0,1:T(1,128)S(1)}, s32[256,1]{0,1:T(1,128)}, u32[]{:S(2)}) copy-start(s32[256,1]{0,1:T(1,128)} %param.8) | copy-start | bytes 3076
  1.8 46.0 %copy-start.4 = (bf16[128,1024]{1,0:T(8,128)(2,1)S(1)}, bf16[128,1024]{1,0:T(8,128)(2,1)}, u32[]{:S(2)}) copy-start(bf16[128,1024]{1,0:T(8,128)(2,1)} %param.10) | copy-start | bytes 786436
  3.0 51.0 %copy-start.1 = (s32[4]{0:T(128)S(1)}, s32[4]{0:T(128)}, u32[]{:S(2)}) copy-start(s32[4]{0:T(128)} %constant.85.clone) | copy-start | bytes 52
  3.0 51.7 %collective-permute-start.2 = (bf16[2,128,1024]{2,1,0:T(8,128)(2,1)S(1)}, bf16[2,128,1024]{2,1,0:T(8,128)(2,1)}, u32[]{:S(2)}, u32[]{:S(2)}) collective-permute-start(bf16[2,128,1024]{2,1,0:T(8,128)(2,1)S(1)} %pad_maximum_fusion.2), channel_id=1, source_target_pairs={{0,508},{4,0},{8,4},{12,8},{16,12},{20,16},{24,20},{28,24},{32,28}... | collective-permute-start | bytes 1572872 | tf_op jit(solution)/shard_map/ppermute | solution.py:16
  8.4 52.3 %collective-permute-start.3 = (bf16[2,128,1024]{2,1,0:T(8,128)(2,1)S(1)}, bf16[2,128,1024]{2,1,0:T(8,128)(2,1)}, u32[]{:S(2)}, u32[]{:S(2)}) collective-permute-start(bf16[2,128,1024]{2,1,0:T(8,128)(2,1)S(1)} %pad_maximum_fusion.2), channel_id=1, source_target_pairs={{0,4},{4,8},{8,12},{12,16},{16,20},{20,24},{24,28},{28,32},{32,36}... | collective-permute-start | bytes 1572872 | tf_op jit(solution)/shard_map/ppermute | solution.py:16
  10.3 66.5 %collective-permute-start.4 = (bf16[2,128,1024]{2,1,0:T(8,128)(2,1)S(1)}, bf16[2,128,1024]{2,1,0:T(8,128)(2,1)}, u32[]{:S(2)}, u32[]{:S(2)}) collective-permute-start(bf16[2,128,1024]{2,1,0:T(8,128)(2,1)S(1)} %pad_maximum_fusion.2), channel_id=1, source_target_pairs={{0,504},{4,508},{8,0},{12,4},{16,8},{20,12},{24,16},{28,20},{32,24... | collective-permute-start | bytes 1572872 | tf_op jit(solution)/shard_map/ppermute | solution.py:16
  13.3 65.3 %collective-permute-start.5 = (bf16[2,128,1024]{2,1,0:T(8,128)(2,1)S(1)}, bf16[2,128,1024]{2,1,0:T(8,128)(2,1)}, u32[]{:S(2)}, u32[]{:S(2)}) collective-permute-start(bf16[2,128,1024]{2,1,0:T(8,128)(2,1)S(1)} %pad_maximum_fusion.2), channel_id=1, source_target_pairs={{0,8},{4,12},{8,16},{12,20},{16,24},{20,28},{24,32},{28,36},{32,40... | collective-permute-start | bytes 1572872 | tf_op jit(solution)/shard_map/ppermute | solution.py:16
  16.2 68.6 %collective-permute-start.6 = (bf16[2,128,1024]{2,1,0:T(8,128)(2,1)S(1)}, bf16[2,128,1024]{2,1,0:T(8,128)(2,1)}, u32[]{:S(2)}, u32[]{:S(2)}) collective-permute-start(bf16[2,128,1024]{2,1,0:T(8,128)(2,1)S(1)} %pad_maximum_fusion.2), channel_id=1, source_target_pairs={{0,500},{4,504},{8,508},{12,0},{16,4},{20,8},{24,12},{28,16},{32,2... | collective-permute-start | bytes 1572872 | tf_op jit(solution)/shard_map/ppermute | solution.py:16
  25.9 46.2 %all-to-all-start = ((bf16[128,4,256]{2,1,0:T(4,128)(2,1)}), bf16[128,4,256]{2,1,0:T(4,128)(2,1)S(1)}, u32[]{:S(2)}, u32[]{:S(2)}) async-start(bf16[128,4,256]{2,1,0:T(4,128)(2,1)} %reshape.916), calls=%async_computation | async-start | bytes 524288 | tf_op jit(solution)/shard_map/all_to_all | solution.py:82
  54.7 31.9 %collective-permute-start.7 = (bf16[2,128,1024]{2,1,0:T(8,128)(2,1)S(1)}, bf16[2,128,1024]{2,1,0:T(8,128)(2,1)}, u32[]{:S(2)}, u32[]{:S(2)}) collective-permute-start(bf16[2,128,1024]{2,1,0:T(8,128)(2,1)S(1)} %pad_maximum_fusion.2), channel_id=1, source_target_pairs={{0,12},{4,16},{8,20},{12,24},{16,28},{20,32},{24,36},{28,40},{32,4... | collective-permute-start | bytes 1572872 | tf_op jit(solution)/shard_map/ppermute | solution.py:16
  72.2 9.8 %collective-permute-start = (bf16[512,256]{1,0:T(8,128)(2,1)S(1)}, bf16[512,256]{1,0:T(8,128)(2,1)S(1)}, u32[]{:S(2)}, u32[]{:S(2)}) collective-permute-start(bf16[512,256]{1,0:T(8,128)(2,1)S(1)} %reshape.917), channel_id=1, source_target_pairs={{0,2},{1,3},{2,0},{3,1},{4,6},{5,7},{6,4},{7,5},{8,10},{9,11},{10,... | collective-permute-start | bytes 786440 | tf_op jit(solution)/shard_map/ppermute | solution.py:21
  82.9 8.7 %collective-permute-start.1 = (bf16[2,512,256]{2,1,0:T(8,128)(2,1)}, bf16[2,512,256]{2,1,0:T(8,128)(2,1)}, u32[]{:S(2)}, u32[]{:S(2)}) collective-permute-start(bf16[2,512,256]{2,1,0:T(8,128)(2,1)} %pad_maximum_fusion.1), channel_id=1, source_target_pairs={{0,1},{1,0},{2,3},{3,2},{4,5},{5,4},{6,7},{7,6},{8,9},{9,8},{10,11... | collective-permute-start | bytes 1572872 | tf_op jit(solution)/shard_map/ppermute | solution.py:21
  96.9 1.5 copy-start.2
  99.8 1.3 copy-start.3
  101.9 4.1 %collective-permute-start.8 = (bf16[2,512,256]{1,2,0:T(8,128)(2,1)S(1)}, bf16[2,512,256]{1,2,0:T(8,128)(2,1)S(1)}, u32[]{:S(2)}, u32[]{:S(2)}) collective-permute-start(bf16[2,512,256]{1,2,0:T(8,128)(2,1)S(1)} %pad_maximum_fusion.3), channel_id=1, source_target_pairs={{0,1},{1,0},{2,3},{3,2},{4,5},{5,4},{6,7},{7,6},{8,9},{9,8},{10,11... | collective-permute-start | bytes 1572872 | tf_op jit(solution)/shard_map/ppermute | solution.py:21
  106.7 11.8 %collective-permute-start.9 = (bf16[512,256]{0,1:T(8,128)(2,1)S(1)}, bf16[512,256]{0,1:T(8,128)(2,1)S(1)}, u32[]{:S(2)}, u32[]{:S(2)}) collective-permute-start(bf16[512,256]{0,1:T(8,128)(2,1)S(1)} %fusion.15), channel_id=1, source_target_pairs={{0,2},{1,3},{2,0},{3,1},{4,6},{5,7},{6,4},{7,5},{8,10},{9,11},{10,... | collective-permute-start | bytes 786440 | tf_op jit(solution)/shard_map/ppermute | solution.py:21
  119.6 36.0 %all-to-all-start.1 = ((bf16[128,4,250]{2,1,0:T(4,128)(2,1)}), bf16[128,4,250]{2,1,0:T(4,128)(2,1)S(1)}, u32[]{:S(2)}, u32[]{:S(2)}) async-start(bf16[128,4,250]{2,1,0:T(4,128)(2,1)} %reshape.922), calls=%async_computation.1 | async-start | bytes 524288 | tf_op jit(solution)/shard_map/all_to_all | solution.py:135

commit v9 on v8

--- a/solution.py
+++ b/solution.py
@@ -1,8 +1,11 @@
+import functools
 import math
 
 import jax
 import jax.numpy as jnp
 from jax import lax
+from jax.experimental import pallas as pl
+from jax.experimental.pallas import tpu as pltpu
 from jax.sharding import PartitionSpec as P
 
 REACH = 3
@@ -47,6 +50,58 @@
     theirs = jnp.exp(other_top - highest)
     merged = kept * mine[:, None] + other * theirs[:, None]
     return merged, highest, total * mine + other_total * theirs
+
+
+def band_kernel(scale, count, query_ref, row_ref, *refs):
+    blocks = refs[:count]
+    accum_ref, top_ref, total_ref, score_ref, weight_ref = refs[count:]
+    rows = blocks[0].shape[1]
+    query = query_ref[...]
+    for b in range(count):
+        cut = slice(b * rows, (b + 1) * rows)
+        part = lax.dot_general(
+            query, blocks[b][0], (((1,), (1,)), ((), ())), preferred_element_type=jnp.float32
+        )
+        score_ref[:, cut] = part * scale + row_ref[:, cut]
+    scores = score_ref[...]
+    top = jnp.max(scores, axis=1, keepdims=True)
+    weight = jnp.exp(scores - top)
+    total = jnp.sum(weight, axis=1, keepdims=True)
+    weight_ref[...] = weight.astype(jnp.bfloat16)
+    top_ref[...] = jnp.broadcast_to(top, top_ref.shape)
+    total_ref[...] = jnp.broadcast_to(total, total_ref.shape)
+    accum = jnp.zeros(accum_ref.shape, jnp.float32)
+    for b in range(count):
+        cut = slice(b * rows, (b + 1) * rows)
+        accum = accum + jnp.dot(weight_ref[:, cut], blocks[b][1], preferred_element_type=jnp.float32)
+    accum_ref[...] = accum
+
+
+def band(query_full, row, blocks, scale):
+    slots, depth = query_full.shape
+    count = len(blocks)
+    rows, width = blocks[0].shape[1], blocks[0].shape[2]
+    band_rows = count * rows
+    out_shape = [
+        jax.ShapeDtypeStruct((slots, width), jnp.float32),
+        jax.ShapeDtypeStruct((slots, 128), jnp.float32),
+        jax.ShapeDtypeStruct((slots, 128), jnp.float32),
+    ]
+    cost = pl.CostEstimate(
+        flops=2 * slots * band_rows * (depth + width),
+        transcendentals=slots * band_rows,
+        bytes_accessed=2 * slots * depth + 2 * band_rows * (depth + width) + 4 * slots * width,
+    )
+    accum, top, total = pl.pallas_call(
+        functools.partial(band_kernel, scale, count),
+        out_shape=out_shape,
+        scratch_shapes=[
+            pltpu.VMEM((slots, band_rows), jnp.float32),
+            pltpu.VMEM((slots, band_rows), jnp.bfloat16),
+        ],
+        cost_estimate=cost,
+    )(query_full, row, *blocks)
+    return accum, top[:, 0], total[:, 0]
 
 
 def body(queries, assign, band_mask, keys, labels, prior):
@@ -93,20 +148,13 @@
     order = jnp.array([0, 2, 1, 3], jnp.int32)[jnp.arange(feats, dtype=jnp.int32) ^ feat_index]
     query_full = jnp.swapaxes(jnp.take(parts, order, axis=0), 0, 1).reshape(slots, feats * queries.shape[1])
 
-    band_keys = jnp.stack([b[0] for b in blocks]).reshape(len(offsets) * rows, depth)
-    band_labels = jnp.stack([b[1] for b in blocks]).reshape(len(offsets) * rows, feats * group)
-    band_prior = band_labels[:, quarter]
     mask_row = band_mask[cluster_index]
     live_blocks = jnp.stack([mask_row[REACH + o] > 0 for o in offsets])
     live = jnp.repeat(live_blocks, rows)
+    band_prior = jnp.concatenate([b[1][:, quarter] for b in blocks]).astype(jnp.float32)
+    row = jnp.where(live, band_prior, -jnp.inf)[None, :]
     scale = temper / math.sqrt(depth)
-    scores = jnp.einsum("qd,kd->qk", query_full, band_keys, preferred_element_type=jnp.float32) * scale
-    scores = scores + band_prior.astype(jnp.float32)[None, :]
-    scores = jnp.where(live[None, :], scores, -jnp.inf)
-    top = jnp.max(scores, axis=1)
-    weight = jnp.exp(scores - top[:, None])
-    total = jnp.sum(weight, axis=1)
-    accum = jnp.dot(weight.astype(jnp.bfloat16), band_labels, preferred_element_type=jnp.float32)
+    accum, top, total = band(query_full, row, blocks, scale)
 
     column = lax.broadcasted_iota(jnp.int32, (slots, group), 1)
 

time: 159 us -> 163 us (1.025)
  Pallas kernels: 0 us -> 11.7 us
  local copies, waits for them, and re-layouts: 27.8 us -> 18.4 us
  waiting for transfers between devices: 41 us -> 46.6 us
  matrix products: 4.32 us -> 0 us
    unnamed x19 -> x26, local copies, waits for them, and re-layouts: 11.9 us -> 0.18 us
    pallas_call x0 -> x1, Pallas kernels: none -> 11.7 us  [band(): pl.pallas_call(functools.partial(band_kernel, scale, count), out_shape=ou...]
    ppermute x4, waiting for transfers between devices: 8.61 us -> 13 us  [swapped(): return lax.ppermute(array, axis, [(i, i ^ bit) for i in range(peers)])]
    dot_general x2 -> x0, matrix products: 4.32 us -> none  [the longest x1 2.89 us: body(): jnp.einsum('qd,kd->qk', query_full, band_keys, preferred_element_type=jnp...]
    squeeze x3 -> x6, local copies, waits for them, and re-layouts: 0.33 us -> 2.96 us  [body(): b[1][:, quarter]]
    dynamic_slice x0 -> x2, local copies, waits for them, and re-layouts: none -> 1.83 us  [body(): pick = lambda g: lax.dynamic_index_in_dim(grid, g, axis=1, keepdims=False)]
    another operation x4 -> x3, local copies, waits for them, and re-layouts: 1.79 us -> 0.02 us  [the longest x1 1.77 us: body(): jnp.stack([b[0] for b in blocks]).reshape(len(offsets) * rows, depth)]
    reshape x1 -> x2, local copies, waits for them, and re-layouts: 2.46 us -> 3.39 us  [the longest x1 2.26 us: body(): grid = accum.reshape(slots, feats, group)]
  transfers between devices with their start and end apart: 12 -> 12, of which waited for: 4 -> 6; matrix products, arithmetic and copies ran while one was open for 14% -> 7% of each run, Pallas kernels for 0% -> 0%
where the time goes in v9:
time: 163 us; the launch traced here: 162 us
  starting transfers between devices  72.7 us (45%)
  waiting for transfers between devices  46.6 us (29%)
  local copies, waits for them, and re-layouts  18.4 us (11%)
  Pallas kernels  11.7 us (7%)
  other arithmetic  8.03 us (5%)
  between operations  5.01 us (3%)
    ppermute x6, starting transfers between devices, shifted(): lax.ppermute(array, axis, [(i, (i - by) % peers) for i in range(peers)])  23.8 us
    all_to_all x1, waiting for transfers between devices, body(): lax.all_to_all(shares.reshape(clusters, capacity, quarter), 'cluster', sp...  22.6 us
    all_to_all x1, starting transfers between devices, body(): lax.all_to_all(outgoing.reshape(clusters, capacity, queries.shape[1]), 'c...  21.9 us
    all_to_all x1, starting transfers between devices, body(): lax.all_to_all(shares.reshape(clusters, capacity, quarter), 'cluster', sp...  13.5 us
    ppermute x4, starting transfers between devices, swapped(): return lax.ppermute(array, axis, [(i, i ^ bit) for i in range(peers)])  13.4 us
    ppermute x4, waiting for transfers between devices, swapped(): return lax.ppermute(array, axis, [(i, i ^ bit) for i in range(peers)])  13 us
    pallas_call x1, Pallas kernels, band(): pl.pallas_call(functools.partial(band_kernel, scale, count), out_shape=ou...  11.7 us
    all_to_all x1, waiting for transfers between devices, body(): lax.all_to_all(outgoing.reshape(clusters, capacity, queries.shape[1]), 'c...  11 us
  transfers between devices with their start and end apart: 12, of which 6 were waited for; matrix products, arithmetic and copies ran while one was open for 7% of the time, Pallas kernels for 0%

profile of v9, /device:TPU:32, one launch (start us, length us, event | category | flops | bytes accessed | tf_op | source)
XLA Modules:
  0.0 162.4 jit_solution(10034565889533623625)
XLA Ops:
  0.0 1.0 reshape.960
  1.1 0.7 and_select_fusion
  1.8 0.1 copy.31
  2.0 1.0 pad_maximum_fusion.2.refs_0_
  3.0 5.4 %collective-permute-start.2 = (bf16[2,128,1024]{2,1,0:T(8,128)(2,1)S(1)}, bf16[2,128,1024]{2,1,0:T(8,128)(2,1)S(1)}, u32[]{:S(2)}, u32[]{:S(2)}) collective-permute-start(bf16[2,128,1024]{2,1,0:T(8,128)(2,1)S(1)} %pad_maximum_fusion.2.refs_0_), channel_id=1, source_target_pairs={{0,508},{4,0},{8,4},{12,8},{16,12},{20,16},{24,20},{28,24},{32,28}... | collective-permute-start | bytes 1572872 | tf_op jit(solution)/shard_map/ppermute | solution.py:19
  8.4 1.9 %collective-permute-start.3 = (bf16[2,128,1024]{2,1,0:T(8,128)(2,1)S(1)}, bf16[2,128,1024]{2,1,0:T(8,128)(2,1)S(1)}, u32[]{:S(2)}, u32[]{:S(2)}) collective-permute-start(bf16[2,128,1024]{2,1,0:T(8,128)(2,1)S(1)} %pad_maximum_fusion.2.refs_0_), channel_id=1, source_target_pairs={{0,4},{4,8},{8,12},{12,16},{16,20},{20,24},{24,28},{28,32},{32,36}... | collective-permute-start | bytes 1572872 | tf_op jit(solution)/shard_map/ppermute | solution.py:19
  10.3 3.0 %collective-permute-start.4 = (bf16[2,128,1024]{2,1,0:T(8,128)(2,1)S(1)}, bf16[2,128,1024]{2,1,0:T(8,128)(2,1)S(1)}, u32[]{:S(2)}, u32[]{:S(2)}) collective-permute-start(bf16[2,128,1024]{2,1,0:T(8,128)(2,1)S(1)} %pad_maximum_fusion.2.refs_0_), channel_id=1, source_target_pairs={{0,504},{4,508},{8,0},{12,4},{16,8},{20,12},{24,16},{28,20},{32,24... | collective-permute-start | bytes 1572872 | tf_op jit(solution)/shard_map/ppermute | solution.py:19
  13.3 2.8 %collective-permute-start.5 = (bf16[2,128,1024]{2,1,0:T(8,128)(2,1)S(1)}, bf16[2,128,1024]{2,1,0:T(8,128)(2,1)}, u32[]{:S(2)}, u32[]{:S(2)}) collective-permute-start(bf16[2,128,1024]{2,1,0:T(8,128)(2,1)S(1)} %pad_maximum_fusion.2.refs_0_), channel_id=1, source_target_pairs={{0,8},{4,12},{8,16},{12,20},{16,24},{20,28},{24,32},{28,36},{32,40... | collective-permute-start | bytes 1572872 | tf_op jit(solution)/shard_map/ppermute | solution.py:19
  16.2 6.4 %collective-permute-start.6 = (bf16[2,128,1024]{2,1,0:T(8,128)(2,1)S(1)}, bf16[2,128,1024]{2,1,0:T(8,128)(2,1)}, u32[]{:S(2)}, u32[]{:S(2)}) collective-permute-start(bf16[2,128,1024]{2,1,0:T(8,128)(2,1)S(1)} %pad_maximum_fusion.2.refs_0_), channel_id=1, source_target_pairs={{0,500},{4,504},{8,508},{12,0},{16,4},{20,8},{24,12},{28,16},{32,2... | collective-permute-start | bytes 1572872 | tf_op jit(solution)/shard_map/ppermute | solution.py:19
  22.6 0.1 copy.23
  22.7 0.2 fusion.42
  23.0 0.2 fusion.44
  23.2 1.9 %scatter_custom_fusion = bf16[512,256]{1,0:T(8,128)(2,1)S(1)} fusion(s32[256]{0:T(256)S(1)} %bitcast.158, bf16[256,256]{1,0:T(8,128)(2,1)} %param.7, bf16[]{:T(256)} %constant.39.clone.1), kind=kCustom, calls=%fused_computation.116 | custom fusion | bytes 262656 | tf_op jit(solution)/shard_map/scatter | solution.py:136
  25.1 0.8 reshape.956
  25.9 21.9 %all-to-all-start = ((bf16[128,4,256]{2,1,0:T(4,128)(2,1)}), bf16[128,4,256]{2,1,0:T(4,128)(2,1)S(1)}, u32[]{:S(2)}, u32[]{:S(2)}) async-start(bf16[128,4,256]{2,1,0:T(4,128)(2,1)} %reshape.956), calls=%async_computation | async-start | bytes 524288 | tf_op jit(solution)/shard_map/all_to_all | solution.py:137
  47.9 0.1 constant_dynamic-slice_fusion.3
  47.9 0.6 fusion.54
  52.9 0.1 stack.65
  53.1 0.1 broadcast_bitcast_fusion
  53.1 0.6 gather_fusion
  53.9 4.3 %collective-permute-start.7 = (bf16[2,128,1024]{2,1,0:T(8,128)(2,1)S(1)}, bf16[2,128,1024]{2,1,0:T(8,128)(2,1)}, u32[]{:S(2)}, u32[]{:S(2)}) collective-permute-start(bf16[2,128,1024]{2,1,0:T(8,128)(2,1)S(1)} %pad_maximum_fusion.2.refs_0_), channel_id=1, source_target_pairs={{0,12},{4,16},{8,20},{12,24},{16,28},{20,32},{24,36},{28,40},{32,4... | collective-permute-start | bytes 1572872 | tf_op jit(solution)/shard_map/ppermute | solution.py:19
  58.2 0.2 slice_reduce_fusion.5
  58.4 0.2 slice_reduce_fusion.4
  58.6 0.2 slice_reduce_fusion.3
  58.8 1.0 slice_bitcast_fusion.4
  59.8 0.2 slice_reduce_fusion.2
  60.0 1.0 slice_bitcast_fusion.3
  61.0 0.2 slice_reduce_fusion.1
  61.2 11.0 %all-to-all-done = bf16[128,4,256]{2,1,0:T(4,128)(2,1)S(1)} async-done(((bf16[128,4,256]{2,1,0:T(4,128)(2,1)}), bf16[128,4,256]{2,1,0:T(4,128)(2,1)S(1)}, u32[]{:S(2)}, u32[]{:S(2)}) %all-to-all-start) | async-done | bytes 262176 | tf_op jit(solution)/shard_map/all_to_all | solution.py:137
  72.2 4.6 %collective-permute-start = (bf16[512,256]{1,0:T(8,128)(2,1)S(1)}, bf16[512,256]{1,0:T(8,128)(2,1)S(1)}, u32[]{:S(2)}, u32[]{:S(2)}) collective-permute-start(bf16[512,256]{1,0:T(8,128)(2,1)S(1)} %reshape.957), channel_id=1, source_target_pairs={{0,2},{1,3},{2,0},{3,1},{4,6},{5,7},{6,4},{7,5},{8,10},{9,11},{10,... | collective-permute-start | bytes 786440 | tf_op jit(solution)/shard_map/ppermute | solution.py:24
  76.9 1.0 slice_bitcast_fusion.2
  78.0 4.0 %collective-permute-done = bf16[512,256]{1,0:T(8,128)(2,1)S(1)} collective-permute-done((bf16[512,256]{1,0:T(8,128)(2,1)S(1)}, bf16[512,256]{1,0:T(8,128)(2,1)S(1)}, u32[]{:S(2)}, u32[]{:S(2)}) %collective-permute-start) | collective-permute-done | bytes 262176 | tf_op jit(solution)/shard_map/ppermute | solution.py:24
  82.1 2.1 %collective-permute-start.1 = (bf16[2,512,256]{2,1,0:T(8,128)(2,1)S(1)}, bf16[2,512,256]{2,1,0:T(8,128)(2,1)S(1)}, u32[]{:S(2)}, u32[]{:S(2)}) collective-permute-start(bf16[2,512,256]{2,1,0:T(8,128)(2,1)S(1)} %pad_maximum_fusion.1), channel_id=1, source_target_pairs={{0,1},{1,0},{2,3},{3,2},{4,5},{5,4},{6,7},{7,6},{8,9},{9,8},{10,11... | collective-permute-start | bytes 1572872 | tf_op jit(solution)/shard_map/ppermute | solution.py:24
  84.2 0.2 slice_reduce_fusion
  84.4 0.6 bitcast_select_fusion.row_ref
  85.0 0.9 collective-permute-done.1
  85.9 0.1 pad_maximum_fusion
  86.0 0.6 gather_fusion.1
  86.6 0.2 select_bitcast_fusion
  86.8 1.1 copy.36
  87.9 11.7 %shard_map.73 = (f32[512,1024]{1,0:T(8,128)}, f32[512,128]{1,0:T(8,128)}, f32[512,128]{1,0:T(8,128)}) custom-call(bf16[512,1024]{1,0:T(8,128)(2,1)} %bitcast.146, f32[1,896]{1,0:T(1,128)} %bitcast_select_fusion.row_ref, bf16[2,128,1024]{2,1,0:T(8,128)(2,1)} %copy-done.4, bf16[2,128,1024]{2,1,0:T(8,128)(2,1)} %copy-done.5, bf16[2,128,1024]{2,1,0:T(8,128)(2,1)} %copy-done.6, ...), custom_call_target="tpu_custom_call" | custom-call | flops 1879048192 | bytes 6815744 | tf_op jit(solution)/shard_map/pallas_call | solution.py:95
  99.6 2.3 %reshape.961 = f32[512,4,256]{2,1,0:T(4,128)S(1)} reshape(f32[512,1024]{1,0:T(8,128)} %get-tuple-element.8) | data formatting | bytes 4194304 | tf_op jit(solution)/shard_map/reshape | solution.py:166
  101.9 0.5 convert_reduce_fusion.8
  102.4 0.9 constant_dynamic-slice_fusion
  103.3 0.5 fusion.23
  103.8 0.8 pad_maximum_fusion.3
  104.6 2.0 %collective-permute-start.8 = (bf16[2,512,256]{2,1,0:T(8,128)(2,1)}, bf16[2,512,256]{2,1,0:T(8,128)(2,1)S(1)}, u32[]{:S(2)}, u32[]{:S(2)}) collective-permute-start(bf16[2,512,256]{2,1,0:T(8,128)(2,1)} %pad_maximum_fusion.3), channel_id=1, source_target_pairs={{0,1},{1,0},{2,3},{3,2},{4,5},{5,4},{6,7},{7,6},{8,9},{9,8},{10,11... | collective-permute-start | bytes 1572872 | tf_op jit(solution)/shard_map/ppermute | solution.py:24
  106.7 0.9 constant_dynamic-slice_fusion.2
  107.7 1.0 collective-permute-done.8
  108.6 0.1 convert_element_type.144
  108.7 0.7 convert_reduce_fusion.5
  109.4 0.2 fusion.28
  109.7 0.3 convert_reduce_fusion.2
  110.0 0.2 fusion
  110.2 0.5 fusion.9
  110.7 4.6 %collective-permute-start.9 = (bf16[512,256]{1,0:T(8,128)(2,1)S(1)}, bf16[512,256]{1,0:T(8,128)(2,1)S(1)}, u32[]{:S(2)}, u32[]{:S(2)}) collective-permute-start(bf16[512,256]{1,0:T(8,128)(2,1)S(1)} %fusion.9), channel_id=1, source_target_pairs={{0,2},{1,3},{2,0},{3,1},{4,6},{5,7},{6,4},{7,5},{8,10},{9,11},{10,... | collective-permute-start | bytes 786440 | tf_op jit(solution)/shard_map/ppermute | solution.py:24
  115.4 7.1 %collective-permute-done.9 = bf16[512,256]{1,0:T(8,128)(2,1)S(1)} collective-permute-done((bf16[512,256]{1,0:T(8,128)(2,1)S(1)}, bf16[512,256]{1,0:T(8,128)(2,1)S(1)}, u32[]{:S(2)}, u32[]{:S(2)}) %collective-permute-start.9) | collective-permute-done | bytes 262176 | tf_op jit(solution)/shard_map/ppermute | solution.py:24
  122.5 0.7 fusion.37
  123.2 0.3 fusion.24
  123.4 0.8 reshape.962
  124.2 13.5 %all-to-all-start.1 = ((bf16[128,4,250]{2,1,0:T(4,128)(2,1)}), bf16[128,4,250]{2,1,0:T(4,128)(2,1)S(1)}, u32[]{:S(2)}, u32[]{:S(2)}) async-start(bf16[128,4,250]{2,1,0:T(4,128)(2,1)} %reshape.962), calls=%async_computation.1 | async-start | bytes 524288 | tf_op jit(solution)/shard_map/all_to_all | solution.py:183
  137.8 22.6 %all-to-all-done.1 = bf16[128,4,250]{2,1,0:T(4,128)(2,1)S(1)} async-done(((bf16[128,4,250]{2,1,0:T(4,128)(2,1)}), bf16[128,4,250]{2,1,0:T(4,128)(2,1)S(1)}, u32[]{:S(2)}, u32[]{:S(2)}) %all-to-all-start.1) | async-done | bytes 256032 | tf_op jit(solution)/shard_map/all_to_all | solution.py:183
  160.4 0.2 reshape.963
  160.6 1.8 %gather_fusion.2 = bf16[256,250]{1,0:T(8,128)(2,1)} fusion(bf16[512,250]{1,0:T(8,128)(2,1)S(1)} %reshape.963, s32[1024]{0:T(1024)S(1)} %pad_clamp_fusion), kind=kCustom, calls=%fused_computation.2 | custom fusion | bytes 257024 | tf_op jit(solution)/shard_map/gather | solution.py:190
  (59 shorter events, 0.7 us)
Async XLA Ops:
  0.0 47.9 %copy-start = (s32[128,7]{0,1:T(8,128)S(1)}, s32[128,7]{0,1:T(8,128)}, u32[]{:S(2)}) copy-start(s32[128,7]{0,1:T(8,128)} %param.9) | copy-start | bytes 10756
  0.0 22.6 %copy-start.8 = (s32[256,1]{0,1:T(1,128)S(1)}, s32[256,1]{0,1:T(1,128)}, u32[]{:S(2)}) copy-start(s32[256,1]{0,1:T(1,128)} %param.8) | copy-start | bytes 3076
  1.8 51.3 %copy-start.1 = (s32[4]{0:T(128)S(1)}, s32[4]{0:T(128)}, u32[]{:S(2)}) copy-start(s32[4]{0:T(128)} %constant.81.clone) | copy-start | bytes 52
  3.0 55.6 %copy-start.4 = (bf16[2,128,1024]{2,1,0:T(8,128)(2,1)}, bf16[2,128,1024]{2,1,0:T(8,128)(2,1)S(1)}, u32[]{:S(2)}) copy-start(bf16[2,128,1024]{2,1,0:T(8,128)(2,1)S(1)} %pad_maximum_fusion.2.refs_0_) | copy-start | bytes 1572868
  3.0 50.9 %collective-permute-start.2 = (bf16[2,128,1024]{2,1,0:T(8,128)(2,1)S(1)}, bf16[2,128,1024]{2,1,0:T(8,128)(2,1)S(1)}, u32[]{:S(2)}, u32[]{:S(2)}) collective-permute-start(bf16[2,128,1024]{2,1,0:T(8,128)(2,1)S(1)} %pad_maximum_fusion.2.refs_0_), channel_id=1, source_target_pairs={{0,508},{4,0},{8,4},{12,8},{16,12},{20,16},{24,20},{28,24},{32,28}... | collective-permute-start | bytes 1572872 | tf_op jit(solution)/shard_map/ppermute | solution.py:19
  8.4 50.0 %collective-permute-start.3 = (bf16[2,128,1024]{2,1,0:T(8,128)(2,1)S(1)}, bf16[2,128,1024]{2,1,0:T(8,128)(2,1)S(1)}, u32[]{:S(2)}, u32[]{:S(2)}) collective-permute-start(bf16[2,128,1024]{2,1,0:T(8,128)(2,1)S(1)} %pad_maximum_fusion.2.refs_0_), channel_id=1, source_target_pairs={{0,4},{4,8},{8,12},{12,16},{16,20},{20,24},{24,28},{28,32},{32,36}... | collective-permute-start | bytes 1572872 | tf_op jit(solution)/shard_map/ppermute | solution.py:19
  10.3 48.2 %collective-permute-start.4 = (bf16[2,128,1024]{2,1,0:T(8,128)(2,1)S(1)}, bf16[2,128,1024]{2,1,0:T(8,128)(2,1)S(1)}, u32[]{:S(2)}, u32[]{:S(2)}) collective-permute-start(bf16[2,128,1024]{2,1,0:T(8,128)(2,1)S(1)} %pad_maximum_fusion.2.refs_0_), channel_id=1, source_target_pairs={{0,504},{4,508},{8,0},{12,4},{16,8},{20,12},{24,16},{28,20},{32,24... | collective-permute-start | bytes 1572872 | tf_op jit(solution)/shard_map/ppermute | solution.py:19
  13.3 45.5 %collective-permute-start.5 = (bf16[2,128,1024]{2,1,0:T(8,128)(2,1)S(1)}, bf16[2,128,1024]{2,1,0:T(8,128)(2,1)}, u32[]{:S(2)}, u32[]{:S(2)}) collective-permute-start(bf16[2,128,1024]{2,1,0:T(8,128)(2,1)S(1)} %pad_maximum_fusion.2.refs_0_), channel_id=1, source_target_pairs={{0,8},{4,12},{8,16},{12,20},{16,24},{20,28},{24,32},{28,36},{32,40... | collective-permute-start | bytes 1572872 | tf_op jit(solution)/shard_map/ppermute | solution.py:19
  16.2 43.8 %collective-permute-start.6 = (bf16[2,128,1024]{2,1,0:T(8,128)(2,1)S(1)}, bf16[2,128,1024]{2,1,0:T(8,128)(2,1)}, u32[]{:S(2)}, u32[]{:S(2)}) collective-permute-start(bf16[2,128,1024]{2,1,0:T(8,128)(2,1)S(1)} %pad_maximum_fusion.2.refs_0_), channel_id=1, source_target_pairs={{0,500},{4,504},{8,508},{12,0},{16,4},{20,8},{24,12},{28,16},{32,2... | collective-permute-start | bytes 1572872 | tf_op jit(solution)/shard_map/ppermute | solution.py:19
  25.9 46.3 %all-to-all-start = ((bf16[128,4,256]{2,1,0:T(4,128)(2,1)}), bf16[128,4,256]{2,1,0:T(4,128)(2,1)S(1)}, u32[]{:S(2)}, u32[]{:S(2)}) async-start(bf16[128,4,256]{2,1,0:T(4,128)(2,1)} %reshape.956), calls=%async_computation | async-start | bytes 524288 | tf_op jit(solution)/shard_map/all_to_all | solution.py:137
  53.9 24.1 %copy-start.5 = (bf16[2,128,1024]{2,1,0:T(8,128)(2,1)}, bf16[2,128,1024]{2,1,0:T(8,128)(2,1)S(1)}, u32[]{:S(2)}) copy-start(bf16[2,128,1024]{2,1,0:T(8,128)(2,1)S(1)} %collective-permute-done.2.refs_1_) | copy-start | bytes 1572868
  53.9 23.0 %collective-permute-start.7 = (bf16[2,128,1024]{2,1,0:T(8,128)(2,1)S(1)}, bf16[2,128,1024]{2,1,0:T(8,128)(2,1)}, u32[]{:S(2)}, u32[]{:S(2)}) collective-permute-start(bf16[2,128,1024]{2,1,0:T(8,128)(2,1)S(1)} %pad_maximum_fusion.2.refs_0_), channel_id=1, source_target_pairs={{0,12},{4,16},{8,20},{12,24},{16,28},{20,32},{24,36},{28,40},{32,4... | collective-permute-start | bytes 1572872 | tf_op jit(solution)/shard_map/ppermute | solution.py:19
  58.4 2.8 %copy-start.6 = (bf16[2,128,1024]{2,1,0:T(8,128)(2,1)}, bf16[2,128,1024]{2,1,0:T(8,128)(2,1)S(1)}, u32[]{:S(2)}) copy-start(bf16[2,128,1024]{2,1,0:T(8,128)(2,1)S(1)} %collective-permute-done.3.refs_2_) | copy-start | bytes 1572868
  58.6 2.6 %copy-start.7 = (bf16[2,128,1024]{2,1,0:T(8,128)(2,1)}, bf16[2,128,1024]{2,1,0:T(8,128)(2,1)S(1)}, u32[]{:S(2)}) copy-start(bf16[2,128,1024]{2,1,0:T(8,128)(2,1)S(1)} %collective-permute-done.4.refs_3_) | copy-start | bytes 1572868
  72.2 9.8 %collective-permute-start = (bf16[512,256]{1,0:T(8,128)(2,1)S(1)}, bf16[512,256]{1,0:T(8,128)(2,1)S(1)}, u32[]{:S(2)}, u32[]{:S(2)}) collective-permute-start(bf16[512,256]{1,0:T(8,128)(2,1)S(1)} %reshape.957), channel_id=1, source_target_pairs={{0,2},{1,3},{2,0},{3,1},{4,6},{5,7},{6,4},{7,5},{8,10},{9,11},{10,... | collective-permute-start | bytes 786440 | tf_op jit(solution)/shard_map/ppermute | solution.py:24
  82.1 3.8 %collective-permute-start.1 = (bf16[2,512,256]{2,1,0:T(8,128)(2,1)S(1)}, bf16[2,512,256]{2,1,0:T(8,128)(2,1)S(1)}, u32[]{:S(2)}, u32[]{:S(2)}) collective-permute-start(bf16[2,512,256]{2,1,0:T(8,128)(2,1)S(1)} %pad_maximum_fusion.1), channel_id=1, source_target_pairs={{0,1},{1,0},{2,3},{3,2},{4,5},{5,4},{6,7},{7,6},{8,9},{9,8},{10,11... | collective-permute-start | bytes 1572872 | tf_op jit(solution)/shard_map/ppermute | solution.py:24
  99.6 2.3 %copy-start.2 = (f32[512,128]{1,0:T(8,128)S(1)}, f32[512,128]{1,0:T(8,128)}, u32[]{:S(2)}) copy-start(f32[512,128]{1,0:T(8,128)} %get-tuple-element.9) | copy-start | bytes 786436
  99.6 2.3 %copy-start.3 = (f32[512,128]{1,0:T(8,128)S(1)}, f32[512,128]{1,0:T(8,128)}, u32[]{:S(2)}) copy-start(f32[512,128]{1,0:T(8,128)} %get-tuple-element.10) | copy-start | bytes 786436
  104.6 4.0 %collective-permute-start.8 = (bf16[2,512,256]{2,1,0:T(8,128)(2,1)}, bf16[2,512,256]{2,1,0:T(8,128)(2,1)S(1)}, u32[]{:S(2)}, u32[]{:S(2)}) collective-permute-start(bf16[2,512,256]{2,1,0:T(8,128)(2,1)} %pad_maximum_fusion.3), channel_id=1, source_target_pairs={{0,1},{1,0},{2,3},{3,2},{4,5},{5,4},{6,7},{7,6},{8,9},{9,8},{10,11... | collective-permute-start | bytes 1572872 | tf_op jit(solution)/shard_map/ppermute | solution.py:24
  110.7 11.7 %collective-permute-start.9 = (bf16[512,256]{1,0:T(8,128)(2,1)S(1)}, bf16[512,256]{1,0:T(8,128)(2,1)S(1)}, u32[]{:S(2)}, u32[]{:S(2)}) collective-permute-start(bf16[512,256]{1,0:T(8,128)(2,1)S(1)} %fusion.9), channel_id=1, source_target_pairs={{0,2},{1,3},{2,0},{3,1},{4,6},{5,7},{6,4},{7,5},{8,10},{9,11},{10,... | collective-permute-start | bytes 786440 | tf_op jit(solution)/shard_map/ppermute | solution.py:24
  124.2 36.2 %all-to-all-start.1 = ((bf16[128,4,250]{2,1,0:T(4,128)(2,1)}), bf16[128,4,250]{2,1,0:T(4,128)(2,1)S(1)}, u32[]{:S(2)}, u32[]{:S(2)}) async-start(bf16[128,4,250]{2,1,0:T(4,128)(2,1)} %reshape.962), calls=%async_computation.1 | async-start | bytes 524288 | tf_op jit(solution)/shard_map/all_to_all | solution.py:183

commit v10 on v9

--- a/solution.py
+++ b/solution.py
@@ -70,14 +70,13 @@
     weight_ref[...] = weight.astype(jnp.bfloat16)
     top_ref[...] = jnp.broadcast_to(top, top_ref.shape)
     total_ref[...] = jnp.broadcast_to(total, total_ref.shape)
-    accum = jnp.zeros(accum_ref.shape, jnp.float32)
-    for b in range(count):
+    accum_ref[...] = jnp.dot(weight_ref[:, :rows], blocks[0][1], preferred_element_type=jnp.float32)
+    for b in range(1, count):
         cut = slice(b * rows, (b + 1) * rows)
-        accum = accum + jnp.dot(weight_ref[:, cut], blocks[b][1], preferred_element_type=jnp.float32)
-    accum_ref[...] = accum
-
-
-def band(query_full, row, blocks, scale):
+        accum_ref[...] += jnp.dot(weight_ref[:, cut], blocks[b][1], preferred_element_type=jnp.float32)
+
+
+def band(query_full, row, blocks, scale, tile=128):
     slots, depth = query_full.shape
     count = len(blocks)
     rows, width = blocks[0].shape[1], blocks[0].shape[2]
@@ -92,12 +91,24 @@
         transcendentals=slots * band_rows,
         bytes_accessed=2 * slots * depth + 2 * band_rows * (depth + width) + 4 * slots * width,
     )
+    whole = pl.BlockSpec(blocks[0].shape, lambda i: (0, 0, 0))
     accum, top, total = pl.pallas_call(
         functools.partial(band_kernel, scale, count),
         out_shape=out_shape,
+        grid=(slots // tile,),
+        in_specs=[
+            pl.BlockSpec((tile, depth), lambda i: (i, 0)),
+            pl.BlockSpec((1, band_rows), lambda i: (0, 0)),
+        ]
+        + [whole] * count,
+        out_specs=[
+            pl.BlockSpec((tile, width), lambda i: (i, 0)),
+            pl.BlockSpec((tile, 128), lambda i: (i, 0)),
+            pl.BlockSpec((tile, 128), lambda i: (i, 0)),
+        ],
         scratch_shapes=[
-            pltpu.VMEM((slots, band_rows), jnp.float32),
-            pltpu.VMEM((slots, band_rows), jnp.bfloat16),
+            pltpu.VMEM((tile, band_rows), jnp.float32),
+            pltpu.VMEM((tile, band_rows), jnp.bfloat16),
         ],
         cost_estimate=cost,
     )(query_full, row, *blocks)

time: 163 us -> 163 us (level)
  no operation moved by 1% of the time
where the time goes in v10:
time: 163 us; the launch traced here: 162 us
  starting transfers between devices  72.4 us (44%)
  waiting for transfers between devices  46.6 us (29%)
  local copies, waits for them, and re-layouts  18.4 us (11%)
  Pallas kernels  12 us (7%)
  other arithmetic  8.03 us (5%)
  between operations  5.02 us (3%)
    ppermute x6, starting transfers between devices, shifted(): lax.ppermute(array, axis, [(i, (i - by) % peers) for i in range(peers)])  23.8 us
    all_to_all x1, waiting for transfers between devices, body(): lax.all_to_all(shares.reshape(clusters, capacity, quarter), 'cluster', sp...  22.6 us
    all_to_all x1, starting transfers between devices, body(): lax.all_to_all(outgoing.reshape(clusters, capacity, queries.shape[1]), 'c...  21.9 us
    ppermute x4, starting transfers between devices, swapped(): return lax.ppermute(array, axis, [(i, i ^ bit) for i in range(peers)])  13.4 us
    all_to_all x1, starting transfers between devices, body(): lax.all_to_all(shares.reshape(clusters, capacity, quarter), 'cluster', sp...  13.3 us
    ppermute x4, waiting for transfers between devices, swapped(): return lax.ppermute(array, axis, [(i, i ^ bit) for i in range(peers)])  13 us
    pallas_call x1, Pallas kernels, band(): pl.pallas_call(functools.partial(band_kernel, scale, count), out_shape=ou...  12 us
    all_to_all x1, waiting for transfers between devices, body(): lax.all_to_all(outgoing.reshape(clusters, capacity, queries.shape[1]), 'c...  11 us
  transfers between devices with their start and end apart: 12, of which 6 were waited for; matrix products, arithmetic and copies ran while one was open for 7% of the time, Pallas kernels for 0%

profile of v10, /device:TPU:32, one launch (start us, length us, event | category | flops | bytes accessed | tf_op | source)
XLA Modules:
  0.0 162.5 jit_solution(8846872999935023759)
XLA Ops:
  0.0 1.0 reshape.960
  1.1 0.7 and_select_fusion
  1.8 0.1 copy.31
  2.0 1.0 pad_maximum_fusion.2.refs_0_
  3.0 5.4 %collective-permute-start.2 = (bf16[2,128,1024]{2,1,0:T(8,128)(2,1)S(1)}, bf16[2,128,1024]{2,1,0:T(8,128)(2,1)S(1)}, u32[]{:S(2)}, u32[]{:S(2)}) collective-permute-start(bf16[2,128,1024]{2,1,0:T(8,128)(2,1)S(1)} %pad_maximum_fusion.2.refs_0_), channel_id=1, source_target_pairs={{0,508},{4,0},{8,4},{12,8},{16,12},{20,16},{24,20},{28,24},{32,28}... | collective-permute-start | bytes 1572872 | tf_op jit(solution)/shard_map/ppermute | solution.py:19
  8.4 1.9 %collective-permute-start.3 = (bf16[2,128,1024]{2,1,0:T(8,128)(2,1)S(1)}, bf16[2,128,1024]{2,1,0:T(8,128)(2,1)S(1)}, u32[]{:S(2)}, u32[]{:S(2)}) collective-permute-start(bf16[2,128,1024]{2,1,0:T(8,128)(2,1)S(1)} %pad_maximum_fusion.2.refs_0_), channel_id=1, source_target_pairs={{0,4},{4,8},{8,12},{12,16},{16,20},{20,24},{24,28},{28,32},{32,36}... | collective-permute-start | bytes 1572872 | tf_op jit(solution)/shard_map/ppermute | solution.py:19
  10.3 3.0 %collective-permute-start.4 = (bf16[2,128,1024]{2,1,0:T(8,128)(2,1)S(1)}, bf16[2,128,1024]{2,1,0:T(8,128)(2,1)S(1)}, u32[]{:S(2)}, u32[]{:S(2)}) collective-permute-start(bf16[2,128,1024]{2,1,0:T(8,128)(2,1)S(1)} %pad_maximum_fusion.2.refs_0_), channel_id=1, source_target_pairs={{0,504},{4,508},{8,0},{12,4},{16,8},{20,12},{24,16},{28,20},{32,24... | collective-permute-start | bytes 1572872 | tf_op jit(solution)/shard_map/ppermute | solution.py:19
  13.3 2.8 %collective-permute-start.5 = (bf16[2,128,1024]{2,1,0:T(8,128)(2,1)S(1)}, bf16[2,128,1024]{2,1,0:T(8,128)(2,1)}, u32[]{:S(2)}, u32[]{:S(2)}) collective-permute-start(bf16[2,128,1024]{2,1,0:T(8,128)(2,1)S(1)} %pad_maximum_fusion.2.refs_0_), channel_id=1, source_target_pairs={{0,8},{4,12},{8,16},{12,20},{16,24},{20,28},{24,32},{28,36},{32,40... | collective-permute-start | bytes 1572872 | tf_op jit(solution)/shard_map/ppermute | solution.py:19
  16.2 6.4 %collective-permute-start.6 = (bf16[2,128,1024]{2,1,0:T(8,128)(2,1)S(1)}, bf16[2,128,1024]{2,1,0:T(8,128)(2,1)}, u32[]{:S(2)}, u32[]{:S(2)}) collective-permute-start(bf16[2,128,1024]{2,1,0:T(8,128)(2,1)S(1)} %pad_maximum_fusion.2.refs_0_), channel_id=1, source_target_pairs={{0,500},{4,504},{8,508},{12,0},{16,4},{20,8},{24,12},{28,16},{32,2... | collective-permute-start | bytes 1572872 | tf_op jit(solution)/shard_map/ppermute | solution.py:19
  22.6 0.1 copy.23
  22.7 0.2 fusion.42
  23.0 0.2 fusion.44
  23.2 1.9 %scatter_custom_fusion = bf16[512,256]{1,0:T(8,128)(2,1)S(1)} fusion(s32[256]{0:T(256)S(1)} %bitcast.158, bf16[256,256]{1,0:T(8,128)(2,1)} %param.7, bf16[]{:T(256)} %constant.39.clone.1), kind=kCustom, calls=%fused_computation.116 | custom fusion | bytes 262656 | tf_op jit(solution)/shard_map/scatter | solution.py:147
  25.1 0.8 reshape.956
  25.9 21.9 %all-to-all-start = ((bf16[128,4,256]{2,1,0:T(4,128)(2,1)}), bf16[128,4,256]{2,1,0:T(4,128)(2,1)S(1)}, u32[]{:S(2)}, u32[]{:S(2)}) async-start(bf16[128,4,256]{2,1,0:T(4,128)(2,1)} %reshape.956), calls=%async_computation | async-start | bytes 524288 | tf_op jit(solution)/shard_map/all_to_all | solution.py:148
  47.9 0.1 constant_dynamic-slice_fusion.3
  47.9 0.6 fusion.54
  52.9 0.1 stack.65
  53.1 0.1 broadcast_bitcast_fusion
  53.1 0.6 gather_fusion
  53.9 4.3 %collective-permute-start.7 = (bf16[2,128,1024]{2,1,0:T(8,128)(2,1)S(1)}, bf16[2,128,1024]{2,1,0:T(8,128)(2,1)}, u32[]{:S(2)}, u32[]{:S(2)}) collective-permute-start(bf16[2,128,1024]{2,1,0:T(8,128)(2,1)S(1)} %pad_maximum_fusion.2.refs_0_), channel_id=1, source_target_pairs={{0,12},{4,16},{8,20},{12,24},{16,28},{20,32},{24,36},{28,40},{32,4... | collective-permute-start | bytes 1572872 | tf_op jit(solution)/shard_map/ppermute | solution.py:19
  58.2 0.2 slice_reduce_fusion.5
  58.4 0.2 slice_reduce_fusion.4
  58.6 0.2 slice_reduce_fusion.3
  58.8 1.0 slice_bitcast_fusion.4
  59.8 0.2 slice_reduce_fusion.2
  60.0 1.0 slice_bitcast_fusion.3
  61.0 0.2 slice_reduce_fusion.1
  61.2 11.0 %all-to-all-done = bf16[128,4,256]{2,1,0:T(4,128)(2,1)S(1)} async-done(((bf16[128,4,256]{2,1,0:T(4,128)(2,1)}), bf16[128,4,256]{2,1,0:T(4,128)(2,1)S(1)}, u32[]{:S(2)}, u32[]{:S(2)}) %all-to-all-start) | async-done | bytes 262176 | tf_op jit(solution)/shard_map/all_to_all | solution.py:148
  72.2 4.6 %collective-permute-start = (bf16[512,256]{1,0:T(8,128)(2,1)S(1)}, bf16[512,256]{1,0:T(8,128)(2,1)S(1)}, u32[]{:S(2)}, u32[]{:S(2)}) collective-permute-start(bf16[512,256]{1,0:T(8,128)(2,1)S(1)} %reshape.957), channel_id=1, source_target_pairs={{0,2},{1,3},{2,0},{3,1},{4,6},{5,7},{6,4},{7,5},{8,10},{9,11},{10,... | collective-permute-start | bytes 786440 | tf_op jit(solution)/shard_map/ppermute | solution.py:24
  76.9 1.0 slice_bitcast_fusion.2
  78.0 4.0 %collective-permute-done = bf16[512,256]{1,0:T(8,128)(2,1)S(1)} collective-permute-done((bf16[512,256]{1,0:T(8,128)(2,1)S(1)}, bf16[512,256]{1,0:T(8,128)(2,1)S(1)}, u32[]{:S(2)}, u32[]{:S(2)}) %collective-permute-start) | collective-permute-done | bytes 262176 | tf_op jit(solution)/shard_map/ppermute | solution.py:24
  82.1 1.9 %collective-permute-start.1 = (bf16[2,512,256]{2,1,0:T(8,128)(2,1)S(1)}, bf16[2,512,256]{2,1,0:T(8,128)(2,1)S(1)}, u32[]{:S(2)}, u32[]{:S(2)}) collective-permute-start(bf16[2,512,256]{2,1,0:T(8,128)(2,1)S(1)} %pad_maximum_fusion.1), channel_id=1, source_target_pairs={{0,1},{1,0},{2,3},{3,2},{4,5},{5,4},{6,7},{7,6},{8,9},{9,8},{10,11... | collective-permute-start | bytes 1572872 | tf_op jit(solution)/shard_map/ppermute | solution.py:24
  84.0 0.2 slice_reduce_fusion
  84.2 0.6 bitcast_select_fusion.row_ref
  84.8 1.1 collective-permute-done.1
  85.9 0.1 pad_maximum_fusion
  86.0 0.6 gather_fusion.1
  86.6 0.2 select_bitcast_fusion
  86.8 1.1 copy.36
  87.9 12.0 %shard_map.73 = (f32[512,1024]{1,0:T(8,128)}, f32[512,128]{1,0:T(8,128)}, f32[512,128]{1,0:T(8,128)}) custom-call(bf16[512,1024]{1,0:T(8,128)(2,1)} %bitcast.146, f32[1,896]{1,0:T(1,128)} %bitcast_select_fusion.row_ref, bf16[2,128,1024]{2,1,0:T(8,128)(2,1)} %copy-done.4, bf16[2,128,1024]{2,1,0:T(8,128)(2,1)} %copy-done.5, bf16[2,128,1024]{2,1,0:T(8,128)(2,1)} %copy-done.6, ...), custom_call_target="tpu_custom_call" | custom-call | flops 1879048192 | bytes 6815744 | tf_op jit(solution)/shard_map/pallas_call | solution.py:95
  99.9 2.3 %reshape.961 = f32[512,4,256]{2,1,0:T(4,128)S(1)} reshape(f32[512,1024]{1,0:T(8,128)} %get-tuple-element.8) | data formatting | bytes 4194304 | tf_op jit(solution)/shard_map/reshape | solution.py:177
  102.2 0.5 convert_reduce_fusion.8
  102.7 0.9 constant_dynamic-slice_fusion
  103.6 0.5 fusion.23
  104.1 0.8 pad_maximum_fusion.3
  105.0 2.2 %collective-permute-start.8 = (bf16[2,512,256]{2,1,0:T(8,128)(2,1)}, bf16[2,512,256]{2,1,0:T(8,128)(2,1)S(1)}, u32[]{:S(2)}, u32[]{:S(2)}) collective-permute-start(bf16[2,512,256]{2,1,0:T(8,128)(2,1)} %pad_maximum_fusion.3), channel_id=1, source_target_pairs={{0,1},{1,0},{2,3},{3,2},{4,5},{5,4},{6,7},{7,6},{8,9},{9,8},{10,11... | collective-permute-start | bytes 1572872 | tf_op jit(solution)/shard_map/ppermute | solution.py:24
  107.2 0.9 constant_dynamic-slice_fusion.2
  108.2 0.8 collective-permute-done.8
  109.0 0.1 convert_element_type.144
  109.0 0.7 convert_reduce_fusion.5
  109.7 0.2 fusion.28
  110.0 0.3 convert_reduce_fusion.2
  110.3 0.2 fusion
  110.5 0.5 fusion.9
  111.0 4.6 %collective-permute-start.9 = (bf16[512,256]{1,0:T(8,128)(2,1)S(1)}, bf16[512,256]{1,0:T(8,128)(2,1)S(1)}, u32[]{:S(2)}, u32[]{:S(2)}) collective-permute-start(bf16[512,256]{1,0:T(8,128)(2,1)S(1)} %fusion.9), channel_id=1, source_target_pairs={{0,2},{1,3},{2,0},{3,1},{4,6},{5,7},{6,4},{7,5},{8,10},{9,11},{10,... | collective-permute-start | bytes 786440 | tf_op jit(solution)/shard_map/ppermute | solution.py:24
  115.7 7.1 %collective-permute-done.9 = bf16[512,256]{1,0:T(8,128)(2,1)S(1)} collective-permute-done((bf16[512,256]{1,0:T(8,128)(2,1)S(1)}, bf16[512,256]{1,0:T(8,128)(2,1)S(1)}, u32[]{:S(2)}, u32[]{:S(2)}) %collective-permute-start.9) | collective-permute-done | bytes 262176 | tf_op jit(solution)/shard_map/ppermute | solution.py:24
  122.8 0.7 fusion.37
  123.5 0.3 fusion.24
  123.8 0.8 reshape.962
  124.5 13.3 %all-to-all-start.1 = ((bf16[128,4,250]{2,1,0:T(4,128)(2,1)}), bf16[128,4,250]{2,1,0:T(4,128)(2,1)S(1)}, u32[]{:S(2)}, u32[]{:S(2)}) async-start(bf16[128,4,250]{2,1,0:T(4,128)(2,1)} %reshape.962), calls=%async_computation.1 | async-start | bytes 524288 | tf_op jit(solution)/shard_map/all_to_all | solution.py:194
  137.9 22.6 %all-to-all-done.1 = bf16[128,4,250]{2,1,0:T(4,128)(2,1)S(1)} async-done(((bf16[128,4,250]{2,1,0:T(4,128)(2,1)}), bf16[128,4,250]{2,1,0:T(4,128)(2,1)S(1)}, u32[]{:S(2)}, u32[]{:S(2)}) %all-to-all-start.1) | async-done | bytes 256032 | tf_op jit(solution)/shard_map/all_to_all | solution.py:194
  160.5 0.2 reshape.963
  160.7 1.8 %gather_fusion.2 = bf16[256,250]{1,0:T(8,128)(2,1)} fusion(bf16[512,250]{1,0:T(8,128)(2,1)S(1)} %reshape.963, s32[1024]{0:T(1024)S(1)} %pad_clamp_fusion), kind=kCustom, calls=%fused_computation.2 | custom fusion | bytes 257024 | tf_op jit(solution)/shard_map/gather | solution.py:201
  (59 shorter events, 0.7 us)
Async XLA Ops:
  0.0 47.9 %copy-start = (s32[128,7]{0,1:T(8,128)S(1)}, s32[128,7]{0,1:T(8,128)}, u32[]{:S(2)}) copy-start(s32[128,7]{0,1:T(8,128)} %param.9) | copy-start | bytes 10756
  0.0 22.6 %copy-start.8 = (s32[256,1]{0,1:T(1,128)S(1)}, s32[256,1]{0,1:T(1,128)}, u32[]{:S(2)}) copy-start(s32[256,1]{0,1:T(1,128)} %param.8) | copy-start | bytes 3076
  1.8 51.3 %copy-start.1 = (s32[4]{0:T(128)S(1)}, s32[4]{0:T(128)}, u32[]{:S(2)}) copy-start(s32[4]{0:T(128)} %constant.81.clone) | copy-start | bytes 52
  3.0 55.6 %copy-start.4 = (bf16[2,128,1024]{2,1,0:T(8,128)(2,1)}, bf16[2,128,1024]{2,1,0:T(8,128)(2,1)S(1)}, u32[]{:S(2)}) copy-start(bf16[2,128,1024]{2,1,0:T(8,128)(2,1)S(1)} %pad_maximum_fusion.2.refs_0_) | copy-start | bytes 1572868
  3.0 50.9 %collective-permute-start.2 = (bf16[2,128,1024]{2,1,0:T(8,128)(2,1)S(1)}, bf16[2,128,1024]{2,1,0:T(8,128)(2,1)S(1)}, u32[]{:S(2)}, u32[]{:S(2)}) collective-permute-start(bf16[2,128,1024]{2,1,0:T(8,128)(2,1)S(1)} %pad_maximum_fusion.2.refs_0_), channel_id=1, source_target_pairs={{0,508},{4,0},{8,4},{12,8},{16,12},{20,16},{24,20},{28,24},{32,28}... | collective-permute-start | bytes 1572872 | tf_op jit(solution)/shard_map/ppermute | solution.py:19
  8.4 50.0 %collective-permute-start.3 = (bf16[2,128,1024]{2,1,0:T(8,128)(2,1)S(1)}, bf16[2,128,1024]{2,1,0:T(8,128)(2,1)S(1)}, u32[]{:S(2)}, u32[]{:S(2)}) collective-permute-start(bf16[2,128,1024]{2,1,0:T(8,128)(2,1)S(1)} %pad_maximum_fusion.2.refs_0_), channel_id=1, source_target_pairs={{0,4},{4,8},{8,12},{12,16},{16,20},{20,24},{24,28},{28,32},{32,36}... | collective-permute-start | bytes 1572872 | tf_op jit(solution)/shard_map/ppermute | solution.py:19
  10.3 48.2 %collective-permute-start.4 = (bf16[2,128,1024]{2,1,0:T(8,128)(2,1)S(1)}, bf16[2,128,1024]{2,1,0:T(8,128)(2,1)S(1)}, u32[]{:S(2)}, u32[]{:S(2)}) collective-permute-start(bf16[2,128,1024]{2,1,0:T(8,128)(2,1)S(1)} %pad_maximum_fusion.2.refs_0_), channel_id=1, source_target_pairs={{0,504},{4,508},{8,0},{12,4},{16,8},{20,12},{24,16},{28,20},{32,24... | collective-permute-start | bytes 1572872 | tf_op jit(solution)/shard_map/ppermute | solution.py:19
  13.3 45.5 %collective-permute-start.5 = (bf16[2,128,1024]{2,1,0:T(8,128)(2,1)S(1)}, bf16[2,128,1024]{2,1,0:T(8,128)(2,1)}, u32[]{:S(2)}, u32[]{:S(2)}) collective-permute-start(bf16[2,128,1024]{2,1,0:T(8,128)(2,1)S(1)} %pad_maximum_fusion.2.refs_0_), channel_id=1, source_target_pairs={{0,8},{4,12},{8,16},{12,20},{16,24},{20,28},{24,32},{28,36},{32,40... | collective-permute-start | bytes 1572872 | tf_op jit(solution)/shard_map/ppermute | solution.py:19
  16.2 43.8 %collective-permute-start.6 = (bf16[2,128,1024]{2,1,0:T(8,128)(2,1)S(1)}, bf16[2,128,1024]{2,1,0:T(8,128)(2,1)}, u32[]{:S(2)}, u32[]{:S(2)}) collective-permute-start(bf16[2,128,1024]{2,1,0:T(8,128)(2,1)S(1)} %pad_maximum_fusion.2.refs_0_), channel_id=1, source_target_pairs={{0,500},{4,504},{8,508},{12,0},{16,4},{20,8},{24,12},{28,16},{32,2... | collective-permute-start | bytes 1572872 | tf_op jit(solution)/shard_map/ppermute | solution.py:19
  25.9 46.3 %all-to-all-start = ((bf16[128,4,256]{2,1,0:T(4,128)(2,1)}), bf16[128,4,256]{2,1,0:T(4,128)(2,1)S(1)}, u32[]{:S(2)}, u32[]{:S(2)}) async-start(bf16[128,4,256]{2,1,0:T(4,128)(2,1)} %reshape.956), calls=%async_computation | async-start | bytes 524288 | tf_op jit(solution)/shard_map/all_to_all | solution.py:148
  53.9 24.1 %copy-start.5 = (bf16[2,128,1024]{2,1,0:T(8,128)(2,1)}, bf16[2,128,1024]{2,1,0:T(8,128)(2,1)S(1)}, u32[]{:S(2)}) copy-start(bf16[2,128,1024]{2,1,0:T(8,128)(2,1)S(1)} %collective-permute-done.2.refs_1_) | copy-start | bytes 1572868
  53.9 23.0 %collective-permute-start.7 = (bf16[2,128,1024]{2,1,0:T(8,128)(2,1)S(1)}, bf16[2,128,1024]{2,1,0:T(8,128)(2,1)}, u32[]{:S(2)}, u32[]{:S(2)}) collective-permute-start(bf16[2,128,1024]{2,1,0:T(8,128)(2,1)S(1)} %pad_maximum_fusion.2.refs_0_), channel_id=1, source_target_pairs={{0,12},{4,16},{8,20},{12,24},{16,28},{20,32},{24,36},{28,40},{32,4... | collective-permute-start | bytes 1572872 | tf_op jit(solution)/shard_map/ppermute | solution.py:19
  58.4 2.8 %copy-start.6 = (bf16[2,128,1024]{2,1,0:T(8,128)(2,1)}, bf16[2,128,1024]{2,1,0:T(8,128)(2,1)S(1)}, u32[]{:S(2)}) copy-start(bf16[2,128,1024]{2,1,0:T(8,128)(2,1)S(1)} %collective-permute-done.3.refs_2_) | copy-start | bytes 1572868
  58.6 2.6 %copy-start.7 = (bf16[2,128,1024]{2,1,0:T(8,128)(2,1)}, bf16[2,128,1024]{2,1,0:T(8,128)(2,1)S(1)}, u32[]{:S(2)}) copy-start(bf16[2,128,1024]{2,1,0:T(8,128)(2,1)S(1)} %collective-permute-done.4.refs_3_) | copy-start | bytes 1572868
  72.2 9.8 %collective-permute-start = (bf16[512,256]{1,0:T(8,128)(2,1)S(1)}, bf16[512,256]{1,0:T(8,128)(2,1)S(1)}, u32[]{:S(2)}, u32[]{:S(2)}) collective-permute-start(bf16[512,256]{1,0:T(8,128)(2,1)S(1)} %reshape.957), channel_id=1, source_target_pairs={{0,2},{1,3},{2,0},{3,1},{4,6},{5,7},{6,4},{7,5},{8,10},{9,11},{10,... | collective-permute-start | bytes 786440 | tf_op jit(solution)/shard_map/ppermute | solution.py:24
  82.1 3.8 %collective-permute-start.1 = (bf16[2,512,256]{2,1,0:T(8,128)(2,1)S(1)}, bf16[2,512,256]{2,1,0:T(8,128)(2,1)S(1)}, u32[]{:S(2)}, u32[]{:S(2)}) collective-permute-start(bf16[2,512,256]{2,1,0:T(8,128)(2,1)S(1)} %pad_maximum_fusion.1), channel_id=1, source_target_pairs={{0,1},{1,0},{2,3},{3,2},{4,5},{5,4},{6,7},{7,6},{8,9},{9,8},{10,11... | collective-permute-start | bytes 1572872 | tf_op jit(solution)/shard_map/ppermute | solution.py:24
  99.9 2.3 %copy-start.2 = (f32[512,128]{1,0:T(8,128)S(1)}, f32[512,128]{1,0:T(8,128)}, u32[]{:S(2)}) copy-start(f32[512,128]{1,0:T(8,128)} %get-tuple-element.9) | copy-start | bytes 786436
  99.9 2.3 %copy-start.3 = (f32[512,128]{1,0:T(8,128)S(1)}, f32[512,128]{1,0:T(8,128)}, u32[]{:S(2)}) copy-start(f32[512,128]{1,0:T(8,128)} %get-tuple-element.10) | copy-start | bytes 786436
  105.0 4.0 %collective-permute-start.8 = (bf16[2,512,256]{2,1,0:T(8,128)(2,1)}, bf16[2,512,256]{2,1,0:T(8,128)(2,1)S(1)}, u32[]{:S(2)}, u32[]{:S(2)}) collective-permute-start(bf16[2,512,256]{2,1,0:T(8,128)(2,1)} %pad_maximum_fusion.3), channel_id=1, source_target_pairs={{0,1},{1,0},{2,3},{3,2},{4,5},{5,4},{6,7},{7,6},{8,9},{9,8},{10,11... | collective-permute-start | bytes 1572872 | tf_op jit(solution)/shard_map/ppermute | solution.py:24
  111.0 11.7 %collective-permute-start.9 = (bf16[512,256]{1,0:T(8,128)(2,1)S(1)}, bf16[512,256]{1,0:T(8,128)(2,1)S(1)}, u32[]{:S(2)}, u32[]{:S(2)}) collective-permute-start(bf16[512,256]{1,0:T(8,128)(2,1)S(1)} %fusion.9), channel_id=1, source_target_pairs={{0,2},{1,3},{2,0},{3,1},{4,6},{5,7},{6,4},{7,5},{8,10},{9,11},{10,... | collective-permute-start | bytes 786440 | tf_op jit(solution)/shard_map/ppermute | solution.py:24
  124.5 36.0 %all-to-all-start.1 = ((bf16[128,4,250]{2,1,0:T(4,128)(2,1)}), bf16[128,4,250]{2,1,0:T(4,128)(2,1)S(1)}, u32[]{:S(2)}, u32[]{:S(2)}) async-start(bf16[128,4,250]{2,1,0:T(4,128)(2,1)} %reshape.962), calls=%async_computation.1 | async-start | bytes 524288 | tf_op jit(solution)/shard_map/all_to_all | solution.py:194

commit v11 on v8

--- a/solution.py
+++ b/solution.py
@@ -72,7 +72,13 @@
     offsets = [0]
     for reach in range(1, REACH + 1):
         offsets += [reach, -reach]
-    blocks = [block] + [shifted(block, "cluster", o) for o in offsets[1:]]
+    above = shifted(block, "cluster", 1)
+    below = shifted(block, "cluster", -1)
+    pair = jnp.stack([block, above])
+    far_above = shifted(pair, "cluster", 2)
+    far_below = shifted(pair, "cluster", -3)
+    reached = {0: block, 1: above, -1: below, 2: far_above[0], 3: far_above[1], -3: far_below[0], -2: far_below[1]}
+    blocks = [reached[o] for o in offsets]
 
     target = assign[:, 0]
     onehot = (target[:, None] == jnp.arange(clusters, dtype=jnp.int32)[None, :]).astype(jnp.int32)

time: 159 us -> 180 us (1.13)
  waiting for transfers between devices: 41 us -> 63.2 us
    ppermute x4, waiting for transfers between devices: 8.61 us -> 23.2 us  [swapped(): return lax.ppermute(array, axis, [(i, i ^ bit) for i in range(peers)])]
    ppermute x6 -> x4, waiting for transfers between devices: 0.02 us -> 10.2 us  [shifted(): lax.ppermute(array, axis, [(i, (i - by) % peers) for i in range(peers)])]
    all_to_all x1, starting transfers between devices: 13.3 us -> 23.3 us  [body(): lax.all_to_all(shares.reshape(clusters, capacity, quarter), 'cluster', sp...]
    ppermute x6 -> x4, starting transfers between devices: 23.8 us -> 14 us  [shifted(): lax.ppermute(array, axis, [(i, (i - by) % peers) for i in range(peers)])]
    all_to_all x1, waiting for transfers between devices: 9.68 us -> 7.1 us  [body(): lax.all_to_all(outgoing.reshape(clusters, capacity, queries.shape[1]), 'c...]
    another operation x4 -> x5, other arithmetic: 1.26 us -> 3.15 us  [the longest x2 2.9 us: body(): pair = jnp.stack([block, above])]
    unnamed x19 -> x17, local copies, waits for them, and re-layouts: 11.9 us -> 11.9 us
  transfers between devices with their start and end apart: 12 -> 10, of which waited for: 4 -> 6; matrix products, arithmetic and copies ran while one was open for 14% -> 12% of each run, Pallas kernels for 0% -> 0%
where the time goes in v11:
time: 180 us; the launch traced here: 179 us
  starting transfers between devices  71.9 us (40%)
  waiting for transfers between devices  63.2 us (35%)
  local copies, waits for them, and re-layouts  27.8 us (15%)
  other arithmetic  6.91 us (4%)
  between operations  4.9 us (3%)
  matrix products  4.32 us (2%)
    all_to_all x1, starting transfers between devices, body(): lax.all_to_all(shares.reshape(clusters, capacity, quarter), 'cluster', sp...  23.3 us
    ppermute x4, waiting for transfers between devices, swapped(): return lax.ppermute(array, axis, [(i, i ^ bit) for i in range(peers)])  23.2 us
    all_to_all x1, waiting for transfers between devices, body(): lax.all_to_all(shares.reshape(clusters, capacity, quarter), 'cluster', sp...  22.7 us
    all_to_all x1, starting transfers between devices, body(): lax.all_to_all(outgoing.reshape(clusters, capacity, queries.shape[1]), 'c...  21.5 us
    ppermute x4, starting transfers between devices, shifted(): lax.ppermute(array, axis, [(i, (i - by) % peers) for i in range(peers)])  14 us
    ppermute x4, starting transfers between devices, swapped(): return lax.ppermute(array, axis, [(i, i ^ bit) for i in range(peers)])  13.1 us
    unnamed x17, local copies, waits for them, and re-layouts  11.9 us
    ppermute x4, waiting for transfers between devices, shifted(): lax.ppermute(array, axis, [(i, (i - by) % peers) for i in range(peers)])  10.2 us
  transfers between devices with their start and end apart: 10, of which 6 were waited for; matrix products, arithmetic and copies ran while one was open for 12% of the time, Pallas kernels for 0%

profile of v11, /device:TPU:32, one launch (start us, length us, event | category | flops | bytes accessed | tf_op | source)
XLA Modules:
  0.0 179.0 jit_solution(17116534714318436961)
XLA Ops:
  0.0 1.0 reshape.927
  1.1 0.7 and_select_fusion
  1.8 0.1 copy.33
  2.0 1.8 %fusion.60 = (bf16[1,2,128,1024]{3,2,1,0:T(8,128)(2,1)S(1)}, bf16[2,128,1024]{2,1,0:T(8,128)(2,1)}) fusion(bf16[1,128,1024]{2,1,0:T(8,128)(2,1)S(1)} %copy.33, bf16[1,128,1024]{2,1,0:T(8,128)(2,1)} %bitcast.153), kind=kLoop, calls=%fused_computation.154 | loop fusion | flops 262144 | bytes 1572864 | tf_op jit(solution)/shard_map/stack | solution.py:77
  3.8 5.4 %collective-permute-start.2 = (bf16[2,128,1024]{2,1,0:T(8,128)(2,1)}, bf16[2,128,1024]{2,1,0:T(8,128)(2,1)S(1)}, u32[]{:S(2)}, u32[]{:S(2)}) collective-permute-start(bf16[2,128,1024]{2,1,0:T(8,128)(2,1)} %get-tuple-element.29), channel_id=1, source_target_pairs={{0,508},{4,0},{8,4},{12,8},{16,12},{20,16},{24,20},{28,24},{32,28}... | collective-permute-start | bytes 1572872 | tf_op jit(solution)/shard_map/ppermute | solution.py:16
  9.2 1.9 %collective-permute-start.3 = (bf16[2,128,1024]{2,1,0:T(8,128)(2,1)}, bf16[2,128,1024]{2,1,0:T(8,128)(2,1)}, u32[]{:S(2)}, u32[]{:S(2)}) collective-permute-start(bf16[2,128,1024]{2,1,0:T(8,128)(2,1)} %get-tuple-element.29), channel_id=1, source_target_pairs={{0,4},{4,8},{8,12},{12,16},{16,20},{20,24},{24,28},{28,32},{32,36}... | collective-permute-start | bytes 1572872 | tf_op jit(solution)/shard_map/ppermute | solution.py:16
  11.1 0.1 copy.30
  11.3 0.2 fusion.25
  11.6 0.2 fusion.27
  11.7 1.9 %scatter_custom_fusion = bf16[512,256]{1,0:T(8,128)(2,1)S(1)} fusion(s32[256]{0:T(256)S(1)} %bitcast.175, bf16[256,256]{1,0:T(8,128)(2,1)} %param.7, bf16[]{:T(256)} %constant.71.clone.1), kind=kCustom, calls=%fused_computation.67 | custom fusion | bytes 262656 | tf_op jit(solution)/shard_map/scatter | solution.py:87
  13.7 0.8 reshape.924
  14.4 21.5 %all-to-all-start = ((bf16[128,4,256]{2,1,0:T(4,128)(2,1)}), bf16[128,4,256]{2,1,0:T(4,128)(2,1)S(1)}, u32[]{:S(2)}, u32[]{:S(2)}) async-start(bf16[128,4,256]{2,1,0:T(4,128)(2,1)} %reshape.924), calls=%async_computation | async-start | bytes 524288 | tf_op jit(solution)/shard_map/all_to_all | solution.py:88
  35.9 0.1 constant_dynamic-slice_fusion
  36.0 0.6 fusion.61
  41.1 0.6 gather_fusion
  41.7 0.1 stack.77
  41.8 0.1 broadcast_bitcast_fusion
  41.9 1.7 constant_dynamic-update-slice_fusion
  43.6 1.1 pad_maximum_fusion.1
  44.7 4.6 %collective-permute-start.4 = (bf16[2,2,128,1024]{3,2,1,0:T(8,128)(2,1)}, bf16[2,2,128,1024]{3,2,1,0:T(8,128)(2,1)}, u32[]{:S(2)}, u32[]{:S(2)}) collective-permute-start(bf16[2,2,128,1024]{3,2,1,0:T(8,128)(2,1)} %pad_maximum_fusion.1), channel_id=1, source_target_pairs={{0,504},{4,508},{8,0},{12,4},{16,8},{20,12},{24,16},{28,20},{32,24... | collective-permute-start | bytes 3145736 | tf_op jit(solution)/shard_map/ppermute | solution.py:16
  49.3 2.2 %collective-permute-start.5 = (bf16[2,2,128,1024]{3,2,1,0:T(8,128)(2,1)}, bf16[2,2,128,1024]{3,2,1,0:T(8,128)(2,1)}, u32[]{:S(2)}, u32[]{:S(2)}) collective-permute-start(bf16[2,2,128,1024]{3,2,1,0:T(8,128)(2,1)} %pad_maximum_fusion.1), channel_id=1, source_target_pairs={{0,12},{4,16},{8,20},{12,24},{16,28},{20,32},{24,36},{28,40},{32,4... | collective-permute-start | bytes 3145736 | tf_op jit(solution)/shard_map/ppermute | solution.py:16
  51.5 7.1 %all-to-all-done = bf16[128,4,256]{2,1,0:T(4,128)(2,1)S(1)} async-done(((bf16[128,4,256]{2,1,0:T(4,128)(2,1)}), bf16[128,4,256]{2,1,0:T(4,128)(2,1)S(1)}, u32[]{:S(2)}, u32[]{:S(2)}) %all-to-all-start) | async-done | bytes 262176 | tf_op jit(solution)/shard_map/all_to_all | solution.py:88
  58.7 4.6 %collective-permute-start = (bf16[512,256]{1,0:T(8,128)(2,1)S(1)}, bf16[512,256]{1,0:T(8,128)(2,1)S(1)}, u32[]{:S(2)}, u32[]{:S(2)}) collective-permute-start(bf16[512,256]{1,0:T(8,128)(2,1)S(1)} %reshape.925), channel_id=1, source_target_pairs={{0,2},{1,3},{2,0},{3,1},{4,6},{5,7},{6,4},{7,5},{8,10},{9,11},{10,... | collective-permute-start | bytes 786440 | tf_op jit(solution)/shard_map/ppermute | solution.py:21
  63.3 0.7 slice_dynamic-update-slice_fusion.3
  64.0 1.8 slice_dynamic-update-slice_fusion.2
  65.8 0.1 stack_reshape.7
  65.9 15.8 %collective-permute-done = bf16[512,256]{1,0:T(8,128)(2,1)S(1)} collective-permute-done((bf16[512,256]{1,0:T(8,128)(2,1)S(1)}, bf16[512,256]{1,0:T(8,128)(2,1)S(1)}, u32[]{:S(2)}, u32[]{:S(2)}) %collective-permute-start) | collective-permute-done | bytes 262176 | tf_op jit(solution)/shard_map/ppermute | solution.py:21
  81.7 1.9 %collective-permute-start.1 = (bf16[2,512,256]{2,1,0:T(8,128)(2,1)S(1)}, bf16[2,512,256]{2,1,0:T(8,128)(2,1)S(1)}, u32[]{:S(2)}, u32[]{:S(2)}) collective-permute-start(bf16[2,512,256]{2,1,0:T(8,128)(2,1)S(1)} %pad_maximum_fusion.2), channel_id=1, source_target_pairs={{0,1},{1,0},{2,3},{3,2},{4,5},{5,4},{6,7},{7,6},{8,9},{9,8},{10,11... | collective-permute-start | bytes 1572872 | tf_op jit(solution)/shard_map/ppermute | solution.py:21
  83.7 10.2 %collective-permute-done.4 = bf16[2,2,128,1024]{3,2,1,0:T(8,128)(2,1)} collective-permute-done((bf16[2,2,128,1024]{3,2,1,0:T(8,128)(2,1)}, bf16[2,2,128,1024]{3,2,1,0:T(8,128)(2,1)}, u32[]{:S(2)}, u32[]{:S(2)}) %collective-permute-start.4) | collective-permute-done | bytes 1048608 | tf_op jit(solution)/shard_map/ppermute | solution.py:16
  93.9 1.8 fusion.24
  95.6 1.8 fusion.23
  97.4 1.8 fusion.22
  99.2 1.8 fusion.21
  100.9 2.4 %copy.35 = bf16[896,1024]{0,1:T(8,128)(2,1)} copy(bf16[896,1024]{1,0:T(8,128)(2,1)S(1)} %bitcast.148) | data formatting | bytes 3670016 | tf_op jit(solution)/shard_map/reshape | solution.py:103
  103.4 0.7 fusion.32
  104.1 0.1 pad_maximum_fusion
  104.2 0.6 gather_fusion.1
  104.9 0.2 select_bitcast_fusion
  105.0 0.5 copy.32
  105.6 2.9 %fusion.62 = (f32[512]{0:T(512)S(1)}, f32[512,896]{1,0:T(8,128)S(1)}) fusion(f32[896]{0:T(1024)S(1)} %fusion.32, bf16[512,1024]{0,1:T(8,128)(2,1)S(1)} %bitcast.151, bf16[896,1024]{1,0:T(8,128)(2,1)} %bitcast.163, pred[896]{0:T(1024)(128)(4,1)S(1)} %broadcast_bitcast_fusion), kind=kOutput, calls=%fused_computation.156 | convolution fusion | flops 941358592 | bytes 4725120 | tf_op jit(solution)/shard_map/qd,kd->qk/dot_general | solution.py:109
  108.5 0.5 fusion
  109.0 1.0 copy-done.2
  110.0 1.4 fusion.4
  111.4 1.3 copy-done.3
  112.8 0.1 copy.39
  113.0 0.1 copy.40
  113.1 0.3 select_convert_fusion.1
  113.4 1.9 %collective-permute-start.6 = (bf16[2,512,256]{1,2,0:T(8,128)(2,1)S(1)}, bf16[2,512,256]{1,2,0:T(8,128)(2,1)S(1)}, u32[]{:S(2)}, u32[]{:S(2)}) collective-permute-start(bf16[2,512,256]{1,2,0:T(8,128)(2,1)S(1)} %pad_maximum_fusion.4), channel_id=1, source_target_pairs={{0,1},{1,0},{2,3},{3,2},{4,5},{5,4},{6,7},{7,6},{8,9},{9,8},{10,11... | collective-permute-start | bytes 1572872 | tf_op jit(solution)/shard_map/ppermute | solution.py:21
  115.4 1.3 dynamic-slice_bitcast_fusion.3
  116.7 0.2 copy.37
  116.9 0.2 copy.38
  117.1 0.2 collective-permute-done.6
  117.3 0.1 convert_element_type.251
  117.5 0.2 fusion.2
  117.7 0.3 fusion.15
  117.9 4.6 %collective-permute-start.7 = (bf16[512,256]{0,1:T(8,128)(2,1)S(1)}, bf16[512,256]{0,1:T(8,128)(2,1)S(1)}, u32[]{:S(2)}, u32[]{:S(2)}) collective-permute-start(bf16[512,256]{0,1:T(8,128)(2,1)S(1)} %fusion.15), channel_id=1, source_target_pairs={{0,2},{1,3},{2,0},{3,1},{4,6},{5,7},{6,4},{7,5},{8,10},{9,11},{10,... | collective-permute-start | bytes 786440 | tf_op jit(solution)/shard_map/ppermute | solution.py:21
  122.6 7.2 %collective-permute-done.7 = bf16[512,256]{0,1:T(8,128)(2,1)S(1)} collective-permute-done((bf16[512,256]{0,1:T(8,128)(2,1)S(1)}, bf16[512,256]{0,1:T(8,128)(2,1)S(1)}, u32[]{:S(2)}, u32[]{:S(2)}) %collective-permute-start.7) | collective-permute-done | bytes 262176 | tf_op jit(solution)/shard_map/ppermute | solution.py:21
  130.0 0.1 fusion.16
  130.1 0.1 copy.41
  130.3 0.8 reshape.930
  131.1 23.3 %all-to-all-start.1 = ((bf16[128,4,250]{2,1,0:T(4,128)(2,1)}), bf16[128,4,250]{2,1,0:T(4,128)(2,1)S(1)}, u32[]{:S(2)}, u32[]{:S(2)}) async-start(bf16[128,4,250]{2,1,0:T(4,128)(2,1)} %reshape.930), calls=%async_computation.1 | async-start | bytes 524288 | tf_op jit(solution)/shard_map/all_to_all | solution.py:141
  154.3 22.7 %all-to-all-done.1 = bf16[128,4,250]{2,1,0:T(4,128)(2,1)S(1)} async-done(((bf16[128,4,250]{2,1,0:T(4,128)(2,1)}), bf16[128,4,250]{2,1,0:T(4,128)(2,1)S(1)}, u32[]{:S(2)}, u32[]{:S(2)}) %all-to-all-start.1) | async-done | bytes 256032 | tf_op jit(solution)/shard_map/all_to_all | solution.py:141
  177.0 0.2 reshape.931
  177.2 1.8 %gather_fusion.2 = bf16[256,250]{1,0:T(8,128)(2,1)} fusion(bf16[512,250]{1,0:T(8,128)(2,1)S(1)} %reshape.931, s32[1024]{0:T(1024)S(1)} %pad_clamp_fusion), kind=kCustom, calls=%fused_computation.2 | custom fusion | bytes 257024 | tf_op jit(solution)/shard_map/gather | solution.py:148
  (45 shorter events, 0.6 us)
Async XLA Ops:
  0.0 35.9 %copy-start = (s32[128,7]{0,1:T(8,128)S(1)}, s32[128,7]{0,1:T(8,128)}, u32[]{:S(2)}) copy-start(s32[128,7]{0,1:T(8,128)} %param.9) | copy-start | bytes 10756
  0.0 11.1 %copy-start.4 = (s32[256,1]{0,1:T(1,128)S(1)}, s32[256,1]{0,1:T(1,128)}, u32[]{:S(2)}) copy-start(s32[256,1]{0,1:T(1,128)} %param.8) | copy-start | bytes 3076
  2.0 39.1 %copy-start.1 = (s32[4]{0:T(128)S(1)}, s32[4]{0:T(128)}, u32[]{:S(2)}) copy-start(s32[4]{0:T(128)} %constant.85.clone) | copy-start | bytes 52
  3.8 39.8 %collective-permute-start.2 = (bf16[2,128,1024]{2,1,0:T(8,128)(2,1)}, bf16[2,128,1024]{2,1,0:T(8,128)(2,1)S(1)}, u32[]{:S(2)}, u32[]{:S(2)}) collective-permute-start(bf16[2,128,1024]{2,1,0:T(8,128)(2,1)} %get-tuple-element.29), channel_id=1, source_target_pairs={{0,508},{4,0},{8,4},{12,8},{16,12},{20,16},{24,20},{28,24},{32,28}... | collective-permute-start | bytes 1572872 | tf_op jit(solution)/shard_map/ppermute | solution.py:16
  9.2 54.8 %collective-permute-start.3 = (bf16[2,128,1024]{2,1,0:T(8,128)(2,1)}, bf16[2,128,1024]{2,1,0:T(8,128)(2,1)}, u32[]{:S(2)}, u32[]{:S(2)}) collective-permute-start(bf16[2,128,1024]{2,1,0:T(8,128)(2,1)} %get-tuple-element.29), channel_id=1, source_target_pairs={{0,4},{4,8},{8,12},{12,16},{16,20},{20,24},{24,28},{28,32},{32,36}... | collective-permute-start | bytes 1572872 | tf_op jit(solution)/shard_map/ppermute | solution.py:16
  14.4 44.2 %all-to-all-start = ((bf16[128,4,256]{2,1,0:T(4,128)(2,1)}), bf16[128,4,256]{2,1,0:T(4,128)(2,1)S(1)}, u32[]{:S(2)}, u32[]{:S(2)}) async-start(bf16[128,4,256]{2,1,0:T(4,128)(2,1)} %reshape.924), calls=%async_computation | async-start | bytes 524288 | tf_op jit(solution)/shard_map/all_to_all | solution.py:88
  44.7 49.2 %collective-permute-start.4 = (bf16[2,2,128,1024]{3,2,1,0:T(8,128)(2,1)}, bf16[2,2,128,1024]{3,2,1,0:T(8,128)(2,1)}, u32[]{:S(2)}, u32[]{:S(2)}) collective-permute-start(bf16[2,2,128,1024]{3,2,1,0:T(8,128)(2,1)} %pad_maximum_fusion.1), channel_id=1, source_target_pairs={{0,504},{4,508},{8,0},{12,4},{16,8},{20,12},{24,16},{28,20},{32,24... | collective-permute-start | bytes 3145736 | tf_op jit(solution)/shard_map/ppermute | solution.py:16
  49.3 46.3 %collective-permute-start.5 = (bf16[2,2,128,1024]{3,2,1,0:T(8,128)(2,1)}, bf16[2,2,128,1024]{3,2,1,0:T(8,128)(2,1)}, u32[]{:S(2)}, u32[]{:S(2)}) collective-permute-start(bf16[2,2,128,1024]{3,2,1,0:T(8,128)(2,1)} %pad_maximum_fusion.1), channel_id=1, source_target_pairs={{0,12},{4,16},{8,20},{12,24},{16,28},{20,32},{24,36},{28,40},{32,4... | collective-permute-start | bytes 3145736 | tf_op jit(solution)/shard_map/ppermute | solution.py:16
  58.7 23.0 %collective-permute-start = (bf16[512,256]{1,0:T(8,128)(2,1)S(1)}, bf16[512,256]{1,0:T(8,128)(2,1)S(1)}, u32[]{:S(2)}, u32[]{:S(2)}) collective-permute-start(bf16[512,256]{1,0:T(8,128)(2,1)S(1)} %reshape.925), channel_id=1, source_target_pairs={{0,2},{1,3},{2,0},{3,1},{4,6},{5,7},{6,4},{7,5},{8,10},{9,11},{10,... | collective-permute-start | bytes 786440 | tf_op jit(solution)/shard_map/ppermute | solution.py:21
  81.7 22.4 %collective-permute-start.1 = (bf16[2,512,256]{2,1,0:T(8,128)(2,1)S(1)}, bf16[2,512,256]{2,1,0:T(8,128)(2,1)S(1)}, u32[]{:S(2)}, u32[]{:S(2)}) collective-permute-start(bf16[2,512,256]{2,1,0:T(8,128)(2,1)S(1)} %pad_maximum_fusion.2), channel_id=1, source_target_pairs={{0,1},{1,0},{2,3},{3,2},{4,5},{5,4},{6,7},{7,6},{8,9},{9,8},{10,11... | collective-permute-start | bytes 1572872 | tf_op jit(solution)/shard_map/ppermute | solution.py:21
  108.5 1.5 copy-start.2
  111.4 1.3 copy-start.3
  113.4 3.8 %collective-permute-start.6 = (bf16[2,512,256]{1,2,0:T(8,128)(2,1)S(1)}, bf16[2,512,256]{1,2,0:T(8,128)(2,1)S(1)}, u32[]{:S(2)}, u32[]{:S(2)}) collective-permute-start(bf16[2,512,256]{1,2,0:T(8,128)(2,1)S(1)} %pad_maximum_fusion.4), channel_id=1, source_target_pairs={{0,1},{1,0},{2,3},{3,2},{4,5},{5,4},{6,7},{7,6},{8,9},{9,8},{10,11... | collective-permute-start | bytes 1572872 | tf_op jit(solution)/shard_map/ppermute | solution.py:21
  117.9 11.9 %collective-permute-start.7 = (bf16[512,256]{0,1:T(8,128)(2,1)S(1)}, bf16[512,256]{0,1:T(8,128)(2,1)S(1)}, u32[]{:S(2)}, u32[]{:S(2)}) collective-permute-start(bf16[512,256]{0,1:T(8,128)(2,1)S(1)} %fusion.15), channel_id=1, source_target_pairs={{0,2},{1,3},{2,0},{3,1},{4,6},{5,7},{6,4},{7,5},{8,10},{9,11},{10,... | collective-permute-start | bytes 786440 | tf_op jit(solution)/shard_map/ppermute | solution.py:21
  131.1 46.0 %all-to-all-start.1 = ((bf16[128,4,250]{2,1,0:T(4,128)(2,1)}), bf16[128,4,250]{2,1,0:T(4,128)(2,1)S(1)}, u32[]{:S(2)}, u32[]{:S(2)}) async-start(bf16[128,4,250]{2,1,0:T(4,128)(2,1)} %reshape.930), calls=%async_computation.1 | async-start | bytes 524288 | tf_op jit(solution)/shard_map/all_to_all | solution.py:141

commit v12 on v8

--- a/solution.py
+++ b/solution.py
@@ -78,7 +78,8 @@
     onehot = (target[:, None] == jnp.arange(clusters, dtype=jnp.int32)[None, :]).astype(jnp.int32)
     before = jnp.cumsum(onehot, axis=0) - onehot
     position = target * capacity + jnp.sum(before * onehot, axis=1)
-    outgoing = jnp.zeros((slots, queries.shape[1]), queries.dtype).at[position].set(queries)
+    placed = (lax.broadcasted_iota(jnp.int32, (slots, local_rows), 0) == position[None, :]).astype(queries.dtype)
+    outgoing = jnp.dot(placed, queries, preferred_element_type=jnp.float32).astype(queries.dtype)
     arrived = lax.all_to_all(
         outgoing.reshape(clusters, capacity, queries.shape[1]),
         "cluster",
@@ -139,7 +140,9 @@
         concat_axis=0,
         tiled=True,
     )
-    return returned.reshape(slots, quarter)[position]
+    return jnp.dot(
+        placed.T, returned.reshape(slots, quarter), preferred_element_type=jnp.float32
+    ).astype(returned.dtype)
 
 
 def solution(mesh):

time: 159 us -> 157 us (0.987)
  blocking collectives: 0 us -> 35.3 us
  waiting for transfers between devices: 41 us -> 18.3 us
  starting transfers between devices: 72.7 us -> 59.3 us
  local copies, waits for them, and re-layouts: 27.8 us -> 24.3 us
  other arithmetic: 6.87 us -> 8.48 us
    all_to_all x0 -> x1, blocking collectives: none -> 35.3 us  [body(): lax.all_to_all(shares.reshape(clusters, capacity, quarter), 'cluster', sp...]
    all_to_all x1 -> x0, waiting for transfers between devices: 22.7 us -> none  [body(): lax.all_to_all(shares.reshape(clusters, capacity, quarter), 'cluster', sp...]
    all_to_all x1 -> x0, starting transfers between devices: 13.3 us -> none  [body(): lax.all_to_all(shares.reshape(clusters, capacity, quarter), 'cluster', sp...]
    scatter x1 -> x0, local copies, waits for them, and re-layouts: 1.91 us -> none  [body(): jnp.zeros((slots, queries.shape[1]), queries.dtype).at[position]]
    gather x1 -> x0, local copies, waits for them, and re-layouts: 1.81 us -> none  [body(): return returned.reshape(slots, quarter)[position]]
    unnamed x19 -> x33, local copies, waits for them, and re-layouts: 11.9 us -> 12.2 us
  transfers between devices with their start and end apart: 12 -> 11, of which waited for: 4 -> 3; matrix products, arithmetic and copies ran while one was open for 14% -> 14% of each run, Pallas kernels for 0% -> 0%
where the time goes in v12:
time: 157 us; the launch traced here: 156 us
  starting transfers between devices  59.3 us (38%)
  blocking collectives  35.3 us (22%)
  local copies, waits for them, and re-layouts  24.3 us (15%)
  waiting for transfers between devices  18.3 us (12%)
  other arithmetic  8.48 us (5%)
  matrix products  5.61 us (4%)
  between operations  4.85 us (3%)
    all_to_all x1, blocking collectives, body(): lax.all_to_all(shares.reshape(clusters, capacity, quarter), 'cluster', sp...  35.3 us
    ppermute x6, starting transfers between devices, shifted(): lax.ppermute(array, axis, [(i, (i - by) % peers) for i in range(peers)])  23.8 us
    all_to_all x1, starting transfers between devices, body(): lax.all_to_all(outgoing.reshape(clusters, capacity, queries.shape[1]), 'c...  21.9 us
    ppermute x4, starting transfers between devices, swapped(): return lax.ppermute(array, axis, [(i, i ^ bit) for i in range(peers)])  13.6 us
    unnamed x33, local copies, waits for them, and re-layouts  12.2 us
    all_to_all x1, waiting for transfers between devices, body(): lax.all_to_all(outgoing.reshape(clusters, capacity, queries.shape[1]), 'c...  9.65 us
    ppermute x4, waiting for transfers between devices, swapped(): return lax.ppermute(array, axis, [(i, i ^ bit) for i in range(peers)])  8.6 us
  transfers between devices with their start and end apart: 11, of which 3 were waited for; matrix products, arithmetic and copies ran while one was open for 14% of the time, Pallas kernels for 0%

profile of v12, /device:TPU:32, one launch (start us, length us, event | category | flops | bytes accessed | tf_op | source)
XLA Modules:
  0.0 156.1 jit_solution(444296555871274861)
XLA Ops:
  0.0 1.1 reshape.926
  1.1 0.7 and_select_fusion
  1.8 0.1 copy.33
  2.0 1.1 pad_maximum_fusion.2
  3.1 5.4 %collective-permute-start.2 = (bf16[2,128,1024]{2,1,0:T(8,128)(2,1)S(1)}, bf16[2,128,1024]{2,1,0:T(8,128)(2,1)}, u32[]{:S(2)}, u32[]{:S(2)}) collective-permute-start(bf16[2,128,1024]{2,1,0:T(8,128)(2,1)S(1)} %pad_maximum_fusion.2), channel_id=1, source_target_pairs={{0,508},{4,0},{8,4},{12,8},{16,12},{20,16},{24,20},{28,24},{32,28}... | collective-permute-start | bytes 1572872 | tf_op jit(solution)/shard_map/ppermute | solution.py:16
  8.5 1.9 %collective-permute-start.3 = (bf16[2,128,1024]{2,1,0:T(8,128)(2,1)S(1)}, bf16[2,128,1024]{2,1,0:T(8,128)(2,1)}, u32[]{:S(2)}, u32[]{:S(2)}) collective-permute-start(bf16[2,128,1024]{2,1,0:T(8,128)(2,1)S(1)} %pad_maximum_fusion.2), channel_id=1, source_target_pairs={{0,4},{4,8},{8,12},{12,16},{16,20},{20,24},{24,28},{28,32},{32,36}... | collective-permute-start | bytes 1572872 | tf_op jit(solution)/shard_map/ppermute | solution.py:16
  10.4 3.0 %collective-permute-start.4 = (bf16[2,128,1024]{2,1,0:T(8,128)(2,1)S(1)}, bf16[2,128,1024]{2,1,0:T(8,128)(2,1)}, u32[]{:S(2)}, u32[]{:S(2)}) collective-permute-start(bf16[2,128,1024]{2,1,0:T(8,128)(2,1)S(1)} %pad_maximum_fusion.2), channel_id=1, source_target_pairs={{0,504},{4,508},{8,0},{12,4},{16,8},{20,12},{24,16},{28,20},{32,24... | collective-permute-start | bytes 1572872 | tf_op jit(solution)/shard_map/ppermute | solution.py:16
  13.4 2.8 %collective-permute-start.5 = (bf16[2,128,1024]{2,1,0:T(8,128)(2,1)S(1)}, bf16[2,128,1024]{2,1,0:T(8,128)(2,1)}, u32[]{:S(2)}, u32[]{:S(2)}) collective-permute-start(bf16[2,128,1024]{2,1,0:T(8,128)(2,1)S(1)} %pad_maximum_fusion.2), channel_id=1, source_target_pairs={{0,8},{4,12},{8,16},{12,20},{16,24},{20,28},{24,32},{28,36},{32,40... | collective-permute-start | bytes 1572872 | tf_op jit(solution)/shard_map/ppermute | solution.py:16
  16.3 6.4 %collective-permute-start.6 = (bf16[2,128,1024]{2,1,0:T(8,128)(2,1)S(1)}, bf16[2,128,1024]{2,1,0:T(8,128)(2,1)}, u32[]{:S(2)}, u32[]{:S(2)}) collective-permute-start(bf16[2,128,1024]{2,1,0:T(8,128)(2,1)S(1)} %pad_maximum_fusion.2), channel_id=1, source_target_pairs={{0,500},{4,504},{8,508},{12,0},{16,4},{20,8},{24,12},{28,16},{32,2... | collective-permute-start | bytes 1572872 | tf_op jit(solution)/shard_map/ppermute | solution.py:16
  22.7 0.1 copy.30
  22.8 0.2 fusion.19
  23.1 0.2 fusion.21
  23.3 0.2 convolution_convert_fusion
  23.5 0.8 reshape.923
  24.3 21.9 %all-to-all-start = ((bf16[128,4,256]{2,1,0:T(4,128)(2,1)}), bf16[128,4,256]{2,1,0:T(4,128)(2,1)S(1)}, u32[]{:S(2)}, u32[]{:S(2)}) async-start(bf16[128,4,256]{2,1,0:T(4,128)(2,1)} %reshape.923), calls=%async_computation | async-start | bytes 524288 | tf_op jit(solution)/shard_map/all_to_all | solution.py:83
  46.3 0.7 constant_dynamic-update-slice_fusion
  47.1 0.6 fusion.52
  52.0 0.1 stack.68
  52.1 0.6 broadcast_bitcast_fusion
  52.8 0.6 gather_fusion
  53.4 0.5 compare_and_fusion
  54.0 0.6 iota_compare_fusion.6
  54.5 0.5 iota_compare_fusion.8
  55.1 4.3 %collective-permute-start.7 = (bf16[2,128,1024]{2,1,0:T(8,128)(2,1)S(1)}, bf16[2,128,1024]{2,1,0:T(8,128)(2,1)}, u32[]{:S(2)}, u32[]{:S(2)}) collective-permute-start(bf16[2,128,1024]{2,1,0:T(8,128)(2,1)S(1)} %pad_maximum_fusion.2), channel_id=1, source_target_pairs={{0,12},{4,16},{8,20},{12,24},{16,28},{20,32},{24,36},{28,40},{32,4... | collective-permute-start | bytes 1572872 | tf_op jit(solution)/shard_map/ppermute | solution.py:16
  59.3 1.8 %slice_dynamic-update-slice_fusion.11 = (bf16[7,128,1024]{2,1,0:T(8,128)(2,1)}, bf16[7,128,1024]{2,1,0:T(8,128)(2,1)S(1)}) fusion(bf16[7,128,1024]{2,1,0:T(8,128)(2,1)} %get-tuple-element.52, bf16[2,128,1024]{2,1,0:T(8,128)(2,1)} %collective-permute-done.2, bf16[7,128,1024]{2,1,0:T(8,128)(2,1)S(1)} %get-tuple-element.53), kind=kLoop, calls=%fused_computation.50 | loop fusion | bytes 1048576
  61.1 1.8 %slice_dynamic-update-slice_fusion.10 = (bf16[7,128,1024]{2,1,0:T(8,128)(2,1)}, bf16[7,128,1024]{2,1,0:T(8,128)(2,1)S(1)}) fusion(bf16[7,128,1024]{2,1,0:T(8,128)(2,1)} %get-tuple-element.26, bf16[2,128,1024]{2,1,0:T(8,128)(2,1)} %collective-permute-done.3, bf16[7,128,1024]{2,1,0:T(8,128)(2,1)S(1)} %get-tuple-element.27), kind=kLoop, calls=%fused_computation.49 | loop fusion | bytes 1048576
  62.9 9.6 %all-to-all-done = bf16[128,4,256]{2,1,0:T(4,128)(2,1)S(1)} async-done(((bf16[128,4,256]{2,1,0:T(4,128)(2,1)}), bf16[128,4,256]{2,1,0:T(4,128)(2,1)S(1)}, u32[]{:S(2)}, u32[]{:S(2)}) %all-to-all-start) | async-done | bytes 262176 | tf_op jit(solution)/shard_map/all_to_all | solution.py:83
  72.6 4.6 %collective-permute-start = (bf16[512,256]{1,0:T(8,128)(2,1)S(1)}, bf16[512,256]{1,0:T(8,128)(2,1)S(1)}, u32[]{:S(2)}, u32[]{:S(2)}) collective-permute-start(bf16[512,256]{1,0:T(8,128)(2,1)S(1)} %reshape.924), channel_id=1, source_target_pairs={{0,2},{1,3},{2,0},{3,1},{4,6},{5,7},{6,4},{7,5},{8,10},{9,11},{10,... | collective-permute-start | bytes 786440 | tf_op jit(solution)/shard_map/ppermute | solution.py:21
  77.3 1.8 %slice_dynamic-update-slice_fusion.9 = (bf16[7,128,1024]{2,1,0:T(8,128)(2,1)}, bf16[7,128,1024]{2,1,0:T(8,128)(2,1)S(1)}) fusion(bf16[7,128,1024]{2,1,0:T(8,128)(2,1)} %get-tuple-element.24, bf16[2,128,1024]{2,1,0:T(8,128)(2,1)} %collective-permute-done.4, bf16[7,128,1024]{2,1,0:T(8,128)(2,1)S(1)} %get-tuple-element.25), kind=kLoop, calls=%fused_computation.48 | loop fusion | bytes 1048576
  79.0 1.8 %slice_dynamic-update-slice_fusion.8 = (bf16[7,128,1024]{2,1,0:T(8,128)(2,1)}, bf16[7,128,1024]{2,1,0:T(8,128)(2,1)S(1)}) fusion(bf16[7,128,1024]{2,1,0:T(8,128)(2,1)} %get-tuple-element.22, bf16[2,128,1024]{2,1,0:T(8,128)(2,1)} %collective-permute-done.5, bf16[7,128,1024]{2,1,0:T(8,128)(2,1)S(1)} %get-tuple-element.23), kind=kLoop, calls=%fused_computation.47 | loop fusion | bytes 1048576
  80.9 1.5 collective-permute-done
  82.4 0.8 pad_maximum_fusion.1
  83.2 1.9 %collective-permute-start.1 = (bf16[2,512,256]{2,1,0:T(8,128)(2,1)}, bf16[2,512,256]{2,1,0:T(8,128)(2,1)}, u32[]{:S(2)}, u32[]{:S(2)}) collective-permute-start(bf16[2,512,256]{2,1,0:T(8,128)(2,1)} %pad_maximum_fusion.1), channel_id=1, source_target_pairs={{0,1},{1,0},{2,3},{3,2},{4,5},{5,4},{6,7},{7,6},{8,9},{9,8},{10,11... | collective-permute-start | bytes 1572872 | tf_op jit(solution)/shard_map/ppermute | solution.py:21
  85.1 1.8 %slice_dynamic-update-slice_fusion.7 = (bf16[7,128,1024]{2,1,0:T(8,128)(2,1)}, bf16[7,128,1024]{2,1,0:T(8,128)(2,1)S(1)}) fusion(bf16[7,128,1024]{2,1,0:T(8,128)(2,1)} %get-tuple-element.20, bf16[2,128,1024]{2,1,0:T(8,128)(2,1)} %collective-permute-done.6, bf16[7,128,1024]{2,1,0:T(8,128)(2,1)S(1)} %get-tuple-element.21), kind=kLoop, calls=%fused_computation.46 | loop fusion | bytes 1048576
  86.9 1.8 %slice_dynamic-update-slice_fusion.6 = (bf16[7,128,1024]{2,1,0:T(8,128)(2,1)}, bf16[7,128,1024]{2,1,0:T(8,128)(2,1)S(1)}) fusion(bf16[7,128,1024]{2,1,0:T(8,128)(2,1)} %get-tuple-element.18, bf16[2,128,1024]{2,1,0:T(8,128)(2,1)} %collective-permute-done.7, bf16[7,128,1024]{2,1,0:T(8,128)(2,1)S(1)} %get-tuple-element.19), kind=kLoop, calls=%fused_computation.45 | loop fusion | bytes 1048576 | tf_op jit(solution)/shard_map/stack | solution.py:97
  88.7 2.4 %copy.35 = bf16[896,1024]{0,1:T(8,128)(2,1)} copy(bf16[896,1024]{1,0:T(8,128)(2,1)S(1)} %bitcast.113) | data formatting | bytes 3670016 | tf_op jit(solution)/shard_map/reshape | solution.py:98
  91.1 0.7 fusion.24
  91.9 1.1 pad_maximum_fusion
  93.0 0.6 gather_fusion.1
  93.7 0.2 select_bitcast_fusion
  93.8 0.5 copy.32
  94.4 2.9 %fusion.53 = (f32[512]{0:T(512)S(1)}, f32[512,896]{1,0:T(8,128)S(1)}) fusion(f32[896]{0:T(1024)S(1)} %fusion.24, bf16[512,1024]{0,1:T(8,128)(2,1)S(1)} %bitcast.115, bf16[896,1024]{1,0:T(8,128)(2,1)} %bitcast.127, pred[896]{0:T(1024)(128)(4,1)S(1)} %copy-done.12), kind=kOutput, calls=%fused_computation.146 | convolution fusion | flops 941358592 | bytes 4725120 | tf_op jit(solution)/shard_map/qd,kd->qk/dot_general | solution.py:104
  97.3 0.5 fusion
  97.8 1.0 copy-done.2
  98.8 1.4 fusion.4
  100.3 1.3 copy-done.3
  101.7 0.1 copy.39
  101.8 0.1 copy.40
  102.0 0.2 copy-done.7
  102.3 0.3 select_convert_fusion.1
  102.6 2.4 %collective-permute-start.8 = (bf16[2,512,256]{1,2,0:T(8,128)(2,1)S(1)}, bf16[2,512,256]{1,2,0:T(8,128)(2,1)S(1)}, u32[]{:S(2)}, u32[]{:S(2)}) collective-permute-start(bf16[2,512,256]{1,2,0:T(8,128)(2,1)S(1)} %pad_maximum_fusion.3), channel_id=1, source_target_pairs={{0,1},{1,0},{2,3},{3,2},{4,5},{5,4},{6,7},{7,6},{8,9},{9,8},{10,11... | collective-permute-start | bytes 1572872 | tf_op jit(solution)/shard_map/ppermute | solution.py:21
  105.0 1.3 dynamic-slice_bitcast_fusion.3
  106.3 0.2 copy.37
  106.5 0.2 copy.38
  106.7 0.1 convert_element_type.259
  106.9 0.2 fusion.2
  107.1 0.3 fusion.15
  107.4 4.6 %collective-permute-start.9 = (bf16[512,256]{0,1:T(8,128)(2,1)S(1)}, bf16[512,256]{0,1:T(8,128)(2,1)S(1)}, u32[]{:S(2)}, u32[]{:S(2)}) collective-permute-start(bf16[512,256]{0,1:T(8,128)(2,1)S(1)} %fusion.15), channel_id=1, source_target_pairs={{0,2},{1,3},{2,0},{3,1},{4,6},{5,7},{6,4},{7,5},{8,10},{9,11},{10,... | collective-permute-start | bytes 786440 | tf_op jit(solution)/shard_map/ppermute | solution.py:21
  112.1 7.1 %collective-permute-done.9 = bf16[512,256]{0,1:T(8,128)(2,1)S(1)} collective-permute-done((bf16[512,256]{0,1:T(8,128)(2,1)S(1)}, bf16[512,256]{0,1:T(8,128)(2,1)S(1)}, u32[]{:S(2)}, u32[]{:S(2)}) %collective-permute-start.9) | collective-permute-done | bytes 262176 | tf_op jit(solution)/shard_map/ppermute | solution.py:21
  119.3 0.1 fusion.16
  119.5 0.1 copy.41
  119.7 35.3 %all_to_all.10 = bf16[128,4,250]{2,1,0:T(4,128)(2,1)S(1)} all-to-all(bf16[128,4,250]{2,1,0:T(4,128)(2,1)S(1)} %reshape.929), channel_id=1, replica_groups=mesh['cluster'=128,'feat'=4] {'cluster'}, dimensions={0} | all-to-all | bytes 512000 | tf_op jit(solution)/shard_map/all_to_all | solution.py:136
  155.0 0.2 reshape.930
  155.1 1.0 convolution_convert_fusion.1
  (62 shorter events, 0.9 us)
Async XLA Ops:
  0.0 23.3 %copy-start = (bf16[256,256]{1,0:T(8,128)(2,1)S(1)}, bf16[256,256]{1,0:T(8,128)(2,1)}, u32[]{:S(2)}) copy-start(bf16[256,256]{1,0:T(8,128)(2,1)} %param.7) | copy-start | bytes 393220
  0.0 22.7 %copy-start.5 = (s32[256,1]{0,1:T(1,128)S(1)}, s32[256,1]{0,1:T(1,128)}, u32[]{:S(2)}) copy-start(s32[256,1]{0,1:T(1,128)} %param.8) | copy-start | bytes 3076
  2.0 44.3 %copy-start.4 = (bf16[128,1024]{1,0:T(8,128)(2,1)S(1)}, bf16[128,1024]{1,0:T(8,128)(2,1)}, u32[]{:S(2)}) copy-start(bf16[128,1024]{1,0:T(8,128)(2,1)} %param.10) | copy-start | bytes 786436
  3.1 43.9 %copy-start.6 = (s32[128,7]{0,1:T(8,128)S(1)}, s32[128,7]{0,1:T(8,128)}, u32[]{:S(2)}) copy-start(s32[128,7]{0,1:T(8,128)} %param.9) | copy-start | bytes 10756
  3.1 49.7 %copy-start.1 = (s32[4]{0:T(128)S(1)}, s32[4]{0:T(128)}, u32[]{:S(2)}) copy-start(s32[4]{0:T(128)} %constant.81.clone) | copy-start | bytes 52
  3.1 52.0 %collective-permute-start.2 = (bf16[2,128,1024]{2,1,0:T(8,128)(2,1)S(1)}, bf16[2,128,1024]{2,1,0:T(8,128)(2,1)}, u32[]{:S(2)}, u32[]{:S(2)}) collective-permute-start(bf16[2,128,1024]{2,1,0:T(8,128)(2,1)S(1)} %pad_maximum_fusion.2), channel_id=1, source_target_pairs={{0,508},{4,0},{8,4},{12,8},{16,12},{20,16},{24,20},{28,24},{32,28}... | collective-permute-start | bytes 1572872 | tf_op jit(solution)/shard_map/ppermute | solution.py:16
  8.5 52.6 %collective-permute-start.3 = (bf16[2,128,1024]{2,1,0:T(8,128)(2,1)S(1)}, bf16[2,128,1024]{2,1,0:T(8,128)(2,1)}, u32[]{:S(2)}, u32[]{:S(2)}) collective-permute-start(bf16[2,128,1024]{2,1,0:T(8,128)(2,1)S(1)} %pad_maximum_fusion.2), channel_id=1, source_target_pairs={{0,4},{4,8},{8,12},{12,16},{16,20},{20,24},{24,28},{28,32},{32,36}... | collective-permute-start | bytes 1572872 | tf_op jit(solution)/shard_map/ppermute | solution.py:16
  10.4 66.8 %collective-permute-start.4 = (bf16[2,128,1024]{2,1,0:T(8,128)(2,1)S(1)}, bf16[2,128,1024]{2,1,0:T(8,128)(2,1)}, u32[]{:S(2)}, u32[]{:S(2)}) collective-permute-start(bf16[2,128,1024]{2,1,0:T(8,128)(2,1)S(1)} %pad_maximum_fusion.2), channel_id=1, source_target_pairs={{0,504},{4,508},{8,0},{12,4},{16,8},{20,12},{24,16},{28,20},{32,24... | collective-permute-start | bytes 1572872 | tf_op jit(solution)/shard_map/ppermute | solution.py:16
  13.4 65.6 %collective-permute-start.5 = (bf16[2,128,1024]{2,1,0:T(8,128)(2,1)S(1)}, bf16[2,128,1024]{2,1,0:T(8,128)(2,1)}, u32[]{:S(2)}, u32[]{:S(2)}) collective-permute-start(bf16[2,128,1024]{2,1,0:T(8,128)(2,1)S(1)} %pad_maximum_fusion.2), channel_id=1, source_target_pairs={{0,8},{4,12},{8,16},{12,20},{16,24},{20,28},{24,32},{28,36},{32,40... | collective-permute-start | bytes 1572872 | tf_op jit(solution)/shard_map/ppermute | solution.py:16
  16.3 68.8 %collective-permute-start.6 = (bf16[2,128,1024]{2,1,0:T(8,128)(2,1)S(1)}, bf16[2,128,1024]{2,1,0:T(8,128)(2,1)}, u32[]{:S(2)}, u32[]{:S(2)}) collective-permute-start(bf16[2,128,1024]{2,1,0:T(8,128)(2,1)S(1)} %pad_maximum_fusion.2), channel_id=1, source_target_pairs={{0,500},{4,504},{8,508},{12,0},{16,4},{20,8},{24,12},{28,16},{32,2... | collective-permute-start | bytes 1572872 | tf_op jit(solution)/shard_map/ppermute | solution.py:16
  24.3 48.2 %all-to-all-start = ((bf16[128,4,256]{2,1,0:T(4,128)(2,1)}), bf16[128,4,256]{2,1,0:T(4,128)(2,1)S(1)}, u32[]{:S(2)}, u32[]{:S(2)}) async-start(bf16[128,4,256]{2,1,0:T(4,128)(2,1)} %reshape.923), calls=%async_computation | async-start | bytes 524288 | tf_op jit(solution)/shard_map/all_to_all | solution.py:83
  55.1 31.8 %collective-permute-start.7 = (bf16[2,128,1024]{2,1,0:T(8,128)(2,1)S(1)}, bf16[2,128,1024]{2,1,0:T(8,128)(2,1)}, u32[]{:S(2)}, u32[]{:S(2)}) collective-permute-start(bf16[2,128,1024]{2,1,0:T(8,128)(2,1)S(1)} %pad_maximum_fusion.2), channel_id=1, source_target_pairs={{0,12},{4,16},{8,20},{12,24},{16,28},{20,32},{24,36},{28,40},{32,4... | collective-permute-start | bytes 1572872 | tf_op jit(solution)/shard_map/ppermute | solution.py:16
  72.6 9.8 %collective-permute-start = (bf16[512,256]{1,0:T(8,128)(2,1)S(1)}, bf16[512,256]{1,0:T(8,128)(2,1)S(1)}, u32[]{:S(2)}, u32[]{:S(2)}) collective-permute-start(bf16[512,256]{1,0:T(8,128)(2,1)S(1)} %reshape.924), channel_id=1, source_target_pairs={{0,2},{1,3},{2,0},{3,1},{4,6},{5,7},{6,4},{7,5},{8,10},{9,11},{10,... | collective-permute-start | bytes 786440 | tf_op jit(solution)/shard_map/ppermute | solution.py:21
  83.2 8.7 %collective-permute-start.1 = (bf16[2,512,256]{2,1,0:T(8,128)(2,1)}, bf16[2,512,256]{2,1,0:T(8,128)(2,1)}, u32[]{:S(2)}, u32[]{:S(2)}) collective-permute-start(bf16[2,512,256]{2,1,0:T(8,128)(2,1)} %pad_maximum_fusion.1), channel_id=1, source_target_pairs={{0,1},{1,0},{2,3},{3,2},{4,5},{5,4},{6,7},{7,6},{8,9},{9,8},{10,11... | collective-permute-start | bytes 1572872 | tf_op jit(solution)/shard_map/ppermute | solution.py:21
  91.9 1.8 %copy-start.11 = (pred[4]{0:T(512)(128)(4,1)S(1)}, pred[4]{0:T(512)(128)(4,1)}, u32[]{:S(2)}) copy-start(pred[4]{0:T(512)(128)(4,1)} %compare_and_fusion) | copy-start | bytes 16
  93.7 0.7 copy-start.12
  97.3 1.5 copy-start.2
  100.3 1.3 copy-start.3
  101.6 0.6 copy-start.7
  101.6 0.6 copy-start.8
  101.6 0.6 copy-start.9
  101.6 0.6 copy-start.10
  102.6 4.1 %collective-permute-start.8 = (bf16[2,512,256]{1,2,0:T(8,128)(2,1)S(1)}, bf16[2,512,256]{1,2,0:T(8,128)(2,1)S(1)}, u32[]{:S(2)}, u32[]{:S(2)}) collective-permute-start(bf16[2,512,256]{1,2,0:T(8,128)(2,1)S(1)} %pad_maximum_fusion.3), channel_id=1, source_target_pairs={{0,1},{1,0},{2,3},{3,2},{4,5},{5,4},{6,7},{7,6},{8,9},{9,8},{10,11... | collective-permute-start | bytes 1572872 | tf_op jit(solution)/shard_map/ppermute | solution.py:21
  107.4 11.8 %collective-permute-start.9 = (bf16[512,256]{0,1:T(8,128)(2,1)S(1)}, bf16[512,256]{0,1:T(8,128)(2,1)S(1)}, u32[]{:S(2)}, u32[]{:S(2)}) collective-permute-start(bf16[512,256]{0,1:T(8,128)(2,1)S(1)} %fusion.15), channel_id=1, source_target_pairs={{0,2},{1,3},{2,0},{3,1},{4,6},{5,7},{6,4},{7,5},{8,10},{9,11},{10,... | collective-permute-start | bytes 786440 | tf_op jit(solution)/shard_map/ppermute | solution.py:21

commit v13 on v12

--- a/solution.py
+++ b/solution.py
@@ -87,6 +87,9 @@
         concat_axis=0,
         tiled=True,
     )
+    band_keys = jnp.stack([b[0] for b in blocks]).reshape(len(offsets) * rows, depth)
+    band_labels = jnp.stack([b[1] for b in blocks]).reshape(len(offsets) * rows, feats * group)
+    arrived, band_keys, band_labels = lax.optimization_barrier((arrived, band_keys, band_labels))
     own = arrived.reshape(slots, queries.shape[1])
     far = swapped(own, "feat", 2)
     near = swapped(jnp.stack([own, far]), "feat", 1)
@@ -94,8 +97,6 @@
     order = jnp.array([0, 2, 1, 3], jnp.int32)[jnp.arange(feats, dtype=jnp.int32) ^ feat_index]
     query_full = jnp.swapaxes(jnp.take(parts, order, axis=0), 0, 1).reshape(slots, feats * queries.shape[1])
 
-    band_keys = jnp.stack([b[0] for b in blocks]).reshape(len(offsets) * rows, depth)
-    band_labels = jnp.stack([b[1] for b in blocks]).reshape(len(offsets) * rows, feats * group)
     band_prior = band_labels[:, quarter]
     mask_row = band_mask[cluster_index]
     live_blocks = jnp.stack([mask_row[REACH + o] > 0 for o in offsets])

time: 157 us -> 166 us (1.057)
  local copies, waits for them, and re-layouts: 24.3 us -> 27.5 us
  blocking collectives: 35.3 us -> 38.2 us
  other arithmetic: 8.48 us -> 10.5 us
    ppermute x6, waiting for transfers between devices: 0.02 us -> 10.2 us  [shifted(): lax.ppermute(array, axis, [(i, (i - by) % peers) for i in range(peers)])]
    all_to_all x1, waiting for transfers between devices: 9.65 us -> 0.01 us  [body(): lax.all_to_all(outgoing.reshape(clusters, capacity, queries.shape[1]), 'c...]
    dynamic_slice x0 -> x6, local copies, waits for them, and re-layouts: none -> 5.91 us  [body(): pick = lambda g: lax.dynamic_index_in_dim(grid, g, axis=1, keepdims=False)]
    all_to_all x1, blocking collectives: 35.3 us -> 38.2 us  [body(): lax.all_to_all(shares.reshape(clusters, capacity, quarter), 'cluster', sp...]
    another operation x7 -> x4, local copies, waits for them, and re-layouts: 3.47 us -> 0.77 us  [the longest x1 0.75 us: body(): jnp.stack([b[1] for b in blocks])]
    optimization_barrier x0 -> x1, local copies, waits for them, and re-layouts: none -> 2.5 us  [body(): lax.optimization_barrier((arrived, band_keys, band_labels))]
  transfers between devices with their start and end apart: 11 -> 11, of which waited for: 3 -> 3; matrix products, arithmetic and copies ran while one was open for 14% -> 13% of each run, Pallas kernels for 0% -> 0%
where the time goes in v13:
time: 166 us; the launch traced here: 165 us
  starting transfers between devices  59.5 us (36%)
  blocking collectives  38.2 us (23%)
  local copies, waits for them, and re-layouts  27.5 us (17%)
  waiting for transfers between devices  17.6 us (11%)
  other arithmetic  10.5 us (6%)
  matrix products  6.9 us (4%)
  between operations  4.9 us (3%)
    all_to_all x1, blocking collectives, body(): lax.all_to_all(shares.reshape(clusters, capacity, quarter), 'cluster', sp...  38.2 us
    ppermute x6, starting transfers between devices, shifted(): lax.ppermute(array, axis, [(i, (i - by) % peers) for i in range(peers)])  23.8 us
    all_to_all x1, starting transfers between devices, body(): lax.all_to_all(outgoing.reshape(clusters, capacity, queries.shape[1]), 'c...  21.9 us
    ppermute x4, starting transfers between devices, swapped(): return lax.ppermute(array, axis, [(i, i ^ bit) for i in range(peers)])  13.8 us
    unnamed x33, local copies, waits for them, and re-layouts  10.8 us
    ppermute x6, waiting for transfers between devices, shifted(): lax.ppermute(array, axis, [(i, (i - by) % peers) for i in range(peers)])  10.2 us
    ppermute x4, waiting for transfers between devices, swapped(): return lax.ppermute(array, axis, [(i, i ^ bit) for i in range(peers)])  7.42 us
    dynamic_slice x6, local copies, waits for them, and re-layouts, body(): pick = lambda g: lax.dynamic_index_in_dim(grid, g, axis=1, keepdims=False)  5.91 us
  transfers between devices with their start and end apart: 11, of which 3 were waited for; matrix products, arithmetic and copies ran while one was open for 13% of the time, Pallas kernels for 0%

profile of v13, /device:TPU:32, one launch (start us, length us, event | category | flops | bytes accessed | tf_op | source)
XLA Modules:
  0.0 165.1 jit_solution(12020647890796187731)
XLA Ops:
  0.0 1.1 reshape.925
  1.1 0.7 and_select_fusion
  1.8 0.1 copy.29
  2.0 1.1 pad_maximum_fusion.1
  3.1 5.4 %collective-permute-start = (bf16[2,128,1024]{2,1,0:T(8,128)(2,1)S(1)}, bf16[2,128,1024]{2,1,0:T(8,128)(2,1)}, u32[]{:S(2)}, u32[]{:S(2)}) collective-permute-start(bf16[2,128,1024]{2,1,0:T(8,128)(2,1)S(1)} %pad_maximum_fusion.1), channel_id=1, source_target_pairs={{0,508},{4,0},{8,4},{12,8},{16,12},{20,16},{24,20},{28,24},{32,28}... | collective-permute-start | bytes 1572872 | tf_op jit(solution)/shard_map/ppermute | solution.py:16
  8.5 1.9 %collective-permute-start.1 = (bf16[2,128,1024]{2,1,0:T(8,128)(2,1)S(1)}, bf16[2,128,1024]{2,1,0:T(8,128)(2,1)}, u32[]{:S(2)}, u32[]{:S(2)}) collective-permute-start(bf16[2,128,1024]{2,1,0:T(8,128)(2,1)S(1)} %pad_maximum_fusion.1), channel_id=1, source_target_pairs={{0,4},{4,8},{8,12},{12,16},{16,20},{20,24},{24,28},{28,32},{32,36}... | collective-permute-start | bytes 1572872 | tf_op jit(solution)/shard_map/ppermute | solution.py:16
  10.4 3.0 %collective-permute-start.2 = (bf16[2,128,1024]{2,1,0:T(8,128)(2,1)S(1)}, bf16[2,128,1024]{2,1,0:T(8,128)(2,1)}, u32[]{:S(2)}, u32[]{:S(2)}) collective-permute-start(bf16[2,128,1024]{2,1,0:T(8,128)(2,1)S(1)} %pad_maximum_fusion.1), channel_id=1, source_target_pairs={{0,504},{4,508},{8,0},{12,4},{16,8},{20,12},{24,16},{28,20},{32,24... | collective-permute-start | bytes 1572872 | tf_op jit(solution)/shard_map/ppermute | solution.py:16
  13.4 2.8 %collective-permute-start.3 = (bf16[2,128,1024]{2,1,0:T(8,128)(2,1)S(1)}, bf16[2,128,1024]{2,1,0:T(8,128)(2,1)}, u32[]{:S(2)}, u32[]{:S(2)}) collective-permute-start(bf16[2,128,1024]{2,1,0:T(8,128)(2,1)S(1)} %pad_maximum_fusion.1), channel_id=1, source_target_pairs={{0,8},{4,12},{8,16},{12,20},{16,24},{20,28},{24,32},{28,36},{32,40... | collective-permute-start | bytes 1572872 | tf_op jit(solution)/shard_map/ppermute | solution.py:16
  16.3 6.4 %collective-permute-start.4 = (bf16[2,128,1024]{2,1,0:T(8,128)(2,1)S(1)}, bf16[2,128,1024]{2,1,0:T(8,128)(2,1)}, u32[]{:S(2)}, u32[]{:S(2)}) collective-permute-start(bf16[2,128,1024]{2,1,0:T(8,128)(2,1)S(1)} %pad_maximum_fusion.1), channel_id=1, source_target_pairs={{0,500},{4,504},{8,508},{12,0},{16,4},{20,8},{24,12},{28,16},{32,2... | collective-permute-start | bytes 1572872 | tf_op jit(solution)/shard_map/ppermute | solution.py:16
  22.8 0.2 fusion.30
  23.1 0.2 fusion.32
  23.3 0.2 convolution_convert_fusion
  23.5 0.8 reshape.924
  24.3 21.9 %all-to-all-start = ((bf16[128,4,256]{2,1,0:T(4,128)(2,1)}), bf16[128,4,256]{2,1,0:T(4,128)(2,1)S(1)}, u32[]{:S(2)}, u32[]{:S(2)}) async-start(bf16[128,4,256]{2,1,0:T(4,128)(2,1)} %reshape.924), calls=%async_computation | async-start | bytes 524288 | tf_op jit(solution)/shard_map/all_to_all | solution.py:83
  46.3 0.7 constant_dynamic-update-slice_fusion
  47.0 0.6 gather_fusion
  47.7 0.6 fusion.63
  48.3 0.6 iota_compare_fusion.4
  48.9 4.3 %collective-permute-start.5 = (bf16[2,128,1024]{2,1,0:T(8,128)(2,1)S(1)}, bf16[2,128,1024]{2,1,0:T(8,128)(2,1)S(1)}, u32[]{:S(2)}, u32[]{:S(2)}) collective-permute-start(bf16[2,128,1024]{2,1,0:T(8,128)(2,1)S(1)} %pad_maximum_fusion.1), channel_id=1, source_target_pairs={{0,12},{4,16},{8,20},{12,24},{16,28},{20,32},{24,36},{28,40},{32,4... | collective-permute-start | bytes 1572872 | tf_op jit(solution)/shard_map/ppermute | solution.py:16
  53.2 1.8 %slice_dynamic-update-slice_fusion.5 = (bf16[7,128,1024]{2,1,0:T(8,128)(2,1)S(1)}, bf16[7,128,1024]{2,1,0:T(8,128)(2,1)}) fusion(bf16[7,128,1024]{2,1,0:T(8,128)(2,1)S(1)} %get-tuple-element.59, bf16[2,128,1024]{2,1,0:T(8,128)(2,1)} %collective-permute-done, bf16[7,128,1024]{2,1,0:T(8,128)(2,1)} %get-tuple-element.58), kind=kLoop, calls=%fused_computation.51 | loop fusion | bytes 1048576
  55.0 1.8 %slice_dynamic-update-slice_fusion.4 = (bf16[7,128,1024]{2,1,0:T(8,128)(2,1)S(1)}, bf16[7,128,1024]{2,1,0:T(8,128)(2,1)}) fusion(bf16[7,128,1024]{2,1,0:T(8,128)(2,1)S(1)} %get-tuple-element.32, bf16[2,128,1024]{2,1,0:T(8,128)(2,1)} %collective-permute-done.1, bf16[7,128,1024]{2,1,0:T(8,128)(2,1)} %get-tuple-element.33), kind=kLoop, calls=%fused_computation.50 | loop fusion | bytes 1048576
  56.7 1.8 %slice_dynamic-update-slice_fusion.3 = (bf16[7,128,1024]{2,1,0:T(8,128)(2,1)S(1)}, bf16[7,128,1024]{2,1,0:T(8,128)(2,1)}) fusion(bf16[7,128,1024]{2,1,0:T(8,128)(2,1)S(1)} %get-tuple-element.30, bf16[2,128,1024]{2,1,0:T(8,128)(2,1)} %collective-permute-done.2, bf16[7,128,1024]{2,1,0:T(8,128)(2,1)} %get-tuple-element.31), kind=kLoop, calls=%fused_computation.49 | loop fusion | bytes 1048576
  58.5 1.8 %slice_dynamic-update-slice_fusion.2 = (bf16[7,128,1024]{2,1,0:T(8,128)(2,1)S(1)}, bf16[7,128,1024]{2,1,0:T(8,128)(2,1)}) fusion(bf16[7,128,1024]{2,1,0:T(8,128)(2,1)S(1)} %get-tuple-element.28, bf16[2,128,1024]{2,1,0:T(8,128)(2,1)} %collective-permute-done.3, bf16[7,128,1024]{2,1,0:T(8,128)(2,1)} %get-tuple-element.29), kind=kLoop, calls=%fused_computation.48 | loop fusion | bytes 1048576
  60.3 1.8 %slice_dynamic-update-slice_fusion.1 = (bf16[7,128,1024]{2,1,0:T(8,128)(2,1)S(1)}, bf16[7,128,1024]{2,1,0:T(8,128)(2,1)}) fusion(bf16[7,128,1024]{2,1,0:T(8,128)(2,1)S(1)} %get-tuple-element.26, bf16[2,128,1024]{2,1,0:T(8,128)(2,1)} %collective-permute-done.4, bf16[7,128,1024]{2,1,0:T(8,128)(2,1)} %get-tuple-element.27), kind=kLoop, calls=%fused_computation.47 | loop fusion | bytes 1048576
  62.1 10.2 %collective-permute-done.5 = bf16[2,128,1024]{2,1,0:T(8,128)(2,1)S(1)} collective-permute-done((bf16[2,128,1024]{2,1,0:T(8,128)(2,1)S(1)}, bf16[2,128,1024]{2,1,0:T(8,128)(2,1)S(1)}, u32[]{:S(2)}, u32[]{:S(2)}) %collective-permute-start.5) | collective-permute-done | bytes 524320 | tf_op jit(solution)/shard_map/ppermute | solution.py:16
  72.2 0.8 slice_dynamic-update-slice_fusion
  73.1 4.6 %collective-permute-start.6 = (bf16[512,256]{1,0:T(8,128)(2,1)S(1)}, bf16[512,256]{1,0:T(8,128)(2,1)S(1)}, u32[]{:S(2)}, u32[]{:S(2)}) collective-permute-start(bf16[512,256]{1,0:T(8,128)(2,1)S(1)} %reshape.928), channel_id=1, source_target_pairs={{0,2},{1,3},{2,0},{3,1},{4,6},{5,7},{6,4},{7,5},{8,10},{9,11},{10,... | collective-permute-start | bytes 786440 | tf_op jit(solution)/shard_map/ppermute | solution.py:21
  77.7 0.6 iota_compare_fusion.6
  82.8 0.5 iota_compare_fusion.8
  83.4 0.5 collective-permute-done.6
  83.9 1.9 %collective-permute-start.7 = (bf16[2,512,256]{2,1,0:T(8,128)(2,1)S(1)}, bf16[2,512,256]{2,1,0:T(8,128)(2,1)}, u32[]{:S(2)}, u32[]{:S(2)}) collective-permute-start(bf16[2,512,256]{2,1,0:T(8,128)(2,1)S(1)} %pad_maximum_fusion.2), channel_id=1, source_target_pairs={{0,1},{1,0},{2,3},{3,2},{4,5},{5,4},{6,7},{7,6},{8,9},{9,8},{10,11... | collective-permute-start | bytes 1572872 | tf_op jit(solution)/shard_map/ppermute | solution.py:21
  85.9 2.5 %copy.32 = bf16[896,1024]{0,1:T(8,128)(2,1)} copy(bf16[896,1024]{1,0:T(8,128)(2,1)S(1)} %bitcast.129) | data formatting | bytes 3670016 | tf_op jit(solution)/shard_map/optimization_barrier | solution.py:92
  88.4 0.7 fusion.35
  89.2 1.1 pad_maximum_fusion
  90.3 0.6 gather_fusion.1
  91.0 0.2 select_bitcast_fusion
  91.1 0.5 copy.31
  91.7 2.9 %fusion.64 = (f32[512]{0:T(512)S(1)}, f32[512,896]{1,0:T(8,128)S(1)}) fusion(f32[896]{0:T(1024)S(1)} %fusion.35, bf16[512,1024]{0,1:T(8,128)(2,1)S(1)} %bitcast.133, bf16[896,1024]{1,0:T(8,128)(2,1)} %bitcast.145, pred[896]{0:T(1024)(128)(4,1)S(1)} %broadcast_bitcast_fusion), kind=kOutput, calls=%fused_computation.157 | convolution fusion | flops 941358592 | bytes 4725120 | tf_op jit(solution)/shard_map/qd,kd->qk/dot_general | solution.py:105
  94.6 0.5 fusion
  95.1 1.0 copy-done.3
  96.1 2.8 %fusion.3 = f32[512,1024]{1,0:T(8,128)} fusion(bf16[896,1024]{1,0:T(8,128)(2,1)S(1)} %bitcast.130, f32[512,896]{1,0:T(8,128)S(1)} %get-tuple-element.57, f32[512]{0:T(512)S(1)} %get-tuple-element.56), kind=kOutput, calls=%fused_computation.12 | convolution fusion | flops 940441600 | bytes 5769216 | tf_op jit(solution)/shard_map/dot_general | solution.py:111
  98.8 0.6 fusion.51
  99.4 0.6 fusion.52
  100.0 2.2 %reshape.930 = f32[512,4,256]{2,1,0:T(4,128)S(1)} reshape(f32[512,1024]{1,0:T(8,128)} %fusion.3) | data formatting | bytes 4194304 | tf_op jit(solution)/shard_map/reshape | solution.py:120
  102.2 0.9 constant_dynamic-slice_fusion
  103.2 0.7 copy.35
  103.8 0.7 copy.36
  104.5 1.0 fusion.26
  105.5 0.9 pad_maximum_fusion.3
  106.4 2.6 %collective-permute-start.8 = (bf16[2,512,256]{1,2,0:T(8,128)(2,1)}, bf16[2,512,256]{1,2,0:T(8,128)(2,1)S(1)}, u32[]{:S(2)}, u32[]{:S(2)}) collective-permute-start(bf16[2,512,256]{1,2,0:T(8,128)(2,1)} %pad_maximum_fusion.3), channel_id=1, source_target_pairs={{0,1},{1,0},{2,3},{3,2},{4,5},{5,4},{6,7},{7,6},{8,9},{9,8},{10,11... | collective-permute-start | bytes 1572872 | tf_op jit(solution)/shard_map/ppermute | solution.py:21
  109.0 1.7 %constant_dynamic-slice_fusion.2 = (f32[512,1,256]{2,1,0:T(1,128)}, f32[512,1,256]{2,1,0:T(1,128)S(1)}) fusion(f32[512,4,256]{2,1,0:T(4,128)S(1)} %reshape.930, s32[]{:T(128)S(6)} %select_n.205, s32[]{:T(128)S(6)} %select_n.206), kind=kLoop, calls=%fused_computation.129 | loop fusion | bytes 2097160 | tf_op jit(solution)/shard_map/jit(dynamic_index_in_dim)/dynamic_slice | solution.py:121
  110.7 1.2 copy.33
  112.0 0.7 copy.34
  112.7 0.1 convert_element_type.259
  112.9 0.2 fusion.2
  113.1 0.2 copy-done.7
  113.3 0.3 fusion.14
  113.6 4.6 %collective-permute-start.9 = (bf16[512,256]{0,1:T(8,128)(2,1)S(1)}, bf16[512,256]{0,1:T(8,128)(2,1)S(1)}, u32[]{:S(2)}, u32[]{:S(2)}) collective-permute-start(bf16[512,256]{0,1:T(8,128)(2,1)S(1)} %fusion.14), channel_id=1, source_target_pairs={{0,2},{1,3},{2,0},{3,1},{4,6},{5,7},{6,4},{7,5},{8,10},{9,11},{10,... | collective-permute-start | bytes 786440 | tf_op jit(solution)/shard_map/ppermute | solution.py:21
  118.3 6.9 %collective-permute-done.9 = bf16[512,256]{0,1:T(8,128)(2,1)S(1)} collective-permute-done((bf16[512,256]{0,1:T(8,128)(2,1)S(1)}, bf16[512,256]{0,1:T(8,128)(2,1)S(1)}, u32[]{:S(2)}, u32[]{:S(2)}) %collective-permute-start.9) | collective-permute-done | bytes 262176 | tf_op jit(solution)/shard_map/ppermute | solution.py:21
  125.4 0.1 fusion.27
  125.5 0.1 copy.37
  125.7 38.2 %all_to_all.10 = bf16[128,4,250]{2,1,0:T(4,128)(2,1)S(1)} all-to-all(bf16[128,4,250]{2,1,0:T(4,128)(2,1)S(1)} %reshape.931), channel_id=1, replica_groups=mesh['cluster'=128,'feat'=4] {'cluster'}, dimensions={0} | all-to-all | bytes 512000 | tf_op jit(solution)/shard_map/all_to_all | solution.py:137
  164.0 0.2 reshape.932
  164.1 1.0 convolution_convert_fusion.1
  (63 shorter events, 1.1 us)
Async XLA Ops:
  0.0 23.3 %copy-start = (bf16[256,256]{1,0:T(8,128)(2,1)S(1)}, bf16[256,256]{1,0:T(8,128)(2,1)}, u32[]{:S(2)}) copy-start(bf16[256,256]{1,0:T(8,128)(2,1)} %param.7) | copy-start | bytes 393220
  0.0 22.7 %copy-start.5 = (s32[256,1]{0,1:T(1,128)S(1)}, s32[256,1]{0,1:T(1,128)}, u32[]{:S(2)}) copy-start(s32[256,1]{0,1:T(1,128)} %param.8) | copy-start | bytes 3076
  2.0 44.3 %copy-start.4 = (bf16[128,1024]{1,0:T(8,128)(2,1)S(1)}, bf16[128,1024]{1,0:T(8,128)(2,1)}, u32[]{:S(2)}) copy-start(bf16[128,1024]{1,0:T(8,128)(2,1)} %param.10) | copy-start | bytes 786436
  3.1 43.9 %copy-start.1 = (s32[4]{0:T(128)S(1)}, s32[4]{0:T(128)}, u32[]{:S(2)}) copy-start(s32[4]{0:T(128)} %constant.81.clone) | copy-start | bytes 52
  3.1 45.8 %collective-permute-start = (bf16[2,128,1024]{2,1,0:T(8,128)(2,1)S(1)}, bf16[2,128,1024]{2,1,0:T(8,128)(2,1)}, u32[]{:S(2)}, u32[]{:S(2)}) collective-permute-start(bf16[2,128,1024]{2,1,0:T(8,128)(2,1)S(1)} %pad_maximum_fusion.1), channel_id=1, source_target_pairs={{0,508},{4,0},{8,4},{12,8},{16,12},{20,16},{24,20},{28,24},{32,28}... | collective-permute-start | bytes 1572872 | tf_op jit(solution)/shard_map/ppermute | solution.py:16
  8.5 46.5 %collective-permute-start.1 = (bf16[2,128,1024]{2,1,0:T(8,128)(2,1)S(1)}, bf16[2,128,1024]{2,1,0:T(8,128)(2,1)}, u32[]{:S(2)}, u32[]{:S(2)}) collective-permute-start(bf16[2,128,1024]{2,1,0:T(8,128)(2,1)S(1)} %pad_maximum_fusion.1), channel_id=1, source_target_pairs={{0,4},{4,8},{8,12},{12,16},{16,20},{20,24},{24,28},{28,32},{32,36}... | collective-permute-start | bytes 1572872 | tf_op jit(solution)/shard_map/ppermute | solution.py:16
  10.4 46.3 %collective-permute-start.2 = (bf16[2,128,1024]{2,1,0:T(8,128)(2,1)S(1)}, bf16[2,128,1024]{2,1,0:T(8,128)(2,1)}, u32[]{:S(2)}, u32[]{:S(2)}) collective-permute-start(bf16[2,128,1024]{2,1,0:T(8,128)(2,1)S(1)} %pad_maximum_fusion.1), channel_id=1, source_target_pairs={{0,504},{4,508},{8,0},{12,4},{16,8},{20,12},{24,16},{28,20},{32,24... | collective-permute-start | bytes 1572872 | tf_op jit(solution)/shard_map/ppermute | solution.py:16
  13.4 45.1 %collective-permute-start.3 = (bf16[2,128,1024]{2,1,0:T(8,128)(2,1)S(1)}, bf16[2,128,1024]{2,1,0:T(8,128)(2,1)}, u32[]{:S(2)}, u32[]{:S(2)}) collective-permute-start(bf16[2,128,1024]{2,1,0:T(8,128)(2,1)S(1)} %pad_maximum_fusion.1), channel_id=1, source_target_pairs={{0,8},{4,12},{8,16},{12,20},{16,24},{20,28},{24,32},{28,36},{32,40... | collective-permute-start | bytes 1572872 | tf_op jit(solution)/shard_map/ppermute | solution.py:16
  16.3 44.0 %collective-permute-start.4 = (bf16[2,128,1024]{2,1,0:T(8,128)(2,1)S(1)}, bf16[2,128,1024]{2,1,0:T(8,128)(2,1)}, u32[]{:S(2)}, u32[]{:S(2)}) collective-permute-start(bf16[2,128,1024]{2,1,0:T(8,128)(2,1)S(1)} %pad_maximum_fusion.1), channel_id=1, source_target_pairs={{0,500},{4,504},{8,508},{12,0},{16,4},{20,8},{24,12},{28,16},{32,2... | collective-permute-start | bytes 1572872 | tf_op jit(solution)/shard_map/ppermute | solution.py:16
  23.1 24.6 %copy-start.6 = (s32[128,7]{0,1:T(8,128)S(1)}, s32[128,7]{0,1:T(8,128)}, u32[]{:S(2)}) copy-start(s32[128,7]{0,1:T(8,128)} %param.9) | copy-start | bytes 10756
  24.3 48.7 %all-to-all-start = ((bf16[128,4,256]{2,1,0:T(4,128)(2,1)}), bf16[128,4,256]{2,1,0:T(4,128)(2,1)S(1)}, u32[]{:S(2)}, u32[]{:S(2)}) async-start(bf16[128,4,256]{2,1,0:T(4,128)(2,1)} %reshape.924), calls=%async_computation | async-start | bytes 524288 | tf_op jit(solution)/shard_map/all_to_all | solution.py:83
  48.9 23.3 %collective-permute-start.5 = (bf16[2,128,1024]{2,1,0:T(8,128)(2,1)S(1)}, bf16[2,128,1024]{2,1,0:T(8,128)(2,1)S(1)}, u32[]{:S(2)}, u32[]{:S(2)}) collective-permute-start(bf16[2,128,1024]{2,1,0:T(8,128)(2,1)S(1)} %pad_maximum_fusion.1), channel_id=1, source_target_pairs={{0,12},{4,16},{8,20},{12,24},{16,28},{20,32},{24,36},{28,40},{32,4... | collective-permute-start | bytes 1572872 | tf_op jit(solution)/shard_map/ppermute | solution.py:16
  73.0 15.5 %copy-start.2 = (bf16[7,128,1024]{2,1,0:T(8,128)(2,1)}, bf16[7,128,1024]{2,1,0:T(8,128)(2,1)S(1)}, u32[]{:S(2)}) copy-start(bf16[7,128,1024]{2,1,0:T(8,128)(2,1)S(1)} %get-tuple-element.22) | copy-start | bytes 5505028
  73.1 10.8 %collective-permute-start.6 = (bf16[512,256]{1,0:T(8,128)(2,1)S(1)}, bf16[512,256]{1,0:T(8,128)(2,1)S(1)}, u32[]{:S(2)}, u32[]{:S(2)}) collective-permute-start(bf16[512,256]{1,0:T(8,128)(2,1)S(1)} %reshape.928), channel_id=1, source_target_pairs={{0,2},{1,3},{2,0},{3,1},{4,6},{5,7},{6,4},{7,5},{8,10},{9,11},{10,... | collective-permute-start | bytes 786440 | tf_op jit(solution)/shard_map/ppermute | solution.py:21
  83.9 5.3 %collective-permute-start.7 = (bf16[2,512,256]{2,1,0:T(8,128)(2,1)S(1)}, bf16[2,512,256]{2,1,0:T(8,128)(2,1)}, u32[]{:S(2)}, u32[]{:S(2)}) collective-permute-start(bf16[2,512,256]{2,1,0:T(8,128)(2,1)S(1)} %pad_maximum_fusion.2), channel_id=1, source_target_pairs={{0,1},{1,0},{2,3},{3,2},{4,5},{5,4},{6,7},{7,6},{8,9},{9,8},{10,11... | collective-permute-start | bytes 1572872 | tf_op jit(solution)/shard_map/ppermute | solution.py:21
  94.6 1.5 copy-start.3
  106.4 6.3 %collective-permute-start.8 = (bf16[2,512,256]{1,2,0:T(8,128)(2,1)}, bf16[2,512,256]{1,2,0:T(8,128)(2,1)S(1)}, u32[]{:S(2)}, u32[]{:S(2)}) collective-permute-start(bf16[2,512,256]{1,2,0:T(8,128)(2,1)} %pad_maximum_fusion.3), channel_id=1, source_target_pairs={{0,1},{1,0},{2,3},{3,2},{4,5},{5,4},{6,7},{7,6},{8,9},{9,8},{10,11... | collective-permute-start | bytes 1572872 | tf_op jit(solution)/shard_map/ppermute | solution.py:21
  112.6 0.7 copy-start.7
  112.6 0.7 copy-start.8
  112.7 0.7 copy-start.9
  112.7 0.7 copy-start.10
  112.7 0.7 copy-start.11
  112.7 0.6 copy-start.12
  113.6 11.6 %collective-permute-start.9 = (bf16[512,256]{0,1:T(8,128)(2,1)S(1)}, bf16[512,256]{0,1:T(8,128)(2,1)S(1)}, u32[]{:S(2)}, u32[]{:S(2)}) collective-permute-start(bf16[512,256]{0,1:T(8,128)(2,1)S(1)} %fusion.14), channel_id=1, source_target_pairs={{0,2},{1,3},{2,0},{3,1},{4,6},{5,7},{6,4},{7,5},{8,10},{9,11},{10,... | collective-permute-start | bytes 786440 | tf_op jit(solution)/shard_map/ppermute | solution.py:21

commit v14 on v12

--- a/solution.py
+++ b/solution.py
@@ -90,9 +90,10 @@
     own = arrived.reshape(slots, queries.shape[1])
     far = swapped(own, "feat", 2)
     near = swapped(jnp.stack([own, far]), "feat", 1)
-    parts = jnp.stack([own, far, near[0], near[1]])
-    order = jnp.array([0, 2, 1, 3], jnp.int32)[jnp.arange(feats, dtype=jnp.int32) ^ feat_index]
-    query_full = jnp.swapaxes(jnp.take(parts, order, axis=0), 0, 1).reshape(slots, feats * queries.shape[1])
+    width = queries.shape[1]
+    query_full = jnp.zeros((slots, feats * width), queries.dtype)
+    for part, code in ((own, 0), (far, 2), (near[0], 1), (near[1], 3)):
+        query_full = lax.dynamic_update_slice_in_dim(query_full, part, (feat_index ^ code) * width, axis=1)
 
     band_keys = jnp.stack([b[0] for b in blocks]).reshape(len(offsets) * rows, depth)
     band_labels = jnp.stack([b[1] for b in blocks]).reshape(len(offsets) * rows, feats * group)

time: 157 us -> 153 us (0.975)
  local copies, waits for them, and re-layouts: 24.3 us -> 21.2 us
  waiting for transfers between devices: 18.3 us -> 20.5 us
  other arithmetic: 8.48 us -> 6.49 us
    unnamed x33 -> x21, local copies, waits for them, and re-layouts: 12.2 us -> 11.2 us
  transfers between devices with their start and end apart: 11 -> 11, of which waited for: 3 -> 3; matrix products, arithmetic and copies ran while one was open for 14% -> 12% of each run, Pallas kernels for 0% -> 0%
where the time goes in v14:
time: 153 us; the launch traced here: 152 us
  starting transfers between devices  59.5 us (39%)
  blocking collectives  35.3 us (23%)
  local copies, waits for them, and re-layouts  21.2 us (14%)
  waiting for transfers between devices  20.5 us (13%)
  other arithmetic  6.49 us (4%)
  between operations  4.93 us (3%)
  matrix products  4.06 us (3%)
    all_to_all x1, blocking collectives, body(): lax.all_to_all(shares.reshape(clusters, capacity, quarter), 'cluster', sp...  35.3 us
    ppermute x6, starting transfers between devices, shifted(): lax.ppermute(array, axis, [(i, (i - by) % peers) for i in range(peers)])  23.9 us
    all_to_all x1, starting transfers between devices, body(): lax.all_to_all(outgoing.reshape(clusters, capacity, queries.shape[1]), 'c...  21.9 us
    ppermute x4, starting transfers between devices, swapped(): return lax.ppermute(array, axis, [(i, i ^ bit) for i in range(peers)])  13.6 us
    unnamed x21, local copies, waits for them, and re-layouts  11.2 us
    all_to_all x1, waiting for transfers between devices, body(): lax.all_to_all(outgoing.reshape(clusters, capacity, queries.shape[1]), 'c...  10.9 us
    ppermute x4, waiting for transfers between devices, swapped(): return lax.ppermute(array, axis, [(i, i ^ bit) for i in range(peers)])  9.65 us
  transfers between devices with their start and end apart: 11, of which 3 were waited for; matrix products, arithmetic and copies ran while one was open for 12% of the time, Pallas kernels for 0%

profile of v14, /device:TPU:32, one launch (start us, length us, event | category | flops | bytes accessed | tf_op | source)
XLA Modules:
  0.0 151.9 jit_solution(7656479089022012162)
XLA Ops:
  0.0 1.1 reshape.888
  1.1 0.7 and_select_fusion
  1.8 0.1 copy.30
  2.0 1.9 %pad_maximum_fusion.1 = bf16[2,128,1024]{2,1,0:T(8,128)(2,1)} fusion(bf16[1,128,1024]{2,1,0:T(8,128)(2,1)S(1)} %copy.30, bf16[1,128,1024]{2,1,0:T(8,128)(2,1)} %bitcast.116), kind=kLoop, calls=%fused_computation.25 | loop fusion | flops 262144 | bytes 1048576 | tf_op jit(solution)/shard_map/stack | solution.py:71
  3.9 5.5 %collective-permute-start.2 = (bf16[2,128,1024]{2,1,0:T(8,128)(2,1)}, bf16[2,128,1024]{2,1,0:T(8,128)(2,1)}, u32[]{:S(2)}, u32[]{:S(2)}) collective-permute-start(bf16[2,128,1024]{2,1,0:T(8,128)(2,1)} %pad_maximum_fusion.1), channel_id=1, source_target_pairs={{0,508},{4,0},{8,4},{12,8},{16,12},{20,16},{24,20},{28,24},{32,28}... | collective-permute-start | bytes 1572872 | tf_op jit(solution)/shard_map/ppermute | solution.py:16
  9.4 1.9 %collective-permute-start.3 = (bf16[2,128,1024]{2,1,0:T(8,128)(2,1)}, bf16[2,128,1024]{2,1,0:T(8,128)(2,1)}, u32[]{:S(2)}, u32[]{:S(2)}) collective-permute-start(bf16[2,128,1024]{2,1,0:T(8,128)(2,1)} %pad_maximum_fusion.1), channel_id=1, source_target_pairs={{0,4},{4,8},{8,12},{12,16},{16,20},{20,24},{24,28},{28,32},{32,36}... | collective-permute-start | bytes 1572872 | tf_op jit(solution)/shard_map/ppermute | solution.py:16
  11.3 3.0 %collective-permute-start.4 = (bf16[2,128,1024]{2,1,0:T(8,128)(2,1)}, bf16[2,128,1024]{2,1,0:T(8,128)(2,1)}, u32[]{:S(2)}, u32[]{:S(2)}) collective-permute-start(bf16[2,128,1024]{2,1,0:T(8,128)(2,1)} %pad_maximum_fusion.1), channel_id=1, source_target_pairs={{0,504},{4,508},{8,0},{12,4},{16,8},{20,12},{24,16},{28,20},{32,24... | collective-permute-start | bytes 1572872 | tf_op jit(solution)/shard_map/ppermute | solution.py:16
  14.3 2.8 %collective-permute-start.5 = (bf16[2,128,1024]{2,1,0:T(8,128)(2,1)}, bf16[2,128,1024]{2,1,0:T(8,128)(2,1)}, u32[]{:S(2)}, u32[]{:S(2)}) collective-permute-start(bf16[2,128,1024]{2,1,0:T(8,128)(2,1)} %pad_maximum_fusion.1), channel_id=1, source_target_pairs={{0,8},{4,12},{8,16},{12,20},{16,24},{20,28},{24,32},{28,36},{32,40... | collective-permute-start | bytes 1572872 | tf_op jit(solution)/shard_map/ppermute | solution.py:16
  17.2 6.4 %collective-permute-start.6 = (bf16[2,128,1024]{2,1,0:T(8,128)(2,1)}, bf16[2,128,1024]{2,1,0:T(8,128)(2,1)S(1)}, u32[]{:S(2)}, u32[]{:S(2)}) collective-permute-start(bf16[2,128,1024]{2,1,0:T(8,128)(2,1)} %pad_maximum_fusion.1), channel_id=1, source_target_pairs={{0,500},{4,504},{8,508},{12,0},{16,4},{20,8},{24,12},{28,16},{32,2... | collective-permute-start | bytes 1572872 | tf_op jit(solution)/shard_map/ppermute | solution.py:16
  23.6 0.1 copy.28
  23.7 0.2 fusion.21
  24.0 0.2 fusion.23
  24.2 0.2 convolution_convert_fusion
  24.4 0.8 reshape.886
  25.2 21.9 %all-to-all-start = ((bf16[128,4,256]{2,1,0:T(4,128)(2,1)}), bf16[128,4,256]{2,1,0:T(4,128)(2,1)S(1)}, u32[]{:S(2)}, u32[]{:S(2)}) async-start(bf16[128,4,256]{2,1,0:T(4,128)(2,1)} %reshape.886), calls=%async_computation | async-start | bytes 524288 | tf_op jit(solution)/shard_map/all_to_all | solution.py:83
  47.2 0.7 constant_dynamic-update-slice_fusion
  47.9 0.1 constant_dynamic-slice_fusion
  48.0 0.6 fusion.52
  53.0 0.1 stack.63
  53.1 0.1 broadcast_bitcast_fusion
  53.3 4.3 %collective-permute-start.7 = (bf16[2,128,1024]{2,1,0:T(8,128)(2,1)}, bf16[2,128,1024]{2,1,0:T(8,128)(2,1)}, u32[]{:S(2)}, u32[]{:S(2)}) collective-permute-start(bf16[2,128,1024]{2,1,0:T(8,128)(2,1)} %pad_maximum_fusion.1), channel_id=1, source_target_pairs={{0,12},{4,16},{8,20},{12,24},{16,28},{20,32},{24,36},{28,40},{32,4... | collective-permute-start | bytes 1572872 | tf_op jit(solution)/shard_map/ppermute | solution.py:16
  57.5 1.8 %slice_dynamic-update-slice_fusion.11 = (bf16[7,128,1024]{2,1,0:T(8,128)(2,1)}, bf16[7,128,1024]{2,1,0:T(8,128)(2,1)S(1)}) fusion(bf16[7,128,1024]{2,1,0:T(8,128)(2,1)} %get-tuple-element.52, bf16[2,128,1024]{2,1,0:T(8,128)(2,1)} %collective-permute-done.2, bf16[7,128,1024]{2,1,0:T(8,128)(2,1)S(1)} %get-tuple-element.53), kind=kLoop, calls=%fused_computation.46 | loop fusion | bytes 1048576
  59.3 1.8 %slice_dynamic-update-slice_fusion.10 = (bf16[7,128,1024]{2,1,0:T(8,128)(2,1)}, bf16[7,128,1024]{2,1,0:T(8,128)(2,1)S(1)}) fusion(bf16[7,128,1024]{2,1,0:T(8,128)(2,1)} %get-tuple-element.26, bf16[2,128,1024]{2,1,0:T(8,128)(2,1)} %collective-permute-done.3, bf16[7,128,1024]{2,1,0:T(8,128)(2,1)S(1)} %get-tuple-element.27), kind=kLoop, calls=%fused_computation.45 | loop fusion | bytes 1048576
  61.1 1.8 %slice_dynamic-update-slice_fusion.9 = (bf16[7,128,1024]{2,1,0:T(8,128)(2,1)}, bf16[7,128,1024]{2,1,0:T(8,128)(2,1)S(1)}) fusion(bf16[7,128,1024]{2,1,0:T(8,128)(2,1)} %get-tuple-element.24, bf16[2,128,1024]{2,1,0:T(8,128)(2,1)} %collective-permute-done.4, bf16[7,128,1024]{2,1,0:T(8,128)(2,1)S(1)} %get-tuple-element.25), kind=kLoop, calls=%fused_computation.44 | loop fusion | bytes 1048576
  62.8 10.9 %all-to-all-done = bf16[128,4,256]{2,1,0:T(4,128)(2,1)S(1)} async-done(((bf16[128,4,256]{2,1,0:T(4,128)(2,1)}), bf16[128,4,256]{2,1,0:T(4,128)(2,1)S(1)}, u32[]{:S(2)}, u32[]{:S(2)}) %all-to-all-start) | async-done | bytes 262176 | tf_op jit(solution)/shard_map/all_to_all | solution.py:83
  73.7 0.1 reshape.887
  73.8 4.6 %collective-permute-start = (bf16[512,256]{1,0:T(8,128)(2,1)S(1)}, bf16[512,256]{1,0:T(8,128)(2,1)S(1)}, u32[]{:S(2)}, u32[]{:S(2)}) collective-permute-start(bf16[512,256]{1,0:T(8,128)(2,1)S(1)} %reshape.887), channel_id=1, source_target_pairs={{0,2},{1,3},{2,0},{3,1},{4,6},{5,7},{6,4},{7,5},{8,10},{9,11},{10,... | collective-permute-start | bytes 786440 | tf_op jit(solution)/shard_map/ppermute | solution.py:21
  78.4 1.8 %slice_dynamic-update-slice_fusion.8 = (bf16[7,128,1024]{2,1,0:T(8,128)(2,1)}, bf16[7,128,1024]{2,1,0:T(8,128)(2,1)S(1)}) fusion(bf16[7,128,1024]{2,1,0:T(8,128)(2,1)} %get-tuple-element.22, bf16[2,128,1024]{2,1,0:T(8,128)(2,1)} %collective-permute-done.5, bf16[7,128,1024]{2,1,0:T(8,128)(2,1)S(1)} %get-tuple-element.23), kind=kLoop, calls=%fused_computation.43 | loop fusion | bytes 1048576
  80.2 0.7 slice_dynamic-update-slice_fusion.7
  80.9 0.1 stack_reshape.6
  81.0 2.6 %collective-permute-done = bf16[512,256]{1,0:T(8,128)(2,1)S(1)} collective-permute-done((bf16[512,256]{1,0:T(8,128)(2,1)S(1)}, bf16[512,256]{1,0:T(8,128)(2,1)S(1)}, u32[]{:S(2)}, u32[]{:S(2)}) %collective-permute-start) | collective-permute-done | bytes 262176 | tf_op jit(solution)/shard_map/ppermute | solution.py:21
  83.5 0.8 pad_maximum_fusion
  84.4 1.9 %collective-permute-start.1 = (bf16[2,512,256]{2,1,0:T(8,128)(2,1)}, bf16[2,512,256]{2,1,0:T(8,128)(2,1)S(1)}, u32[]{:S(2)}, u32[]{:S(2)}) collective-permute-start(bf16[2,512,256]{2,1,0:T(8,128)(2,1)} %pad_maximum_fusion), channel_id=1, source_target_pairs={{0,1},{1,0},{2,3},{3,2},{4,5},{5,4},{6,7},{7,6},{8,9},{9,8},{10,11... | collective-permute-start | bytes 1572872 | tf_op jit(solution)/shard_map/ppermute | solution.py:21
  86.3 1.8 %slice_dynamic-update-slice_fusion.6 = (bf16[7,128,1024]{2,1,0:T(8,128)(2,1)}, bf16[7,128,1024]{2,1,0:T(8,128)(2,1)S(1)}) fusion(bf16[7,128,1024]{2,1,0:T(8,128)(2,1)} %get-tuple-element.18, bf16[2,128,1024]{2,1,0:T(8,128)(2,1)} %collective-permute-done.7, bf16[7,128,1024]{2,1,0:T(8,128)(2,1)S(1)} %get-tuple-element.19), kind=kLoop, calls=%fused_computation.41 | loop fusion | bytes 1048576 | tf_op jit(solution)/shard_map/stack | solution.py:98
  88.1 2.5 %copy.32 = bf16[896,1024]{0,1:T(8,128)(2,1)} copy(bf16[896,1024]{1,0:T(8,128)(2,1)S(1)} %bitcast.112) | data formatting | bytes 3670016 | tf_op jit(solution)/shard_map/reshape | solution.py:99
  90.5 0.9 fusion.26
  91.4 0.1 broadcast_in_dim.144
  91.7 0.4 copy-done.4
  92.0 1.4 fusion.53
  93.4 0.5 fusion
  93.9 1.0 copy-done.1
  94.9 1.4 fusion.4
  96.4 1.3 copy-done.2
  97.7 0.1 dynamic-slice_bitcast_fusion.1
  97.7 0.1 copy.36
  97.9 0.1 copy.37
  98.0 0.3 select_convert_fusion.1
  98.3 0.1 pad_maximum_fusion.2
  98.4 2.4 %collective-permute-start.8 = (bf16[2,512,256]{1,2,0:T(8,128)(2,1)S(1)}, bf16[2,512,256]{1,2,0:T(8,128)(2,1)S(1)}, u32[]{:S(2)}, u32[]{:S(2)}) collective-permute-start(bf16[2,512,256]{1,2,0:T(8,128)(2,1)S(1)} %pad_maximum_fusion.2), channel_id=1, source_target_pairs={{0,1},{1,0},{2,3},{3,2},{4,5},{5,4},{6,7},{7,6},{8,9},{9,8},{10,11... | collective-permute-start | bytes 1572872 | tf_op jit(solution)/shard_map/ppermute | solution.py:21
  100.8 1.3 dynamic-slice_bitcast_fusion.3
  102.1 0.2 copy.34
  102.3 0.2 copy.35
  102.5 0.1 convert_element_type.259
  102.7 0.2 fusion.2
  102.9 0.3 fusion.15
  103.2 4.6 %collective-permute-start.9 = (bf16[512,256]{0,1:T(8,128)(2,1)S(1)}, bf16[512,256]{0,1:T(8,128)(2,1)S(1)}, u32[]{:S(2)}, u32[]{:S(2)}) collective-permute-start(bf16[512,256]{0,1:T(8,128)(2,1)S(1)} %fusion.15), channel_id=1, source_target_pairs={{0,2},{1,3},{2,0},{3,1},{4,6},{5,7},{6,4},{7,5},{8,10},{9,11},{10,... | collective-permute-start | bytes 786440 | tf_op jit(solution)/shard_map/ppermute | solution.py:21
  107.9 7.1 %collective-permute-done.9 = bf16[512,256]{0,1:T(8,128)(2,1)S(1)} collective-permute-done((bf16[512,256]{0,1:T(8,128)(2,1)S(1)}, bf16[512,256]{0,1:T(8,128)(2,1)S(1)}, u32[]{:S(2)}, u32[]{:S(2)}) %collective-permute-start.9) | collective-permute-done | bytes 262176 | tf_op jit(solution)/shard_map/ppermute | solution.py:21
  115.0 0.1 convert_element_type.273
  115.1 0.1 fusion.16
  115.2 0.1 copy.38
  115.4 0.1 reshape.891
  115.5 35.3 %all_to_all.10 = bf16[128,4,250]{2,1,0:T(4,128)(2,1)S(1)} all-to-all(bf16[128,4,250]{2,1,0:T(4,128)(2,1)S(1)} %reshape.891), channel_id=1, replica_groups=mesh['cluster'=128,'feat'=4] {'cluster'}, dimensions={0} | all-to-all | bytes 512000 | tf_op jit(solution)/shard_map/all_to_all | solution.py:137
  150.7 0.2 reshape.892
  150.9 1.0 convolution_convert_fusion.1
  (45 shorter events, 0.5 us)
Async XLA Ops:
  0.0 24.2 %copy-start = (bf16[256,256]{1,0:T(8,128)(2,1)S(1)}, bf16[256,256]{1,0:T(8,128)(2,1)}, u32[]{:S(2)}) copy-start(bf16[256,256]{1,0:T(8,128)(2,1)} %param.6) | copy-start | bytes 393220
  0.0 23.6 %copy-start.5 = (s32[256,1]{0,1:T(1,128)S(1)}, s32[256,1]{0,1:T(1,128)}, u32[]{:S(2)}) copy-start(s32[256,1]{0,1:T(1,128)} %param.7) | copy-start | bytes 3076
  2.0 45.1 %copy-start.3 = (bf16[128,1024]{1,0:T(8,128)(2,1)S(1)}, bf16[128,1024]{1,0:T(8,128)(2,1)}, u32[]{:S(2)}) copy-start(bf16[128,1024]{1,0:T(8,128)(2,1)} %param.9) | copy-start | bytes 786436
  3.9 44.0 %copy-start.6 = (s32[128,7]{0,1:T(8,128)S(1)}, s32[128,7]{0,1:T(8,128)}, u32[]{:S(2)}) copy-start(s32[128,7]{0,1:T(8,128)} %param.8) | copy-start | bytes 10756
  3.9 49.4 %collective-permute-start.2 = (bf16[2,128,1024]{2,1,0:T(8,128)(2,1)}, bf16[2,128,1024]{2,1,0:T(8,128)(2,1)}, u32[]{:S(2)}, u32[]{:S(2)}) collective-permute-start(bf16[2,128,1024]{2,1,0:T(8,128)(2,1)} %pad_maximum_fusion.1), channel_id=1, source_target_pairs={{0,508},{4,0},{8,4},{12,8},{16,12},{20,16},{24,20},{28,24},{32,28}... | collective-permute-start | bytes 1572872 | tf_op jit(solution)/shard_map/ppermute | solution.py:16
  9.4 49.9 %collective-permute-start.3 = (bf16[2,128,1024]{2,1,0:T(8,128)(2,1)}, bf16[2,128,1024]{2,1,0:T(8,128)(2,1)}, u32[]{:S(2)}, u32[]{:S(2)}) collective-permute-start(bf16[2,128,1024]{2,1,0:T(8,128)(2,1)} %pad_maximum_fusion.1), channel_id=1, source_target_pairs={{0,4},{4,8},{8,12},{12,16},{16,20},{20,24},{24,28},{28,32},{32,36}... | collective-permute-start | bytes 1572872 | tf_op jit(solution)/shard_map/ppermute | solution.py:16
  11.3 49.7 %collective-permute-start.4 = (bf16[2,128,1024]{2,1,0:T(8,128)(2,1)}, bf16[2,128,1024]{2,1,0:T(8,128)(2,1)}, u32[]{:S(2)}, u32[]{:S(2)}) collective-permute-start(bf16[2,128,1024]{2,1,0:T(8,128)(2,1)} %pad_maximum_fusion.1), channel_id=1, source_target_pairs={{0,504},{4,508},{8,0},{12,4},{16,8},{20,12},{24,16},{28,20},{32,24... | collective-permute-start | bytes 1572872 | tf_op jit(solution)/shard_map/ppermute | solution.py:16
  14.3 64.1 %collective-permute-start.5 = (bf16[2,128,1024]{2,1,0:T(8,128)(2,1)}, bf16[2,128,1024]{2,1,0:T(8,128)(2,1)}, u32[]{:S(2)}, u32[]{:S(2)}) collective-permute-start(bf16[2,128,1024]{2,1,0:T(8,128)(2,1)} %pad_maximum_fusion.1), channel_id=1, source_target_pairs={{0,8},{4,12},{8,16},{12,20},{16,24},{20,28},{24,32},{28,36},{32,40... | collective-permute-start | bytes 1572872 | tf_op jit(solution)/shard_map/ppermute | solution.py:16
  17.2 63.0 %collective-permute-start.6 = (bf16[2,128,1024]{2,1,0:T(8,128)(2,1)}, bf16[2,128,1024]{2,1,0:T(8,128)(2,1)S(1)}, u32[]{:S(2)}, u32[]{:S(2)}) collective-permute-start(bf16[2,128,1024]{2,1,0:T(8,128)(2,1)} %pad_maximum_fusion.1), channel_id=1, source_target_pairs={{0,500},{4,504},{8,508},{12,0},{16,4},{20,8},{24,12},{28,16},{32,2... | collective-permute-start | bytes 1572872 | tf_op jit(solution)/shard_map/ppermute | solution.py:16
  25.2 48.5 %all-to-all-start = ((bf16[128,4,256]{2,1,0:T(4,128)(2,1)}), bf16[128,4,256]{2,1,0:T(4,128)(2,1)S(1)}, u32[]{:S(2)}, u32[]{:S(2)}) async-start(bf16[128,4,256]{2,1,0:T(4,128)(2,1)} %reshape.886), calls=%async_computation | async-start | bytes 524288 | tf_op jit(solution)/shard_map/all_to_all | solution.py:83
  53.3 33.0 %collective-permute-start.7 = (bf16[2,128,1024]{2,1,0:T(8,128)(2,1)}, bf16[2,128,1024]{2,1,0:T(8,128)(2,1)}, u32[]{:S(2)}, u32[]{:S(2)}) collective-permute-start(bf16[2,128,1024]{2,1,0:T(8,128)(2,1)} %pad_maximum_fusion.1), channel_id=1, source_target_pairs={{0,12},{4,16},{8,20},{12,24},{16,28},{20,32},{24,36},{28,40},{32,4... | collective-permute-start | bytes 1572872 | tf_op jit(solution)/shard_map/ppermute | solution.py:16
  73.8 9.8 %collective-permute-start = (bf16[512,256]{1,0:T(8,128)(2,1)S(1)}, bf16[512,256]{1,0:T(8,128)(2,1)S(1)}, u32[]{:S(2)}, u32[]{:S(2)}) collective-permute-start(bf16[512,256]{1,0:T(8,128)(2,1)S(1)} %reshape.887), channel_id=1, source_target_pairs={{0,2},{1,3},{2,0},{3,1},{4,6},{5,7},{6,4},{7,5},{8,10},{9,11},{10,... | collective-permute-start | bytes 786440 | tf_op jit(solution)/shard_map/ppermute | solution.py:21
  84.4 7.2 %collective-permute-start.1 = (bf16[2,512,256]{2,1,0:T(8,128)(2,1)}, bf16[2,512,256]{2,1,0:T(8,128)(2,1)S(1)}, u32[]{:S(2)}, u32[]{:S(2)}) collective-permute-start(bf16[2,512,256]{2,1,0:T(8,128)(2,1)} %pad_maximum_fusion), channel_id=1, source_target_pairs={{0,1},{1,0},{2,3},{3,2},{4,5},{5,4},{6,7},{7,6},{8,9},{9,8},{10,11... | collective-permute-start | bytes 1572872 | tf_op jit(solution)/shard_map/ppermute | solution.py:21
  90.5 1.5 copy-start.4
  93.4 1.5 copy-start.1
  96.4 1.3 copy-start.2
  98.4 4.1 %collective-permute-start.8 = (bf16[2,512,256]{1,2,0:T(8,128)(2,1)S(1)}, bf16[2,512,256]{1,2,0:T(8,128)(2,1)S(1)}, u32[]{:S(2)}, u32[]{:S(2)}) collective-permute-start(bf16[2,512,256]{1,2,0:T(8,128)(2,1)S(1)} %pad_maximum_fusion.2), channel_id=1, source_target_pairs={{0,1},{1,0},{2,3},{3,2},{4,5},{5,4},{6,7},{7,6},{8,9},{9,8},{10,11... | collective-permute-start | bytes 1572872 | tf_op jit(solution)/shard_map/ppermute | solution.py:21
  103.2 11.8 %collective-permute-start.9 = (bf16[512,256]{0,1:T(8,128)(2,1)S(1)}, bf16[512,256]{0,1:T(8,128)(2,1)S(1)}, u32[]{:S(2)}, u32[]{:S(2)}) collective-permute-start(bf16[512,256]{0,1:T(8,128)(2,1)S(1)} %fusion.15), channel_id=1, source_target_pairs={{0,2},{1,3},{2,0},{3,1},{4,6},{5,7},{6,4},{7,5},{8,10},{9,11},{10,... | collective-permute-start | bytes 786440 | tf_op jit(solution)/shard_map/ppermute | solution.py:21

commit v15 on v14

--- a/solution.py
+++ b/solution.py
@@ -70,7 +70,7 @@
     grouped = jnp.concatenate([labels.reshape(rows, feats, quarter), spare], axis=2)
     block = jnp.stack([keys, grouped.reshape(rows, feats * group)])
     offsets = [0]
-    for reach in range(1, REACH + 1):
+    for reach in sorted(range(1, REACH + 1), key=lambda r: r == 2):
         offsets += [reach, -reach]
     blocks = [block] + [shifted(block, "cluster", o) for o in offsets[1:]]
 

time: 153 us -> 149 us (0.974)
  waiting for transfers between devices: 20.5 us -> 16.8 us
    all_to_all x1, waiting for transfers between devices: 10.9 us -> 7.09 us  [body(): lax.all_to_all(outgoing.reshape(clusters, capacity, queries.shape[1]), 'c...]
  transfers between devices with their start and end apart: 11 -> 11, of which waited for: 3 -> 3; matrix products, arithmetic and copies ran while one was open for 12% -> 13% of each run, Pallas kernels for 0% -> 0%
where the time goes in v15:
time: 149 us
  starting transfers between devices  59.4 us (40%)
  blocking collectives  35.8 us (24%)
  local copies, waits for them, and re-layouts  21.2 us (14%)
  waiting for transfers between devices  16.8 us (11%)
  other arithmetic  6.49 us (4%)
  between operations  4.93 us (3%)
  matrix products  4.07 us (3%)
    all_to_all x1, blocking collectives, body(): lax.all_to_all(shares.reshape(clusters, capacity, quarter), 'cluster', sp...  35.8 us
    all_to_all x1, starting transfers between devices, body(): lax.all_to_all(outgoing.reshape(clusters, capacity, queries.shape[1]), 'c...  23.2 us
    ppermute x6, starting transfers between devices, shifted(): lax.ppermute(array, axis, [(i, (i - by) % peers) for i in range(peers)])  22.7 us
    ppermute x4, starting transfers between devices, swapped(): return lax.ppermute(array, axis, [(i, i ^ bit) for i in range(peers)])  13.6 us
    unnamed x21, local copies, waits for them, and re-layouts  11.2 us
    ppermute x4, waiting for transfers between devices, swapped(): return lax.ppermute(array, axis, [(i, i ^ bit) for i in range(peers)])  9.66 us
    all_to_all x1, waiting for transfers between devices, body(): lax.all_to_all(outgoing.reshape(clusters, capacity, queries.shape[1]), 'c...  7.09 us
  transfers between devices with their start and end apart: 11, of which 3 were waited for; matrix products, arithmetic and copies ran while one was open for 13% of the time, Pallas kernels for 0%

profile of v15, /device:TPU:32, one launch (start us, length us, event | category | flops | bytes accessed | tf_op | source)
XLA Modules:
  0.0 148.7 jit_solution(9084700783467339469)
XLA Ops:
  0.0 1.1 reshape.888
  1.1 0.7 and_select_fusion
  1.8 0.1 copy.30
  2.0 1.9 %pad_maximum_fusion.1 = bf16[2,128,1024]{2,1,0:T(8,128)(2,1)} fusion(bf16[1,128,1024]{2,1,0:T(8,128)(2,1)S(1)} %copy.30, bf16[1,128,1024]{2,1,0:T(8,128)(2,1)} %bitcast.116), kind=kLoop, calls=%fused_computation.25 | loop fusion | flops 262144 | bytes 1048576 | tf_op jit(solution)/shard_map/stack | solution.py:71
  3.9 5.5 %collective-permute-start.2 = (bf16[2,128,1024]{2,1,0:T(8,128)(2,1)}, bf16[2,128,1024]{2,1,0:T(8,128)(2,1)}, u32[]{:S(2)}, u32[]{:S(2)}) collective-permute-start(bf16[2,128,1024]{2,1,0:T(8,128)(2,1)} %pad_maximum_fusion.1), channel_id=1, source_target_pairs={{0,508},{4,0},{8,4},{12,8},{16,12},{20,16},{24,20},{28,24},{32,28}... | collective-permute-start | bytes 1572872 | tf_op jit(solution)/shard_map/ppermute | solution.py:16
  9.4 1.9 %collective-permute-start.3 = (bf16[2,128,1024]{2,1,0:T(8,128)(2,1)}, bf16[2,128,1024]{2,1,0:T(8,128)(2,1)}, u32[]{:S(2)}, u32[]{:S(2)}) collective-permute-start(bf16[2,128,1024]{2,1,0:T(8,128)(2,1)} %pad_maximum_fusion.1), channel_id=1, source_target_pairs={{0,4},{4,8},{8,12},{12,16},{16,20},{20,24},{24,28},{28,32},{32,36}... | collective-permute-start | bytes 1572872 | tf_op jit(solution)/shard_map/ppermute | solution.py:16
  11.3 5.0 %collective-permute-start.4 = (bf16[2,128,1024]{2,1,0:T(8,128)(2,1)}, bf16[2,128,1024]{2,1,0:T(8,128)(2,1)}, u32[]{:S(2)}, u32[]{:S(2)}) collective-permute-start(bf16[2,128,1024]{2,1,0:T(8,128)(2,1)} %pad_maximum_fusion.1), channel_id=1, source_target_pairs={{0,500},{4,504},{8,508},{12,0},{16,4},{20,8},{24,12},{28,16},{32,2... | collective-permute-start | bytes 1572872 | tf_op jit(solution)/shard_map/ppermute | solution.py:16
  16.3 1.9 %collective-permute-start.5 = (bf16[2,128,1024]{2,1,0:T(8,128)(2,1)}, bf16[2,128,1024]{2,1,0:T(8,128)(2,1)}, u32[]{:S(2)}, u32[]{:S(2)}) collective-permute-start(bf16[2,128,1024]{2,1,0:T(8,128)(2,1)} %pad_maximum_fusion.1), channel_id=1, source_target_pairs={{0,12},{4,16},{8,20},{12,24},{16,28},{20,32},{24,36},{28,40},{32,4... | collective-permute-start | bytes 1572872 | tf_op jit(solution)/shard_map/ppermute | solution.py:16
  18.3 4.9 %collective-permute-start.6 = (bf16[2,128,1024]{2,1,0:T(8,128)(2,1)}, bf16[2,128,1024]{2,1,0:T(8,128)(2,1)S(1)}, u32[]{:S(2)}, u32[]{:S(2)}) collective-permute-start(bf16[2,128,1024]{2,1,0:T(8,128)(2,1)} %pad_maximum_fusion.1), channel_id=1, source_target_pairs={{0,504},{4,508},{8,0},{12,4},{16,8},{20,12},{24,16},{28,20},{32,24... | collective-permute-start | bytes 1572872 | tf_op jit(solution)/shard_map/ppermute | solution.py:16
  23.2 0.1 copy.28
  23.3 0.2 fusion.21
  23.6 0.2 fusion.23
  23.8 0.2 convolution_convert_fusion
  24.1 0.8 reshape.886
  24.8 23.2 %all-to-all-start = ((bf16[128,4,256]{2,1,0:T(4,128)(2,1)}), bf16[128,4,256]{2,1,0:T(4,128)(2,1)S(1)}, u32[]{:S(2)}, u32[]{:S(2)}) async-start(bf16[128,4,256]{2,1,0:T(4,128)(2,1)} %reshape.886), calls=%async_computation | async-start | bytes 524288 | tf_op jit(solution)/shard_map/all_to_all | solution.py:83
  48.1 0.7 constant_dynamic-update-slice_fusion
  48.8 0.1 constant_dynamic-slice_fusion
  48.9 0.6 fusion.52
  53.9 0.1 stack.63
  54.0 0.1 broadcast_bitcast_fusion
  54.1 3.4 %collective-permute-start.7 = (bf16[2,128,1024]{2,1,0:T(8,128)(2,1)}, bf16[2,128,1024]{2,1,0:T(8,128)(2,1)}, u32[]{:S(2)}, u32[]{:S(2)}) collective-permute-start(bf16[2,128,1024]{2,1,0:T(8,128)(2,1)} %pad_maximum_fusion.1), channel_id=1, source_target_pairs={{0,8},{4,12},{8,16},{12,20},{16,24},{20,28},{24,32},{28,36},{32,40... | collective-permute-start | bytes 1572872 | tf_op jit(solution)/shard_map/ppermute | solution.py:16
  57.5 1.8 %slice_dynamic-update-slice_fusion.11 = (bf16[7,128,1024]{2,1,0:T(8,128)(2,1)}, bf16[7,128,1024]{2,1,0:T(8,128)(2,1)S(1)}) fusion(bf16[7,128,1024]{2,1,0:T(8,128)(2,1)} %get-tuple-element.52, bf16[2,128,1024]{2,1,0:T(8,128)(2,1)} %collective-permute-done.2, bf16[7,128,1024]{2,1,0:T(8,128)(2,1)S(1)} %get-tuple-element.53), kind=kLoop, calls=%fused_computation.46 | loop fusion | bytes 1048576
  59.3 1.8 %slice_dynamic-update-slice_fusion.10 = (bf16[7,128,1024]{2,1,0:T(8,128)(2,1)}, bf16[7,128,1024]{2,1,0:T(8,128)(2,1)S(1)}) fusion(bf16[7,128,1024]{2,1,0:T(8,128)(2,1)} %get-tuple-element.26, bf16[2,128,1024]{2,1,0:T(8,128)(2,1)} %collective-permute-done.3, bf16[7,128,1024]{2,1,0:T(8,128)(2,1)S(1)} %get-tuple-element.27), kind=kLoop, calls=%fused_computation.45 | loop fusion | bytes 1048576
  61.1 1.8 %slice_dynamic-update-slice_fusion.9 = (bf16[7,128,1024]{2,1,0:T(8,128)(2,1)}, bf16[7,128,1024]{2,1,0:T(8,128)(2,1)S(1)}) fusion(bf16[7,128,1024]{2,1,0:T(8,128)(2,1)} %get-tuple-element.24, bf16[2,128,1024]{2,1,0:T(8,128)(2,1)} %collective-permute-done.4, bf16[7,128,1024]{2,1,0:T(8,128)(2,1)S(1)} %get-tuple-element.25), kind=kLoop, calls=%fused_computation.44 | loop fusion | bytes 1048576
  62.8 7.1 %all-to-all-done = bf16[128,4,256]{2,1,0:T(4,128)(2,1)S(1)} async-done(((bf16[128,4,256]{2,1,0:T(4,128)(2,1)}), bf16[128,4,256]{2,1,0:T(4,128)(2,1)S(1)}, u32[]{:S(2)}, u32[]{:S(2)}) %all-to-all-start) | async-done | bytes 262176 | tf_op jit(solution)/shard_map/all_to_all | solution.py:83
  69.9 0.1 reshape.887
  70.0 4.6 %collective-permute-start = (bf16[512,256]{1,0:T(8,128)(2,1)S(1)}, bf16[512,256]{1,0:T(8,128)(2,1)S(1)}, u32[]{:S(2)}, u32[]{:S(2)}) collective-permute-start(bf16[512,256]{1,0:T(8,128)(2,1)S(1)} %reshape.887), channel_id=1, source_target_pairs={{0,2},{1,3},{2,0},{3,1},{4,6},{5,7},{6,4},{7,5},{8,10},{9,11},{10,... | collective-permute-start | bytes 786440 | tf_op jit(solution)/shard_map/ppermute | solution.py:21
  74.6 1.8 %slice_dynamic-update-slice_fusion.8 = (bf16[7,128,1024]{2,1,0:T(8,128)(2,1)}, bf16[7,128,1024]{2,1,0:T(8,128)(2,1)S(1)}) fusion(bf16[7,128,1024]{2,1,0:T(8,128)(2,1)} %get-tuple-element.22, bf16[2,128,1024]{2,1,0:T(8,128)(2,1)} %collective-permute-done.5, bf16[7,128,1024]{2,1,0:T(8,128)(2,1)S(1)} %get-tuple-element.23), kind=kLoop, calls=%fused_computation.43 | loop fusion | bytes 1048576
  76.4 0.7 slice_dynamic-update-slice_fusion.7
  77.1 0.1 stack_reshape.6
  77.2 2.6 %collective-permute-done = bf16[512,256]{1,0:T(8,128)(2,1)S(1)} collective-permute-done((bf16[512,256]{1,0:T(8,128)(2,1)S(1)}, bf16[512,256]{1,0:T(8,128)(2,1)S(1)}, u32[]{:S(2)}, u32[]{:S(2)}) %collective-permute-start) | collective-permute-done | bytes 262176 | tf_op jit(solution)/shard_map/ppermute | solution.py:21
  79.8 0.8 pad_maximum_fusion
  80.6 1.9 %collective-permute-start.1 = (bf16[2,512,256]{2,1,0:T(8,128)(2,1)}, bf16[2,512,256]{2,1,0:T(8,128)(2,1)S(1)}, u32[]{:S(2)}, u32[]{:S(2)}) collective-permute-start(bf16[2,512,256]{2,1,0:T(8,128)(2,1)} %pad_maximum_fusion), channel_id=1, source_target_pairs={{0,1},{1,0},{2,3},{3,2},{4,5},{5,4},{6,7},{7,6},{8,9},{9,8},{10,11... | collective-permute-start | bytes 1572872 | tf_op jit(solution)/shard_map/ppermute | solution.py:21
  82.5 1.8 %slice_dynamic-update-slice_fusion.6 = (bf16[7,128,1024]{2,1,0:T(8,128)(2,1)}, bf16[7,128,1024]{2,1,0:T(8,128)(2,1)S(1)}) fusion(bf16[7,128,1024]{2,1,0:T(8,128)(2,1)} %get-tuple-element.18, bf16[2,128,1024]{2,1,0:T(8,128)(2,1)} %collective-permute-done.7, bf16[7,128,1024]{2,1,0:T(8,128)(2,1)S(1)} %get-tuple-element.19), kind=kLoop, calls=%fused_computation.41 | loop fusion | bytes 1048576 | tf_op jit(solution)/shard_map/stack | solution.py:98
  84.3 2.5 %copy.32 = bf16[896,1024]{0,1:T(8,128)(2,1)} copy(bf16[896,1024]{1,0:T(8,128)(2,1)S(1)} %bitcast.112) | data formatting | bytes 3670016 | tf_op jit(solution)/shard_map/reshape | solution.py:99
  86.7 0.9 fusion.26
  87.6 0.1 broadcast_in_dim.144
  87.9 0.4 copy-done.4
  88.3 1.4 fusion.53
  89.7 0.5 fusion
  90.2 1.0 copy-done.1
  91.1 1.4 fusion.4
  92.6 1.3 copy-done.2
  93.9 0.1 dynamic-slice_bitcast_fusion.1
  94.0 0.1 copy.36
  94.1 0.1 copy.37
  94.3 0.3 select_convert_fusion.1
  94.6 0.1 pad_maximum_fusion.2
  94.6 2.4 %collective-permute-start.8 = (bf16[2,512,256]{1,2,0:T(8,128)(2,1)S(1)}, bf16[2,512,256]{1,2,0:T(8,128)(2,1)S(1)}, u32[]{:S(2)}, u32[]{:S(2)}) collective-permute-start(bf16[2,512,256]{1,2,0:T(8,128)(2,1)S(1)} %pad_maximum_fusion.2), channel_id=1, source_target_pairs={{0,1},{1,0},{2,3},{3,2},{4,5},{5,4},{6,7},{7,6},{8,9},{9,8},{10,11... | collective-permute-start | bytes 1572872 | tf_op jit(solution)/shard_map/ppermute | solution.py:21
  97.0 1.3 dynamic-slice_bitcast_fusion.3
  98.3 0.2 copy.34
  98.5 0.2 copy.35
  98.7 0.1 convert_element_type.259
  98.9 0.2 fusion.2
  99.1 0.3 fusion.15
  99.4 4.6 %collective-permute-start.9 = (bf16[512,256]{0,1:T(8,128)(2,1)S(1)}, bf16[512,256]{0,1:T(8,128)(2,1)S(1)}, u32[]{:S(2)}, u32[]{:S(2)}) collective-permute-start(bf16[512,256]{0,1:T(8,128)(2,1)S(1)} %fusion.15), channel_id=1, source_target_pairs={{0,2},{1,3},{2,0},{3,1},{4,6},{5,7},{6,4},{7,5},{8,10},{9,11},{10,... | collective-permute-start | bytes 786440 | tf_op jit(solution)/shard_map/ppermute | solution.py:21
  104.1 7.1 %collective-permute-done.9 = bf16[512,256]{0,1:T(8,128)(2,1)S(1)} collective-permute-done((bf16[512,256]{0,1:T(8,128)(2,1)S(1)}, bf16[512,256]{0,1:T(8,128)(2,1)S(1)}, u32[]{:S(2)}, u32[]{:S(2)}) %collective-permute-start.9) | collective-permute-done | bytes 262176 | tf_op jit(solution)/shard_map/ppermute | solution.py:21
  111.2 0.1 convert_element_type.273
  111.3 0.1 fusion.16
  111.5 0.1 copy.38
  111.6 0.1 reshape.891
  111.7 35.8 %all_to_all.10 = bf16[128,4,250]{2,1,0:T(4,128)(2,1)S(1)} all-to-all(bf16[128,4,250]{2,1,0:T(4,128)(2,1)S(1)} %reshape.891), channel_id=1, replica_groups=mesh['cluster'=128,'feat'=4] {'cluster'}, dimensions={0} | all-to-all | bytes 512000 | tf_op jit(solution)/shard_map/all_to_all | solution.py:137
  147.5 0.2 reshape.892
  147.6 1.0 convolution_convert_fusion.1
  (45 shorter events, 0.5 us)
Async XLA Ops:
  0.0 23.8 %copy-start = (bf16[256,256]{1,0:T(8,128)(2,1)S(1)}, bf16[256,256]{1,0:T(8,128)(2,1)}, u32[]{:S(2)}) copy-start(bf16[256,256]{1,0:T(8,128)(2,1)} %param.6) | copy-start | bytes 393220
  0.0 23.2 %copy-start.5 = (s32[256,1]{0,1:T(1,128)S(1)}, s32[256,1]{0,1:T(1,128)}, u32[]{:S(2)}) copy-start(s32[256,1]{0,1:T(1,128)} %param.7) | copy-start | bytes 3076
  2.0 46.0 %copy-start.3 = (bf16[128,1024]{1,0:T(8,128)(2,1)S(1)}, bf16[128,1024]{1,0:T(8,128)(2,1)}, u32[]{:S(2)}) copy-start(bf16[128,1024]{1,0:T(8,128)(2,1)} %param.9) | copy-start | bytes 786436
  3.9 44.9 %copy-start.6 = (s32[128,7]{0,1:T(8,128)S(1)}, s32[128,7]{0,1:T(8,128)}, u32[]{:S(2)}) copy-start(s32[128,7]{0,1:T(8,128)} %param.8) | copy-start | bytes 10756
  3.9 50.3 %collective-permute-start.2 = (bf16[2,128,1024]{2,1,0:T(8,128)(2,1)}, bf16[2,128,1024]{2,1,0:T(8,128)(2,1)}, u32[]{:S(2)}, u32[]{:S(2)}) collective-permute-start(bf16[2,128,1024]{2,1,0:T(8,128)(2,1)} %pad_maximum_fusion.1), channel_id=1, source_target_pairs={{0,508},{4,0},{8,4},{12,8},{16,12},{20,16},{24,20},{28,24},{32,28}... | collective-permute-start | bytes 1572872 | tf_op jit(solution)/shard_map/ppermute | solution.py:16
  9.4 49.9 %collective-permute-start.3 = (bf16[2,128,1024]{2,1,0:T(8,128)(2,1)}, bf16[2,128,1024]{2,1,0:T(8,128)(2,1)}, u32[]{:S(2)}, u32[]{:S(2)}) collective-permute-start(bf16[2,128,1024]{2,1,0:T(8,128)(2,1)} %pad_maximum_fusion.1), channel_id=1, source_target_pairs={{0,4},{4,8},{8,12},{12,16},{16,20},{20,24},{24,28},{28,32},{32,36}... | collective-permute-start | bytes 1572872 | tf_op jit(solution)/shard_map/ppermute | solution.py:16
  11.3 49.7 %collective-permute-start.4 = (bf16[2,128,1024]{2,1,0:T(8,128)(2,1)}, bf16[2,128,1024]{2,1,0:T(8,128)(2,1)}, u32[]{:S(2)}, u32[]{:S(2)}) collective-permute-start(bf16[2,128,1024]{2,1,0:T(8,128)(2,1)} %pad_maximum_fusion.1), channel_id=1, source_target_pairs={{0,500},{4,504},{8,508},{12,0},{16,4},{20,8},{24,12},{28,16},{32,2... | collective-permute-start | bytes 1572872 | tf_op jit(solution)/shard_map/ppermute | solution.py:16
  16.3 58.3 %collective-permute-start.5 = (bf16[2,128,1024]{2,1,0:T(8,128)(2,1)}, bf16[2,128,1024]{2,1,0:T(8,128)(2,1)}, u32[]{:S(2)}, u32[]{:S(2)}) collective-permute-start(bf16[2,128,1024]{2,1,0:T(8,128)(2,1)} %pad_maximum_fusion.1), channel_id=1, source_target_pairs={{0,12},{4,16},{8,20},{12,24},{16,28},{20,32},{24,36},{28,40},{32,4... | collective-permute-start | bytes 1572872 | tf_op jit(solution)/shard_map/ppermute | solution.py:16
  18.3 58.1 %collective-permute-start.6 = (bf16[2,128,1024]{2,1,0:T(8,128)(2,1)}, bf16[2,128,1024]{2,1,0:T(8,128)(2,1)S(1)}, u32[]{:S(2)}, u32[]{:S(2)}) collective-permute-start(bf16[2,128,1024]{2,1,0:T(8,128)(2,1)} %pad_maximum_fusion.1), channel_id=1, source_target_pairs={{0,504},{4,508},{8,0},{12,4},{16,8},{20,12},{24,16},{28,20},{32,24... | collective-permute-start | bytes 1572872 | tf_op jit(solution)/shard_map/ppermute | solution.py:16
  24.8 45.1 %all-to-all-start = ((bf16[128,4,256]{2,1,0:T(4,128)(2,1)}), bf16[128,4,256]{2,1,0:T(4,128)(2,1)S(1)}, u32[]{:S(2)}, u32[]{:S(2)}) async-start(bf16[128,4,256]{2,1,0:T(4,128)(2,1)} %reshape.886), calls=%async_computation | async-start | bytes 524288 | tf_op jit(solution)/shard_map/all_to_all | solution.py:83
  54.1 28.4 %collective-permute-start.7 = (bf16[2,128,1024]{2,1,0:T(8,128)(2,1)}, bf16[2,128,1024]{2,1,0:T(8,128)(2,1)}, u32[]{:S(2)}, u32[]{:S(2)}) collective-permute-start(bf16[2,128,1024]{2,1,0:T(8,128)(2,1)} %pad_maximum_fusion.1), channel_id=1, source_target_pairs={{0,8},{4,12},{8,16},{12,20},{16,24},{20,28},{24,32},{28,36},{32,40... | collective-permute-start | bytes 1572872 | tf_op jit(solution)/shard_map/ppermute | solution.py:16
  70.0 9.8 %collective-permute-start = (bf16[512,256]{1,0:T(8,128)(2,1)S(1)}, bf16[512,256]{1,0:T(8,128)(2,1)S(1)}, u32[]{:S(2)}, u32[]{:S(2)}) collective-permute-start(bf16[512,256]{1,0:T(8,128)(2,1)S(1)} %reshape.887), channel_id=1, source_target_pairs={{0,2},{1,3},{2,0},{3,1},{4,6},{5,7},{6,4},{7,5},{8,10},{9,11},{10,... | collective-permute-start | bytes 786440 | tf_op jit(solution)/shard_map/ppermute | solution.py:21
  80.6 7.2 %collective-permute-start.1 = (bf16[2,512,256]{2,1,0:T(8,128)(2,1)}, bf16[2,512,256]{2,1,0:T(8,128)(2,1)S(1)}, u32[]{:S(2)}, u32[]{:S(2)}) collective-permute-start(bf16[2,512,256]{2,1,0:T(8,128)(2,1)} %pad_maximum_fusion), channel_id=1, source_target_pairs={{0,1},{1,0},{2,3},{3,2},{4,5},{5,4},{6,7},{7,6},{8,9},{9,8},{10,11... | collective-permute-start | bytes 1572872 | tf_op jit(solution)/shard_map/ppermute | solution.py:21
  86.7 1.5 %copy-start.4 = (bf16[7,128,1024]{2,1,0:T(8,128)(2,1)S(1)}, bf16[7,128,1024]{2,1,0:T(8,128)(2,1)}, u32[]{:S(2)}) copy-start(bf16[7,128,1024]{2,1,0:T(8,128)(2,1)} %get-tuple-element.16) | copy-start | bytes 5505028
  89.6 1.5 %copy-start.1 = (bf16[896,1024]{0,1:T(8,128)(2,1)S(1)}, bf16[896,1024]{0,1:T(8,128)(2,1)}, u32[]{:S(2)}) copy-start(bf16[896,1024]{0,1:T(8,128)(2,1)} %copy.32) | copy-start | bytes 5505028
  92.6 1.3 copy-start.2
  94.6 4.1 %collective-permute-start.8 = (bf16[2,512,256]{1,2,0:T(8,128)(2,1)S(1)}, bf16[2,512,256]{1,2,0:T(8,128)(2,1)S(1)}, u32[]{:S(2)}, u32[]{:S(2)}) collective-permute-start(bf16[2,512,256]{1,2,0:T(8,128)(2,1)S(1)} %pad_maximum_fusion.2), channel_id=1, source_target_pairs={{0,1},{1,0},{2,3},{3,2},{4,5},{5,4},{6,7},{7,6},{8,9},{9,8},{10,11... | collective-permute-start | bytes 1572872 | tf_op jit(solution)/shard_map/ppermute | solution.py:21
  99.4 11.8 %collective-permute-start.9 = (bf16[512,256]{0,1:T(8,128)(2,1)S(1)}, bf16[512,256]{0,1:T(8,128)(2,1)S(1)}, u32[]{:S(2)}, u32[]{:S(2)}) collective-permute-start(bf16[512,256]{0,1:T(8,128)(2,1)S(1)} %fusion.15), channel_id=1, source_target_pairs={{0,2},{1,3},{2,0},{3,1},{4,6},{5,7},{6,4},{7,5},{8,10},{9,11},{10,... | collective-permute-start | bytes 786440 | tf_op jit(solution)/shard_map/ppermute | solution.py:21

commit v16 on v15

--- a/solution.py
+++ b/solution.py
@@ -96,8 +96,8 @@
         query_full = lax.dynamic_update_slice_in_dim(query_full, part, (feat_index ^ code) * width, axis=1)
 
     band_keys = jnp.stack([b[0] for b in blocks]).reshape(len(offsets) * rows, depth)
-    band_labels = jnp.stack([b[1] for b in blocks]).reshape(len(offsets) * rows, feats * group)
-    band_prior = band_labels[:, quarter]
+    band_labels = jnp.concatenate([b[1].T for b in blocks], axis=1)
+    band_prior = jnp.concatenate([b[1][:, quarter] for b in blocks])
     mask_row = band_mask[cluster_index]
     live_blocks = jnp.stack([mask_row[REACH + o] > 0 for o in offsets])
     live = jnp.repeat(live_blocks, rows)
@@ -108,7 +108,7 @@
     top = jnp.max(scores, axis=1)
     weight = jnp.exp(scores - top[:, None])
     total = jnp.sum(weight, axis=1)
-    accum = jnp.dot(weight.astype(jnp.bfloat16), band_labels, preferred_element_type=jnp.float32)
+    accum = jnp.einsum("qk,ck->qc", weight.astype(jnp.bfloat16), band_labels, preferred_element_type=jnp.float32)
 
     column = lax.broadcasted_iota(jnp.int32, (slots, group), 1)
 

time: 149 us -> 157 us (1.054)
  local copies, waits for them, and re-layouts: 21.2 us -> 27.4 us
  waiting for transfers between devices: 16.8 us -> 11.7 us
  blocking collectives: 35.8 us -> 39 us
  other arithmetic: 6.49 us -> 8.68 us
    dynamic_slice x0 -> x6, local copies, waits for them, and re-layouts: none -> 5.88 us  [body(): pick = lambda g: lax.dynamic_index_in_dim(grid, g, axis=1, keepdims=False)]
    all_to_all x1, waiting for transfers between devices: 7.09 us -> 1.67 us  [body(): lax.all_to_all(outgoing.reshape(clusters, capacity, queries.shape[1]), 'c...]
    squeeze x3 -> x6, local copies, waits for them, and re-layouts: 0.33 us -> 5.44 us  [body(): band_prior = jnp.concatenate([b[1][:, quarter] for b in blocks])]
    unnamed x21 -> x38, local copies, waits for them, and re-layouts: 11.2 us -> 6.93 us
    another operation x7 -> x4, local copies, waits for them, and re-layouts: 3.45 us -> 0.16 us  [the longest x1 0.14 us: body(): band_prior = jnp.concatenate([b[1][:, quarter] for b in blocks])]
    all_to_all x1, blocking collectives: 35.8 us -> 39 us  [body(): lax.all_to_all(shares.reshape(clusters, capacity, quarter), 'cluster', sp...]
    concatenate x0 -> x3, local copies, waits for them, and re-layouts: none -> 2.02 us  [the longest x1 1.82 us: body(): band_labels = jnp.concatenate([b[1].T for b in blocks], axis=1)]
    eq x3, other arithmetic: 0.02 us -> 1.74 us  [pack(): column == quarter + i]
  transfers between devices with their start and end apart: 11 -> 11, of which waited for: 3 -> 3; matrix products, arithmetic and copies ran while one was open for 13% -> 15% of each run, Pallas kernels for 0% -> 0%
where the time goes in v16:
time: 157 us
  starting transfers between devices  59.6 us (38%)
  blocking collectives  39 us (25%)
  local copies, waits for them, and re-layouts  27.4 us (17%)
  waiting for transfers between devices  11.7 us (7%)
  other arithmetic  8.68 us (6%)
  matrix products  5.38 us (3%)
  between operations  4.89 us (3%)
    all_to_all x1, blocking collectives, body(): lax.all_to_all(shares.reshape(clusters, capacity, quarter), 'cluster', sp...  39 us
    all_to_all x1, starting transfers between devices, body(): lax.all_to_all(outgoing.reshape(clusters, capacity, queries.shape[1]), 'c...  23.2 us
    ppermute x6, starting transfers between devices, shifted(): lax.ppermute(array, axis, [(i, (i - by) % peers) for i in range(peers)])  22.6 us
    ppermute x4, starting transfers between devices, swapped(): return lax.ppermute(array, axis, [(i, i ^ bit) for i in range(peers)])  13.8 us
    ppermute x4, waiting for transfers between devices, swapped(): return lax.ppermute(array, axis, [(i, i ^ bit) for i in range(peers)])  10 us
    unnamed x38, local copies, waits for them, and re-layouts  6.93 us
    dynamic_slice x6, local copies, waits for them, and re-layouts, body(): pick = lambda g: lax.dynamic_index_in_dim(grid, g, axis=1, keepdims=False)  5.88 us
    squeeze x6, local copies, waits for them, and re-layouts, body(): band_prior = jnp.concatenate([b[1][:, quarter] for b in blocks])  5.44 us
  transfers between devices with their start and end apart: 11, of which 3 were waited for; matrix products, arithmetic and copies ran while one was open for 15% of the time, Pallas kernels for 0%

profile of v16, /device:TPU:32, one launch (start us, length us, event | category | flops | bytes accessed | tf_op | source)
XLA Modules:
  0.0 156.7 jit_solution(13914785390186842268)
XLA Ops:
  0.0 1.1 reshape.936
  1.1 0.7 and_select_fusion
  2.0 1.9 %pad_maximum_fusion.1 = bf16[2,128,1024]{2,1,0:T(8,128)(2,1)} fusion(bf16[1,128,1024]{2,1,0:T(8,128)(2,1)S(1)} %copy.19, bf16[1,128,1024]{2,1,0:T(8,128)(2,1)} %bitcast.168), kind=kLoop, calls=%fused_computation.24 | loop fusion | flops 262144 | bytes 1048576 | tf_op jit(solution)/shard_map/stack | solution.py:71
  3.9 5.5 %collective-permute-start.2 = (bf16[2,128,1024]{2,1,0:T(8,128)(2,1)}, bf16[2,128,1024]{2,1,0:T(8,128)(2,1)S(1)}, u32[]{:S(2)}, u32[]{:S(2)}) collective-permute-start(bf16[2,128,1024]{2,1,0:T(8,128)(2,1)} %pad_maximum_fusion.1), channel_id=1, source_target_pairs={{0,508},{4,0},{8,4},{12,8},{16,12},{20,16},{24,20},{28,24},{32,28}... | collective-permute-start | bytes 1572872 | tf_op jit(solution)/shard_map/ppermute | solution.py:16
  9.4 1.9 %collective-permute-start.3 = (bf16[2,128,1024]{2,1,0:T(8,128)(2,1)}, bf16[2,128,1024]{2,1,0:T(8,128)(2,1)S(1)}, u32[]{:S(2)}, u32[]{:S(2)}) collective-permute-start(bf16[2,128,1024]{2,1,0:T(8,128)(2,1)} %pad_maximum_fusion.1), channel_id=1, source_target_pairs={{0,4},{4,8},{8,12},{12,16},{16,20},{20,24},{24,28},{28,32},{32,36}... | collective-permute-start | bytes 1572872 | tf_op jit(solution)/shard_map/ppermute | solution.py:16
  11.3 5.0 %collective-permute-start.4 = (bf16[2,128,1024]{2,1,0:T(8,128)(2,1)}, bf16[2,128,1024]{2,1,0:T(8,128)(2,1)S(1)}, u32[]{:S(2)}, u32[]{:S(2)}) collective-permute-start(bf16[2,128,1024]{2,1,0:T(8,128)(2,1)} %pad_maximum_fusion.1), channel_id=1, source_target_pairs={{0,500},{4,504},{8,508},{12,0},{16,4},{20,8},{24,12},{28,16},{32,2... | collective-permute-start | bytes 1572872 | tf_op jit(solution)/shard_map/ppermute | solution.py:16
  16.3 1.9 %collective-permute-start.5 = (bf16[2,128,1024]{2,1,0:T(8,128)(2,1)}, bf16[2,128,1024]{2,1,0:T(8,128)(2,1)S(1)}, u32[]{:S(2)}, u32[]{:S(2)}) collective-permute-start(bf16[2,128,1024]{2,1,0:T(8,128)(2,1)} %pad_maximum_fusion.1), channel_id=1, source_target_pairs={{0,12},{4,16},{8,20},{12,24},{16,28},{20,32},{24,36},{28,40},{32,4... | collective-permute-start | bytes 1572872 | tf_op jit(solution)/shard_map/ppermute | solution.py:16
  18.3 4.9 %collective-permute-start.6 = (bf16[2,128,1024]{2,1,0:T(8,128)(2,1)}, bf16[2,128,1024]{2,1,0:T(8,128)(2,1)S(1)}, u32[]{:S(2)}, u32[]{:S(2)}) collective-permute-start(bf16[2,128,1024]{2,1,0:T(8,128)(2,1)} %pad_maximum_fusion.1), channel_id=1, source_target_pairs={{0,504},{4,508},{8,0},{12,4},{16,8},{20,12},{24,16},{28,20},{32,24... | collective-permute-start | bytes 1572872 | tf_op jit(solution)/shard_map/ppermute | solution.py:16
  23.3 0.2 fusion.32
  23.8 0.2 convolution_convert_fusion
  24.1 0.8 reshape.934
  24.8 23.2 %all-to-all-start = ((bf16[128,4,256]{2,1,0:T(4,128)(2,1)}), bf16[128,4,256]{2,1,0:T(4,128)(2,1)S(1)}, u32[]{:S(2)}, u32[]{:S(2)}) async-start(bf16[128,4,256]{2,1,0:T(4,128)(2,1)} %reshape.934), calls=%async_computation | async-start | bytes 524288 | tf_op jit(solution)/shard_map/all_to_all | solution.py:83
  48.0 0.7 constant_dynamic-update-slice_fusion
  48.9 0.6 iota_compare_fusion.4
  49.5 0.6 iota_compare_fusion.6
  50.2 0.6 fusion.62
  55.3 0.7 bitcast_dynamic-update-slice_fusion.6
  56.1 0.6 iota_compare_fusion.8
  56.8 3.4 %collective-permute-start.7 = (bf16[2,128,1024]{2,1,0:T(8,128)(2,1)}, bf16[2,128,1024]{2,1,0:T(8,128)(2,1)}, u32[]{:S(2)}, u32[]{:S(2)}) collective-permute-start(bf16[2,128,1024]{2,1,0:T(8,128)(2,1)} %pad_maximum_fusion.1), channel_id=1, source_target_pairs={{0,8},{4,12},{8,16},{12,20},{16,24},{20,28},{24,32},{28,36},{32,40... | collective-permute-start | bytes 1572872 | tf_op jit(solution)/shard_map/ppermute | solution.py:16
  60.2 0.7 slice_bitcast_fusion.9
  60.9 0.7 bitcast_dynamic-update-slice_fusion.5
  61.6 0.7 slice_bitcast_fusion.8
  62.4 0.7 bitcast_dynamic-update-slice_fusion.4
  63.1 0.7 slice_bitcast_fusion.7
  63.8 0.7 bitcast_dynamic-update-slice_fusion.3
  64.6 0.7 slice_bitcast_fusion.6
  65.5 0.2 slice_reduce_fusion.5
  65.7 0.7 bitcast_dynamic-update-slice_fusion.2
  66.4 0.7 slice_bitcast_fusion.5
  67.3 0.2 slice_reduce_fusion.2
  67.5 0.7 bitcast_dynamic-update-slice_fusion.1
  68.2 1.7 %all-to-all-done = bf16[128,4,256]{2,1,0:T(4,128)(2,1)S(1)} async-done(((bf16[128,4,256]{2,1,0:T(4,128)(2,1)}), bf16[128,4,256]{2,1,0:T(4,128)(2,1)S(1)}, u32[]{:S(2)}, u32[]{:S(2)}) %all-to-all-start) | async-done | bytes 262176 | tf_op jit(solution)/shard_map/all_to_all | solution.py:83
  70.0 4.6 %collective-permute-start = (bf16[512,256]{1,0:T(8,128)(2,1)S(1)}, bf16[512,256]{1,0:T(8,128)(2,1)S(1)}, u32[]{:S(2)}, u32[]{:S(2)}) collective-permute-start(bf16[512,256]{1,0:T(8,128)(2,1)S(1)} %reshape.935), channel_id=1, source_target_pairs={{0,2},{1,3},{2,0},{3,1},{4,6},{5,7},{6,4},{7,5},{8,10},{9,11},{10,... | collective-permute-start | bytes 786440 | tf_op jit(solution)/shard_map/ppermute | solution.py:21
  74.8 1.8 %slice_bitcast_fusion.4 = (bf16[128,1024]{1,0:T(8,128)(2,1)S(1)}, bf16[7,128,1024]{2,1,0:T(8,128)(2,1)}) fusion(bf16[2,128,1024]{2,1,0:T(8,128)(2,1)} %collective-permute-done.7, bf16[7,128,1024]{2,1,0:T(8,128)(2,1)} %get-tuple-element.19), kind=kLoop, calls=%fused_computation.63 | loop fusion | bytes 1048576 | tf_op jit(solution)/shard_map/squeeze | solution.py:100
  76.6 3.1 %collective-permute-done = bf16[512,256]{1,0:T(8,128)(2,1)S(1)} collective-permute-done((bf16[512,256]{1,0:T(8,128)(2,1)S(1)}, bf16[512,256]{1,0:T(8,128)(2,1)S(1)}, u32[]{:S(2)}, u32[]{:S(2)}) %collective-permute-start) | collective-permute-done | bytes 262176 | tf_op jit(solution)/shard_map/ppermute | solution.py:21
  79.8 1.9 %collective-permute-start.1 = (bf16[2,512,256]{2,1,0:T(8,128)(2,1)S(1)}, bf16[2,512,256]{2,1,0:T(8,128)(2,1)S(1)}, u32[]{:S(2)}, u32[]{:S(2)}) collective-permute-start(bf16[2,512,256]{2,1,0:T(8,128)(2,1)S(1)} %pad_maximum_fusion), channel_id=1, source_target_pairs={{0,1},{1,0},{2,3},{3,2},{4,5},{5,4},{6,7},{7,6},{8,9},{9,8},{10,11... | collective-permute-start | bytes 1572872 | tf_op jit(solution)/shard_map/ppermute | solution.py:21
  81.9 0.2 dynamic-update-slice.8
  82.1 0.2 dynamic-update-slice.9
  82.3 0.2 dynamic-update-slice.10
  82.5 0.2 dynamic-update-slice.11
  82.7 0.2 dynamic-update-slice.12
  82.9 0.2 dynamic-update-slice.13
  83.1 1.8 %bitcast_dynamic-update-slice_fusion = bf16[1024,896]{0,1:T(8,128)(2,1)} fusion(bf16[1024,896]{0,1:T(8,128)(2,1)} %bitcast_dynamic-update-slice_fusion.1, bf16[2,128,1024]{2,1,0:T(8,128)(2,1)} %collective-permute-done.7), kind=kLoop, calls=%fused_computation.53 | loop fusion | bytes 524288 | tf_op jit(solution)/shard_map/concatenate | solution.py:99
  85.2 1.4 fusion.63
  86.6 0.5 fusion
  87.1 0.6 fusion.52
  87.7 0.4 copy-done.3
  88.1 2.8 %fusion.3 = f32[512,1024]{1,0:T(8,128)} fusion(bf16[1024,896]{0,1:T(8,128)(2,1)S(1)} %copy-done.3, f32[512,896]{1,0:T(8,128)S(1)} %get-tuple-element.51, f32[512]{0:T(512)S(1)} %get-tuple-element.50), kind=kOutput, calls=%fused_computation.8 | convolution fusion | flops 940441600 | bytes 5769216 | tf_op jit(solution)/shard_map/qk,ck->qc/dot_general | solution.py:111
  90.9 2.2 %reshape.938 = f32[512,4,256]{2,1,0:T(4,128)S(1)} reshape(f32[512,1024]{1,0:T(8,128)} %fusion.3) | data formatting | bytes 4194304 | tf_op jit(solution)/shard_map/reshape | solution.py:120
  93.1 0.9 constant_dynamic-slice_fusion
  94.0 0.7 copy.23
  94.7 0.7 copy.24
  95.4 1.0 fusion.26
  96.4 0.8 pad_maximum_fusion.2
  97.2 2.6 %collective-permute-start.8 = (bf16[2,512,256]{1,2,0:T(8,128)(2,1)}, bf16[2,512,256]{1,2,0:T(8,128)(2,1)S(1)}, u32[]{:S(2)}, u32[]{:S(2)}) collective-permute-start(bf16[2,512,256]{1,2,0:T(8,128)(2,1)} %pad_maximum_fusion.2), channel_id=1, source_target_pairs={{0,1},{1,0},{2,3},{3,2},{4,5},{5,4},{6,7},{7,6},{8,9},{9,8},{10,11... | collective-permute-start | bytes 1572872 | tf_op jit(solution)/shard_map/ppermute | solution.py:21
  99.8 1.7 %constant_dynamic-slice_fusion.2 = (f32[512,1,256]{2,1,0:T(1,128)}, f32[512,1,256]{2,1,0:T(1,128)S(1)}) fusion(f32[512,4,256]{2,1,0:T(4,128)S(1)} %reshape.938, s32[]{:T(128)S(6)} %select_n.182, s32[]{:T(128)S(6)} %select_n.183), kind=kLoop, calls=%fused_computation.103 | loop fusion | bytes 2097160 | tf_op jit(solution)/shard_map/jit(dynamic_index_in_dim)/dynamic_slice | solution.py:121
  101.5 1.2 copy.21
  102.7 0.7 copy.22
  103.7 0.2 fusion.2
  104.1 0.3 fusion.14
  104.4 4.6 %collective-permute-start.9 = (bf16[512,256]{0,1:T(8,128)(2,1)S(1)}, bf16[512,256]{0,1:T(8,128)(2,1)S(1)}, u32[]{:S(2)}, u32[]{:S(2)}) collective-permute-start(bf16[512,256]{0,1:T(8,128)(2,1)S(1)} %fusion.14), channel_id=1, source_target_pairs={{0,2},{1,3},{2,0},{3,1},{4,6},{5,7},{6,4},{7,5},{8,10},{9,11},{10,... | collective-permute-start | bytes 786440 | tf_op jit(solution)/shard_map/ppermute | solution.py:21
  109.1 6.9 %collective-permute-done.9 = bf16[512,256]{0,1:T(8,128)(2,1)S(1)} collective-permute-done((bf16[512,256]{0,1:T(8,128)(2,1)S(1)}, bf16[512,256]{0,1:T(8,128)(2,1)S(1)}, u32[]{:S(2)}, u32[]{:S(2)}) %collective-permute-start.9) | collective-permute-done | bytes 262176 | tf_op jit(solution)/shard_map/ppermute | solution.py:21
  116.5 39.0 %all_to_all.10 = bf16[128,4,250]{2,1,0:T(4,128)(2,1)S(1)} all-to-all(bf16[128,4,250]{2,1,0:T(4,128)(2,1)S(1)} %reshape.939), channel_id=1, replica_groups=mesh['cluster'=128,'feat'=4] {'cluster'}, dimensions={0} | all-to-all | bytes 512000 | tf_op jit(solution)/shard_map/all_to_all | solution.py:137
  155.7 1.0 convolution_convert_fusion.1
  (77 shorter events, 3.4 us)
Async XLA Ops:
  0.0 23.8 %copy-start = (bf16[256,256]{1,0:T(8,128)(2,1)S(1)}, bf16[256,256]{1,0:T(8,128)(2,1)}, u32[]{:S(2)}) copy-start(bf16[256,256]{1,0:T(8,128)(2,1)} %param.6) | copy-start | bytes 393220
  0.0 23.2 %copy-start.4 = (s32[256,1]{0,1:T(1,128)S(1)}, s32[256,1]{0,1:T(1,128)}, u32[]{:S(2)}) copy-start(s32[256,1]{0,1:T(1,128)} %param.7) | copy-start | bytes 3076
  2.0 46.0 %copy-start.1 = (bf16[128,1024]{1,0:T(8,128)(2,1)S(1)}, bf16[128,1024]{1,0:T(8,128)(2,1)}, u32[]{:S(2)}) copy-start(bf16[128,1024]{1,0:T(8,128)(2,1)} %param.9) | copy-start | bytes 786436
  3.9 46.2 %copy-start.5 = (s32[128,7]{0,1:T(8,128)S(1)}, s32[128,7]{0,1:T(8,128)}, u32[]{:S(2)}) copy-start(s32[128,7]{0,1:T(8,128)} %param.8) | copy-start | bytes 10756
  3.9 52.9 %collective-permute-start.2 = (bf16[2,128,1024]{2,1,0:T(8,128)(2,1)}, bf16[2,128,1024]{2,1,0:T(8,128)(2,1)S(1)}, u32[]{:S(2)}, u32[]{:S(2)}) collective-permute-start(bf16[2,128,1024]{2,1,0:T(8,128)(2,1)} %pad_maximum_fusion.1), channel_id=1, source_target_pairs={{0,508},{4,0},{8,4},{12,8},{16,12},{20,16},{24,20},{28,24},{32,28}... | collective-permute-start | bytes 1572872 | tf_op jit(solution)/shard_map/ppermute | solution.py:16
  9.4 52.2 %collective-permute-start.3 = (bf16[2,128,1024]{2,1,0:T(8,128)(2,1)}, bf16[2,128,1024]{2,1,0:T(8,128)(2,1)S(1)}, u32[]{:S(2)}, u32[]{:S(2)}) collective-permute-start(bf16[2,128,1024]{2,1,0:T(8,128)(2,1)} %pad_maximum_fusion.1), channel_id=1, source_target_pairs={{0,4},{4,8},{8,12},{12,16},{16,20},{20,24},{24,28},{28,32},{32,36}... | collective-permute-start | bytes 1572872 | tf_op jit(solution)/shard_map/ppermute | solution.py:16
  11.3 51.8 %collective-permute-start.4 = (bf16[2,128,1024]{2,1,0:T(8,128)(2,1)}, bf16[2,128,1024]{2,1,0:T(8,128)(2,1)S(1)}, u32[]{:S(2)}, u32[]{:S(2)}) collective-permute-start(bf16[2,128,1024]{2,1,0:T(8,128)(2,1)} %pad_maximum_fusion.1), channel_id=1, source_target_pairs={{0,500},{4,504},{8,508},{12,0},{16,4},{20,8},{24,12},{28,16},{32,2... | collective-permute-start | bytes 1572872 | tf_op jit(solution)/shard_map/ppermute | solution.py:16
  16.3 48.2 %collective-permute-start.5 = (bf16[2,128,1024]{2,1,0:T(8,128)(2,1)}, bf16[2,128,1024]{2,1,0:T(8,128)(2,1)S(1)}, u32[]{:S(2)}, u32[]{:S(2)}) collective-permute-start(bf16[2,128,1024]{2,1,0:T(8,128)(2,1)} %pad_maximum_fusion.1), channel_id=1, source_target_pairs={{0,12},{4,16},{8,20},{12,24},{16,28},{20,32},{24,36},{28,40},{32,4... | collective-permute-start | bytes 1572872 | tf_op jit(solution)/shard_map/ppermute | solution.py:16
  18.3 48.1 %collective-permute-start.6 = (bf16[2,128,1024]{2,1,0:T(8,128)(2,1)}, bf16[2,128,1024]{2,1,0:T(8,128)(2,1)S(1)}, u32[]{:S(2)}, u32[]{:S(2)}) collective-permute-start(bf16[2,128,1024]{2,1,0:T(8,128)(2,1)} %pad_maximum_fusion.1), channel_id=1, source_target_pairs={{0,504},{4,508},{8,0},{12,4},{16,8},{20,12},{24,16},{28,20},{32,24... | collective-permute-start | bytes 1572872 | tf_op jit(solution)/shard_map/ppermute | solution.py:16
  24.8 45.1 %all-to-all-start = ((bf16[128,4,256]{2,1,0:T(4,128)(2,1)}), bf16[128,4,256]{2,1,0:T(4,128)(2,1)S(1)}, u32[]{:S(2)}, u32[]{:S(2)}) async-start(bf16[128,4,256]{2,1,0:T(4,128)(2,1)} %reshape.934), calls=%async_computation | async-start | bytes 524288 | tf_op jit(solution)/shard_map/all_to_all | solution.py:83
  56.8 18.0 %collective-permute-start.7 = (bf16[2,128,1024]{2,1,0:T(8,128)(2,1)}, bf16[2,128,1024]{2,1,0:T(8,128)(2,1)}, u32[]{:S(2)}, u32[]{:S(2)}) collective-permute-start(bf16[2,128,1024]{2,1,0:T(8,128)(2,1)} %pad_maximum_fusion.1), channel_id=1, source_target_pairs={{0,8},{4,12},{8,16},{12,20},{16,24},{20,28},{24,32},{28,36},{32,40... | collective-permute-start | bytes 1572872 | tf_op jit(solution)/shard_map/ppermute | solution.py:16
  70.0 9.8 %collective-permute-start = (bf16[512,256]{1,0:T(8,128)(2,1)S(1)}, bf16[512,256]{1,0:T(8,128)(2,1)S(1)}, u32[]{:S(2)}, u32[]{:S(2)}) collective-permute-start(bf16[512,256]{1,0:T(8,128)(2,1)S(1)} %reshape.935), channel_id=1, source_target_pairs={{0,2},{1,3},{2,0},{3,1},{4,6},{5,7},{6,4},{7,5},{8,10},{9,11},{10,... | collective-permute-start | bytes 786440 | tf_op jit(solution)/shard_map/ppermute | solution.py:21
  79.8 5.3 %collective-permute-start.1 = (bf16[2,512,256]{2,1,0:T(8,128)(2,1)S(1)}, bf16[2,512,256]{2,1,0:T(8,128)(2,1)S(1)}, u32[]{:S(2)}, u32[]{:S(2)}) collective-permute-start(bf16[2,512,256]{2,1,0:T(8,128)(2,1)S(1)} %pad_maximum_fusion), channel_id=1, source_target_pairs={{0,1},{1,0},{2,3},{3,2},{4,5},{5,4},{6,7},{7,6},{8,9},{9,8},{10,11... | collective-permute-start | bytes 1572872 | tf_op jit(solution)/shard_map/ppermute | solution.py:21
  83.1 2.1 %copy-start.2 = (bf16[7,128,1024]{2,1,0:T(8,128)(2,1)S(1)}, bf16[7,128,1024]{2,1,0:T(8,128)(2,1)}, u32[]{:S(2)}) copy-start(bf16[7,128,1024]{2,1,0:T(8,128)(2,1)} %get-tuple-element.17) | copy-start | bytes 5505028
  86.6 1.5 copy-start.3
  97.2 6.3 %collective-permute-start.8 = (bf16[2,512,256]{1,2,0:T(8,128)(2,1)}, bf16[2,512,256]{1,2,0:T(8,128)(2,1)S(1)}, u32[]{:S(2)}, u32[]{:S(2)}) collective-permute-start(bf16[2,512,256]{1,2,0:T(8,128)(2,1)} %pad_maximum_fusion.2), channel_id=1, source_target_pairs={{0,1},{1,0},{2,3},{3,2},{4,5},{5,4},{6,7},{7,6},{8,9},{9,8},{10,11... | collective-permute-start | bytes 1572872 | tf_op jit(solution)/shard_map/ppermute | solution.py:21
  103.4 0.6 copy-start.6
  103.4 0.7 copy-start.7
  103.4 0.7 copy-start.8
  103.5 0.7 copy-start.9
  103.5 0.6 copy-start.10
  103.5 0.7 copy-start.11
  104.4 11.6 %collective-permute-start.9 = (bf16[512,256]{0,1:T(8,128)(2,1)S(1)}, bf16[512,256]{0,1:T(8,128)(2,1)S(1)}, u32[]{:S(2)}, u32[]{:S(2)}) collective-permute-start(bf16[512,256]{0,1:T(8,128)(2,1)S(1)} %fusion.14), channel_id=1, source_target_pairs={{0,2},{1,3},{2,0},{3,1},{4,6},{5,7},{6,4},{7,5},{8,10},{9,11},{10,... | collective-permute-start | bytes 786440 | tf_op jit(solution)/shard_map/ppermute | solution.py:21

commit v17 on v15

--- a/solution.py
+++ b/solution.py
@@ -70,7 +70,7 @@
     grouped = jnp.concatenate([labels.reshape(rows, feats, quarter), spare], axis=2)
     block = jnp.stack([keys, grouped.reshape(rows, feats * group)])
     offsets = [0]
-    for reach in sorted(range(1, REACH + 1), key=lambda r: r == 2):
+    for reach in sorted(range(1, REACH + 1), key=lambda r: (r == 2, -r)):
         offsets += [reach, -reach]
     blocks = [block] + [shifted(block, "cluster", o) for o in offsets[1:]]
 

time: 149 us -> 149 us (level)
  blocking collectives: 35.8 us -> 33.6 us
  waiting for transfers between devices: 16.8 us -> 18.4 us
    all_to_all x1, blocking collectives: 35.8 us -> 33.6 us  [body(): lax.all_to_all(shares.reshape(clusters, capacity, quarter), 'cluster', sp...]
    all_to_all x1, waiting for transfers between devices: 7.09 us -> 8.68 us  [body(): lax.all_to_all(outgoing.reshape(clusters, capacity, queries.shape[1]), 'c...]
where the time goes in v17:
time: 149 us; the launch traced here: 148 us
  starting transfers between devices  59.4 us (40%)
  blocking collectives  33.6 us (23%)
  local copies, waits for them, and re-layouts  21.2 us (14%)
  waiting for transfers between devices  18.4 us (12%)
  other arithmetic  6.49 us (4%)
  between operations  4.93 us (3%)
  matrix products  4.06 us (3%)
    all_to_all x1, blocking collectives, body(): lax.all_to_all(shares.reshape(clusters, capacity, quarter), 'cluster', sp...  33.6 us
    all_to_all x1, starting transfers between devices, body(): lax.all_to_all(outgoing.reshape(clusters, capacity, queries.shape[1]), 'c...  23.2 us
    ppermute x6, starting transfers between devices, shifted(): lax.ppermute(array, axis, [(i, (i - by) % peers) for i in range(peers)])  22.7 us
    ppermute x4, starting transfers between devices, swapped(): return lax.ppermute(array, axis, [(i, i ^ bit) for i in range(peers)])  13.6 us
    unnamed x21, local copies, waits for them, and re-layouts  11.2 us
    ppermute x4, waiting for transfers between devices, swapped(): return lax.ppermute(array, axis, [(i, i ^ bit) for i in range(peers)])  9.66 us
    all_to_all x1, waiting for transfers between devices, body(): lax.all_to_all(outgoing.reshape(clusters, capacity, queries.shape[1]), 'c...  8.68 us
  transfers between devices with their start and end apart: 11, of which 3 were waited for; matrix products, arithmetic and copies ran while one was open for 13% of the time, Pallas kernels for 0%

profile of v17, /device:TPU:32, one launch (start us, length us, event | category | flops | bytes accessed | tf_op | source)
XLA Modules:
  0.0 148.0 jit_solution(16574454562174491861)
XLA Ops:
  0.0 1.1 reshape.888
  1.1 0.7 and_select_fusion
  1.8 0.1 copy.30
  2.0 1.9 %pad_maximum_fusion.1 = bf16[2,128,1024]{2,1,0:T(8,128)(2,1)} fusion(bf16[1,128,1024]{2,1,0:T(8,128)(2,1)S(1)} %copy.30, bf16[1,128,1024]{2,1,0:T(8,128)(2,1)} %bitcast.116), kind=kLoop, calls=%fused_computation.25 | loop fusion | flops 262144 | bytes 1048576 | tf_op jit(solution)/shard_map/stack | solution.py:71
  3.9 5.7 %collective-permute-start.2 = (bf16[2,128,1024]{2,1,0:T(8,128)(2,1)}, bf16[2,128,1024]{2,1,0:T(8,128)(2,1)}, u32[]{:S(2)}, u32[]{:S(2)}) collective-permute-start(bf16[2,128,1024]{2,1,0:T(8,128)(2,1)} %pad_maximum_fusion.1), channel_id=1, source_target_pairs={{0,500},{4,504},{8,508},{12,0},{16,4},{20,8},{24,12},{28,16},{32,2... | collective-permute-start | bytes 1572872 | tf_op jit(solution)/shard_map/ppermute | solution.py:16
  9.6 1.9 %collective-permute-start.3 = (bf16[2,128,1024]{2,1,0:T(8,128)(2,1)}, bf16[2,128,1024]{2,1,0:T(8,128)(2,1)}, u32[]{:S(2)}, u32[]{:S(2)}) collective-permute-start(bf16[2,128,1024]{2,1,0:T(8,128)(2,1)} %pad_maximum_fusion.1), channel_id=1, source_target_pairs={{0,12},{4,16},{8,20},{12,24},{16,28},{20,32},{24,36},{28,40},{32,4... | collective-permute-start | bytes 1572872 | tf_op jit(solution)/shard_map/ppermute | solution.py:16
  11.5 7.0 %collective-permute-start.4 = (bf16[2,128,1024]{2,1,0:T(8,128)(2,1)}, bf16[2,128,1024]{2,1,0:T(8,128)(2,1)}, u32[]{:S(2)}, u32[]{:S(2)}) collective-permute-start(bf16[2,128,1024]{2,1,0:T(8,128)(2,1)} %pad_maximum_fusion.1), channel_id=1, source_target_pairs={{0,508},{4,0},{8,4},{12,8},{16,12},{20,16},{24,20},{28,24},{32,28}... | collective-permute-start | bytes 1572872 | tf_op jit(solution)/shard_map/ppermute | solution.py:16
  18.6 1.9 %collective-permute-start.5 = (bf16[2,128,1024]{2,1,0:T(8,128)(2,1)}, bf16[2,128,1024]{2,1,0:T(8,128)(2,1)}, u32[]{:S(2)}, u32[]{:S(2)}) collective-permute-start(bf16[2,128,1024]{2,1,0:T(8,128)(2,1)} %pad_maximum_fusion.1), channel_id=1, source_target_pairs={{0,4},{4,8},{8,12},{12,16},{16,20},{20,24},{24,28},{28,32},{32,36}... | collective-permute-start | bytes 1572872 | tf_op jit(solution)/shard_map/ppermute | solution.py:16
  20.5 2.7 %collective-permute-start.6 = (bf16[2,128,1024]{2,1,0:T(8,128)(2,1)}, bf16[2,128,1024]{2,1,0:T(8,128)(2,1)S(1)}, u32[]{:S(2)}, u32[]{:S(2)}) collective-permute-start(bf16[2,128,1024]{2,1,0:T(8,128)(2,1)} %pad_maximum_fusion.1), channel_id=1, source_target_pairs={{0,504},{4,508},{8,0},{12,4},{16,8},{20,12},{24,16},{28,20},{32,24... | collective-permute-start | bytes 1572872 | tf_op jit(solution)/shard_map/ppermute | solution.py:16
  23.2 0.1 copy.28
  23.3 0.2 fusion.21
  23.6 0.2 fusion.23
  23.8 0.2 convolution_convert_fusion
  24.1 0.8 reshape.886
  24.8 23.2 %all-to-all-start = ((bf16[128,4,256]{2,1,0:T(4,128)(2,1)}), bf16[128,4,256]{2,1,0:T(4,128)(2,1)S(1)}, u32[]{:S(2)}, u32[]{:S(2)}) async-start(bf16[128,4,256]{2,1,0:T(4,128)(2,1)} %reshape.886), calls=%async_computation | async-start | bytes 524288 | tf_op jit(solution)/shard_map/all_to_all | solution.py:83
  48.1 0.7 constant_dynamic-update-slice_fusion
  48.8 0.1 constant_dynamic-slice_fusion
  48.9 0.6 fusion.52
  53.9 0.1 stack.63
  54.0 0.1 broadcast_bitcast_fusion
  54.1 3.4 %collective-permute-start.7 = (bf16[2,128,1024]{2,1,0:T(8,128)(2,1)}, bf16[2,128,1024]{2,1,0:T(8,128)(2,1)}, u32[]{:S(2)}, u32[]{:S(2)}) collective-permute-start(bf16[2,128,1024]{2,1,0:T(8,128)(2,1)} %pad_maximum_fusion.1), channel_id=1, source_target_pairs={{0,8},{4,12},{8,16},{12,20},{16,24},{20,28},{24,32},{28,36},{32,40... | collective-permute-start | bytes 1572872 | tf_op jit(solution)/shard_map/ppermute | solution.py:16
  57.5 1.8 %slice_dynamic-update-slice_fusion.11 = (bf16[7,128,1024]{2,1,0:T(8,128)(2,1)}, bf16[7,128,1024]{2,1,0:T(8,128)(2,1)S(1)}) fusion(bf16[7,128,1024]{2,1,0:T(8,128)(2,1)} %get-tuple-element.52, bf16[2,128,1024]{2,1,0:T(8,128)(2,1)} %collective-permute-done.2, bf16[7,128,1024]{2,1,0:T(8,128)(2,1)S(1)} %get-tuple-element.53), kind=kLoop, calls=%fused_computation.46 | loop fusion | bytes 1048576
  59.3 1.8 %slice_dynamic-update-slice_fusion.10 = (bf16[7,128,1024]{2,1,0:T(8,128)(2,1)}, bf16[7,128,1024]{2,1,0:T(8,128)(2,1)S(1)}) fusion(bf16[7,128,1024]{2,1,0:T(8,128)(2,1)} %get-tuple-element.26, bf16[2,128,1024]{2,1,0:T(8,128)(2,1)} %collective-permute-done.3, bf16[7,128,1024]{2,1,0:T(8,128)(2,1)S(1)} %get-tuple-element.27), kind=kLoop, calls=%fused_computation.45 | loop fusion | bytes 1048576
  61.1 1.8 %slice_dynamic-update-slice_fusion.9 = (bf16[7,128,1024]{2,1,0:T(8,128)(2,1)}, bf16[7,128,1024]{2,1,0:T(8,128)(2,1)S(1)}) fusion(bf16[7,128,1024]{2,1,0:T(8,128)(2,1)} %get-tuple-element.24, bf16[2,128,1024]{2,1,0:T(8,128)(2,1)} %collective-permute-done.4, bf16[7,128,1024]{2,1,0:T(8,128)(2,1)S(1)} %get-tuple-element.25), kind=kLoop, calls=%fused_computation.44 | loop fusion | bytes 1048576
  62.8 8.7 %all-to-all-done = bf16[128,4,256]{2,1,0:T(4,128)(2,1)S(1)} async-done(((bf16[128,4,256]{2,1,0:T(4,128)(2,1)}), bf16[128,4,256]{2,1,0:T(4,128)(2,1)S(1)}, u32[]{:S(2)}, u32[]{:S(2)}) %all-to-all-start) | async-done | bytes 262176 | tf_op jit(solution)/shard_map/all_to_all | solution.py:83
  71.5 0.1 reshape.887
  71.6 4.6 %collective-permute-start = (bf16[512,256]{1,0:T(8,128)(2,1)S(1)}, bf16[512,256]{1,0:T(8,128)(2,1)S(1)}, u32[]{:S(2)}, u32[]{:S(2)}) collective-permute-start(bf16[512,256]{1,0:T(8,128)(2,1)S(1)} %reshape.887), channel_id=1, source_target_pairs={{0,2},{1,3},{2,0},{3,1},{4,6},{5,7},{6,4},{7,5},{8,10},{9,11},{10,... | collective-permute-start | bytes 786440 | tf_op jit(solution)/shard_map/ppermute | solution.py:21
  76.2 1.8 %slice_dynamic-update-slice_fusion.8 = (bf16[7,128,1024]{2,1,0:T(8,128)(2,1)}, bf16[7,128,1024]{2,1,0:T(8,128)(2,1)S(1)}) fusion(bf16[7,128,1024]{2,1,0:T(8,128)(2,1)} %get-tuple-element.22, bf16[2,128,1024]{2,1,0:T(8,128)(2,1)} %collective-permute-done.5, bf16[7,128,1024]{2,1,0:T(8,128)(2,1)S(1)} %get-tuple-element.23), kind=kLoop, calls=%fused_computation.43 | loop fusion | bytes 1048576
  78.0 0.7 slice_dynamic-update-slice_fusion.7
  78.7 0.1 stack_reshape.6
  78.8 2.6 %collective-permute-done = bf16[512,256]{1,0:T(8,128)(2,1)S(1)} collective-permute-done((bf16[512,256]{1,0:T(8,128)(2,1)S(1)}, bf16[512,256]{1,0:T(8,128)(2,1)S(1)}, u32[]{:S(2)}, u32[]{:S(2)}) %collective-permute-start) | collective-permute-done | bytes 262176 | tf_op jit(solution)/shard_map/ppermute | solution.py:21
  81.3 0.8 pad_maximum_fusion
  82.2 1.9 %collective-permute-start.1 = (bf16[2,512,256]{2,1,0:T(8,128)(2,1)}, bf16[2,512,256]{2,1,0:T(8,128)(2,1)S(1)}, u32[]{:S(2)}, u32[]{:S(2)}) collective-permute-start(bf16[2,512,256]{2,1,0:T(8,128)(2,1)} %pad_maximum_fusion), channel_id=1, source_target_pairs={{0,1},{1,0},{2,3},{3,2},{4,5},{5,4},{6,7},{7,6},{8,9},{9,8},{10,11... | collective-permute-start | bytes 1572872 | tf_op jit(solution)/shard_map/ppermute | solution.py:21
  84.1 1.8 %slice_dynamic-update-slice_fusion.6 = (bf16[7,128,1024]{2,1,0:T(8,128)(2,1)}, bf16[7,128,1024]{2,1,0:T(8,128)(2,1)S(1)}) fusion(bf16[7,128,1024]{2,1,0:T(8,128)(2,1)} %get-tuple-element.18, bf16[2,128,1024]{2,1,0:T(8,128)(2,1)} %collective-permute-done.7, bf16[7,128,1024]{2,1,0:T(8,128)(2,1)S(1)} %get-tuple-element.19), kind=kLoop, calls=%fused_computation.41 | loop fusion | bytes 1048576 | tf_op jit(solution)/shard_map/stack | solution.py:98
  85.9 2.5 %copy.32 = bf16[896,1024]{0,1:T(8,128)(2,1)} copy(bf16[896,1024]{1,0:T(8,128)(2,1)S(1)} %bitcast.112) | data formatting | bytes 3670016 | tf_op jit(solution)/shard_map/reshape | solution.py:99
  88.3 0.9 fusion.26
  89.2 0.1 broadcast_in_dim.144
  89.5 0.4 copy-done.4
  89.8 1.4 fusion.53
  91.2 0.5 fusion
  91.7 1.0 copy-done.1
  92.7 1.4 fusion.4
  94.2 1.3 copy-done.2
  95.5 0.1 dynamic-slice_bitcast_fusion.1
  95.6 0.1 copy.36
  95.7 0.1 copy.37
  95.8 0.3 select_convert_fusion.1
  96.1 0.1 pad_maximum_fusion.2
  96.2 2.4 %collective-permute-start.8 = (bf16[2,512,256]{1,2,0:T(8,128)(2,1)S(1)}, bf16[2,512,256]{1,2,0:T(8,128)(2,1)S(1)}, u32[]{:S(2)}, u32[]{:S(2)}) collective-permute-start(bf16[2,512,256]{1,2,0:T(8,128)(2,1)S(1)} %pad_maximum_fusion.2), channel_id=1, source_target_pairs={{0,1},{1,0},{2,3},{3,2},{4,5},{5,4},{6,7},{7,6},{8,9},{9,8},{10,11... | collective-permute-start | bytes 1572872 | tf_op jit(solution)/shard_map/ppermute | solution.py:21
  98.6 1.3 dynamic-slice_bitcast_fusion.3
  99.9 0.2 copy.34
  100.1 0.2 copy.35
  100.3 0.1 convert_element_type.259
  100.5 0.2 fusion.2
  100.7 0.3 fusion.15
  101.0 4.6 %collective-permute-start.9 = (bf16[512,256]{0,1:T(8,128)(2,1)S(1)}, bf16[512,256]{0,1:T(8,128)(2,1)S(1)}, u32[]{:S(2)}, u32[]{:S(2)}) collective-permute-start(bf16[512,256]{0,1:T(8,128)(2,1)S(1)} %fusion.15), channel_id=1, source_target_pairs={{0,2},{1,3},{2,0},{3,1},{4,6},{5,7},{6,4},{7,5},{8,10},{9,11},{10,... | collective-permute-start | bytes 786440 | tf_op jit(solution)/shard_map/ppermute | solution.py:21
  105.7 7.1 %collective-permute-done.9 = bf16[512,256]{0,1:T(8,128)(2,1)S(1)} collective-permute-done((bf16[512,256]{0,1:T(8,128)(2,1)S(1)}, bf16[512,256]{0,1:T(8,128)(2,1)S(1)}, u32[]{:S(2)}, u32[]{:S(2)}) %collective-permute-start.9) | collective-permute-done | bytes 262176 | tf_op jit(solution)/shard_map/ppermute | solution.py:21
  112.8 0.1 convert_element_type.273
  112.9 0.1 fusion.16
  113.0 0.1 copy.38
  113.2 0.1 reshape.891
  113.3 33.6 %all_to_all.10 = bf16[128,4,250]{2,1,0:T(4,128)(2,1)S(1)} all-to-all(bf16[128,4,250]{2,1,0:T(4,128)(2,1)S(1)} %reshape.891), channel_id=1, replica_groups=mesh['cluster'=128,'feat'=4] {'cluster'}, dimensions={0} | all-to-all | bytes 512000 | tf_op jit(solution)/shard_map/all_to_all | solution.py:137
  146.9 0.2 reshape.892
  147.0 1.0 convolution_convert_fusion.1
  (45 shorter events, 0.5 us)
Async XLA Ops:
  0.0 23.8 %copy-start = (bf16[256,256]{1,0:T(8,128)(2,1)S(1)}, bf16[256,256]{1,0:T(8,128)(2,1)}, u32[]{:S(2)}) copy-start(bf16[256,256]{1,0:T(8,128)(2,1)} %param.6) | copy-start | bytes 393220
  0.0 23.2 %copy-start.5 = (s32[256,1]{0,1:T(1,128)S(1)}, s32[256,1]{0,1:T(1,128)}, u32[]{:S(2)}) copy-start(s32[256,1]{0,1:T(1,128)} %param.7) | copy-start | bytes 3076
  2.0 46.0 %copy-start.3 = (bf16[128,1024]{1,0:T(8,128)(2,1)S(1)}, bf16[128,1024]{1,0:T(8,128)(2,1)}, u32[]{:S(2)}) copy-start(bf16[128,1024]{1,0:T(8,128)(2,1)} %param.9) | copy-start | bytes 786436
  3.9 44.9 %copy-start.6 = (s32[128,7]{0,1:T(8,128)S(1)}, s32[128,7]{0,1:T(8,128)}, u32[]{:S(2)}) copy-start(s32[128,7]{0,1:T(8,128)} %param.8) | copy-start | bytes 10756
  3.9 50.3 %collective-permute-start.2 = (bf16[2,128,1024]{2,1,0:T(8,128)(2,1)}, bf16[2,128,1024]{2,1,0:T(8,128)(2,1)}, u32[]{:S(2)}, u32[]{:S(2)}) collective-permute-start(bf16[2,128,1024]{2,1,0:T(8,128)(2,1)} %pad_maximum_fusion.1), channel_id=1, source_target_pairs={{0,500},{4,504},{8,508},{12,0},{16,4},{20,8},{24,12},{28,16},{32,2... | collective-permute-start | bytes 1572872 | tf_op jit(solution)/shard_map/ppermute | solution.py:16
  9.6 49.7 %collective-permute-start.3 = (bf16[2,128,1024]{2,1,0:T(8,128)(2,1)}, bf16[2,128,1024]{2,1,0:T(8,128)(2,1)}, u32[]{:S(2)}, u32[]{:S(2)}) collective-permute-start(bf16[2,128,1024]{2,1,0:T(8,128)(2,1)} %pad_maximum_fusion.1), channel_id=1, source_target_pairs={{0,12},{4,16},{8,20},{12,24},{16,28},{20,32},{24,36},{28,40},{32,4... | collective-permute-start | bytes 1572872 | tf_op jit(solution)/shard_map/ppermute | solution.py:16
  11.5 49.6 %collective-permute-start.4 = (bf16[2,128,1024]{2,1,0:T(8,128)(2,1)}, bf16[2,128,1024]{2,1,0:T(8,128)(2,1)}, u32[]{:S(2)}, u32[]{:S(2)}) collective-permute-start(bf16[2,128,1024]{2,1,0:T(8,128)(2,1)} %pad_maximum_fusion.1), channel_id=1, source_target_pairs={{0,508},{4,0},{8,4},{12,8},{16,12},{20,16},{24,20},{28,24},{32,28}... | collective-permute-start | bytes 1572872 | tf_op jit(solution)/shard_map/ppermute | solution.py:16
  18.6 57.7 %collective-permute-start.5 = (bf16[2,128,1024]{2,1,0:T(8,128)(2,1)}, bf16[2,128,1024]{2,1,0:T(8,128)(2,1)}, u32[]{:S(2)}, u32[]{:S(2)}) collective-permute-start(bf16[2,128,1024]{2,1,0:T(8,128)(2,1)} %pad_maximum_fusion.1), channel_id=1, source_target_pairs={{0,4},{4,8},{8,12},{12,16},{16,20},{20,24},{24,28},{28,32},{32,36}... | collective-permute-start | bytes 1572872 | tf_op jit(solution)/shard_map/ppermute | solution.py:16
  20.5 57.5 %collective-permute-start.6 = (bf16[2,128,1024]{2,1,0:T(8,128)(2,1)}, bf16[2,128,1024]{2,1,0:T(8,128)(2,1)S(1)}, u32[]{:S(2)}, u32[]{:S(2)}) collective-permute-start(bf16[2,128,1024]{2,1,0:T(8,128)(2,1)} %pad_maximum_fusion.1), channel_id=1, source_target_pairs={{0,504},{4,508},{8,0},{12,4},{16,8},{20,12},{24,16},{28,20},{32,24... | collective-permute-start | bytes 1572872 | tf_op jit(solution)/shard_map/ppermute | solution.py:16
  24.8 46.7 %all-to-all-start = ((bf16[128,4,256]{2,1,0:T(4,128)(2,1)}), bf16[128,4,256]{2,1,0:T(4,128)(2,1)S(1)}, u32[]{:S(2)}, u32[]{:S(2)}) async-start(bf16[128,4,256]{2,1,0:T(4,128)(2,1)} %reshape.886), calls=%async_computation | async-start | bytes 524288 | tf_op jit(solution)/shard_map/all_to_all | solution.py:83
  54.1 29.9 %collective-permute-start.7 = (bf16[2,128,1024]{2,1,0:T(8,128)(2,1)}, bf16[2,128,1024]{2,1,0:T(8,128)(2,1)}, u32[]{:S(2)}, u32[]{:S(2)}) collective-permute-start(bf16[2,128,1024]{2,1,0:T(8,128)(2,1)} %pad_maximum_fusion.1), channel_id=1, source_target_pairs={{0,8},{4,12},{8,16},{12,20},{16,24},{20,28},{24,32},{28,36},{32,40... | collective-permute-start | bytes 1572872 | tf_op jit(solution)/shard_map/ppermute | solution.py:16
  71.6 9.8 %collective-permute-start = (bf16[512,256]{1,0:T(8,128)(2,1)S(1)}, bf16[512,256]{1,0:T(8,128)(2,1)S(1)}, u32[]{:S(2)}, u32[]{:S(2)}) collective-permute-start(bf16[512,256]{1,0:T(8,128)(2,1)S(1)} %reshape.887), channel_id=1, source_target_pairs={{0,2},{1,3},{2,0},{3,1},{4,6},{5,7},{6,4},{7,5},{8,10},{9,11},{10,... | collective-permute-start | bytes 786440 | tf_op jit(solution)/shard_map/ppermute | solution.py:21
  82.2 7.2 %collective-permute-start.1 = (bf16[2,512,256]{2,1,0:T(8,128)(2,1)}, bf16[2,512,256]{2,1,0:T(8,128)(2,1)S(1)}, u32[]{:S(2)}, u32[]{:S(2)}) collective-permute-start(bf16[2,512,256]{2,1,0:T(8,128)(2,1)} %pad_maximum_fusion), channel_id=1, source_target_pairs={{0,1},{1,0},{2,3},{3,2},{4,5},{5,4},{6,7},{7,6},{8,9},{9,8},{10,11... | collective-permute-start | bytes 1572872 | tf_op jit(solution)/shard_map/ppermute | solution.py:21
  88.3 1.5 %copy-start.4 = (bf16[7,128,1024]{2,1,0:T(8,128)(2,1)S(1)}, bf16[7,128,1024]{2,1,0:T(8,128)(2,1)}, u32[]{:S(2)}) copy-start(bf16[7,128,1024]{2,1,0:T(8,128)(2,1)} %get-tuple-element.16) | copy-start | bytes 5505028
  91.2 1.5 %copy-start.1 = (bf16[896,1024]{0,1:T(8,128)(2,1)S(1)}, bf16[896,1024]{0,1:T(8,128)(2,1)}, u32[]{:S(2)}) copy-start(bf16[896,1024]{0,1:T(8,128)(2,1)} %copy.32) | copy-start | bytes 5505028
  94.2 1.3 copy-start.2
  96.2 4.1 %collective-permute-start.8 = (bf16[2,512,256]{1,2,0:T(8,128)(2,1)S(1)}, bf16[2,512,256]{1,2,0:T(8,128)(2,1)S(1)}, u32[]{:S(2)}, u32[]{:S(2)}) collective-permute-start(bf16[2,512,256]{1,2,0:T(8,128)(2,1)S(1)} %pad_maximum_fusion.2), channel_id=1, source_target_pairs={{0,1},{1,0},{2,3},{3,2},{4,5},{5,4},{6,7},{7,6},{8,9},{9,8},{10,11... | collective-permute-start | bytes 1572872 | tf_op jit(solution)/shard_map/ppermute | solution.py:21
  101.0 11.8 %collective-permute-start.9 = (bf16[512,256]{0,1:T(8,128)(2,1)S(1)}, bf16[512,256]{0,1:T(8,128)(2,1)S(1)}, u32[]{:S(2)}, u32[]{:S(2)}) collective-permute-start(bf16[512,256]{0,1:T(8,128)(2,1)S(1)} %fusion.15), channel_id=1, source_target_pairs={{0,2},{1,3},{2,0},{3,1},{4,6},{5,7},{6,4},{7,5},{8,10},{9,11},{10,... | collective-permute-start | bytes 786440 | tf_op jit(solution)/shard_map/ppermute | solution.py:21

commit v18 on v17

--- a/solution.py
+++ b/solution.py
@@ -63,12 +63,10 @@
 
     quarter = classes // feats
     group = -(-(quarter + 6) // 128) * 128
-    first = (lax.broadcasted_iota(jnp.int32, (rows, feats, group - quarter), 1) == 0) & (
-        lax.broadcasted_iota(jnp.int32, (rows, feats, group - quarter), 2) == 0
-    )
-    spare = jnp.where(first, prior[:, None, None], jnp.zeros((), prior.dtype))
-    grouped = jnp.concatenate([labels.reshape(rows, feats, quarter), spare], axis=2)
-    block = jnp.stack([keys, grouped.reshape(rows, feats * group)])
+    lane = lax.broadcasted_iota(jnp.int32, (rows, feats * group), 1)
+    padded = jnp.pad(labels.reshape(rows, feats, quarter), ((0, 0), (0, 0), (0, group - quarter)))
+    grouped = jnp.where(lane == quarter, prior[:, None], padded.reshape(rows, feats * group))
+    block = jnp.stack([keys, grouped])
     offsets = [0]
     for reach in sorted(range(1, REACH + 1), key=lambda r: (r == 2, -r)):
         offsets += [reach, -reach]

time: 149 us -> 148 us (level)
  no operation moved by 1% of the time
where the time goes in v18:
time: 148 us; the launch traced here: 147 us
  starting transfers between devices  59.3 us (40%)
  blocking collectives  33.6 us (23%)
  local copies, waits for them, and re-layouts  21.2 us (14%)
  waiting for transfers between devices  18.4 us (12%)
  other arithmetic  5.49 us (4%)
  between operations  4.94 us (3%)
  matrix products  4.06 us (3%)
    all_to_all x1, blocking collectives, body(): lax.all_to_all(shares.reshape(clusters, capacity, quarter), 'cluster', sp...  33.6 us
    all_to_all x1, starting transfers between devices, body(): lax.all_to_all(outgoing.reshape(clusters, capacity, queries.shape[1]), 'c...  23.2 us
    ppermute x6, starting transfers between devices, shifted(): lax.ppermute(array, axis, [(i, (i - by) % peers) for i in range(peers)])  22.5 us
    ppermute x4, starting transfers between devices, swapped(): return lax.ppermute(array, axis, [(i, i ^ bit) for i in range(peers)])  13.6 us
    unnamed x21, local copies, waits for them, and re-layouts  11.2 us
    ppermute x4, waiting for transfers between devices, swapped(): return lax.ppermute(array, axis, [(i, i ^ bit) for i in range(peers)])  9.67 us
    all_to_all x1, waiting for transfers between devices, body(): lax.all_to_all(outgoing.reshape(clusters, capacity, queries.shape[1]), 'c...  8.69 us
  transfers between devices with their start and end apart: 11, of which 3 were waited for; matrix products, arithmetic and copies ran while one was open for 13% of the time, Pallas kernels for 0%

profile of v18, /device:TPU:32, one launch (start us, length us, event | category | flops | bytes accessed | tf_op | source)
XLA Modules:
  0.0 147.0 jit_solution(2080394652927340971)
XLA Ops:
  0.0 1.1 reshape.938
  1.1 0.1 copy.28
  1.3 0.8 constant_dynamic-update-slice_fusion.1
  2.1 0.9 pad_maximum_fusion.1
  2.9 5.6 %collective-permute-start.2 = (bf16[2,128,1024]{2,1,0:T(8,128)(2,1)}, bf16[2,128,1024]{2,1,0:T(8,128)(2,1)}, u32[]{:S(2)}, u32[]{:S(2)}) collective-permute-start(bf16[2,128,1024]{2,1,0:T(8,128)(2,1)} %pad_maximum_fusion.1), channel_id=1, source_target_pairs={{0,500},{4,504},{8,508},{12,0},{16,4},{20,8},{24,12},{28,16},{32,2... | collective-permute-start | bytes 1572872 | tf_op jit(solution)/shard_map/ppermute | solution.py:16
  8.5 1.9 %collective-permute-start.3 = (bf16[2,128,1024]{2,1,0:T(8,128)(2,1)}, bf16[2,128,1024]{2,1,0:T(8,128)(2,1)}, u32[]{:S(2)}, u32[]{:S(2)}) collective-permute-start(bf16[2,128,1024]{2,1,0:T(8,128)(2,1)} %pad_maximum_fusion.1), channel_id=1, source_target_pairs={{0,12},{4,16},{8,20},{12,24},{16,28},{20,32},{24,36},{28,40},{32,4... | collective-permute-start | bytes 1572872 | tf_op jit(solution)/shard_map/ppermute | solution.py:16
  10.4 7.0 %collective-permute-start.4 = (bf16[2,128,1024]{2,1,0:T(8,128)(2,1)}, bf16[2,128,1024]{2,1,0:T(8,128)(2,1)}, u32[]{:S(2)}, u32[]{:S(2)}) collective-permute-start(bf16[2,128,1024]{2,1,0:T(8,128)(2,1)} %pad_maximum_fusion.1), channel_id=1, source_target_pairs={{0,508},{4,0},{8,4},{12,8},{16,12},{20,16},{24,20},{28,24},{32,28}... | collective-permute-start | bytes 1572872 | tf_op jit(solution)/shard_map/ppermute | solution.py:16
  17.5 1.9 %collective-permute-start.5 = (bf16[2,128,1024]{2,1,0:T(8,128)(2,1)}, bf16[2,128,1024]{2,1,0:T(8,128)(2,1)}, u32[]{:S(2)}, u32[]{:S(2)}) collective-permute-start(bf16[2,128,1024]{2,1,0:T(8,128)(2,1)} %pad_maximum_fusion.1), channel_id=1, source_target_pairs={{0,4},{4,8},{8,12},{12,16},{16,20},{20,24},{24,28},{28,32},{32,36}... | collective-permute-start | bytes 1572872 | tf_op jit(solution)/shard_map/ppermute | solution.py:16
  19.4 2.7 %collective-permute-start.6 = (bf16[2,128,1024]{2,1,0:T(8,128)(2,1)}, bf16[2,128,1024]{2,1,0:T(8,128)(2,1)S(1)}, u32[]{:S(2)}, u32[]{:S(2)}) collective-permute-start(bf16[2,128,1024]{2,1,0:T(8,128)(2,1)} %pad_maximum_fusion.1), channel_id=1, source_target_pairs={{0,504},{4,508},{8,0},{12,4},{16,8},{20,12},{24,16},{28,20},{32,24... | collective-permute-start | bytes 1572872 | tf_op jit(solution)/shard_map/ppermute | solution.py:16
  22.1 0.1 copy.26
  22.2 0.2 fusion.21
  22.5 0.2 fusion.23
  22.7 0.2 convolution_convert_fusion
  23.0 0.8 reshape.936
  23.8 23.2 %all-to-all-start = ((bf16[128,4,256]{2,1,0:T(4,128)(2,1)}), bf16[128,4,256]{2,1,0:T(4,128)(2,1)S(1)}, u32[]{:S(2)}, u32[]{:S(2)}) async-start(bf16[128,4,256]{2,1,0:T(4,128)(2,1)} %reshape.936), calls=%async_computation | async-start | bytes 524288 | tf_op jit(solution)/shard_map/all_to_all | solution.py:81
  47.0 0.7 constant_dynamic-update-slice_fusion
  47.7 0.1 constant_dynamic-slice_fusion
  47.8 0.6 fusion.52
  52.8 0.1 stack.64
  52.9 0.1 broadcast_bitcast_fusion
  53.0 3.4 %collective-permute-start.7 = (bf16[2,128,1024]{2,1,0:T(8,128)(2,1)}, bf16[2,128,1024]{2,1,0:T(8,128)(2,1)}, u32[]{:S(2)}, u32[]{:S(2)}) collective-permute-start(bf16[2,128,1024]{2,1,0:T(8,128)(2,1)} %pad_maximum_fusion.1), channel_id=1, source_target_pairs={{0,8},{4,12},{8,16},{12,20},{16,24},{20,28},{24,32},{28,36},{32,40... | collective-permute-start | bytes 1572872 | tf_op jit(solution)/shard_map/ppermute | solution.py:16
  56.4 1.8 %slice_dynamic-update-slice_fusion.11 = (bf16[7,128,1024]{2,1,0:T(8,128)(2,1)}, bf16[7,128,1024]{2,1,0:T(8,128)(2,1)S(1)}) fusion(bf16[7,128,1024]{2,1,0:T(8,128)(2,1)} %constant_dynamic-update-slice_fusion, bf16[2,128,1024]{2,1,0:T(8,128)(2,1)} %collective-permute-done.2, bf16[7,128,1024]{2,1,0:T(8,128)(2,1)S(1)} %get-tuple-element.11), kind=kLoop, calls=%fused_computation.46 | loop fusion | bytes 1048576
  58.2 1.8 %slice_dynamic-update-slice_fusion.10 = (bf16[7,128,1024]{2,1,0:T(8,128)(2,1)}, bf16[7,128,1024]{2,1,0:T(8,128)(2,1)S(1)}) fusion(bf16[7,128,1024]{2,1,0:T(8,128)(2,1)} %get-tuple-element.28, bf16[2,128,1024]{2,1,0:T(8,128)(2,1)} %collective-permute-done.3, bf16[7,128,1024]{2,1,0:T(8,128)(2,1)S(1)} %get-tuple-element.29), kind=kLoop, calls=%fused_computation.45 | loop fusion | bytes 1048576
  60.0 1.8 %slice_dynamic-update-slice_fusion.9 = (bf16[7,128,1024]{2,1,0:T(8,128)(2,1)}, bf16[7,128,1024]{2,1,0:T(8,128)(2,1)S(1)}) fusion(bf16[7,128,1024]{2,1,0:T(8,128)(2,1)} %get-tuple-element.26, bf16[2,128,1024]{2,1,0:T(8,128)(2,1)} %collective-permute-done.4, bf16[7,128,1024]{2,1,0:T(8,128)(2,1)S(1)} %get-tuple-element.27), kind=kLoop, calls=%fused_computation.44 | loop fusion | bytes 1048576
  61.7 8.7 %all-to-all-done = bf16[128,4,256]{2,1,0:T(4,128)(2,1)S(1)} async-done(((bf16[128,4,256]{2,1,0:T(4,128)(2,1)}), bf16[128,4,256]{2,1,0:T(4,128)(2,1)S(1)}, u32[]{:S(2)}, u32[]{:S(2)}) %all-to-all-start) | async-done | bytes 262176 | tf_op jit(solution)/shard_map/all_to_all | solution.py:81
  70.4 0.1 reshape.937
  70.5 4.6 %collective-permute-start = (bf16[512,256]{1,0:T(8,128)(2,1)S(1)}, bf16[512,256]{1,0:T(8,128)(2,1)S(1)}, u32[]{:S(2)}, u32[]{:S(2)}) collective-permute-start(bf16[512,256]{1,0:T(8,128)(2,1)S(1)} %reshape.937), channel_id=1, source_target_pairs={{0,2},{1,3},{2,0},{3,1},{4,6},{5,7},{6,4},{7,5},{8,10},{9,11},{10,... | collective-permute-start | bytes 786440 | tf_op jit(solution)/shard_map/ppermute | solution.py:21
  75.1 1.8 %slice_dynamic-update-slice_fusion.8 = (bf16[7,128,1024]{2,1,0:T(8,128)(2,1)}, bf16[7,128,1024]{2,1,0:T(8,128)(2,1)S(1)}) fusion(bf16[7,128,1024]{2,1,0:T(8,128)(2,1)} %get-tuple-element.24, bf16[2,128,1024]{2,1,0:T(8,128)(2,1)} %collective-permute-done.5, bf16[7,128,1024]{2,1,0:T(8,128)(2,1)S(1)} %get-tuple-element.25), kind=kLoop, calls=%fused_computation.43 | loop fusion | bytes 1048576
  76.9 0.7 slice_dynamic-update-slice_fusion.7
  77.6 0.1 stack_reshape.3
  77.7 2.6 %collective-permute-done = bf16[512,256]{1,0:T(8,128)(2,1)S(1)} collective-permute-done((bf16[512,256]{1,0:T(8,128)(2,1)S(1)}, bf16[512,256]{1,0:T(8,128)(2,1)S(1)}, u32[]{:S(2)}, u32[]{:S(2)}) %collective-permute-start) | collective-permute-done | bytes 262176 | tf_op jit(solution)/shard_map/ppermute | solution.py:21
  80.3 0.8 pad_maximum_fusion
  81.1 1.9 %collective-permute-start.1 = (bf16[2,512,256]{2,1,0:T(8,128)(2,1)}, bf16[2,512,256]{2,1,0:T(8,128)(2,1)S(1)}, u32[]{:S(2)}, u32[]{:S(2)}) collective-permute-start(bf16[2,512,256]{2,1,0:T(8,128)(2,1)} %pad_maximum_fusion), channel_id=1, source_target_pairs={{0,1},{1,0},{2,3},{3,2},{4,5},{5,4},{6,7},{7,6},{8,9},{9,8},{10,11... | collective-permute-start | bytes 1572872 | tf_op jit(solution)/shard_map/ppermute | solution.py:21
  83.0 1.8 %slice_dynamic-update-slice_fusion.6 = (bf16[7,128,1024]{2,1,0:T(8,128)(2,1)}, bf16[7,128,1024]{2,1,0:T(8,128)(2,1)S(1)}) fusion(bf16[7,128,1024]{2,1,0:T(8,128)(2,1)} %get-tuple-element.20, bf16[2,128,1024]{2,1,0:T(8,128)(2,1)} %collective-permute-done.7, bf16[7,128,1024]{2,1,0:T(8,128)(2,1)S(1)} %get-tuple-element.21), kind=kLoop, calls=%fused_computation.41 | loop fusion | bytes 1048576 | tf_op jit(solution)/shard_map/stack | solution.py:96
  84.8 2.5 %copy.29 = bf16[896,1024]{0,1:T(8,128)(2,1)} copy(bf16[896,1024]{1,0:T(8,128)(2,1)S(1)} %bitcast.112) | data formatting | bytes 3670016 | tf_op jit(solution)/shard_map/reshape | solution.py:97
  87.3 0.9 fusion.26
  88.1 0.1 broadcast_in_dim.140
  88.4 0.4 copy-done.4
  88.8 1.4 fusion.53
  90.2 0.5 fusion
  90.7 1.0 copy-done.1
  91.7 1.4 fusion.4
  93.1 1.3 copy-done.2
  94.5 0.1 dynamic-slice_bitcast_fusion.1
  94.5 0.1 copy.33
  94.7 0.1 copy.34
  94.8 0.3 select_convert_fusion.1
  95.1 0.1 pad_maximum_fusion.2
  95.1 2.4 %collective-permute-start.8 = (bf16[2,512,256]{1,2,0:T(8,128)(2,1)S(1)}, bf16[2,512,256]{1,2,0:T(8,128)(2,1)S(1)}, u32[]{:S(2)}, u32[]{:S(2)}) collective-permute-start(bf16[2,512,256]{1,2,0:T(8,128)(2,1)S(1)} %pad_maximum_fusion.2), channel_id=1, source_target_pairs={{0,1},{1,0},{2,3},{3,2},{4,5},{5,4},{6,7},{7,6},{8,9},{9,8},{10,11... | collective-permute-start | bytes 1572872 | tf_op jit(solution)/shard_map/ppermute | solution.py:21
  97.6 1.3 dynamic-slice_bitcast_fusion.3
  98.8 0.2 copy.31
  99.1 0.2 copy.32
  99.3 0.1 convert_element_type.261
  99.5 0.2 fusion.2
  99.7 0.3 fusion.15
  100.0 4.6 %collective-permute-start.9 = (bf16[512,256]{0,1:T(8,128)(2,1)S(1)}, bf16[512,256]{0,1:T(8,128)(2,1)S(1)}, u32[]{:S(2)}, u32[]{:S(2)}) collective-permute-start(bf16[512,256]{0,1:T(8,128)(2,1)S(1)} %fusion.15), channel_id=1, source_target_pairs={{0,2},{1,3},{2,0},{3,1},{4,6},{5,7},{6,4},{7,5},{8,10},{9,11},{10,... | collective-permute-start | bytes 786440 | tf_op jit(solution)/shard_map/ppermute | solution.py:21
  104.6 7.1 %collective-permute-done.9 = bf16[512,256]{0,1:T(8,128)(2,1)S(1)} collective-permute-done((bf16[512,256]{0,1:T(8,128)(2,1)S(1)}, bf16[512,256]{0,1:T(8,128)(2,1)S(1)}, u32[]{:S(2)}, u32[]{:S(2)}) %collective-permute-start.9) | collective-permute-done | bytes 262176 | tf_op jit(solution)/shard_map/ppermute | solution.py:21
  111.7 0.1 convert_element_type.275
  111.9 0.1 fusion.16
  112.0 0.1 copy.35
  112.1 0.1 reshape.942
  112.2 33.6 %all_to_all.10 = bf16[128,4,250]{2,1,0:T(4,128)(2,1)S(1)} all-to-all(bf16[128,4,250]{2,1,0:T(4,128)(2,1)S(1)} %reshape.942), channel_id=1, replica_groups=mesh['cluster'=128,'feat'=4] {'cluster'}, dimensions={0} | all-to-all | bytes 512000 | tf_op jit(solution)/shard_map/all_to_all | solution.py:135
  145.8 0.2 reshape.943
  146.0 1.0 convolution_convert_fusion.1
  (43 shorter events, 0.4 us)
Async XLA Ops:
  0.0 22.7 %copy-start = (bf16[256,256]{1,0:T(8,128)(2,1)S(1)}, bf16[256,256]{1,0:T(8,128)(2,1)}, u32[]{:S(2)}) copy-start(bf16[256,256]{1,0:T(8,128)(2,1)} %param.6) | copy-start | bytes 393220
  0.0 2.1 %copy-start.3 = (bf16[128,1024]{1,0:T(8,128)(2,1)S(1)}, bf16[128,1024]{1,0:T(8,128)(2,1)}, u32[]{:S(2)}) copy-start(bf16[128,1024]{1,0:T(8,128)(2,1)} %param.9) | copy-start | bytes 786436
  0.0 22.1 %copy-start.5 = (s32[256,1]{0,1:T(1,128)S(1)}, s32[256,1]{0,1:T(1,128)}, u32[]{:S(2)}) copy-start(s32[256,1]{0,1:T(1,128)} %param.7) | copy-start | bytes 3076
  2.1 45.6 %copy-start.6 = (s32[128,7]{0,1:T(8,128)S(1)}, s32[128,7]{0,1:T(8,128)}, u32[]{:S(2)}) copy-start(s32[128,7]{0,1:T(8,128)} %param.8) | copy-start | bytes 10756
  2.9 50.1 %collective-permute-start.2 = (bf16[2,128,1024]{2,1,0:T(8,128)(2,1)}, bf16[2,128,1024]{2,1,0:T(8,128)(2,1)}, u32[]{:S(2)}, u32[]{:S(2)}) collective-permute-start(bf16[2,128,1024]{2,1,0:T(8,128)(2,1)} %pad_maximum_fusion.1), channel_id=1, source_target_pairs={{0,500},{4,504},{8,508},{12,0},{16,4},{20,8},{24,12},{28,16},{32,2... | collective-permute-start | bytes 1572872 | tf_op jit(solution)/shard_map/ppermute | solution.py:16
  8.5 49.7 %collective-permute-start.3 = (bf16[2,128,1024]{2,1,0:T(8,128)(2,1)}, bf16[2,128,1024]{2,1,0:T(8,128)(2,1)}, u32[]{:S(2)}, u32[]{:S(2)}) collective-permute-start(bf16[2,128,1024]{2,1,0:T(8,128)(2,1)} %pad_maximum_fusion.1), channel_id=1, source_target_pairs={{0,12},{4,16},{8,20},{12,24},{16,28},{20,32},{24,36},{28,40},{32,4... | collective-permute-start | bytes 1572872 | tf_op jit(solution)/shard_map/ppermute | solution.py:16
  10.4 49.5 %collective-permute-start.4 = (bf16[2,128,1024]{2,1,0:T(8,128)(2,1)}, bf16[2,128,1024]{2,1,0:T(8,128)(2,1)}, u32[]{:S(2)}, u32[]{:S(2)}) collective-permute-start(bf16[2,128,1024]{2,1,0:T(8,128)(2,1)} %pad_maximum_fusion.1), channel_id=1, source_target_pairs={{0,508},{4,0},{8,4},{12,8},{16,12},{20,16},{24,20},{28,24},{32,28}... | collective-permute-start | bytes 1572872 | tf_op jit(solution)/shard_map/ppermute | solution.py:16
  17.5 57.7 %collective-permute-start.5 = (bf16[2,128,1024]{2,1,0:T(8,128)(2,1)}, bf16[2,128,1024]{2,1,0:T(8,128)(2,1)}, u32[]{:S(2)}, u32[]{:S(2)}) collective-permute-start(bf16[2,128,1024]{2,1,0:T(8,128)(2,1)} %pad_maximum_fusion.1), channel_id=1, source_target_pairs={{0,4},{4,8},{8,12},{12,16},{16,20},{20,24},{24,28},{28,32},{32,36}... | collective-permute-start | bytes 1572872 | tf_op jit(solution)/shard_map/ppermute | solution.py:16
  19.4 57.5 %collective-permute-start.6 = (bf16[2,128,1024]{2,1,0:T(8,128)(2,1)}, bf16[2,128,1024]{2,1,0:T(8,128)(2,1)S(1)}, u32[]{:S(2)}, u32[]{:S(2)}) collective-permute-start(bf16[2,128,1024]{2,1,0:T(8,128)(2,1)} %pad_maximum_fusion.1), channel_id=1, source_target_pairs={{0,504},{4,508},{8,0},{12,4},{16,8},{20,12},{24,16},{28,20},{32,24... | collective-permute-start | bytes 1572872 | tf_op jit(solution)/shard_map/ppermute | solution.py:16
  23.8 46.7 %all-to-all-start = ((bf16[128,4,256]{2,1,0:T(4,128)(2,1)}), bf16[128,4,256]{2,1,0:T(4,128)(2,1)S(1)}, u32[]{:S(2)}, u32[]{:S(2)}) async-start(bf16[128,4,256]{2,1,0:T(4,128)(2,1)} %reshape.936), calls=%async_computation | async-start | bytes 524288 | tf_op jit(solution)/shard_map/all_to_all | solution.py:81
  53.0 30.0 %collective-permute-start.7 = (bf16[2,128,1024]{2,1,0:T(8,128)(2,1)}, bf16[2,128,1024]{2,1,0:T(8,128)(2,1)}, u32[]{:S(2)}, u32[]{:S(2)}) collective-permute-start(bf16[2,128,1024]{2,1,0:T(8,128)(2,1)} %pad_maximum_fusion.1), channel_id=1, source_target_pairs={{0,8},{4,12},{8,16},{12,20},{16,24},{20,28},{24,32},{28,36},{32,40... | collective-permute-start | bytes 1572872 | tf_op jit(solution)/shard_map/ppermute | solution.py:16
  70.5 9.8 %collective-permute-start = (bf16[512,256]{1,0:T(8,128)(2,1)S(1)}, bf16[512,256]{1,0:T(8,128)(2,1)S(1)}, u32[]{:S(2)}, u32[]{:S(2)}) collective-permute-start(bf16[512,256]{1,0:T(8,128)(2,1)S(1)} %reshape.937), channel_id=1, source_target_pairs={{0,2},{1,3},{2,0},{3,1},{4,6},{5,7},{6,4},{7,5},{8,10},{9,11},{10,... | collective-permute-start | bytes 786440 | tf_op jit(solution)/shard_map/ppermute | solution.py:21
  81.1 7.2 %collective-permute-start.1 = (bf16[2,512,256]{2,1,0:T(8,128)(2,1)}, bf16[2,512,256]{2,1,0:T(8,128)(2,1)S(1)}, u32[]{:S(2)}, u32[]{:S(2)}) collective-permute-start(bf16[2,512,256]{2,1,0:T(8,128)(2,1)} %pad_maximum_fusion), channel_id=1, source_target_pairs={{0,1},{1,0},{2,3},{3,2},{4,5},{5,4},{6,7},{7,6},{8,9},{9,8},{10,11... | collective-permute-start | bytes 1572872 | tf_op jit(solution)/shard_map/ppermute | solution.py:21
  87.3 1.5 %copy-start.4 = (bf16[7,128,1024]{2,1,0:T(8,128)(2,1)S(1)}, bf16[7,128,1024]{2,1,0:T(8,128)(2,1)}, u32[]{:S(2)}) copy-start(bf16[7,128,1024]{2,1,0:T(8,128)(2,1)} %get-tuple-element.18) | copy-start | bytes 5505028
  90.2 1.5 %copy-start.1 = (bf16[896,1024]{0,1:T(8,128)(2,1)S(1)}, bf16[896,1024]{0,1:T(8,128)(2,1)}, u32[]{:S(2)}) copy-start(bf16[896,1024]{0,1:T(8,128)(2,1)} %copy.29) | copy-start | bytes 5505028
  93.1 1.3 copy-start.2
  95.1 4.1 %collective-permute-start.8 = (bf16[2,512,256]{1,2,0:T(8,128)(2,1)S(1)}, bf16[2,512,256]{1,2,0:T(8,128)(2,1)S(1)}, u32[]{:S(2)}, u32[]{:S(2)}) collective-permute-start(bf16[2,512,256]{1,2,0:T(8,128)(2,1)S(1)} %pad_maximum_fusion.2), channel_id=1, source_target_pairs={{0,1},{1,0},{2,3},{3,2},{4,5},{5,4},{6,7},{7,6},{8,9},{9,8},{10,11... | collective-permute-start | bytes 1572872 | tf_op jit(solution)/shard_map/ppermute | solution.py:21
  100.0 11.8 %collective-permute-start.9 = (bf16[512,256]{0,1:T(8,128)(2,1)S(1)}, bf16[512,256]{0,1:T(8,128)(2,1)S(1)}, u32[]{:S(2)}, u32[]{:S(2)}) collective-permute-start(bf16[512,256]{0,1:T(8,128)(2,1)S(1)} %fusion.15), channel_id=1, source_target_pairs={{0,2},{1,3},{2,0},{3,1},{4,6},{5,7},{6,4},{7,5},{8,10},{9,11},{10,... | collective-permute-start | bytes 786440 | tf_op jit(solution)/shard_map/ppermute | solution.py:21

commit v19 on v18

--- a/solution.py
+++ b/solution.py
@@ -63,10 +63,11 @@
 
     quarter = classes // feats
     group = -(-(quarter + 6) // 128) * 128
-    lane = lax.broadcasted_iota(jnp.int32, (rows, feats * group), 1)
+    lane = lax.broadcasted_iota(jnp.int32, (2, rows, feats * group), 2)
+    plane = lax.broadcasted_iota(jnp.int32, (2, rows, feats * group), 0)
     padded = jnp.pad(labels.reshape(rows, feats, quarter), ((0, 0), (0, 0), (0, group - quarter)))
-    grouped = jnp.where(lane == quarter, prior[:, None], padded.reshape(rows, feats * group))
-    block = jnp.stack([keys, grouped])
+    grouped = jnp.where(lane == quarter, prior[None, :, None], padded.reshape(1, rows, feats * group))
+    block = jnp.where(plane == 0, keys[None], grouped)
     offsets = [0]
     for reach in sorted(range(1, REACH + 1), key=lambda r: (r == 2, -r)):
         offsets += [reach, -reach]

time: 148 us -> 148 us (level)
  local copies, waits for them, and re-layouts: 21.2 us -> 23.8 us
  waiting for transfers between devices: 18.4 us -> 16.7 us
    reshape x2 -> x0, local copies, waits for them, and re-layouts: 2.62 us -> none  [the longest x1 2.48 us: body(): jnp.stack([b[1] for b in blocks])]
    dot_general x0 -> x1, local copies, waits for them, and re-layouts: none -> 2.45 us  [body(): jnp.dot(weight.astype(jnp.bfloat16), band_labels, preferred_element_type=...]
    dynamic_update_slice x4, local copies, waits for them, and re-layouts: 0.12 us -> 2.12 us  [body(): lax.dynamic_update_slice_in_dim(query_full, part, (feat_index ^ code) * w...]
    unnamed x21 -> x27, local copies, waits for them, and re-layouts: 11.2 us -> 11.2 us
  transfers between devices with their start and end apart: 11 -> 11, of which waited for: 3 -> 3; matrix products, arithmetic and copies ran while one was open for 13% -> 14% of each run, Pallas kernels for 0% -> 0%
where the time goes in v19:
time: 148 us
  starting transfers between devices  59.3 us (40%)
  blocking collectives  33.6 us (23%)
  local copies, waits for them, and re-layouts  23.8 us (16%)
  waiting for transfers between devices  16.7 us (11%)
  other arithmetic  5.42 us (4%)
  between operations  4.76 us (3%)
  matrix products  4.06 us (3%)
    all_to_all x1, blocking collectives, body(): lax.all_to_all(shares.reshape(clusters, capacity, quarter), 'cluster', sp...  33.6 us
    all_to_all x1, starting transfers between devices, body(): lax.all_to_all(outgoing.reshape(clusters, capacity, queries.shape[1]), 'c...  23.2 us
    ppermute x6, starting transfers between devices, shifted(): lax.ppermute(array, axis, [(i, (i - by) % peers) for i in range(peers)])  22.5 us
    ppermute x4, starting transfers between devices, swapped(): return lax.ppermute(array, axis, [(i, i ^ bit) for i in range(peers)])  13.5 us
    unnamed x27, local copies, waits for them, and re-layouts  11.2 us
    ppermute x4, waiting for transfers between devices, swapped(): return lax.ppermute(array, axis, [(i, i ^ bit) for i in range(peers)])  8.69 us
    all_to_all x1, waiting for transfers between devices, body(): lax.all_to_all(outgoing.reshape(clusters, capacity, queries.shape[1]), 'c...  8.03 us
  transfers between devices with their start and end apart: 11, of which 3 were waited for; matrix products, arithmetic and copies ran while one was open for 14% of the time, Pallas kernels for 0%

profile of v19, /device:TPU:32, one launch (start us, length us, event | category | flops | bytes accessed | tf_op | source)
XLA Modules:
  0.0 147.6 jit_solution(1596080768281061160)
XLA Ops:
  0.0 1.1 reshape.891
  1.1 0.1 copy.25
  1.3 1.1 select_select_fusion
  2.4 5.6 %collective-permute-start.2 = (bf16[2,128,1024]{2,1,0:T(8,128)(2,1)S(1)}, bf16[2,128,1024]{2,1,0:T(8,128)(2,1)}, u32[]{:S(2)}, u32[]{:S(2)}) collective-permute-start(bf16[2,128,1024]{2,1,0:T(8,128)(2,1)S(1)} %select_select_fusion), channel_id=1, source_target_pairs={{0,500},{4,504},{8,508},{12,0},{16,4},{20,8},{24,12},{28,16},{32,2... | collective-permute-start | bytes 1572872 | tf_op jit(solution)/shard_map/ppermute | solution.py:16
  7.9 1.9 %collective-permute-start.3 = (bf16[2,128,1024]{2,1,0:T(8,128)(2,1)S(1)}, bf16[2,128,1024]{2,1,0:T(8,128)(2,1)}, u32[]{:S(2)}, u32[]{:S(2)}) collective-permute-start(bf16[2,128,1024]{2,1,0:T(8,128)(2,1)S(1)} %select_select_fusion), channel_id=1, source_target_pairs={{0,12},{4,16},{8,20},{12,24},{16,28},{20,32},{24,36},{28,40},{32,4... | collective-permute-start | bytes 1572872 | tf_op jit(solution)/shard_map/ppermute | solution.py:16
  9.9 7.0 %collective-permute-start.4 = (bf16[2,128,1024]{2,1,0:T(8,128)(2,1)S(1)}, bf16[2,128,1024]{2,1,0:T(8,128)(2,1)S(1)}, u32[]{:S(2)}, u32[]{:S(2)}) collective-permute-start(bf16[2,128,1024]{2,1,0:T(8,128)(2,1)S(1)} %select_select_fusion), channel_id=1, source_target_pairs={{0,508},{4,0},{8,4},{12,8},{16,12},{20,16},{24,20},{28,24},{32,28}... | collective-permute-start | bytes 1572872 | tf_op jit(solution)/shard_map/ppermute | solution.py:16
  16.9 1.9 %collective-permute-start.5 = (bf16[2,128,1024]{2,1,0:T(8,128)(2,1)S(1)}, bf16[2,128,1024]{2,1,0:T(8,128)(2,1)}, u32[]{:S(2)}, u32[]{:S(2)}) collective-permute-start(bf16[2,128,1024]{2,1,0:T(8,128)(2,1)S(1)} %select_select_fusion), channel_id=1, source_target_pairs={{0,4},{4,8},{8,12},{12,16},{16,20},{20,24},{24,28},{28,32},{32,36}... | collective-permute-start | bytes 1572872 | tf_op jit(solution)/shard_map/ppermute | solution.py:16
  18.9 2.7 %collective-permute-start.6 = (bf16[2,128,1024]{2,1,0:T(8,128)(2,1)S(1)}, bf16[2,128,1024]{2,1,0:T(8,128)(2,1)}, u32[]{:S(2)}, u32[]{:S(2)}) collective-permute-start(bf16[2,128,1024]{2,1,0:T(8,128)(2,1)S(1)} %select_select_fusion), channel_id=1, source_target_pairs={{0,504},{4,508},{8,0},{12,4},{16,8},{20,12},{24,16},{28,20},{32,24... | collective-permute-start | bytes 1572872 | tf_op jit(solution)/shard_map/ppermute | solution.py:16
  21.6 0.1 copy.23
  21.7 0.2 fusion.21
  22.0 0.2 fusion.23
  22.2 0.2 convolution_convert_fusion
  22.4 0.8 reshape.889
  23.2 23.2 %all-to-all-start = ((bf16[128,4,256]{2,1,0:T(4,128)(2,1)}), bf16[128,4,256]{2,1,0:T(4,128)(2,1)S(1)}, u32[]{:S(2)}, u32[]{:S(2)}) async-start(bf16[128,4,256]{2,1,0:T(4,128)(2,1)} %reshape.889), calls=%async_computation | async-start | bytes 524288 | tf_op jit(solution)/shard_map/all_to_all | solution.py:82
  46.4 0.7 slice_dynamic-update-slice_fusion.13
  47.2 0.1 constant_dynamic-slice_fusion
  47.2 0.6 fusion.51
  52.1 0.1 stack.57
  52.2 0.6 broadcast_bitcast_fusion
  52.9 0.5 iota_compare_fusion.7
  53.4 0.6 iota_compare_fusion.9
  54.0 3.4 %collective-permute-start.7 = (bf16[2,128,1024]{2,1,0:T(8,128)(2,1)S(1)}, bf16[2,128,1024]{2,1,0:T(8,128)(2,1)}, u32[]{:S(2)}, u32[]{:S(2)}) collective-permute-start(bf16[2,128,1024]{2,1,0:T(8,128)(2,1)S(1)} %select_select_fusion), channel_id=1, source_target_pairs={{0,8},{4,12},{8,16},{12,20},{16,24},{20,28},{24,32},{28,36},{32,40... | collective-permute-start | bytes 1572872 | tf_op jit(solution)/shard_map/ppermute | solution.py:16
  57.4 1.8 %slice_dynamic-update-slice_fusion.12 = (bf16[7,128,1024]{2,1,0:T(8,128)(2,1)}, bf16[7,128,1024]{2,1,0:T(8,128)(2,1)S(1)}) fusion(bf16[7,128,1024]{2,1,0:T(8,128)(2,1)} %get-tuple-element.28, bf16[2,128,1024]{2,1,0:T(8,128)(2,1)} %collective-permute-done.2, bf16[7,128,1024]{2,1,0:T(8,128)(2,1)S(1)} %get-tuple-element.29), kind=kLoop, calls=%fused_computation.48 | loop fusion | bytes 1048576
  59.1 1.8 %slice_dynamic-update-slice_fusion.11 = (bf16[7,128,1024]{2,1,0:T(8,128)(2,1)}, bf16[7,128,1024]{2,1,0:T(8,128)(2,1)S(1)}) fusion(bf16[7,128,1024]{2,1,0:T(8,128)(2,1)} %get-tuple-element.26, bf16[2,128,1024]{2,1,0:T(8,128)(2,1)} %collective-permute-done.3, bf16[7,128,1024]{2,1,0:T(8,128)(2,1)S(1)} %get-tuple-element.27), kind=kLoop, calls=%fused_computation.47 | loop fusion | bytes 1048576
  60.9 0.7 slice_dynamic-update-slice_fusion.10
  61.6 8.0 %all-to-all-done = bf16[128,4,256]{2,1,0:T(4,128)(2,1)S(1)} async-done(((bf16[128,4,256]{2,1,0:T(4,128)(2,1)}), bf16[128,4,256]{2,1,0:T(4,128)(2,1)S(1)}, u32[]{:S(2)}, u32[]{:S(2)}) %all-to-all-start) | async-done | bytes 262176 | tf_op jit(solution)/shard_map/all_to_all | solution.py:82
  69.7 0.1 reshape.890
  69.7 4.6 %collective-permute-start = (bf16[512,256]{1,0:T(8,128)(2,1)S(1)}, bf16[512,256]{1,0:T(8,128)(2,1)S(1)}, u32[]{:S(2)}, u32[]{:S(2)}) collective-permute-start(bf16[512,256]{1,0:T(8,128)(2,1)S(1)} %reshape.890), channel_id=1, source_target_pairs={{0,2},{1,3},{2,0},{3,1},{4,6},{5,7},{6,4},{7,5},{8,10},{9,11},{10,... | collective-permute-start | bytes 786440 | tf_op jit(solution)/shard_map/ppermute | solution.py:21
  74.4 1.8 %slice_dynamic-update-slice_fusion.9 = (bf16[7,128,1024]{2,1,0:T(8,128)(2,1)}, bf16[7,128,1024]{2,1,0:T(8,128)(2,1)S(1)}) fusion(bf16[7,128,1024]{2,1,0:T(8,128)(2,1)} %get-tuple-element.22, bf16[2,128,1024]{2,1,0:T(8,128)(2,1)} %collective-permute-done.5, bf16[7,128,1024]{2,1,0:T(8,128)(2,1)S(1)} %get-tuple-element.23), kind=kLoop, calls=%fused_computation.45 | loop fusion | bytes 1048576
  76.1 1.8 %slice_dynamic-update-slice_fusion.8 = (bf16[7,128,1024]{2,1,0:T(8,128)(2,1)}, bf16[7,128,1024]{2,1,0:T(8,128)(2,1)S(1)}) fusion(bf16[7,128,1024]{2,1,0:T(8,128)(2,1)} %get-tuple-element.20, bf16[2,128,1024]{2,1,0:T(8,128)(2,1)} %collective-permute-done.6, bf16[7,128,1024]{2,1,0:T(8,128)(2,1)S(1)} %get-tuple-element.21), kind=kLoop, calls=%fused_computation.44 | loop fusion | bytes 1048576
  77.9 0.1 stack_reshape.3
  77.9 1.6 %collective-permute-done = bf16[512,256]{1,0:T(8,128)(2,1)S(1)} collective-permute-done((bf16[512,256]{1,0:T(8,128)(2,1)S(1)}, bf16[512,256]{1,0:T(8,128)(2,1)S(1)}, u32[]{:S(2)}, u32[]{:S(2)}) %collective-permute-start) | collective-permute-done | bytes 262176 | tf_op jit(solution)/shard_map/ppermute | solution.py:21
  79.5 0.8 pad_maximum_fusion
  80.3 1.9 %collective-permute-start.1 = (bf16[2,512,256]{2,1,0:T(8,128)(2,1)}, bf16[2,512,256]{2,1,0:T(8,128)(2,1)}, u32[]{:S(2)}, u32[]{:S(2)}) collective-permute-start(bf16[2,512,256]{2,1,0:T(8,128)(2,1)} %pad_maximum_fusion), channel_id=1, source_target_pairs={{0,1},{1,0},{2,3},{3,2},{4,5},{5,4},{6,7},{7,6},{8,9},{9,8},{10,11... | collective-permute-start | bytes 1572872 | tf_op jit(solution)/shard_map/ppermute | solution.py:21
  82.3 1.8 %slice_dynamic-update-slice_fusion.7 = (bf16[7,128,1024]{2,1,0:T(8,128)(2,1)}, bf16[7,128,1024]{2,1,0:T(8,128)(2,1)S(1)}) fusion(bf16[7,128,1024]{2,1,0:T(8,128)(2,1)} %get-tuple-element.18, bf16[2,128,1024]{2,1,0:T(8,128)(2,1)} %collective-permute-done.7, bf16[7,128,1024]{2,1,0:T(8,128)(2,1)S(1)} %get-tuple-element.19), kind=kLoop, calls=%fused_computation.43 | loop fusion | bytes 1048576 | tf_op jit(solution)/shard_map/stack | solution.py:97
  84.0 2.5 %copy.26 = bf16[1024,896]{1,0:T(8,128)(2,1)} copy(bf16[1024,896]{0,1:T(8,128)(2,1)S(1)} %bitcast.110) | data formatting | bytes 3670016 | tf_op jit(solution)/shard_map/dot_general | solution.py:110
  86.5 0.2 convert_reduce_fusion
  86.7 0.1 broadcast_in_dim.159
  87.0 1.1 fusion.18
  88.0 1.0 fusion.17
  89.1 1.4 fusion.52
  90.4 0.5 fusion
  90.9 1.0 copy-done.1
  91.9 1.4 fusion.4
  93.4 1.3 copy-done.2
  94.8 0.1 copy.29
  94.9 0.1 copy.30
  95.1 0.3 copy-done.6
  95.4 0.3 select_convert_fusion.1
  95.7 2.4 %collective-permute-start.8 = (bf16[2,512,256]{1,2,0:T(8,128)(2,1)S(1)}, bf16[2,512,256]{1,2,0:T(8,128)(2,1)S(1)}, u32[]{:S(2)}, u32[]{:S(2)}) collective-permute-start(bf16[2,512,256]{1,2,0:T(8,128)(2,1)S(1)} %pad_maximum_fusion.1), channel_id=1, source_target_pairs={{0,1},{1,0},{2,3},{3,2},{4,5},{5,4},{6,7},{7,6},{8,9},{9,8},{10,11... | collective-permute-start | bytes 1572872 | tf_op jit(solution)/shard_map/ppermute | solution.py:21
  98.2 1.3 dynamic-slice_bitcast_fusion.3
  99.4 0.2 copy.27
  99.6 0.2 copy.28
  99.9 0.1 convert_element_type.261
  100.1 0.2 fusion.2
  100.3 0.3 fusion.15
  100.5 4.6 %collective-permute-start.9 = (bf16[512,256]{0,1:T(8,128)(2,1)S(1)}, bf16[512,256]{0,1:T(8,128)(2,1)S(1)}, u32[]{:S(2)}, u32[]{:S(2)}) collective-permute-start(bf16[512,256]{0,1:T(8,128)(2,1)S(1)} %fusion.15), channel_id=1, source_target_pairs={{0,2},{1,3},{2,0},{3,1},{4,6},{5,7},{6,4},{7,5},{8,10},{9,11},{10,... | collective-permute-start | bytes 786440 | tf_op jit(solution)/shard_map/ppermute | solution.py:21
  105.2 7.1 %collective-permute-done.9 = bf16[512,256]{0,1:T(8,128)(2,1)S(1)} collective-permute-done((bf16[512,256]{0,1:T(8,128)(2,1)S(1)}, bf16[512,256]{0,1:T(8,128)(2,1)S(1)}, u32[]{:S(2)}, u32[]{:S(2)}) %collective-permute-start.9) | collective-permute-done | bytes 262176 | tf_op jit(solution)/shard_map/ppermute | solution.py:21
  112.5 0.1 fusion.16
  112.6 0.1 copy.31
  112.7 0.1 reshape.894
  112.8 33.6 %all_to_all.10 = bf16[128,4,250]{2,1,0:T(4,128)(2,1)S(1)} all-to-all(bf16[128,4,250]{2,1,0:T(4,128)(2,1)S(1)} %reshape.894), channel_id=1, replica_groups=mesh['cluster'=128,'feat'=4] {'cluster'}, dimensions={0} | all-to-all | bytes 512000 | tf_op jit(solution)/shard_map/all_to_all | solution.py:136
  146.4 0.2 reshape.895
  146.6 1.0 convolution_convert_fusion.1
  (49 shorter events, 0.6 us)
Async XLA Ops:
  0.0 22.2 %copy-start = (bf16[256,256]{1,0:T(8,128)(2,1)S(1)}, bf16[256,256]{1,0:T(8,128)(2,1)}, u32[]{:S(2)}) copy-start(bf16[256,256]{1,0:T(8,128)(2,1)} %param.6) | copy-start | bytes 393220
  0.0 21.6 %copy-start.4 = (s32[256,1]{0,1:T(1,128)S(1)}, s32[256,1]{0,1:T(1,128)}, u32[]{:S(2)}) copy-start(s32[256,1]{0,1:T(1,128)} %param.7) | copy-start | bytes 3076
  2.3 44.8 %copy-start.5 = (s32[128,7]{0,1:T(8,128)S(1)}, s32[128,7]{0,1:T(8,128)}, u32[]{:S(2)}) copy-start(s32[128,7]{0,1:T(8,128)} %param.8) | copy-start | bytes 10756
  2.4 51.6 %collective-permute-start.2 = (bf16[2,128,1024]{2,1,0:T(8,128)(2,1)S(1)}, bf16[2,128,1024]{2,1,0:T(8,128)(2,1)}, u32[]{:S(2)}, u32[]{:S(2)}) collective-permute-start(bf16[2,128,1024]{2,1,0:T(8,128)(2,1)S(1)} %select_select_fusion), channel_id=1, source_target_pairs={{0,500},{4,504},{8,508},{12,0},{16,4},{20,8},{24,12},{28,16},{32,2... | collective-permute-start | bytes 1572872 | tf_op jit(solution)/shard_map/ppermute | solution.py:16
  7.9 51.2 %collective-permute-start.3 = (bf16[2,128,1024]{2,1,0:T(8,128)(2,1)S(1)}, bf16[2,128,1024]{2,1,0:T(8,128)(2,1)}, u32[]{:S(2)}, u32[]{:S(2)}) collective-permute-start(bf16[2,128,1024]{2,1,0:T(8,128)(2,1)S(1)} %select_select_fusion), channel_id=1, source_target_pairs={{0,12},{4,16},{8,20},{12,24},{16,28},{20,32},{24,36},{28,40},{32,4... | collective-permute-start | bytes 1572872 | tf_op jit(solution)/shard_map/ppermute | solution.py:16
  9.9 51.0 %collective-permute-start.4 = (bf16[2,128,1024]{2,1,0:T(8,128)(2,1)S(1)}, bf16[2,128,1024]{2,1,0:T(8,128)(2,1)S(1)}, u32[]{:S(2)}, u32[]{:S(2)}) collective-permute-start(bf16[2,128,1024]{2,1,0:T(8,128)(2,1)S(1)} %select_select_fusion), channel_id=1, source_target_pairs={{0,508},{4,0},{8,4},{12,8},{16,12},{20,16},{24,20},{28,24},{32,28}... | collective-permute-start | bytes 1572872 | tf_op jit(solution)/shard_map/ppermute | solution.py:16
  16.9 57.4 %collective-permute-start.5 = (bf16[2,128,1024]{2,1,0:T(8,128)(2,1)S(1)}, bf16[2,128,1024]{2,1,0:T(8,128)(2,1)}, u32[]{:S(2)}, u32[]{:S(2)}) collective-permute-start(bf16[2,128,1024]{2,1,0:T(8,128)(2,1)S(1)} %select_select_fusion), channel_id=1, source_target_pairs={{0,4},{4,8},{8,12},{12,16},{16,20},{20,24},{24,28},{28,32},{32,36}... | collective-permute-start | bytes 1572872 | tf_op jit(solution)/shard_map/ppermute | solution.py:16
  18.9 57.3 %collective-permute-start.6 = (bf16[2,128,1024]{2,1,0:T(8,128)(2,1)S(1)}, bf16[2,128,1024]{2,1,0:T(8,128)(2,1)}, u32[]{:S(2)}, u32[]{:S(2)}) collective-permute-start(bf16[2,128,1024]{2,1,0:T(8,128)(2,1)S(1)} %select_select_fusion), channel_id=1, source_target_pairs={{0,504},{4,508},{8,0},{12,4},{16,8},{20,12},{24,16},{28,20},{32,24... | collective-permute-start | bytes 1572872 | tf_op jit(solution)/shard_map/ppermute | solution.py:16
  23.2 46.4 %all-to-all-start = ((bf16[128,4,256]{2,1,0:T(4,128)(2,1)}), bf16[128,4,256]{2,1,0:T(4,128)(2,1)S(1)}, u32[]{:S(2)}, u32[]{:S(2)}) async-start(bf16[128,4,256]{2,1,0:T(4,128)(2,1)} %reshape.889), calls=%async_computation | async-start | bytes 524288 | tf_op jit(solution)/shard_map/all_to_all | solution.py:82
  54.0 28.3 %collective-permute-start.7 = (bf16[2,128,1024]{2,1,0:T(8,128)(2,1)S(1)}, bf16[2,128,1024]{2,1,0:T(8,128)(2,1)}, u32[]{:S(2)}, u32[]{:S(2)}) collective-permute-start(bf16[2,128,1024]{2,1,0:T(8,128)(2,1)S(1)} %select_select_fusion), channel_id=1, source_target_pairs={{0,8},{4,12},{8,16},{12,20},{16,24},{20,28},{24,32},{28,36},{32,40... | collective-permute-start | bytes 1572872 | tf_op jit(solution)/shard_map/ppermute | solution.py:16
  69.7 9.8 %collective-permute-start = (bf16[512,256]{1,0:T(8,128)(2,1)S(1)}, bf16[512,256]{1,0:T(8,128)(2,1)S(1)}, u32[]{:S(2)}, u32[]{:S(2)}) collective-permute-start(bf16[512,256]{1,0:T(8,128)(2,1)S(1)} %reshape.890), channel_id=1, source_target_pairs={{0,2},{1,3},{2,0},{3,1},{4,6},{5,7},{6,4},{7,5},{8,10},{9,11},{10,... | collective-permute-start | bytes 786440 | tf_op jit(solution)/shard_map/ppermute | solution.py:21
  80.3 6.6 %collective-permute-start.1 = (bf16[2,512,256]{2,1,0:T(8,128)(2,1)}, bf16[2,512,256]{2,1,0:T(8,128)(2,1)}, u32[]{:S(2)}, u32[]{:S(2)}) collective-permute-start(bf16[2,512,256]{2,1,0:T(8,128)(2,1)} %pad_maximum_fusion), channel_id=1, source_target_pairs={{0,1},{1,0},{2,3},{3,2},{4,5},{5,4},{6,7},{7,6},{8,9},{9,8},{10,11... | collective-permute-start | bytes 1572872 | tf_op jit(solution)/shard_map/ppermute | solution.py:21
  86.5 2.5 %copy-start.3 = (bf16[7,128,1024]{2,1,0:T(8,128)(2,1)S(1)}, bf16[7,128,1024]{2,1,0:T(8,128)(2,1)}, u32[]{:S(2)}) copy-start(bf16[7,128,1024]{2,1,0:T(8,128)(2,1)} %get-tuple-element.16) | copy-start | bytes 5505028
  86.5 2.5 %copy-start.9 = (pred[896]{0:T(1024)(128)(4,1)S(1)}, pred[896]{0:T(1024)(128)(4,1)}, u32[]{:S(2)}) copy-start(pred[896]{0:T(1024)(128)(4,1)} %broadcast_bitcast_fusion) | copy-start | bytes 2692
  90.4 1.5 %copy-start.1 = (bf16[1024,896]{1,0:T(8,128)(2,1)S(1)}, bf16[1024,896]{1,0:T(8,128)(2,1)}, u32[]{:S(2)}) copy-start(bf16[1024,896]{1,0:T(8,128)(2,1)} %copy.26) | copy-start | bytes 5505028
  93.4 1.3 copy-start.2
  94.7 0.6 copy-start.6
  94.7 0.6 copy-start.7
  94.7 0.7 copy-start.8
  95.7 4.1 %collective-permute-start.8 = (bf16[2,512,256]{1,2,0:T(8,128)(2,1)S(1)}, bf16[2,512,256]{1,2,0:T(8,128)(2,1)S(1)}, u32[]{:S(2)}, u32[]{:S(2)}) collective-permute-start(bf16[2,512,256]{1,2,0:T(8,128)(2,1)S(1)} %pad_maximum_fusion.1), channel_id=1, source_target_pairs={{0,1},{1,0},{2,3},{3,2},{4,5},{5,4},{6,7},{7,6},{8,9},{9,8},{10,11... | collective-permute-start | bytes 1572872 | tf_op jit(solution)/shard_map/ppermute | solution.py:21
  100.5 11.8 %collective-permute-start.9 = (bf16[512,256]{0,1:T(8,128)(2,1)S(1)}, bf16[512,256]{0,1:T(8,128)(2,1)S(1)}, u32[]{:S(2)}, u32[]{:S(2)}) collective-permute-start(bf16[512,256]{0,1:T(8,128)(2,1)S(1)} %fusion.15), channel_id=1, source_target_pairs={{0,2},{1,3},{2,0},{3,1},{4,6},{5,7},{6,4},{7,5},{8,10},{9,11},{10,... | collective-permute-start | bytes 786440 | tf_op jit(solution)/shard_map/ppermute | solution.py:21

commit v20 on v18

--- a/solution.py
+++ b/solution.py
@@ -95,7 +95,7 @@
 
     band_keys = jnp.stack([b[0] for b in blocks]).reshape(len(offsets) * rows, depth)
     band_labels = jnp.stack([b[1] for b in blocks]).reshape(len(offsets) * rows, feats * group)
-    band_prior = band_labels[:, quarter]
+    band_prior = jnp.concatenate([b[1][:, quarter] for b in blocks])
     mask_row = band_mask[cluster_index]
     live_blocks = jnp.stack([mask_row[REACH + o] > 0 for o in offsets])
     live = jnp.repeat(live_blocks, rows)

time: 148 us -> 150 us (1.014)
  local copies, waits for them, and re-layouts: 21.2 us -> 25.4 us
  waiting for transfers between devices: 18.4 us -> 14.7 us
  blocking collectives: 33.6 us -> 35.3 us
    squeeze x0 -> x6, local copies, waits for them, and re-layouts: none -> 9.81 us  [body(): band_prior = jnp.concatenate([b[1][:, quarter] for b in blocks])]
    unnamed x21 -> x24, local copies, waits for them, and re-layouts: 11.2 us -> 5.54 us
    all_to_all x1, waiting for transfers between devices: 8.69 us -> 3.89 us  [body(): lax.all_to_all(outgoing.reshape(clusters, capacity, queries.shape[1]), 'c...]
    another operation x4 -> x3, local copies, waits for them, and re-layouts: 1.79 us -> 0.02 us  [the longest x1 1.77 us: body(): jnp.stack([b[0] for b in blocks]).reshape(len(offsets) * rows, depth)]
    all_to_all x1, blocking collectives: 33.6 us -> 35.3 us  [body(): lax.all_to_all(shares.reshape(clusters, capacity, quarter), 'cluster', sp...]
    slice x0 -> x7, local copies, waits for them, and re-layouts: none -> 1.64 us  [body(): band_prior = jnp.concatenate([b[1][:, quarter] for b in blocks])]
  transfers between devices with their start and end apart: 11 -> 11, of which waited for: 3 -> 3; matrix products, arithmetic and copies ran while one was open for 13% -> 15% of each run, Pallas kernels for 0% -> 0%
where the time goes in v20:
time: 150 us; the launch traced here: 149 us
  starting transfers between devices  59.5 us (40%)
  blocking collectives  35.3 us (24%)
  local copies, waits for them, and re-layouts  25.4 us (17%)
  waiting for transfers between devices  14.7 us (10%)
  other arithmetic  5.28 us (4%)
  between operations  4.88 us (3%)
  matrix products  4.06 us (3%)
    all_to_all x1, blocking collectives, body(): lax.all_to_all(shares.reshape(clusters, capacity, quarter), 'cluster', sp...  35.3 us
    all_to_all x1, starting transfers between devices, body(): lax.all_to_all(outgoing.reshape(clusters, capacity, queries.shape[1]), 'c...  23.2 us
    ppermute x6, starting transfers between devices, shifted(): lax.ppermute(array, axis, [(i, (i - by) % peers) for i in range(peers)])  22.5 us
    ppermute x4, starting transfers between devices, swapped(): return lax.ppermute(array, axis, [(i, i ^ bit) for i in range(peers)])  13.8 us
    ppermute x4, waiting for transfers between devices, swapped(): return lax.ppermute(array, axis, [(i, i ^ bit) for i in range(peers)])  10.8 us
    squeeze x6, local copies, waits for them, and re-layouts, body(): band_prior = jnp.concatenate([b[1][:, quarter] for b in blocks])  9.81 us
    unnamed x24, local copies, waits for them, and re-layouts  5.54 us
    all_to_all x1, waiting for transfers between devices, body(): lax.all_to_all(outgoing.reshape(clusters, capacity, queries.shape[1]), 'c...  3.89 us
  transfers between devices with their start and end apart: 11, of which 3 were waited for; matrix products, arithmetic and copies ran while one was open for 15% of the time, Pallas kernels for 0%

profile of v20, /device:TPU:32, one launch (start us, length us, event | category | flops | bytes accessed | tf_op | source)
XLA Modules:
  0.0 149.1 jit_solution(12809033009453437333)
XLA Ops:
  0.0 1.1 reshape.990
  1.1 0.1 copy.26
  1.3 0.8 constant_dynamic-update-slice_fusion.1
  2.1 0.9 pad_maximum_fusion.1
  2.9 5.6 %collective-permute-start.2 = (bf16[2,128,1024]{2,1,0:T(8,128)(2,1)}, bf16[2,128,1024]{2,1,0:T(8,128)(2,1)}, u32[]{:S(2)}, u32[]{:S(2)}) collective-permute-start(bf16[2,128,1024]{2,1,0:T(8,128)(2,1)} %pad_maximum_fusion.1), channel_id=1, source_target_pairs={{0,500},{4,504},{8,508},{12,0},{16,4},{20,8},{24,12},{28,16},{32,2... | collective-permute-start | bytes 1572872 | tf_op jit(solution)/shard_map/ppermute | solution.py:16
  8.5 1.9 %collective-permute-start.3 = (bf16[2,128,1024]{2,1,0:T(8,128)(2,1)}, bf16[2,128,1024]{2,1,0:T(8,128)(2,1)}, u32[]{:S(2)}, u32[]{:S(2)}) collective-permute-start(bf16[2,128,1024]{2,1,0:T(8,128)(2,1)} %pad_maximum_fusion.1), channel_id=1, source_target_pairs={{0,12},{4,16},{8,20},{12,24},{16,28},{20,32},{24,36},{28,40},{32,4... | collective-permute-start | bytes 1572872 | tf_op jit(solution)/shard_map/ppermute | solution.py:16
  10.4 7.0 %collective-permute-start.4 = (bf16[2,128,1024]{2,1,0:T(8,128)(2,1)}, bf16[2,128,1024]{2,1,0:T(8,128)(2,1)}, u32[]{:S(2)}, u32[]{:S(2)}) collective-permute-start(bf16[2,128,1024]{2,1,0:T(8,128)(2,1)} %pad_maximum_fusion.1), channel_id=1, source_target_pairs={{0,508},{4,0},{8,4},{12,8},{16,12},{20,16},{24,20},{28,24},{32,28}... | collective-permute-start | bytes 1572872 | tf_op jit(solution)/shard_map/ppermute | solution.py:16
  17.5 1.9 %collective-permute-start.5 = (bf16[2,128,1024]{2,1,0:T(8,128)(2,1)}, bf16[2,128,1024]{2,1,0:T(8,128)(2,1)}, u32[]{:S(2)}, u32[]{:S(2)}) collective-permute-start(bf16[2,128,1024]{2,1,0:T(8,128)(2,1)} %pad_maximum_fusion.1), channel_id=1, source_target_pairs={{0,4},{4,8},{8,12},{12,16},{16,20},{20,24},{24,28},{28,32},{32,36}... | collective-permute-start | bytes 1572872 | tf_op jit(solution)/shard_map/ppermute | solution.py:16
  19.4 2.7 %collective-permute-start.6 = (bf16[2,128,1024]{2,1,0:T(8,128)(2,1)}, bf16[2,128,1024]{2,1,0:T(8,128)(2,1)S(1)}, u32[]{:S(2)}, u32[]{:S(2)}) collective-permute-start(bf16[2,128,1024]{2,1,0:T(8,128)(2,1)} %pad_maximum_fusion.1), channel_id=1, source_target_pairs={{0,504},{4,508},{8,0},{12,4},{16,8},{20,12},{24,16},{28,20},{32,24... | collective-permute-start | bytes 1572872 | tf_op jit(solution)/shard_map/ppermute | solution.py:16
  22.3 0.2 fusion.21
  22.6 0.2 fusion.23
  22.8 0.2 convolution_convert_fusion
  23.0 0.8 reshape.988
  23.8 23.2 %all-to-all-start = ((bf16[128,4,256]{2,1,0:T(4,128)(2,1)}), bf16[128,4,256]{2,1,0:T(4,128)(2,1)S(1)}, u32[]{:S(2)}, u32[]{:S(2)}) async-start(bf16[128,4,256]{2,1,0:T(4,128)(2,1)} %reshape.988), calls=%async_computation | async-start | bytes 524288 | tf_op jit(solution)/shard_map/all_to_all | solution.py:81
  47.0 0.7 constant_dynamic-update-slice_fusion
  47.7 0.6 slice.202
  48.4 0.6 fusion.52
  53.4 0.7 fusion.51
  54.2 0.2 dynamic-update-slice.7
  54.4 3.4 %collective-permute-start.7 = (bf16[2,128,1024]{2,1,0:T(8,128)(2,1)}, bf16[2,128,1024]{2,1,0:T(8,128)(2,1)}, u32[]{:S(2)}, u32[]{:S(2)}) collective-permute-start(bf16[2,128,1024]{2,1,0:T(8,128)(2,1)} %pad_maximum_fusion.1), channel_id=1, source_target_pairs={{0,8},{4,12},{8,16},{12,20},{16,24},{20,28},{24,32},{28,36},{32,40... | collective-permute-start | bytes 1572872 | tf_op jit(solution)/shard_map/ppermute | solution.py:16
  57.8 1.8 %slice_bitcast_fusion.9 = (bf16[128,1024]{1,0:T(8,128)(2,1)S(1)}, bf16[7,128,1024]{2,1,0:T(8,128)(2,1)S(1)}, bf16[7,128,1024]{2,1,0:T(8,128)(2,1)}) fusion(bf16[2,128,1024]{2,1,0:T(8,128)(2,1)} %collective-permute-done.2, bf16[7,128,1024]{2,1,0:T(8,128)(2,1)S(1)} %get-tuple-element.11, bf16[7,128,1024]{2,1,0:T(8,128)(2,1)} %constant_dynamic-update-slice_fusion), kind=kLoop, calls=%fused_computation.60 | loop fusion | bytes 1310720 | tf_op jit(solution)/shard_map/squeeze | solution.py:98
  59.6 1.8 %slice_bitcast_fusion.8 = (bf16[128,1024]{1,0:T(8,128)(2,1)S(1)}, bf16[7,128,1024]{2,1,0:T(8,128)(2,1)S(1)}, bf16[7,128,1024]{2,1,0:T(8,128)(2,1)}) fusion(bf16[2,128,1024]{2,1,0:T(8,128)(2,1)} %collective-permute-done.3, bf16[7,128,1024]{2,1,0:T(8,128)(2,1)S(1)} %get-tuple-element.34, bf16[7,128,1024]{2,1,0:T(8,128)(2,1)} %get-tuple-element.35), kind=kLoop, calls=%fused_computation.58 | loop fusion | bytes 1310720 | tf_op jit(solution)/shard_map/squeeze | solution.py:98
  61.4 1.8 %slice_bitcast_fusion.7 = (bf16[128,1024]{1,0:T(8,128)(2,1)S(1)}, bf16[7,128,1024]{2,1,0:T(8,128)(2,1)S(1)}, bf16[7,128,1024]{2,1,0:T(8,128)(2,1)}) fusion(bf16[2,128,1024]{2,1,0:T(8,128)(2,1)} %collective-permute-done.4, bf16[7,128,1024]{2,1,0:T(8,128)(2,1)S(1)} %get-tuple-element.31, bf16[7,128,1024]{2,1,0:T(8,128)(2,1)} %get-tuple-element.32), kind=kLoop, calls=%fused_computation.56 | loop fusion | bytes 1310720 | tf_op jit(solution)/shard_map/squeeze | solution.py:98
  63.2 1.8 %slice_bitcast_fusion.6 = (bf16[128,1024]{1,0:T(8,128)(2,1)S(1)}, bf16[7,128,1024]{2,1,0:T(8,128)(2,1)S(1)}, bf16[7,128,1024]{2,1,0:T(8,128)(2,1)}) fusion(bf16[2,128,1024]{2,1,0:T(8,128)(2,1)} %collective-permute-done.5, bf16[7,128,1024]{2,1,0:T(8,128)(2,1)S(1)} %get-tuple-element.28, bf16[7,128,1024]{2,1,0:T(8,128)(2,1)} %get-tuple-element.29), kind=kLoop, calls=%fused_computation.54 | loop fusion | bytes 1310720 | tf_op jit(solution)/shard_map/squeeze | solution.py:98
  65.0 0.2 slice_reduce_fusion.2
  65.2 0.2 slice_reduce_fusion.3
  65.4 0.2 slice_reduce_fusion.4
  65.5 0.2 slice_reduce_fusion.5
  65.7 0.2 dynamic-update-slice.8
  66.0 0.2 dynamic-update-slice.9
  66.2 0.2 dynamic-update-slice.10
  66.3 0.2 dynamic-update-slice.11
  66.5 3.9 %all-to-all-done = bf16[128,4,256]{2,1,0:T(4,128)(2,1)S(1)} async-done(((bf16[128,4,256]{2,1,0:T(4,128)(2,1)}), bf16[128,4,256]{2,1,0:T(4,128)(2,1)S(1)}, u32[]{:S(2)}, u32[]{:S(2)}) %all-to-all-start) | async-done | bytes 262176 | tf_op jit(solution)/shard_map/all_to_all | solution.py:81
  70.5 4.6 %collective-permute-start = (bf16[512,256]{1,0:T(8,128)(2,1)S(1)}, bf16[512,256]{1,0:T(8,128)(2,1)S(1)}, u32[]{:S(2)}, u32[]{:S(2)}) collective-permute-start(bf16[512,256]{1,0:T(8,128)(2,1)S(1)} %reshape.989), channel_id=1, source_target_pairs={{0,2},{1,3},{2,0},{3,1},{4,6},{5,7},{6,4},{7,5},{8,10},{9,11},{10,... | collective-permute-start | bytes 786440 | tf_op jit(solution)/shard_map/ppermute | solution.py:21
  75.2 0.8 slice_bitcast_fusion.5
  75.9 0.2 slice_reduce_fusion.1
  76.1 0.2 dynamic-update-slice.12
  76.4 3.9 %collective-permute-done = bf16[512,256]{1,0:T(8,128)(2,1)S(1)} collective-permute-done((bf16[512,256]{1,0:T(8,128)(2,1)S(1)}, bf16[512,256]{1,0:T(8,128)(2,1)S(1)}, u32[]{:S(2)}, u32[]{:S(2)}) %collective-permute-start) | collective-permute-done | bytes 262176 | tf_op jit(solution)/shard_map/ppermute | solution.py:21
  80.3 0.8 pad_maximum_fusion
  81.1 1.9 %collective-permute-start.1 = (bf16[2,512,256]{2,1,0:T(8,128)(2,1)}, bf16[2,512,256]{2,1,0:T(8,128)(2,1)S(1)}, u32[]{:S(2)}, u32[]{:S(2)}) collective-permute-start(bf16[2,512,256]{2,1,0:T(8,128)(2,1)} %pad_maximum_fusion), channel_id=1, source_target_pairs={{0,1},{1,0},{2,3},{3,2},{4,5},{5,4},{6,7},{7,6},{8,9},{9,8},{10,11... | collective-permute-start | bytes 1572872 | tf_op jit(solution)/shard_map/ppermute | solution.py:21
  83.0 1.8 %slice_bitcast_fusion.4 = (bf16[128,1024]{1,0:T(8,128)(2,1)S(1)}, bf16[7,128,1024]{2,1,0:T(8,128)(2,1)S(1)}, bf16[7,128,1024]{2,1,0:T(8,128)(2,1)}) fusion(bf16[2,128,1024]{2,1,0:T(8,128)(2,1)} %collective-permute-done.7, bf16[7,128,1024]{2,1,0:T(8,128)(2,1)S(1)} %get-tuple-element.22, bf16[7,128,1024]{2,1,0:T(8,128)(2,1)} %get-tuple-element.23), kind=kLoop, calls=%fused_computation.50 | loop fusion | bytes 1310720 | tf_op jit(solution)/shard_map/squeeze | solution.py:98
  84.9 0.2 slice_reduce_fusion
  85.0 0.2 dynamic-update-slice.13
  85.3 2.4 %copy.27 = bf16[896,1024]{0,1:T(8,128)(2,1)} copy(bf16[896,1024]{1,0:T(8,128)(2,1)S(1)} %bitcast.127) | data formatting | bytes 3670016 | tf_op jit(solution)/shard_map/reshape | solution.py:97
  88.0 1.2 copy-done.4
  89.2 1.4 fusion.53
  90.6 0.5 fusion
  91.1 1.0 copy-done.1
  92.1 1.4 fusion.4
  93.6 1.3 copy-done.2
  94.9 0.1 copy.30
  95.1 0.1 copy.31
  95.2 0.3 select_convert_fusion.1
  95.6 2.4 %collective-permute-start.8 = (bf16[2,512,256]{1,2,0:T(8,128)(2,1)S(1)}, bf16[2,512,256]{1,2,0:T(8,128)(2,1)S(1)}, u32[]{:S(2)}, u32[]{:S(2)}) collective-permute-start(bf16[2,512,256]{1,2,0:T(8,128)(2,1)S(1)} %pad_maximum_fusion.2), channel_id=1, source_target_pairs={{0,1},{1,0},{2,3},{3,2},{4,5},{5,4},{6,7},{7,6},{8,9},{9,8},{10,11... | collective-permute-start | bytes 1572872 | tf_op jit(solution)/shard_map/ppermute | solution.py:21
  98.0 1.3 dynamic-slice_bitcast_fusion.3
  99.3 0.2 copy.28
  99.5 0.2 copy.29
  99.9 0.2 fusion.2
  100.1 0.3 fusion.15
  100.4 4.8 %collective-permute-start.9 = (bf16[512,256]{0,1:T(8,128)(2,1)S(1)}, bf16[512,256]{0,1:T(8,128)(2,1)S(1)}, u32[]{:S(2)}, u32[]{:S(2)}) collective-permute-start(bf16[512,256]{0,1:T(8,128)(2,1)S(1)} %fusion.15), channel_id=1, source_target_pairs={{0,2},{1,3},{2,0},{3,1},{4,6},{5,7},{6,4},{7,5},{8,10},{9,11},{10,... | collective-permute-start | bytes 786440 | tf_op jit(solution)/shard_map/ppermute | solution.py:21
  105.3 6.9 %collective-permute-done.9 = bf16[512,256]{0,1:T(8,128)(2,1)S(1)} collective-permute-done((bf16[512,256]{0,1:T(8,128)(2,1)S(1)}, bf16[512,256]{0,1:T(8,128)(2,1)S(1)}, u32[]{:S(2)}, u32[]{:S(2)}) %collective-permute-start.9) | collective-permute-done | bytes 262176 | tf_op jit(solution)/shard_map/ppermute | solution.py:21
  112.7 35.3 %all_to_all.10 = bf16[128,4,250]{2,1,0:T(4,128)(2,1)S(1)} all-to-all(bf16[128,4,250]{2,1,0:T(4,128)(2,1)S(1)} %reshape.995), channel_id=1, replica_groups=mesh['cluster'=128,'feat'=4] {'cluster'}, dimensions={0} | all-to-all | bytes 512000 | tf_op jit(solution)/shard_map/all_to_all | solution.py:135
  148.0 0.2 reshape.996
  148.1 1.0 convolution_convert_fusion.1
  (61 shorter events, 1.7 us)
Async XLA Ops:
  0.0 22.8 %copy-start = (bf16[256,256]{1,0:T(8,128)(2,1)S(1)}, bf16[256,256]{1,0:T(8,128)(2,1)}, u32[]{:S(2)}) copy-start(bf16[256,256]{1,0:T(8,128)(2,1)} %param.6) | copy-start | bytes 393220
  0.0 2.1 %copy-start.3 = (bf16[128,1024]{1,0:T(8,128)(2,1)S(1)}, bf16[128,1024]{1,0:T(8,128)(2,1)}, u32[]{:S(2)}) copy-start(bf16[128,1024]{1,0:T(8,128)(2,1)} %param.9) | copy-start | bytes 786436
  0.0 22.1 %copy-start.5 = (s32[256,1]{0,1:T(1,128)S(1)}, s32[256,1]{0,1:T(1,128)}, u32[]{:S(2)}) copy-start(s32[256,1]{0,1:T(1,128)} %param.7) | copy-start | bytes 3076
  2.1 46.2 %copy-start.6 = (s32[128,7]{0,1:T(8,128)S(1)}, s32[128,7]{0,1:T(8,128)}, u32[]{:S(2)}) copy-start(s32[128,7]{0,1:T(8,128)} %param.8) | copy-start | bytes 10756
  2.1 51.4 %copy-start.7 = (bf16[128]{0:T(256)(128)(2,1)S(1)}, bf16[128]{0:T(256)(128)(2,1)}, u32[]{:S(2)}) copy-start(bf16[128]{0:T(256)(128)(2,1)} %param.11) | copy-start | bytes 772
  2.9 51.5 %collective-permute-start.2 = (bf16[2,128,1024]{2,1,0:T(8,128)(2,1)}, bf16[2,128,1024]{2,1,0:T(8,128)(2,1)}, u32[]{:S(2)}, u32[]{:S(2)}) collective-permute-start(bf16[2,128,1024]{2,1,0:T(8,128)(2,1)} %pad_maximum_fusion.1), channel_id=1, source_target_pairs={{0,500},{4,504},{8,508},{12,0},{16,4},{20,8},{24,12},{28,16},{32,2... | collective-permute-start | bytes 1572872 | tf_op jit(solution)/shard_map/ppermute | solution.py:16
  8.5 51.1 %collective-permute-start.3 = (bf16[2,128,1024]{2,1,0:T(8,128)(2,1)}, bf16[2,128,1024]{2,1,0:T(8,128)(2,1)}, u32[]{:S(2)}, u32[]{:S(2)}) collective-permute-start(bf16[2,128,1024]{2,1,0:T(8,128)(2,1)} %pad_maximum_fusion.1), channel_id=1, source_target_pairs={{0,12},{4,16},{8,20},{12,24},{16,28},{20,32},{24,36},{28,40},{32,4... | collective-permute-start | bytes 1572872 | tf_op jit(solution)/shard_map/ppermute | solution.py:16
  10.4 50.9 %collective-permute-start.4 = (bf16[2,128,1024]{2,1,0:T(8,128)(2,1)}, bf16[2,128,1024]{2,1,0:T(8,128)(2,1)}, u32[]{:S(2)}, u32[]{:S(2)}) collective-permute-start(bf16[2,128,1024]{2,1,0:T(8,128)(2,1)} %pad_maximum_fusion.1), channel_id=1, source_target_pairs={{0,508},{4,0},{8,4},{12,8},{16,12},{20,16},{24,20},{28,24},{32,28}... | collective-permute-start | bytes 1572872 | tf_op jit(solution)/shard_map/ppermute | solution.py:16
  17.5 45.7 %collective-permute-start.5 = (bf16[2,128,1024]{2,1,0:T(8,128)(2,1)}, bf16[2,128,1024]{2,1,0:T(8,128)(2,1)}, u32[]{:S(2)}, u32[]{:S(2)}) collective-permute-start(bf16[2,128,1024]{2,1,0:T(8,128)(2,1)} %pad_maximum_fusion.1), channel_id=1, source_target_pairs={{0,4},{4,8},{8,12},{12,16},{16,20},{20,24},{24,28},{28,32},{32,36}... | collective-permute-start | bytes 1572872 | tf_op jit(solution)/shard_map/ppermute | solution.py:16
  19.4 55.7 %collective-permute-start.6 = (bf16[2,128,1024]{2,1,0:T(8,128)(2,1)}, bf16[2,128,1024]{2,1,0:T(8,128)(2,1)S(1)}, u32[]{:S(2)}, u32[]{:S(2)}) collective-permute-start(bf16[2,128,1024]{2,1,0:T(8,128)(2,1)} %pad_maximum_fusion.1), channel_id=1, source_target_pairs={{0,504},{4,508},{8,0},{12,4},{16,8},{20,12},{24,16},{28,20},{32,24... | collective-permute-start | bytes 1572872 | tf_op jit(solution)/shard_map/ppermute | solution.py:16
  23.8 46.7 %all-to-all-start = ((bf16[128,4,256]{2,1,0:T(4,128)(2,1)}), bf16[128,4,256]{2,1,0:T(4,128)(2,1)S(1)}, u32[]{:S(2)}, u32[]{:S(2)}) async-start(bf16[128,4,256]{2,1,0:T(4,128)(2,1)} %reshape.988), calls=%async_computation | async-start | bytes 524288 | tf_op jit(solution)/shard_map/all_to_all | solution.py:81
  54.4 28.6 %collective-permute-start.7 = (bf16[2,128,1024]{2,1,0:T(8,128)(2,1)}, bf16[2,128,1024]{2,1,0:T(8,128)(2,1)}, u32[]{:S(2)}, u32[]{:S(2)}) collective-permute-start(bf16[2,128,1024]{2,1,0:T(8,128)(2,1)} %pad_maximum_fusion.1), channel_id=1, source_target_pairs={{0,8},{4,12},{8,16},{12,20},{16,24},{20,28},{24,32},{28,36},{32,40... | collective-permute-start | bytes 1572872 | tf_op jit(solution)/shard_map/ppermute | solution.py:16
  70.5 9.8 %collective-permute-start = (bf16[512,256]{1,0:T(8,128)(2,1)S(1)}, bf16[512,256]{1,0:T(8,128)(2,1)S(1)}, u32[]{:S(2)}, u32[]{:S(2)}) collective-permute-start(bf16[512,256]{1,0:T(8,128)(2,1)S(1)} %reshape.989), channel_id=1, source_target_pairs={{0,2},{1,3},{2,0},{3,1},{4,6},{5,7},{6,4},{7,5},{8,10},{9,11},{10,... | collective-permute-start | bytes 786440 | tf_op jit(solution)/shard_map/ppermute | solution.py:21
  81.1 6.8 %collective-permute-start.1 = (bf16[2,512,256]{2,1,0:T(8,128)(2,1)}, bf16[2,512,256]{2,1,0:T(8,128)(2,1)S(1)}, u32[]{:S(2)}, u32[]{:S(2)}) collective-permute-start(bf16[2,512,256]{2,1,0:T(8,128)(2,1)} %pad_maximum_fusion), channel_id=1, source_target_pairs={{0,1},{1,0},{2,3},{3,2},{4,5},{5,4},{6,7},{7,6},{8,9},{9,8},{10,11... | collective-permute-start | bytes 1572872 | tf_op jit(solution)/shard_map/ppermute | solution.py:21
  87.7 1.5 %copy-start.4 = (bf16[7,128,1024]{2,1,0:T(8,128)(2,1)S(1)}, bf16[7,128,1024]{2,1,0:T(8,128)(2,1)}, u32[]{:S(2)}) copy-start(bf16[7,128,1024]{2,1,0:T(8,128)(2,1)} %get-tuple-element.20) | copy-start | bytes 5505028
  90.6 1.5 %copy-start.1 = (bf16[896,1024]{0,1:T(8,128)(2,1)S(1)}, bf16[896,1024]{0,1:T(8,128)(2,1)}, u32[]{:S(2)}) copy-start(bf16[896,1024]{0,1:T(8,128)(2,1)} %copy.27) | copy-start | bytes 5505028
  93.5 1.3 copy-start.2
  95.6 4.1 %collective-permute-start.8 = (bf16[2,512,256]{1,2,0:T(8,128)(2,1)S(1)}, bf16[2,512,256]{1,2,0:T(8,128)(2,1)S(1)}, u32[]{:S(2)}, u32[]{:S(2)}) collective-permute-start(bf16[2,512,256]{1,2,0:T(8,128)(2,1)S(1)} %pad_maximum_fusion.2), channel_id=1, source_target_pairs={{0,1},{1,0},{2,3},{3,2},{4,5},{5,4},{6,7},{7,6},{8,9},{9,8},{10,11... | collective-permute-start | bytes 1572872 | tf_op jit(solution)/shard_map/ppermute | solution.py:21
  100.4 11.8 %collective-permute-start.9 = (bf16[512,256]{0,1:T(8,128)(2,1)S(1)}, bf16[512,256]{0,1:T(8,128)(2,1)S(1)}, u32[]{:S(2)}, u32[]{:S(2)}) collective-permute-start(bf16[512,256]{0,1:T(8,128)(2,1)S(1)} %fusion.15), channel_id=1, source_target_pairs={{0,2},{1,3},{2,0},{3,1},{4,6},{5,7},{6,4},{7,5},{8,10},{9,11},{10,... | collective-permute-start | bytes 786440 | tf_op jit(solution)/shard_map/ppermute | solution.py:21

commit v21 on v18

--- a/solution.py
+++ b/solution.py
@@ -70,7 +70,7 @@
     offsets = [0]
     for reach in sorted(range(1, REACH + 1), key=lambda r: (r == 2, -r)):
         offsets += [reach, -reach]
-    blocks = [block] + [shifted(block, "cluster", o) for o in offsets[1:]]
+    early = {o: shifted(block, "cluster", o) for o in offsets[1:] if abs(o) != 2}
 
     target = assign[:, 0]
     onehot = (target[:, None] == jnp.arange(clusters, dtype=jnp.int32)[None, :]).astype(jnp.int32)
@@ -87,6 +87,9 @@
     )
     own = arrived.reshape(slots, queries.shape[1])
     far = swapped(own, "feat", 2)
+    late_block, own = lax.optimization_barrier((block, own))
+    early.update({o: shifted(late_block, "cluster", o) for o in offsets[1:] if abs(o) == 2})
+    blocks = [block] + [early[o] for o in offsets[1:]]
     near = swapped(jnp.stack([own, far]), "feat", 1)
     width = queries.shape[1]
     query_full = jnp.zeros((slots, feats * width), queries.dtype)

time: 148 us -> 160 us (1.081)
  waiting for transfers between devices: 18.4 us -> 27.9 us
  blocking collectives: 33.6 us -> 38.8 us
  starting transfers between devices: 59.3 us -> 56.2 us
    ppermute x6, waiting for transfers between devices: 0.02 us -> 7.85 us  [shifted(): lax.ppermute(array, axis, [(i, (i - by) % peers) for i in range(peers)])]
    all_to_all x1, blocking collectives: 33.6 us -> 38.8 us  [body(): lax.all_to_all(shares.reshape(clusters, capacity, quarter), 'cluster', sp...]
    ppermute x4, starting transfers between devices: 13.6 us -> 11.2 us  [swapped(): return lax.ppermute(array, axis, [(i, i ^ bit) for i in range(peers)])]
    all_to_all x1, waiting for transfers between devices: 8.69 us -> 10.7 us  [body(): lax.all_to_all(outgoing.reshape(clusters, capacity, queries.shape[1]), 'c...]
    dynamic_update_slice x4, local copies, waits for them, and re-layouts: 0.12 us -> 2.01 us  [body(): lax.dynamic_update_slice_in_dim(query_full, part, (feat_index ^ code) * w...]
    unnamed x21 -> x19, local copies, waits for them, and re-layouts: 11.2 us -> 9.8 us
  transfers between devices with their start and end apart: 11 -> 11, of which waited for: 3 -> 5; matrix products, arithmetic and copies ran while one was open for 13% -> 10% of each run, Pallas kernels for 0% -> 0%
where the time goes in v21:
time: 160 us; the launch traced here: 159 us
  starting transfers between devices  56.2 us (35%)
  blocking collectives  38.8 us (24%)
  waiting for transfers between devices  27.9 us (17%)
  local copies, waits for them, and re-layouts  20.6 us (13%)
  matrix products  5.57 us (3%)
  other arithmetic  5.31 us (3%)
  between operations  4.95 us (3%)
    all_to_all x1, blocking collectives, body(): lax.all_to_all(shares.reshape(clusters, capacity, quarter), 'cluster', sp...  38.8 us
    all_to_all x1, starting transfers between devices, body(): lax.all_to_all(outgoing.reshape(clusters, capacity, queries.shape[1]), 'c...  22.5 us
    ppermute x6, starting transfers between devices, shifted(): lax.ppermute(array, axis, [(i, (i - by) % peers) for i in range(peers)])  22.5 us
    ppermute x4, starting transfers between devices, swapped(): return lax.ppermute(array, axis, [(i, i ^ bit) for i in range(peers)])  11.2 us
    all_to_all x1, waiting for transfers between devices, body(): lax.all_to_all(outgoing.reshape(clusters, capacity, queries.shape[1]), 'c...  10.7 us
    unnamed x19, local copies, waits for them, and re-layouts  9.8 us
    ppermute x4, waiting for transfers between devices, swapped(): return lax.ppermute(array, axis, [(i, i ^ bit) for i in range(peers)])  9.37 us
    ppermute x6, waiting for transfers between devices, shifted(): lax.ppermute(array, axis, [(i, (i - by) % peers) for i in range(peers)])  7.85 us
  transfers between devices with their start and end apart: 11, of which 5 were waited for; matrix products, arithmetic and copies ran while one was open for 10% of the time, Pallas kernels for 0%

profile of v21, /device:TPU:32, one launch (start us, length us, event | category | flops | bytes accessed | tf_op | source)
XLA Modules:
  0.0 159.3 jit_solution(3581343597965288839)
XLA Ops:
  0.0 1.1 reshape.936
  1.1 0.1 copy.28
  1.3 0.8 constant_dynamic-update-slice_fusion.1
  2.1 0.8 pad_maximum_fusion
  2.9 5.6 %collective-permute-start.2 = (bf16[2,128,1024]{2,1,0:T(8,128)(2,1)}, bf16[2,128,1024]{2,1,0:T(8,128)(2,1)}, u32[]{:S(2)}, u32[]{:S(2)}) collective-permute-start(bf16[2,128,1024]{2,1,0:T(8,128)(2,1)} %pad_maximum_fusion), channel_id=1, source_target_pairs={{0,500},{4,504},{8,508},{12,0},{16,4},{20,8},{24,12},{28,16},{32,2... | collective-permute-start | bytes 1572872 | tf_op jit(solution)/shard_map/ppermute | solution.py:16
  8.5 1.9 %collective-permute-start.3 = (bf16[2,128,1024]{2,1,0:T(8,128)(2,1)}, bf16[2,128,1024]{2,1,0:T(8,128)(2,1)}, u32[]{:S(2)}, u32[]{:S(2)}) collective-permute-start(bf16[2,128,1024]{2,1,0:T(8,128)(2,1)} %pad_maximum_fusion), channel_id=1, source_target_pairs={{0,12},{4,16},{8,20},{12,24},{16,28},{20,32},{24,36},{28,40},{32,4... | collective-permute-start | bytes 1572872 | tf_op jit(solution)/shard_map/ppermute | solution.py:16
  10.4 7.0 %collective-permute-start.4 = (bf16[2,128,1024]{2,1,0:T(8,128)(2,1)}, bf16[2,128,1024]{2,1,0:T(8,128)(2,1)}, u32[]{:S(2)}, u32[]{:S(2)}) collective-permute-start(bf16[2,128,1024]{2,1,0:T(8,128)(2,1)} %pad_maximum_fusion), channel_id=1, source_target_pairs={{0,508},{4,0},{8,4},{12,8},{16,12},{20,16},{24,20},{28,24},{32,28}... | collective-permute-start | bytes 1572872 | tf_op jit(solution)/shard_map/ppermute | solution.py:16
  17.5 1.9 %collective-permute-start.5 = (bf16[2,128,1024]{2,1,0:T(8,128)(2,1)}, bf16[2,128,1024]{2,1,0:T(8,128)(2,1)S(1)}, u32[]{:S(2)}, u32[]{:S(2)}) collective-permute-start(bf16[2,128,1024]{2,1,0:T(8,128)(2,1)} %pad_maximum_fusion), channel_id=1, source_target_pairs={{0,4},{4,8},{8,12},{12,16},{16,20},{20,24},{24,28},{28,32},{32,36}... | collective-permute-start | bytes 1572872 | tf_op jit(solution)/shard_map/ppermute | solution.py:16
  19.4 0.1 copy.26
  19.5 0.2 fusion.21
  19.8 0.2 fusion.23
  20.0 0.2 convolution_convert_fusion
  20.3 0.8 reshape.938
  21.0 22.5 %all-to-all-start = ((bf16[128,4,256]{2,1,0:T(4,128)(2,1)}), bf16[128,4,256]{2,1,0:T(4,128)(2,1)S(1)}, u32[]{:S(2)}, u32[]{:S(2)}) async-start(bf16[128,4,256]{2,1,0:T(4,128)(2,1)} %reshape.938), calls=%async_computation | async-start | bytes 524288 | tf_op jit(solution)/shard_map/all_to_all | solution.py:81
  43.6 0.7 constant_dynamic-update-slice_fusion
  44.3 0.1 constant_dynamic-slice_fusion
  44.4 0.6 fusion.52
  49.4 0.1 stack.67
  49.5 0.1 broadcast_bitcast_fusion
  49.7 1.8 %slice_dynamic-update-slice_fusion.11 = (bf16[7,128,1024]{2,1,0:T(8,128)(2,1)}, bf16[7,128,1024]{2,1,0:T(8,128)(2,1)S(1)}) fusion(bf16[7,128,1024]{2,1,0:T(8,128)(2,1)} %constant_dynamic-update-slice_fusion, bf16[2,128,1024]{2,1,0:T(8,128)(2,1)} %collective-permute-done.2, bf16[7,128,1024]{2,1,0:T(8,128)(2,1)S(1)} %get-tuple-element.15), kind=kLoop, calls=%fused_computation.46 | loop fusion | bytes 1048576
  51.4 1.8 %slice_dynamic-update-slice_fusion.10 = (bf16[7,128,1024]{2,1,0:T(8,128)(2,1)}, bf16[7,128,1024]{2,1,0:T(8,128)(2,1)S(1)}) fusion(bf16[7,128,1024]{2,1,0:T(8,128)(2,1)} %get-tuple-element.32, bf16[2,128,1024]{2,1,0:T(8,128)(2,1)} %collective-permute-done.3, bf16[7,128,1024]{2,1,0:T(8,128)(2,1)S(1)} %get-tuple-element.33), kind=kLoop, calls=%fused_computation.45 | loop fusion | bytes 1048576
  53.2 1.8 %slice_dynamic-update-slice_fusion.9 = (bf16[7,128,1024]{2,1,0:T(8,128)(2,1)}, bf16[7,128,1024]{2,1,0:T(8,128)(2,1)S(1)}) fusion(bf16[7,128,1024]{2,1,0:T(8,128)(2,1)} %get-tuple-element.30, bf16[2,128,1024]{2,1,0:T(8,128)(2,1)} %collective-permute-done.4, bf16[7,128,1024]{2,1,0:T(8,128)(2,1)S(1)} %get-tuple-element.31), kind=kLoop, calls=%fused_computation.44 | loop fusion | bytes 1048576
  55.0 10.7 %all-to-all-done = bf16[128,4,256]{2,1,0:T(4,128)(2,1)S(1)} async-done(((bf16[128,4,256]{2,1,0:T(4,128)(2,1)}), bf16[128,4,256]{2,1,0:T(4,128)(2,1)S(1)}, u32[]{:S(2)}, u32[]{:S(2)}) %all-to-all-start) | async-done | bytes 262176 | tf_op jit(solution)/shard_map/all_to_all | solution.py:81
  65.6 0.1 reshape.939
  65.7 4.6 %collective-permute-start = (bf16[512,256]{1,0:T(8,128)(2,1)S(1)}, bf16[512,256]{1,0:T(8,128)(2,1)S(1)}, u32[]{:S(2)}, u32[]{:S(2)}) collective-permute-start(bf16[512,256]{1,0:T(8,128)(2,1)S(1)} %reshape.939), channel_id=1, source_target_pairs={{0,2},{1,3},{2,0},{3,1},{4,6},{5,7},{6,4},{7,5},{8,10},{9,11},{10,... | collective-permute-start | bytes 786440 | tf_op jit(solution)/shard_map/ppermute | solution.py:21
  70.3 4.1 %collective-permute-start.6 = (bf16[2,128,1024]{2,1,0:T(8,128)(2,1)}, bf16[2,128,1024]{2,1,0:T(8,128)(2,1)S(1)}, u32[]{:S(2)}, u32[]{:S(2)}) collective-permute-start(bf16[2,128,1024]{2,1,0:T(8,128)(2,1)} %pad_maximum_fusion), channel_id=1, source_target_pairs={{0,504},{4,508},{8,0},{12,4},{16,8},{20,12},{24,16},{28,20},{32,24... | collective-permute-start | bytes 1572872 | tf_op jit(solution)/shard_map/ppermute | solution.py:16
  74.5 0.7 slice_dynamic-update-slice_fusion.8
  75.2 1.9 %collective-permute-start.7 = (bf16[2,128,1024]{2,1,0:T(8,128)(2,1)}, bf16[2,128,1024]{2,1,0:T(8,128)(2,1)S(1)}, u32[]{:S(2)}, u32[]{:S(2)}) collective-permute-start(bf16[2,128,1024]{2,1,0:T(8,128)(2,1)} %pad_maximum_fusion), channel_id=1, source_target_pairs={{0,8},{4,12},{8,16},{12,20},{16,24},{20,28},{24,32},{28,36},{32,40... | collective-permute-start | bytes 1572872 | tf_op jit(solution)/shard_map/ppermute | solution.py:16
  77.1 0.1 broadcast_in_dim.140
  77.3 0.8 pad_maximum_fusion.1
  78.1 1.9 %collective-permute-start.1 = (bf16[2,512,256]{2,1,0:T(8,128)(2,1)}, bf16[2,512,256]{2,1,0:T(8,128)(2,1)}, u32[]{:S(2)}, u32[]{:S(2)}) collective-permute-start(bf16[2,512,256]{2,1,0:T(8,128)(2,1)} %pad_maximum_fusion.1), channel_id=1, source_target_pairs={{0,1},{1,0},{2,3},{3,2},{4,5},{5,4},{6,7},{7,6},{8,9},{9,8},{10,11... | collective-permute-start | bytes 1572872 | tf_op jit(solution)/shard_map/ppermute | solution.py:21
  80.1 2.7 %collective-permute-done.6 = bf16[2,128,1024]{2,1,0:T(8,128)(2,1)S(1)} collective-permute-done((bf16[2,128,1024]{2,1,0:T(8,128)(2,1)}, bf16[2,128,1024]{2,1,0:T(8,128)(2,1)S(1)}, u32[]{:S(2)}, u32[]{:S(2)}) %collective-permute-start.6) | collective-permute-done | bytes 524320 | tf_op jit(solution)/shard_map/ppermute | solution.py:16
  82.8 0.7 slice_dynamic-update-slice_fusion.7
  83.5 5.1 %collective-permute-done.7 = bf16[2,128,1024]{2,1,0:T(8,128)(2,1)S(1)} collective-permute-done((bf16[2,128,1024]{2,1,0:T(8,128)(2,1)}, bf16[2,128,1024]{2,1,0:T(8,128)(2,1)S(1)}, u32[]{:S(2)}, u32[]{:S(2)}) %collective-permute-start.7) | collective-permute-done | bytes 524320 | tf_op jit(solution)/shard_map/ppermute | solution.py:16
  88.6 0.7 slice_dynamic-update-slice_fusion.6
  89.4 2.4 %copy.29 = bf16[896,1024]{0,1:T(8,128)(2,1)} copy(bf16[896,1024]{1,0:T(8,128)(2,1)S(1)} %bitcast.113) | data formatting | bytes 3670016 | tf_op jit(solution)/shard_map/reshape | solution.py:100
  91.8 0.7 fusion.26
  92.6 1.0 fusion.18
  93.5 1.0 fusion.17
  94.5 2.9 %fusion.53 = (f32[512]{0:T(512)S(1)}, f32[512,896]{1,0:T(8,128)S(1)}) fusion(f32[896]{0:T(1024)S(1)} %fusion.26, bf16[512,1024]{1,0:T(8,128)(2,1)S(1)} %fusion.17, bf16[896,1024]{1,0:T(8,128)(2,1)} %bitcast.126, pred[896]{0:T(1024)(128)(4,1)S(1)} %broadcast_bitcast_fusion), kind=kOutput, calls=%fused_computation.138 | convolution fusion | flops 941358592 | bytes 4725120 | tf_op jit(solution)/shard_map/qd,kd->qk/dot_general | solution.py:106
  97.4 0.5 fusion
  97.9 1.0 copy-done.1
  98.9 1.4 fusion.4
  100.4 1.3 copy-done.2
  101.7 0.1 dynamic-slice_bitcast_fusion.1
  101.8 0.1 copy.33
  101.9 0.1 copy.34
  102.0 0.3 select_convert_fusion.1
  102.4 1.9 %collective-permute-start.8 = (bf16[2,512,256]{1,2,0:T(8,128)(2,1)S(1)}, bf16[2,512,256]{1,2,0:T(8,128)(2,1)S(1)}, u32[]{:S(2)}, u32[]{:S(2)}) collective-permute-start(bf16[2,512,256]{1,2,0:T(8,128)(2,1)S(1)} %pad_maximum_fusion.2), channel_id=1, source_target_pairs={{0,1},{1,0},{2,3},{3,2},{4,5},{5,4},{6,7},{7,6},{8,9},{9,8},{10,11... | collective-permute-start | bytes 1572872 | tf_op jit(solution)/shard_map/ppermute | solution.py:21
  104.3 1.3 dynamic-slice_bitcast_fusion.3
  105.6 0.2 copy.31
  105.8 0.2 copy.32
  106.0 0.2 collective-permute-done.8
  106.2 0.1 convert_element_type.261
  106.4 0.2 fusion.2
  106.6 0.3 fusion.15
  106.9 2.7 %collective-permute-start.9 = (bf16[512,256]{0,1:T(8,128)(2,1)S(1)}, bf16[512,256]{0,1:T(8,128)(2,1)S(1)}, u32[]{:S(2)}, u32[]{:S(2)}) collective-permute-start(bf16[512,256]{0,1:T(8,128)(2,1)S(1)} %fusion.15), channel_id=1, source_target_pairs={{0,2},{1,3},{2,0},{3,1},{4,6},{5,7},{6,4},{7,5},{8,10},{9,11},{10,... | collective-permute-start | bytes 786440 | tf_op jit(solution)/shard_map/ppermute | solution.py:21
  109.6 9.2 %collective-permute-done.9 = bf16[512,256]{0,1:T(8,128)(2,1)S(1)} collective-permute-done((bf16[512,256]{0,1:T(8,128)(2,1)S(1)}, bf16[512,256]{0,1:T(8,128)(2,1)S(1)}, u32[]{:S(2)}, u32[]{:S(2)}) %collective-permute-start.9) | collective-permute-done | bytes 262176 | tf_op jit(solution)/shard_map/ppermute | solution.py:21
  118.9 0.1 fusion.16
  119.0 0.1 copy.35
  119.2 0.1 reshape.942
  119.3 38.8 %all_to_all.10 = bf16[128,4,250]{2,1,0:T(4,128)(2,1)S(1)} all-to-all(bf16[128,4,250]{2,1,0:T(4,128)(2,1)S(1)} %reshape.942), channel_id=1, replica_groups=mesh['cluster'=128,'feat'=4] {'cluster'}, dimensions={0} | all-to-all | bytes 512000 | tf_op jit(solution)/shard_map/all_to_all | solution.py:138
  158.1 0.2 reshape.943
  158.3 1.0 convolution_convert_fusion.1
  (40 shorter events, 0.5 us)
Async XLA Ops:
  0.0 20.0 %copy-start = (bf16[256,256]{1,0:T(8,128)(2,1)S(1)}, bf16[256,256]{1,0:T(8,128)(2,1)}, u32[]{:S(2)}) copy-start(bf16[256,256]{1,0:T(8,128)(2,1)} %param.6) | copy-start | bytes 393220
  0.0 2.1 %copy-start.3 = (bf16[128,1024]{1,0:T(8,128)(2,1)S(1)}, bf16[128,1024]{1,0:T(8,128)(2,1)}, u32[]{:S(2)}) copy-start(bf16[128,1024]{1,0:T(8,128)(2,1)} %param.9) | copy-start | bytes 786436
  0.0 19.4 %copy-start.4 = (s32[256,1]{0,1:T(1,128)S(1)}, s32[256,1]{0,1:T(1,128)}, u32[]{:S(2)}) copy-start(s32[256,1]{0,1:T(1,128)} %param.7) | copy-start | bytes 3076
  2.1 42.2 %copy-start.5 = (s32[128,7]{0,1:T(8,128)S(1)}, s32[128,7]{0,1:T(8,128)}, u32[]{:S(2)}) copy-start(s32[128,7]{0,1:T(8,128)} %param.8) | copy-start | bytes 10756
  2.9 46.7 %collective-permute-start.2 = (bf16[2,128,1024]{2,1,0:T(8,128)(2,1)}, bf16[2,128,1024]{2,1,0:T(8,128)(2,1)}, u32[]{:S(2)}, u32[]{:S(2)}) collective-permute-start(bf16[2,128,1024]{2,1,0:T(8,128)(2,1)} %pad_maximum_fusion), channel_id=1, source_target_pairs={{0,500},{4,504},{8,508},{12,0},{16,4},{20,8},{24,12},{28,16},{32,2... | collective-permute-start | bytes 1572872 | tf_op jit(solution)/shard_map/ppermute | solution.py:16
  8.5 42.9 %collective-permute-start.3 = (bf16[2,128,1024]{2,1,0:T(8,128)(2,1)}, bf16[2,128,1024]{2,1,0:T(8,128)(2,1)}, u32[]{:S(2)}, u32[]{:S(2)}) collective-permute-start(bf16[2,128,1024]{2,1,0:T(8,128)(2,1)} %pad_maximum_fusion), channel_id=1, source_target_pairs={{0,12},{4,16},{8,20},{12,24},{16,28},{20,32},{24,36},{28,40},{32,4... | collective-permute-start | bytes 1572872 | tf_op jit(solution)/shard_map/ppermute | solution.py:16
  10.4 42.8 %collective-permute-start.4 = (bf16[2,128,1024]{2,1,0:T(8,128)(2,1)}, bf16[2,128,1024]{2,1,0:T(8,128)(2,1)}, u32[]{:S(2)}, u32[]{:S(2)}) collective-permute-start(bf16[2,128,1024]{2,1,0:T(8,128)(2,1)} %pad_maximum_fusion), channel_id=1, source_target_pairs={{0,508},{4,0},{8,4},{12,8},{16,12},{20,16},{24,20},{28,24},{32,28}... | collective-permute-start | bytes 1572872 | tf_op jit(solution)/shard_map/ppermute | solution.py:16
  17.5 57.0 %collective-permute-start.5 = (bf16[2,128,1024]{2,1,0:T(8,128)(2,1)}, bf16[2,128,1024]{2,1,0:T(8,128)(2,1)S(1)}, u32[]{:S(2)}, u32[]{:S(2)}) collective-permute-start(bf16[2,128,1024]{2,1,0:T(8,128)(2,1)} %pad_maximum_fusion), channel_id=1, source_target_pairs={{0,4},{4,8},{8,12},{12,16},{16,20},{20,24},{24,28},{28,32},{32,36}... | collective-permute-start | bytes 1572872 | tf_op jit(solution)/shard_map/ppermute | solution.py:16
  21.0 44.6 %all-to-all-start = ((bf16[128,4,256]{2,1,0:T(4,128)(2,1)}), bf16[128,4,256]{2,1,0:T(4,128)(2,1)S(1)}, u32[]{:S(2)}, u32[]{:S(2)}) async-start(bf16[128,4,256]{2,1,0:T(4,128)(2,1)} %reshape.938), calls=%async_computation | async-start | bytes 524288 | tf_op jit(solution)/shard_map/all_to_all | solution.py:81
  65.7 11.6 %collective-permute-start = (bf16[512,256]{1,0:T(8,128)(2,1)S(1)}, bf16[512,256]{1,0:T(8,128)(2,1)S(1)}, u32[]{:S(2)}, u32[]{:S(2)}) collective-permute-start(bf16[512,256]{1,0:T(8,128)(2,1)S(1)} %reshape.939), channel_id=1, source_target_pairs={{0,2},{1,3},{2,0},{3,1},{4,6},{5,7},{6,4},{7,5},{8,10},{9,11},{10,... | collective-permute-start | bytes 786440 | tf_op jit(solution)/shard_map/ppermute | solution.py:21
  70.3 12.5 %collective-permute-start.6 = (bf16[2,128,1024]{2,1,0:T(8,128)(2,1)}, bf16[2,128,1024]{2,1,0:T(8,128)(2,1)S(1)}, u32[]{:S(2)}, u32[]{:S(2)}) collective-permute-start(bf16[2,128,1024]{2,1,0:T(8,128)(2,1)} %pad_maximum_fusion), channel_id=1, source_target_pairs={{0,504},{4,508},{8,0},{12,4},{16,8},{20,12},{24,16},{28,20},{32,24... | collective-permute-start | bytes 1572872 | tf_op jit(solution)/shard_map/ppermute | solution.py:16
  75.2 13.5 %collective-permute-start.7 = (bf16[2,128,1024]{2,1,0:T(8,128)(2,1)}, bf16[2,128,1024]{2,1,0:T(8,128)(2,1)S(1)}, u32[]{:S(2)}, u32[]{:S(2)}) collective-permute-start(bf16[2,128,1024]{2,1,0:T(8,128)(2,1)} %pad_maximum_fusion), channel_id=1, source_target_pairs={{0,8},{4,12},{8,16},{12,20},{16,24},{20,28},{24,32},{28,36},{32,40... | collective-permute-start | bytes 1572872 | tf_op jit(solution)/shard_map/ppermute | solution.py:16
  78.1 14.4 %collective-permute-start.1 = (bf16[2,512,256]{2,1,0:T(8,128)(2,1)}, bf16[2,512,256]{2,1,0:T(8,128)(2,1)}, u32[]{:S(2)}, u32[]{:S(2)}) collective-permute-start(bf16[2,512,256]{2,1,0:T(8,128)(2,1)} %pad_maximum_fusion.1), channel_id=1, source_target_pairs={{0,1},{1,0},{2,3},{3,2},{4,5},{5,4},{6,7},{7,6},{8,9},{9,8},{10,11... | collective-permute-start | bytes 1572872 | tf_op jit(solution)/shard_map/ppermute | solution.py:21
  97.4 1.5 copy-start.1
  100.4 1.3 copy-start.2
  102.4 3.8 %collective-permute-start.8 = (bf16[2,512,256]{1,2,0:T(8,128)(2,1)S(1)}, bf16[2,512,256]{1,2,0:T(8,128)(2,1)S(1)}, u32[]{:S(2)}, u32[]{:S(2)}) collective-permute-start(bf16[2,512,256]{1,2,0:T(8,128)(2,1)S(1)} %pad_maximum_fusion.2), channel_id=1, source_target_pairs={{0,1},{1,0},{2,3},{3,2},{4,5},{5,4},{6,7},{7,6},{8,9},{9,8},{10,11... | collective-permute-start | bytes 1572872 | tf_op jit(solution)/shard_map/ppermute | solution.py:21
  106.9 11.9 %collective-permute-start.9 = (bf16[512,256]{0,1:T(8,128)(2,1)S(1)}, bf16[512,256]{0,1:T(8,128)(2,1)S(1)}, u32[]{:S(2)}, u32[]{:S(2)}) collective-permute-start(bf16[512,256]{0,1:T(8,128)(2,1)S(1)} %fusion.15), channel_id=1, source_target_pairs={{0,2},{1,3},{2,0},{3,1},{4,6},{5,7},{6,4},{7,5},{8,10},{9,11},{10,... | collective-permute-start | bytes 786440 | tf_op jit(solution)/shard_map/ppermute | solution.py:21
